TPU v7x, 32 devices: a whole 2x2x4 slice. The times are simulated.
32 devices in a mesh: gx: 2 (over x), gy: 2 (over y), gz: 8 (over z, core).
Axes of the slice: x: 2, y: 2, z: 4, core: 2. Of those that a mesh axis runs over, the one named last changes fastest.
Arguments:
- edge_coeffs_x: float32 [4, 4, 16, 5, 1280], P('gx', None, 'gy', None, 'gz'), may hold values from -3 to 3
- edge_coeffs_y: float32 [4, 5, 16, 4, 1280], P('gx', None, 'gy', None, 'gz'), may hold values from -3 to 3
- edge_coeffs_z: float32 [4, 5, 16, 5, 1024], P('gx', None, 'gy', None, 'gz'), may hold values from -3 to 3
- flips: int32 [3, 4, 16, 256], P(None, 'gx', 'gy', 'gz'), may hold values from 0 to 1
- flags: int32 [16, 64, 1024], P('gx', 'gy', 'gz'), may hold values 0 or 1
Outputs:
- field_out: float32 [3, 16, 64, 1024], P(None, 'gx', 'gy', 'gz')
Inputs may be any that keep to these rules, and one draw needn't show every extreme that they name: `flips`: 1 marks an element whose reference direction of that component is reversed. `flags`: 1 marks a constrained node, whose assembled value is set to zero.
All inputs are finite; a program needn't handle non-finite values. No bound on the sum of `flags` on one device may be relied on, other than what follows from the above.
Results may differ from a plain program's by a relative error of at most 0.000068.
Values sent between devices are 32-bit elements; how exact they have to be, the bound alone decides.
No kernel may reach another device: no remote copies, remote signals or barrier semaphores. Data moves between devices by JAX's collectives and lax.ppermute only.
A program may use at most 64 MiB of HBM per device.

v0:
```python
import math

import jax
import jax.numpy as jnp
import numpy as np
from jax import lax
from jax.sharding import PartitionSpec as P


def passed_along(block, axis, distance):
    devices = range(lax.axis_size(axis))
    route = [((i - distance) % len(devices), i) for i in devices]
    return lax.ppermute(block, axis, route)


def with_halo(cells, sides, width):
    for axis, dim in sides:
        count = lax.axis_size(axis)
        head = lax.slice_in_dim(cells, 0, width, axis=dim)
        tail = lax.slice_in_dim(cells, cells.shape[dim] - width, cells.shape[dim], axis=dim)
        cells = jnp.concatenate(
            [
                lax.ppermute(tail, axis, [(i, (i + 1) % count) for i in range(count)]),
                cells,
                lax.ppermute(head, axis, [((i + 1) % count, i) for i in range(count)]),
            ],
            axis=dim,
        )
    return cells


def lagrange_table(points, targets):
    table = np.ones((len(targets), len(points)))
    for row_pos in range(len(targets)):
        for col_pos in range(len(points)):
            for other in range(len(points)):
                if other != col_pos:
                    table[row_pos, col_pos] *= (targets[row_pos] - points[other]) / (
                        points[col_pos] - points[other]
                    )
    return table


def basis_tables():
    spread = math.sqrt(3.0 / 7.0)
    targets = [0.0, (1.0 - spread) / 2.0, 0.5, (1.0 + spread) / 2.0, 1.0]
    closed = [0.0, 0.25, 0.5, 0.75, 1.0]
    inner = math.sqrt(3.0 / 7.0 - 2.0 / 7.0 * math.sqrt(6.0 / 5.0))
    outer = math.sqrt(3.0 / 7.0 + 2.0 / 7.0 * math.sqrt(6.0 / 5.0))
    gauss = [(1.0 - outer) / 2.0, (1.0 - inner) / 2.0, (1.0 + inner) / 2.0, (1.0 + outer) / 2.0]
    return (lagrange_table(closed, targets), lagrange_table(gauss, targets))


def depth_matrix(table, count):
    size_z = table.shape[1]
    matrix = np.zeros((size_z * count, 4 * count + 1))
    for elem_pos in range(count):
        matrix[
            size_z * elem_pos : size_z * elem_pos + size_z, 4 * elem_pos : 4 * elem_pos + 5
        ] += table.T
    return jnp.asarray(matrix, dtype=jnp.float32)


def interpolate(coef, flip, table_x, table_y, table_z):
    merged = coef.shape[4]
    size_z = table_z.shape[1]
    count = merged // size_z
    precise = lax.Precision.HIGHEST
    orient = jnp.repeat((1 - 2 * flip).astype(jnp.float32), size_z, axis=2)
    signed = coef * orient[:, None, :, None, :]
    map_x = jnp.asarray(table_x, dtype=jnp.float32)
    map_y = jnp.asarray(table_y, dtype=jnp.float32)
    partial_value = jnp.einsum("ai,xiyjw->xayjw", map_x, signed, precision=precise)
    partial_value = jnp.einsum("bj,xayjw->xaybw", map_y, partial_value, precision=precise)
    return jnp.einsum(
        "xaybw,wn->xaybn", partial_value, depth_matrix(table_z, count), precision=precise
    )


def merge_pair(array, axis_pos):
    shape_list = array.shape
    return array.reshape(
        shape_list[:axis_pos]
        + (shape_list[axis_pos] * shape_list[axis_pos + 1],)
        + shape_list[axis_pos + 2 :]
    )


def assemble_dim(nodal, axis_pos):
    leading = merge_pair(lax.slice_in_dim(nodal, 0, 4, axis=axis_pos + 1), axis_pos)
    upper = lax.slice_in_dim(nodal, 4, 5, axis=axis_pos + 1)
    zero_shape = list(upper.shape)
    zero_shape[axis_pos + 1] = 3
    trailing = merge_pair(
        jnp.concatenate([jnp.zeros(tuple(zero_shape), nodal.dtype), upper], axis=axis_pos + 1),
        axis_pos,
    )
    right_pad = [(0, 0)] * leading.ndim
    right_pad[axis_pos] = (0, 1)
    left_pad = [(0, 0)] * leading.ndim
    left_pad[axis_pos] = (1, 0)
    return jnp.pad(leading, right_pad) + jnp.pad(trailing, left_pad)


def assemble_plane(nodal):
    return assemble_dim(assemble_dim(nodal, 1), 2)


def upper_plane(extended, axis_pos):
    length = extended.shape[axis_pos]
    return lax.slice_in_dim(extended, length - 1, length, axis=axis_pos)


def add_plane(extended, axis_pos, arrived):
    length = extended.shape[axis_pos]
    first_plane = lax.slice_in_dim(extended, 0, 1, axis=axis_pos) + arrived
    return jnp.concatenate(
        [first_plane, lax.slice_in_dim(extended, 1, length - 1, axis=axis_pos)], axis=axis_pos
    )


def fold_depth(extended):
    arrived = passed_along(upper_plane(extended, 3), "gz", 1)
    return add_plane(extended, 3, arrived)


def window(padded_array, axis_pos, offset):
    starts = [0, 2, 2, 2]
    limits = [
        padded_array.shape[0],
        padded_array.shape[1] - 2,
        padded_array.shape[2] - 2,
        padded_array.shape[3] - 2,
    ]
    starts[axis_pos] = offset
    limits[axis_pos] = offset + padded_array.shape[axis_pos] - 4
    return lax.slice(padded_array, tuple(starts), tuple(limits))


def stencil_apply(padded_array):
    total = 8.0 * window(padded_array, 1, 2)
    for axis_pos in (1, 2, 3):
        near = window(padded_array, axis_pos, 1) + window(padded_array, axis_pos, 3)
        far = window(padded_array, axis_pos, 0) + window(padded_array, axis_pos, 4)
        total = total - 4.0 / 3.0 * near + 1.0 / 12.0 * far
    return 0.25 * total


def body(edge_coeffs_x, edge_coeffs_y, edge_coeffs_z, flips, flags):
    closed_map, open_map = basis_tables()
    nodal_x = interpolate(edge_coeffs_x, flips[0], open_map, closed_map, closed_map)
    nodal_y = interpolate(edge_coeffs_y, flips[1], closed_map, open_map, closed_map)
    nodal_z = interpolate(edge_coeffs_z, flips[2], closed_map, closed_map, open_map)
    stacked = jnp.stack([nodal_x, nodal_y, nodal_z])
    extended = assemble_plane(stacked)
    arrived = passed_along(upper_plane(extended, 1), "gx", 1)
    extended = add_plane(extended, 1, arrived)
    arrived = passed_along(upper_plane(extended, 2), "gy", 1)
    extended = add_plane(extended, 2, arrived)
    extended = fold_depth(extended)
    masked = extended * (1 - flags).astype(jnp.float32)[None]
    padded_array = with_halo(masked, (("gx", 1), ("gy", 2), ("gz", 3)), 2)
    return stencil_apply(padded_array)


def solution(mesh):
    in_specs = (
        P("gx", None, "gy", None, "gz"),
        P("gx", None, "gy", None, "gz"),
        P("gx", None, "gy", None, "gz"),
        P(None, "gx", "gy", "gz"),
        P("gx", "gy", "gz"),
    )
    out_specs = P(None, "gx", "gy", "gz")
    return jax.shard_map(body, mesh=mesh, in_specs=in_specs, out_specs=out_specs, check_vma=False)
```

profile of v0, /device:TPU:0, one launch (start us, length us, event | category | flops | bytes accessed | tf_op | source)
XLA Modules:
  0.0 55.0 jit_solution(17961571941493109561)
XLA Ops:
  0.0 0.7 %convert_bitcast_fusion.2 = (f32[2,8,32]{2,1,0:T(8,128)S(1)}, f32[2,8,32]{2,1,0:T(8,128)S(1)}, f32[2,8,32]{2,1,0:T(8,128)S(1)}) fusion(s32[3,2,8,32]{3,2,1,0:T(8,128)} %param.17), kind=kLoop, calls=%fused_computation.85 | loop fusion | flops 4608 | bytes 12288 | tf_op jit(solution)/shard_map/convert_element_type | solution.py:69
  0.9 1.0 %broadcast_multiply_fusion.2 = f32[2,5,8,5,128]{4,2,3,1,0:T(8,128)S(1)} fusion(f32[2,5,8,5,128]{4,2,3,1,0:T(8,128)} %param.16, f32[2,8,128]{2,1,0:T(8,128)S(1)} %copy.43), kind=kLoop, calls=%fused_computation.77 | loop fusion | flops 51200 | bytes 417792 | tf_op jit(solution)/shard_map/mul | solution.py:70
  1.9 1.2 %convolution_bitcast_fusion.8 = f32[2,5,8,5,128]{4,1,3,2,0:T(8,128)S(1)} fusion(f32[5,5,1,1,1]{1,0,4,3,2:T(8,128)} %constant.43, f32[2,5,8,5,128]{4,2,3,1,0:T(8,128)S(1)} %broadcast_multiply_fusion.2), kind=kOutput, calls=%fused_computation.11 | convolution fusion | flops 3072000 | bytes 409700 | tf_op jit(solution)/shard_map/ai,xiyjw->xayjw/dot_general | solution.py:73
  3.1 1.1 %convolution_bitcast_fusion.7 = f32[2,5,8,5,128]{4,3,2,1,0:T(8,128)S(1)} fusion(f32[5,5,1,1,1]{1,0,4,3,2:T(8,128)} %constant.43, f32[2,5,8,5,128]{4,1,3,2,0:T(8,128)S(1)} %convolution_bitcast_fusion.8), kind=kOutput, calls=%fused_computation.10 | convolution fusion | flops 3072000 | bytes 409700 | tf_op jit(solution)/shard_map/bj,xayjw->xaybw/dot_general | solution.py:74
  4.2 0.1 broadcast_in_dim.12
  4.3 0.2 mul.81
  4.5 0.1 broadcast_in_dim.13
  4.6 0.2 mul.85
  4.9 0.7 %convolution_bitcast_fusion.3 = f32[2,5,8,4,160]{4,1,3,2,0:T(8,128)S(1)} fusion(f32[5,5,1,1,1]{1,0,4,3,2:T(8,128)S(1)} %copy-done.7, f32[2,5,8,4,160]{4,3,2,1,0:T(4,128)S(1)} %broadcast_multiply_fusion), kind=kOutput, calls=%fused_computation.5 | convolution fusion | flops 3072000 | bytes 409700 | tf_op jit(solution)/shard_map/ai,xiyjw->xayjw/dot_general | solution.py:73
  5.7 0.7 %convolution_bitcast_fusion = f32[2,5,8,5,160]{4,3,2,1,0:T(8,128)S(1)} fusion(f32[5,4,1,1,1]{0,1,4,3,2:T(4,128)S(1)} %copy-done.8, f32[2,5,8,4,160]{4,1,3,2,0:T(8,128)S(1)} %convolution_bitcast_fusion.3), kind=kOutput, calls=%fused_computation.2 | convolution fusion | flops 3072000 | bytes 460880 | tf_op jit(solution)/shard_map/bj,xayjw->xaybw/dot_general | solution.py:74
  6.5 0.7 %convolution_bitcast_fusion.1 = f32[2,5,8,5,160]{4,1,3,2,0:T(8,128)S(1)} fusion(f32[5,4,1,1,1]{0,1,4,3,2:T(4,128)S(1)} %copy-done.8, f32[2,4,8,5,160]{4,2,3,1,0:T(8,128)S(1)} %broadcast_multiply_fusion.1), kind=kOutput, calls=%fused_computation.3 | convolution fusion | flops 3072000 | bytes 460880 | tf_op jit(solution)/shard_map/ai,xiyjw->xayjw/dot_general | solution.py:73
  7.3 0.8 %convolution_bitcast_fusion.2 = f32[2,5,8,5,160]{4,3,2,1,0:T(8,128)S(1)} fusion(f32[5,5,1,1,1]{1,0,4,3,2:T(8,128)S(1)} %copy-done.7, f32[2,5,8,5,160]{4,1,3,2,0:T(8,128)S(1)} %convolution_bitcast_fusion.1), kind=kOutput, calls=%fused_computation.4 | convolution fusion | flops 3840000 | bytes 512100 | tf_op jit(solution)/shard_map/bj,xayjw->xaybw/dot_general | solution.py:74
  8.1 0.6 %convolution_bitcast_fusion.5 = f32[1,2,5,8,5,129]{5,3,4,2,1,0:T(8,128)S(1)} fusion(f32[160,129,1,1,1]{0,1,4,3,2:T(8,128)S(1)} %copy-done, f32[2,5,8,5,160]{4,3,2,1,0:T(8,128)S(1)} %convolution_bitcast_fusion), kind=kOutput, calls=%fused_computation.8 | convolution fusion | flops 99072000 | bytes 544960 | tf_op jit(solution)/shard_map/xaybw,wn->xaybn/dot_general | solution.py:75
  8.6 0.6 %convolution_bitcast_fusion.6 = f32[1,2,5,8,5,129]{5,3,4,2,1,0:T(8,128)S(1)} fusion(f32[160,129,1,1,1]{0,1,4,3,2:T(8,128)S(1)} %copy-done, f32[2,5,8,5,160]{4,3,2,1,0:T(8,128)S(1)} %convolution_bitcast_fusion.2), kind=kOutput, calls=%fused_computation.9 | convolution fusion | flops 99072000 | bytes 544960 | tf_op jit(solution)/shard_map/xaybw,wn->xaybn/dot_general | solution.py:75
  9.2 0.5 convolution_bitcast_fusion.4
  9.8 0.1 pad_maximum_fusion
  10.0 0.4 copy.48
  10.4 0.4 copy.47
  10.9 0.4 pad_add_fusion.1
  11.3 0.3 fusion
  11.6 0.3 reshape.33
  12.0 0.3 concatenate.47
  12.2 0.3 reshape.34
  12.6 3.0 %collective-permute-start = (f32[3,1,33,129]{3,2,1,0:T(8,128)S(1)}, f32[3,1,33,129]{3,2,1,0:T(8,128)S(1)}, u32[]{:S(2)}, u32[]{:S(2)}) collective-permute-start(f32[3,1,33,129]{3,2,1,0:T(8,128)S(1)} %pad_add_fusion.2), channel_id=1, source_target_pairs={{16,0},{0,16},{17,1},{1,17},{18,2},{2,18},{19,3},{3,19},{20,4},{4,... | collective-permute-start | bytes 153260 | tf_op jit(solution)/shard_map/ppermute | solution.py:13
  15.6 0.1 pad_add_fusion
  15.7 3.2 %collective-permute-done = f32[3,1,33,129]{3,2,1,0:T(8,128)S(1)} collective-permute-done((f32[3,1,33,129]{3,2,1,0:T(8,128)S(1)}, f32[3,1,33,129]{3,2,1,0:T(8,128)S(1)}, u32[]{:S(2)}, u32[]{:S(2)}) %collective-permute-start) | collective-permute-done | bytes 51116 | tf_op jit(solution)/shard_map/ppermute | solution.py:13
  19.0 1.8 %collective-permute-start.1 = (f32[3,8,1,129]{3,2,1,0:T(1,128)S(1)}, f32[3,8,1,129]{3,2,1,0:T(1,128)S(1)}, u32[]{:S(2)}, u32[]{:S(2)}) collective-permute-start(f32[3,8,1,129]{3,2,1,0:T(1,128)S(1)} %pad_maximum_fusion.18), channel_id=1, source_target_pairs={{8,0},{0,8},{9,1},{1,9},{10,2},{2,10},{11,3},{3,11},{12,4},{4,12},... | collective-permute-start | bytes 37160 | tf_op jit(solution)/shard_map/ppermute | solution.py:13
  20.8 2.1 %collective-permute-done.1 = f32[3,8,1,129]{3,2,1,0:T(1,128)S(1)} collective-permute-done((f32[3,8,1,129]{3,2,1,0:T(1,128)S(1)}, f32[3,8,1,129]{3,2,1,0:T(1,128)S(1)}, u32[]{:S(2)}, u32[]{:S(2)}) %collective-permute-start.1) | collective-permute-done | bytes 12416 | tf_op jit(solution)/shard_map/ppermute | solution.py:13
  23.1 0.2 slice.153
  23.3 8.8 %collective-permute-done.2 = f32[3,8,32,1]{3,2,1,0:T(8,128)S(1)} collective-permute-done((f32[3,8,32,1]{3,2,1,0:T(8,128)S(1)}, f32[3,8,32,1]{3,2,1,0:T(8,128)S(1)}, u32[]{:S(2)}, u32[]{:S(2)}) %collective-permute-start.2) | collective-permute-done | bytes 3104 | tf_op jit(solution)/shard_map/ppermute | solution.py:13
  32.2 0.2 maximum_multiply_fusion
  32.4 1.8 %collective-permute-start.3 = (f32[3,2,32,128]{3,2,1,0:T(8,128)S(1)}, f32[3,2,32,128]{3,2,1,0:T(8,128)S(1)}, u32[]{:S(2)}, u32[]{:S(2)}) collective-permute-start(f32[3,2,32,128]{3,2,1,0:T(8,128)S(1)} %get-tuple-element.11), channel_id=1, source_target_pairs={{0,16},{16,0},{1,17},{17,1},{2,18},{18,2},{3,19},{19,3},{4,20},{20... | collective-permute-start | bytes 294920 | tf_op jit(solution)/shard_map/ppermute | solution.py:23
  34.2 0.3 collective-permute-start.4
  34.4 2.6 %collective-permute-done.3 = f32[3,2,32,128]{3,2,1,0:T(8,128)S(1)} collective-permute-done((f32[3,2,32,128]{3,2,1,0:T(8,128)S(1)}, f32[3,2,32,128]{3,2,1,0:T(8,128)S(1)}, u32[]{:S(2)}, u32[]{:S(2)}) %collective-permute-start.3) | collective-permute-done | bytes 98336 | tf_op jit(solution)/shard_map/ppermute | solution.py:23
  37.0 1.7 %collective-permute-done.4 = f32[3,2,32,128]{3,2,1,0:T(8,128)S(1)} collective-permute-done((f32[3,2,32,128]{3,2,1,0:T(8,128)S(1)}, f32[3,2,32,128]{3,2,1,0:T(8,128)S(1)}, u32[]{:S(2)}, u32[]{:S(2)}) %collective-permute-start.4) | collective-permute-done | bytes 98336 | tf_op jit(solution)/shard_map/ppermute | solution.py:25
  38.8 1.6 %collective-permute-start.5 = (f32[3,12,2,128]{3,2,1,0:T(2,128)S(1)}, f32[3,12,2,128]{3,2,1,0:T(2,128)S(1)}, u32[]{:S(2)}, u32[]{:S(2)}) collective-permute-start(f32[3,12,2,128]{3,2,1,0:T(2,128)S(1)} %get-tuple-element.9), channel_id=1, source_target_pairs={{0,8},{8,0},{1,9},{9,1},{2,10},{10,2},{3,11},{11,3},{4,12},{12,4},... | collective-permute-start | bytes 110600 | tf_op jit(solution)/shard_map/ppermute | solution.py:23
  40.4 0.5 collective-permute-start.6
  40.9 1.9 %collective-permute-done.5 = f32[3,12,2,128]{3,2,1,0:T(2,128)S(1)} collective-permute-done((f32[3,12,2,128]{3,2,1,0:T(2,128)S(1)}, f32[3,12,2,128]{3,2,1,0:T(2,128)S(1)}, u32[]{:S(2)}, u32[]{:S(2)}) %collective-permute-start.5) | collective-permute-done | bytes 36896 | tf_op jit(solution)/shard_map/ppermute | solution.py:23
  42.8 1.5 %collective-permute-done.6 = f32[3,12,2,128]{3,2,1,0:T(2,128)S(1)} collective-permute-done((f32[3,12,2,128]{3,2,1,0:T(2,128)S(1)}, f32[3,12,2,128]{3,2,1,0:T(2,128)S(1)}, u32[]{:S(2)}, u32[]{:S(2)}) %collective-permute-start.6) | collective-permute-done | bytes 36896 | tf_op jit(solution)/shard_map/ppermute | solution.py:25
  44.4 0.3 fusion.29
  44.7 0.4 copy.49
  45.1 0.4 copy.51
  45.6 0.5 collective-permute-start.7
  46.1 0.1 maximum_maximum_fusion
  46.2 4.7 %collective-permute-done.7 = f32[3,12,36,2]{2,1,3,0:T(8,128)S(1)} collective-permute-done((f32[3,12,36,2]{2,1,3,0:T(8,128)S(1)}, f32[3,12,36,2]{2,1,3,0:T(8,128)S(1)}, u32[]{:S(2)}, u32[]{:S(2)}) %collective-permute-start.7) | collective-permute-done | bytes 10400 | tf_op jit(solution)/shard_map/ppermute | solution.py:23
  51.0 0.4 copy.50
  51.4 1.2 %copy.52 = f32[3,12,36,2]{3,2,1,0:T(8,128)S(1)} copy(f32[3,12,36,2]{2,1,3,0:T(8,128)} %collective-permute-done.8) | data formatting | bytes 20736 | tf_op jit(solution)/shard_map/ppermute | solution.py:25
  52.5 2.5 %fusion.15 = f32[3,8,32,128]{3,2,1,0:T(8,128)} fusion(f32[3,8,32,128]{3,2,1,0:T(8,128)S(1)} %maximum_multiply_fusion, f32[3,2,32,128]{3,2,1,0:T(8,128)S(1)} %collective-permute-done.4, f32[3,2,32,128]{3,2,1,0:T(8,128)S(1)} %collective-permute-done.3, f32[3,12,36,2]{3,2,1,0:T(8,128)S(1)} %copy.52, f32[3,12,2,128]{3,2,1,0:T(2,128)} %copy-done.2, ...), kind=kLoop, calls=%fused_computation.40 | loop fusion | flops 4325376 | bytes 2650368 | tf_op jit(solution)/shard_map/mul | solution.py:146
  (39 shorter events, 1.0 us)
Async XLA Ops:
  0.8 4.0 %copy-start.3 = (f32[2,5,8,4,160]{4,3,2,1,0:T(4,128)S(1)}, f32[2,5,8,4,160]{4,3,2,1,0:T(4,128)}, u32[]{:S(2)}) copy-start(f32[2,5,8,4,160]{4,3,2,1,0:T(4,128)} %param.15) | copy-start | bytes 614404
  1.9 3.0 %copy-start.7 = (f32[5,5,1,1,1]{1,0,4,3,2:T(8,128)S(1)}, f32[5,5,1,1,1]{1,0,4,3,2:T(8,128)}, u32[]{:S(2)}) copy-start(f32[5,5,1,1,1]{1,0,4,3,2:T(8,128)} %constant.43) | copy-start | bytes 304
  4.2 1.5 %copy-start.8 = (f32[5,4,1,1,1]{0,1,4,3,2:T(4,128)S(1)}, f32[5,4,1,1,1]{0,1,4,3,2:T(4,128)}, u32[]{:S(2)}) copy-start(f32[5,4,1,1,1]{0,1,4,3,2:T(4,128)} %constant.42) | copy-start | bytes 244
  4.5 1.9 %copy-start.4 = (f32[2,4,8,5,160]{4,2,3,1,0:T(8,128)S(1)}, f32[2,4,8,5,160]{4,2,3,1,0:T(8,128)}, u32[]{:S(2)}) copy-start(f32[2,4,8,5,160]{4,2,3,1,0:T(8,128)} %param.14) | copy-start | bytes 614404
  6.4 1.6 %copy-start = (f32[160,129,1,1,1]{0,1,4,3,2:T(8,128)S(1)}, f32[160,129,1,1,1]{0,1,4,3,2:T(8,128)}, u32[]{:S(2)}) copy-start(f32[160,129,1,1,1]{0,1,4,3,2:T(8,128)} %constant.44) | copy-start | bytes 247684
  7.2 2.0 %copy-start.6 = (f32[128,129,1,1,1]{0,1,4,3,2:T(8,128)S(1)}, f32[128,129,1,1,1]{0,1,4,3,2:T(8,128)}, u32[]{:S(2)}) copy-start(f32[128,129,1,1,1]{0,1,4,3,2:T(8,128)} %constant.45) | copy-start | bytes 198148
  12.6 6.3 %collective-permute-start = (f32[3,1,33,129]{3,2,1,0:T(8,128)S(1)}, f32[3,1,33,129]{3,2,1,0:T(8,128)S(1)}, u32[]{:S(2)}, u32[]{:S(2)}) collective-permute-start(f32[3,1,33,129]{3,2,1,0:T(8,128)S(1)} %pad_add_fusion.2), channel_id=1, source_target_pairs={{16,0},{0,16},{17,1},{1,17},{18,2},{2,18},{19,3},{3,19},{20,4},{4,... | collective-permute-start | bytes 153260 | tf_op jit(solution)/shard_map/ppermute | solution.py:13
  19.0 4.1 %copy-start.5 = (s32[8,32,128]{2,1,0:T(8,128)S(1)}, s32[8,32,128]{2,1,0:T(8,128)}, u32[]{:S(2)}) copy-start(s32[8,32,128]{2,1,0:T(8,128)} %param.18) | copy-start | bytes 393220
  19.0 3.9 %collective-permute-start.1 = (f32[3,8,1,129]{3,2,1,0:T(1,128)S(1)}, f32[3,8,1,129]{3,2,1,0:T(1,128)S(1)}, u32[]{:S(2)}, u32[]{:S(2)}) collective-permute-start(f32[3,8,1,129]{3,2,1,0:T(1,128)S(1)} %pad_maximum_fusion.18), channel_id=1, source_target_pairs={{8,0},{0,8},{9,1},{1,9},{10,2},{2,10},{11,3},{3,11},{12,4},{4,12},... | collective-permute-start | bytes 37160 | tf_op jit(solution)/shard_map/ppermute | solution.py:13
  23.0 9.1 %collective-permute-start.2 = (f32[3,8,32,1]{3,2,1,0:T(8,128)S(1)}, f32[3,8,32,1]{3,2,1,0:T(8,128)S(1)}, u32[]{:S(2)}, u32[]{:S(2)}) collective-permute-start(f32[3,8,32,1]{3,2,1,0:T(8,128)S(1)} %slice.152), channel_id=1, source_target_pairs={{7,0},{0,1},{1,2},{2,3},{3,4},{4,5},{5,6},{6,7},{15,8},{8,9},{9,10... | collective-permute-start | bytes 9224 | tf_op jit(solution)/shard_map/ppermute | solution.py:13
  32.4 4.7 %collective-permute-start.3 = (f32[3,2,32,128]{3,2,1,0:T(8,128)S(1)}, f32[3,2,32,128]{3,2,1,0:T(8,128)S(1)}, u32[]{:S(2)}, u32[]{:S(2)}) collective-permute-start(f32[3,2,32,128]{3,2,1,0:T(8,128)S(1)} %get-tuple-element.11), channel_id=1, source_target_pairs={{0,16},{16,0},{1,17},{17,1},{2,18},{18,2},{3,19},{19,3},{4,20},{20... | collective-permute-start | bytes 294920 | tf_op jit(solution)/shard_map/ppermute | solution.py:23
  34.2 4.6 %collective-permute-start.4 = (f32[3,2,32,128]{3,2,1,0:T(8,128)S(1)}, f32[3,2,32,128]{3,2,1,0:T(8,128)S(1)}, u32[]{:S(2)}, u32[]{:S(2)}) collective-permute-start(f32[3,2,32,128]{3,2,1,0:T(8,128)S(1)} %get-tuple-element.12), channel_id=1, source_target_pairs={{16,0},{0,16},{17,1},{1,17},{18,2},{2,18},{19,3},{3,19},{20,4},{4,... | collective-permute-start | bytes 294920 | tf_op jit(solution)/shard_map/ppermute | solution.py:25
  38.8 4.0 %collective-permute-start.5 = (f32[3,12,2,128]{3,2,1,0:T(2,128)S(1)}, f32[3,12,2,128]{3,2,1,0:T(2,128)S(1)}, u32[]{:S(2)}, u32[]{:S(2)}) collective-permute-start(f32[3,12,2,128]{3,2,1,0:T(2,128)S(1)} %get-tuple-element.9), channel_id=1, source_target_pairs={{0,8},{8,0},{1,9},{9,1},{2,10},{10,2},{3,11},{11,3},{4,12},{12,4},... | collective-permute-start | bytes 110600 | tf_op jit(solution)/shard_map/ppermute | solution.py:23
  40.4 4.0 %collective-permute-start.6 = (f32[3,12,2,128]{3,2,1,0:T(2,128)S(1)}, f32[3,12,2,128]{3,2,1,0:T(2,128)S(1)}, u32[]{:S(2)}, u32[]{:S(2)}) collective-permute-start(f32[3,12,2,128]{3,2,1,0:T(2,128)S(1)} %get-tuple-element.10), channel_id=1, source_target_pairs={{8,0},{0,8},{9,1},{1,9},{10,2},{2,10},{11,3},{3,11},{12,4},{4,12},... | collective-permute-start | bytes 110600 | tf_op jit(solution)/shard_map/ppermute | solution.py:25
  42.8 3.3 %copy-start.1 = (f32[3,12,2,128]{3,2,1,0:T(2,128)}, f32[3,12,2,128]{3,2,1,0:T(2,128)S(1)}, u32[]{:S(2)}) copy-start(f32[3,12,2,128]{3,2,1,0:T(2,128)S(1)} %collective-permute-done.5) | copy-start | bytes 110596
  44.3 1.9 %copy-start.2 = (f32[3,12,2,128]{3,2,1,0:T(2,128)}, f32[3,12,2,128]{3,2,1,0:T(2,128)S(1)}, u32[]{:S(2)}) copy-start(f32[3,12,2,128]{3,2,1,0:T(2,128)S(1)} %collective-permute-done.6) | copy-start | bytes 110596
  45.5 5.8 %collective-permute-start.8 = (f32[3,12,36,2]{2,1,3,0:T(8,128)S(1)}, f32[3,12,36,2]{2,1,3,0:T(8,128)}, u32[]{:S(2)}, u32[]{:S(2)}) collective-permute-start(f32[3,12,36,2]{2,1,3,0:T(8,128)S(1)} %copy.51), channel_id=1, source_target_pairs={{1,0},{2,1},{3,2},{4,3},{5,4},{6,5},{7,6},{0,7},{9,8},{10,9},{11,1... | collective-permute-start | bytes 31112 | tf_op jit(solution)/shard_map/ppermute | solution.py:25
  45.6 5.4 %collective-permute-start.7 = (f32[3,12,36,2]{2,1,3,0:T(8,128)S(1)}, f32[3,12,36,2]{2,1,3,0:T(8,128)S(1)}, u32[]{:S(2)}, u32[]{:S(2)}) collective-permute-start(f32[3,12,36,2]{2,1,3,0:T(8,128)S(1)} %copy.49), channel_id=1, source_target_pairs={{0,1},{1,2},{2,3},{3,4},{4,5},{5,6},{6,7},{7,0},{8,9},{9,10},{10,1... | collective-permute-start | bytes 31112 | tf_op jit(solution)/shard_map/ppermute | solution.py:23
where the time goes:
time: 55.4 us; the launch traced here: 55 us
  waiting for transfers between devices  26.5 us (48%)
  starting transfers between devices  9.62 us (17%)
  matrix products  6.94 us (13%)
  other arithmetic  6.04 us (11%)
  local copies, waits for them, and re-layouts  5.47 us (10%)
    ppermute x3, waiting for transfers between devices, passed_along(): return lax.ppermute(block, axis, route)  14 us
    ppermute x3, waiting for transfers between devices, with_halo(): lax.ppermute(tail, axis, [(i, (i + 1) % count) for i in range(count)])  9.26 us
    ppermute x3, starting transfers between devices, passed_along(): return lax.ppermute(block, axis, route)  4.89 us
    ppermute x3, starting transfers between devices, with_halo(): lax.ppermute(tail, axis, [(i, (i + 1) % count) for i in range(count)])  3.88 us
    ppermute x3, waiting for transfers between devices, with_halo(): lax.ppermute(head, axis, [((i + 1) % count, i) for i in range(count)])  3.26 us
    dot_general x3, matrix products, interpolate(): jnp.einsum('ai,xiyjw->xayjw', map_x, signed, precision=precise)  2.67 us
    dot_general x3, matrix products, interpolate(): jnp.einsum('bj,xayjw->xaybw', map_y, partial_value, precision=precise)  2.66 us
    mul x1, other arithmetic, stencil_apply(): return 0.25 * total  2.52 us
  transfers between devices with their start and end apart: 9, of which 8 were waited for; matrix products, arithmetic and copies ran while one was open for 1% of the time, Pallas kernels for 0%

commit v1 on v0

v1 whole, which is shorter than its diff:
```python
import math

import jax
import jax.numpy as jnp
import numpy as np
from jax import lax
from jax.sharding import PartitionSpec as P


def lagrange_table(points, targets):
    table = np.ones((len(targets), len(points)))
    for row_pos in range(len(targets)):
        for col_pos in range(len(points)):
            for other in range(len(points)):
                if other != col_pos:
                    table[row_pos, col_pos] *= (targets[row_pos] - points[other]) / (
                        points[col_pos] - points[other]
                    )
    return table


def basis_tables():
    spread = math.sqrt(3.0 / 7.0)
    targets = [0.0, (1.0 - spread) / 2.0, 0.5, (1.0 + spread) / 2.0, 1.0]
    closed = [0.0, 0.25, 0.5, 0.75, 1.0]
    inner = math.sqrt(3.0 / 7.0 - 2.0 / 7.0 * math.sqrt(6.0 / 5.0))
    outer = math.sqrt(3.0 / 7.0 + 2.0 / 7.0 * math.sqrt(6.0 / 5.0))
    gauss = [(1.0 - outer) / 2.0, (1.0 - inner) / 2.0, (1.0 + inner) / 2.0, (1.0 + outer) / 2.0]
    closed_map = np.asarray(lagrange_table(closed, targets), dtype=np.float32).astype(np.float64)
    open_map = np.asarray(lagrange_table(gauss, targets), dtype=np.float32).astype(np.float64)
    return closed_map, open_map


def assembly_matrix(table, count):
    size = table.shape[1]
    matrix = np.zeros((4 * count + 1, count * size))
    for elem_pos in range(count):
        matrix[4 * elem_pos : 4 * elem_pos + 5, size * elem_pos : size * elem_pos + size] += table
    return matrix


def interpolate(coef, flip, table_x, table_y, table_z):
    ex_count, size_x, ey_count, size_y, merged = coef.shape
    size_z = table_z.shape[1]
    ez_count = merged // size_z
    precise = lax.Precision.HIGHEST
    orient = jnp.repeat((1 - 2 * flip).astype(jnp.float32), size_z, axis=2)
    signed = (coef * orient[:, None, :, None, :]).reshape(ex_count * size_x * ey_count * size_y, merged)
    plane_map = np.kron(assembly_matrix(table_x, ex_count), assembly_matrix(table_y, ey_count))
    depth_map = assembly_matrix(table_z, ez_count)
    deep = jnp.dot(signed, jnp.asarray(depth_map.T, jnp.float32), precision=precise)
    nodal = jnp.dot(jnp.asarray(plane_map, jnp.float32), deep, precision=precise)
    return nodal.reshape(4 * ex_count + 1, 4 * ey_count + 1, 4 * ez_count + 1)


def from_neighbours(up, down, axis, dim):
    count = lax.axis_size(axis)
    if count == 1:
        return up, down
    if count == 2:
        both = lax.ppermute(jnp.concatenate([up, down], axis=dim), axis, [(0, 1), (1, 0)])
        rows = up.shape[dim]
        return (
            lax.slice_in_dim(both, 0, rows, axis=dim),
            lax.slice_in_dim(both, rows, both.shape[dim], axis=dim),
        )
    from_prev = lax.ppermute(up, axis, [(i, (i + 1) % count) for i in range(count)])
    from_next = lax.ppermute(down, axis, [(i, (i - 1) % count) for i in range(count)])
    return from_prev, from_next


def fold_and_halo(partial, axis, dim):
    n = partial.shape[dim] - 1
    up = lax.slice_in_dim(partial, n - 2, n + 1, axis=dim)
    down = lax.slice_in_dim(partial, 0, 2, axis=dim)
    from_prev, from_next = from_neighbours(up, down, axis, dim)
    return jnp.concatenate(
        [
            lax.slice_in_dim(from_prev, 0, 2, axis=dim),
            lax.slice_in_dim(partial, 0, 1, axis=dim) + lax.slice_in_dim(from_prev, 2, 3, axis=dim),
            lax.slice_in_dim(partial, 1, n, axis=dim),
            lax.slice_in_dim(partial, n, n + 1, axis=dim) + lax.slice_in_dim(from_next, 0, 1, axis=dim),
            lax.slice_in_dim(from_next, 1, 2, axis=dim),
        ],
        axis=dim,
    )


def halo(cells, axis, dim):
    n = cells.shape[dim]
    up = lax.slice_in_dim(cells, n - 2, n, axis=dim)
    down = lax.slice_in_dim(cells, 0, 2, axis=dim)
    from_prev, from_next = from_neighbours(up, down, axis, dim)
    return jnp.concatenate([from_prev, cells, from_next], axis=dim)


def window(padded_array, axis_pos, offset):
    starts = [0, 2, 2, 2]
    limits = [
        padded_array.shape[0],
        padded_array.shape[1] - 2,
        padded_array.shape[2] - 2,
        padded_array.shape[3] - 2,
    ]
    starts[axis_pos] = offset
    limits[axis_pos] = offset + padded_array.shape[axis_pos] - 4
    return lax.slice(padded_array, tuple(starts), tuple(limits))


def stencil_apply(padded_array):
    total = 8.0 * window(padded_array, 1, 2)
    for axis_pos in (1, 2, 3):
        near = window(padded_array, axis_pos, 1) + window(padded_array, axis_pos, 3)
        far = window(padded_array, axis_pos, 0) + window(padded_array, axis_pos, 4)
        total = total - 4.0 / 3.0 * near + 1.0 / 12.0 * far
    return 0.25 * total


def body(edge_coeffs_x, edge_coeffs_y, edge_coeffs_z, flips, flags):
    closed_map, open_map = basis_tables()
    keep = (1 - flags).astype(jnp.float32)
    for axis, dim in (("gz", 2), ("gy", 1), ("gx", 0)):
        keep = halo(keep, axis, dim)
    nodal_x = interpolate(edge_coeffs_x, flips[0], open_map, closed_map, closed_map)
    nodal_y = interpolate(edge_coeffs_y, flips[1], closed_map, open_map, closed_map)
    nodal_z = interpolate(edge_coeffs_z, flips[2], closed_map, closed_map, open_map)
    extended = jnp.stack([nodal_x, nodal_y, nodal_z])
    for axis, dim in (("gz", 3), ("gy", 2), ("gx", 1)):
        extended = fold_and_halo(extended, axis, dim)
    return stencil_apply(extended * keep[None])


def solution(mesh):
    in_specs = (
        P("gx", None, "gy", None, "gz"),
        P("gx", None, "gy", None, "gz"),
        P("gx", None, "gy", None, "gz"),
        P(None, "gx", "gy", "gz"),
        P("gx", "gy", "gz"),
    )
    out_specs = P(None, "gx", "gy", "gz")
    return jax.shard_map(body, mesh=mesh, in_specs=in_specs, out_specs=out_specs, check_vma=False)
```

time: 55.4 us -> 49.5 us (0.89)
  the two profiles are of different devices: /device:TPU:0 before, /device:TPU:8 now
where the time goes in v1:
time: 49.5 us; the launch traced here: 49.2 us
  waiting for transfers between devices  20.5 us (41%)
  local copies, waits for them, and re-layouts  11.3 us (23%)
  starting transfers between devices  8.38 us (17%)
  other arithmetic  4.85 us (10%)
  matrix products  3.7 us (7%)
    ppermute x4, waiting for transfers between devices, from_neighbours(): lax.ppermute(jnp.concatenate([up, down], axis=dim), axis, [(0, 1), (1, 0)])  20.5 us
    ppermute x4, starting transfers between devices, from_neighbours(): lax.ppermute(jnp.concatenate([up, down], axis=dim), axis, [(0, 1), (1, 0)])  4.82 us
    unnamed x32, local copies, waits for them, and re-layouts  4.03 us
    ppermute x2, starting transfers between devices, from_neighbours(): lax.ppermute(down, axis, [(i, (i - 1) % count) for i in range(count)])  3.51 us
    concatenate x3, local copies, waits for them, and re-layouts, fold_and_halo(): jnp.concatenate([lax.slice_in_dim(from_prev, 0, 2, axis=dim), lax.slice_i...  3.1 us
    mul x1, other arithmetic, stencil_apply(): return 0.25 * total  2.03 us
    dot_general x3, matrix products, interpolate(): jnp.dot(jnp.asarray(plane_map, jnp.float32), deep, precision=precise)  1.98 us
    dot_general x3, matrix products, interpolate(): jnp.dot(signed, jnp.asarray(depth_map.T, jnp.float32), precision=precise)  1.71 us
  transfers between devices with their start and end apart: 8, of which 2 were waited for; matrix products, arithmetic and copies ran while one was open for 30% of the time, Pallas kernels for 0%

profile of v1, /device:TPU:8, one launch (start us, length us, event | category | flops | bytes accessed | tf_op | source)
XLA Modules:
  0.0 49.2 jit_solution(2825969194314822957)
XLA Ops:
  0.0 1.0 %subtract_convert_fusion = f32[8,32,128]{2,1,0:T(8,128)S(1)} fusion(s32[8,32,128]{2,1,0:T(8,128)} %param.15), kind=kLoop, calls=%fused_computation.39 | loop fusion | flops 65536 | bytes 262144 | tf_op jit(solution)/shard_map/convert_element_type | solution.py:121
  1.0 0.8 %fusion.18 = (f32[8,32,2]{2,1,0:T(8,128)}, f32[8,32,2]{2,1,0:T(8,128)S(1)}) fusion(f32[8,32,128]{2,1,0:T(8,128)S(1)} %subtract_convert_fusion), kind=kLoop, calls=%fused_computation.60 | loop fusion | bytes 8192 | tf_op jit(solution)/shard_map/slice | solution.py:91
  1.7 1.7 %collective-permute-start.5 = (f32[8,32,2]{2,1,0:T(8,128)S(1)}, f32[8,32,2]{2,1,0:T(8,128)S(1)}, u32[]{:S(2)}, u32[]{:S(2)}) collective-permute-start(f32[8,32,2]{2,1,0:T(8,128)S(1)} %get-tuple-element.13), channel_id=1, source_target_pairs={{0,7},{1,0},{2,1},{3,2},{4,3},{5,4},{6,5},{7,6},{8,15},{9,8},{10,9... | collective-permute-start | bytes 6152 | tf_op jit(solution)/shard_map/ppermute | solution.py:68
  3.5 0.7 %convert_bitcast_fusion = (f32[2,8,32]{2,1,0:T(8,128)S(1)}, f32[2,8,32]{2,1,0:T(8,128)S(1)}, f32[2,8,32]{2,1,0:T(8,128)S(1)}) fusion(s32[3,2,8,32]{3,2,1,0:T(8,128)} %param.14), kind=kLoop, calls=%fused_computation.56 | loop fusion | flops 4608 | bytes 12288 | tf_op jit(solution)/shard_map/convert_element_type | solution.py:47
  4.2 0.1 broadcast_in_dim.10
  4.3 0.2 mul.81
  4.6 0.1 copy.22
  4.8 0.4 copy-done.4
  5.1 0.6 %fusion.21 = f32[320,129]{0,1:T(8,128)S(1)} fusion(f32[320,160]{1,0:T(8,128)S(1)} %reshape.28, f32[160,129]{1,0:T(8,128)S(1)} %copy-done.4), kind=kOutput, calls=%fused_computation.63 | convolution fusion | flops 79257600 | bytes 452480 | tf_op jit(solution)/shard_map/dot_general | solution.py:51
  5.8 0.7 %fusion.22 = f32[297,129]{1,0:T(8,128)S(1)} fusion(f32[297,320]{1,0:T(8,128)S(1)} %copy-done.7, f32[320,129]{0,1:T(8,128)S(1)} %fusion.21), kind=kOutput, calls=%fused_computation.64 | convolution fusion | flops 147121920 | bytes 698532 | tf_op jit(solution)/shard_map/dot_general | solution.py:52
  6.6 0.1 broadcast_in_dim.11
  6.7 0.2 mul.85
  6.9 0.1 broadcast_multiply_fusion.1
  6.9 0.1 reshape.29
  7.1 0.6 %fusion.23 = f32[320,129]{0,1:T(8,128)S(1)} fusion(f32[320,160]{1,0:T(8,128)S(1)} %reshape.29, f32[160,129]{1,0:T(8,128)S(1)} %copy-done.4), kind=kOutput, calls=%fused_computation.65 | convolution fusion | flops 79257600 | bytes 452480 | tf_op jit(solution)/shard_map/dot_general | solution.py:51
  7.7 0.7 %fusion.24 = f32[297,129]{1,0:T(8,128)S(1)} fusion(f32[297,320]{1,0:T(8,128)S(1)} %copy-done.6, f32[320,129]{0,1:T(8,128)S(1)} %fusion.23), kind=kOutput, calls=%fused_computation.66 | convolution fusion | flops 147121920 | bytes 698532 | tf_op jit(solution)/shard_map/dot_general | solution.py:52
  8.5 0.1 copy.25
  8.7 0.1 copy.27
  8.8 0.5 %copy-done.11 = f32[128,129]{1,0:T(8,128)S(1)} copy-done((f32[128,129]{1,0:T(8,128)S(1)}, f32[128,129]{1,0:T(8,128)}, u32[]{:S(2)}) %copy-start.11) | copy-done | bytes 66072
  9.3 0.4 fusion.25
  9.8 0.7 %fusion.26 = f32[297,129]{1,0:T(8,128)S(1)} fusion(f32[297,400]{1,0:T(8,128)S(1)} %copy-done.5, f32[400,129]{0,1:T(8,128)S(1)} %fusion.25), kind=kOutput, calls=%fused_computation.68 | convolution fusion | flops 183902400 | bytes 834852 | tf_op jit(solution)/shard_map/dot_general | solution.py:52
  10.5 0.2 slice.224
  10.8 0.3 copy.29
  11.1 0.3 copy.32
  11.4 1.8 %collective-permute-start.1 = (f32[3,9,33,2]{2,3,1,0:T(2,128)S(1)}, f32[3,9,33,2]{2,3,1,0:T(2,128)S(1)}, u32[]{:S(2)}, u32[]{:S(2)}) collective-permute-start(f32[3,9,33,2]{2,3,1,0:T(2,128)S(1)} %copy.32), channel_id=1, source_target_pairs={{0,7},{1,0},{2,1},{3,2},{4,3},{5,4},{6,5},{7,6},{8,15},{9,8},{10,9... | collective-permute-start | bytes 21392 | tf_op jit(solution)/shard_map/ppermute | solution.py:68
  13.2 1.0 %slice.228 = f32[3,9,33,127]{3,2,1,0:T(8,128)} slice(f32[3,9,33,129]{3,2,1,0:T(8,128)S(1)} %constant_dynamic-update-slice_fusion), slice={[0:3], [0:9], [0:33], [1:128]} | slice | bytes 905256 | tf_op jit(solution)/shard_map/slice | solution.py:81
  14.2 0.1 fusion.16
  14.4 1.6 %collective-permute-start.6 = (f32[8,4,132]{2,1,0:T(4,128)S(1)}, f32[8,4,132]{2,1,0:T(4,128)S(1)}, u32[]{:S(2)}, u32[]{:S(2)}) collective-permute-start(f32[8,4,132]{2,1,0:T(4,128)S(1)} %fusion.16), channel_id=1, source_target_pairs={{0,8},{8,0},{1,9},{9,1},{2,10},{10,2},{3,11},{11,3},{4,12},{12,4},... | collective-permute-start | bytes 50696 | tf_op jit(solution)/shard_map/ppermute | solution.py:61
  16.0 0.3 copy.40
  16.3 1.1 %copy.41 = f32[3,9,33,1]{3,2,1,0:T(8,128)} copy(f32[3,9,33,1]{2,3,1,0:T(1,128)S(1)} %get-tuple-element.16) | data formatting | bytes 7128
  17.4 0.3 copy.39
  17.8 1.1 %copy.38 = f32[3,9,33,2]{3,2,1,0:T(8,128)} copy(f32[3,9,33,2]{2,3,1,0:T(2,128)S(1)} %slice.225) | data formatting | bytes 14256
  18.9 0.2 slice_add_fusion
  19.1 2.0 %concatenate.30 = f32[3,9,33,132]{3,2,1,0:T(8,128)S(1)} concatenate(f32[3,9,33,2]{3,2,1,0:T(8,128)} %copy.38, f32[3,9,33,1]{3,2,1,0:T(8,128)S(1)} %get-tuple-element.8, f32[3,9,33,127]{3,2,1,0:T(8,128)} %slice.228, f32[3,9,33,1]{3,2,1,0:T(8,128)S(1)} %get-tuple-element.7, f32[3,9,33,1]{3,2,1,0:T(8,128)} %copy.41), dimensions={3} | concatenate | bytes 940896 | tf_op jit(solution)/shard_map/concatenate | solution.py:77
  21.2 0.1 slice.238
  21.4 0.6 %collective-permute-start.2 = (f32[3,9,5,132]{3,2,1,0:T(8,128)S(1)}, f32[3,9,5,132]{3,2,1,0:T(8,128)S(1)}, u32[]{:S(2)}, u32[]{:S(2)}) collective-permute-start(f32[3,9,5,132]{3,2,1,0:T(8,128)S(1)} %pad_maximum_fusion.2), channel_id=1, source_target_pairs={{0,8},{8,0},{1,9},{9,1},{2,10},{10,2},{3,11},{11,3},{4,12},{12,4},... | collective-permute-start | bytes 213848 | tf_op jit(solution)/shard_map/ppermute | solution.py:61
  22.0 0.1 copy-done.3
  22.1 0.1 fusion.13
  22.2 1.6 %collective-permute-start.7 = (f32[4,36,132]{2,1,0:T(8,128)S(1)}, f32[4,36,132]{2,1,0:T(8,128)S(1)}, u32[]{:S(2)}, u32[]{:S(2)}) collective-permute-start(f32[4,36,132]{2,1,0:T(8,128)S(1)} %fusion.13), channel_id=1, source_target_pairs={{0,16},{16,0},{1,17},{17,1},{2,18},{18,2},{3,19},{19,3},{4,20},{20... | collective-permute-start | bytes 228104 | tf_op jit(solution)/shard_map/ppermute | solution.py:61
  23.8 5.9 %collective-permute-done.2 = f32[3,9,5,132]{3,2,1,0:T(8,128)S(1)} collective-permute-done((f32[3,9,5,132]{3,2,1,0:T(8,128)S(1)}, f32[3,9,5,132]{3,2,1,0:T(8,128)S(1)}, u32[]{:S(2)}, u32[]{:S(2)}) %collective-permute-start.2) | collective-permute-done | bytes 71312 | tf_op jit(solution)/shard_map/ppermute | solution.py:61
  29.7 0.1 slice_add_fusion.10
  29.8 1.1 %concatenate.32 = f32[3,9,36,132]{3,2,1,0:T(8,128)S(1)} concatenate(f32[3,9,2,132]{3,2,1,0:T(2,128)S(1)} %slice.235, f32[3,9,1,132]{3,2,1,0:T(1,128)S(1)} %get-tuple-element.6, f32[3,9,31,132]{3,2,1,0:T(8,128)S(1)} %slice.238, f32[3,9,1,132]{3,2,1,0:T(1,128)S(1)} %get-tuple-element.5, f32[3,9,1,132]{3,2,1,0:T(1,128)S(1)} %get-tuple-element.9), dimensions={2} | concatenate | bytes 1026432 | tf_op jit(solution)/shard_map/concatenate | solution.py:77
  31.0 1.1 %collective-permute-start.3 = (f32[3,5,36,132]{3,2,1,0:T(8,128)S(1)}, f32[3,5,36,132]{3,2,1,0:T(8,128)S(1)}, u32[]{:S(2)}, u32[]{:S(2)}) collective-permute-start(f32[3,5,36,132]{3,2,1,0:T(8,128)S(1)} %pad_maximum_fusion), channel_id=1, source_target_pairs={{0,16},{16,0},{1,17},{17,1},{2,18},{18,2},{3,19},{19,3},{4,20},{20... | collective-permute-start | bytes 855368 | tf_op jit(solution)/shard_map/ppermute | solution.py:61
  32.1 0.2 pad_maximum_fusion.1
  32.3 14.5 %collective-permute-done.3 = f32[3,5,36,132]{3,2,1,0:T(8,128)S(1)} collective-permute-done((f32[3,5,36,132]{3,2,1,0:T(8,128)S(1)}, f32[3,5,36,132]{3,2,1,0:T(8,128)S(1)}, u32[]{:S(2)}, u32[]{:S(2)}) %collective-permute-start.3) | collective-permute-done | bytes 285152 | tf_op jit(solution)/shard_map/ppermute | solution.py:61
  46.9 0.1 slice_dynamic-update-slice_fusion
  47.0 0.1 broadcast_multiply_fusion
  47.2 2.0 %fusion.2 = f32[3,8,32,128]{3,2,1,0:T(8,128)} fusion(f32[3,12,36,132]{3,2,1,0:T(8,128)S(1)} %broadcast_multiply_fusion), kind=kLoop, calls=%fused_computation.9 | loop fusion | flops 1966080 | bytes 5505024 | tf_op jit(solution)/shard_map/mul | solution.py:116
  (58 shorter events, 1.0 us)
Async XLA Ops:
  0.0 4.5 %copy-start.8 = (f32[2,4,8,5,160]{4,2,3,1,0:T(8,128)S(1)}, f32[2,4,8,5,160]{4,2,3,1,0:T(8,128)}, u32[]{:S(2)}) copy-start(f32[2,4,8,5,160]{4,2,3,1,0:T(8,128)} %param.11) | copy-start | bytes 614404
  1.7 12.5 %collective-permute-start.4 = (f32[8,32,2]{2,1,0:T(8,128)}, f32[8,32,2]{2,1,0:T(8,128)S(1)}, u32[]{:S(2)}, u32[]{:S(2)}) collective-permute-start(f32[8,32,2]{2,1,0:T(8,128)} %get-tuple-element.12), channel_id=1, source_target_pairs={{0,1},{1,2},{2,3},{3,4},{4,5},{5,6},{6,7},{7,0},{8,9},{9,10},{10,1... | collective-permute-start | bytes 6152 | tf_op jit(solution)/shard_map/ppermute | solution.py:67
  1.7 12.5 %collective-permute-start.5 = (f32[8,32,2]{2,1,0:T(8,128)S(1)}, f32[8,32,2]{2,1,0:T(8,128)S(1)}, u32[]{:S(2)}, u32[]{:S(2)}) collective-permute-start(f32[8,32,2]{2,1,0:T(8,128)S(1)} %get-tuple-element.13), channel_id=1, source_target_pairs={{0,7},{1,0},{2,1},{3,2},{4,3},{5,4},{6,5},{7,6},{8,15},{9,8},{10,9... | collective-permute-start | bytes 6152 | tf_op jit(solution)/shard_map/ppermute | solution.py:68
  4.2 0.9 %copy-start.4 = (f32[160,129]{1,0:T(8,128)S(1)}, f32[160,129]{1,0:T(8,128)}, u32[]{:S(2)}) copy-start(f32[160,129]{1,0:T(8,128)} %constant.10.clone) | copy-start | bytes 247684
  4.5 1.3 %copy-start.7 = (f32[297,320]{1,0:T(8,128)S(1)}, f32[297,320]{1,0:T(8,128)}, u32[]{:S(2)}) copy-start(f32[297,320]{1,0:T(8,128)} %constant.24.clone) | copy-start | bytes 1140484
  5.8 1.1 %copy-start.9 = (f32[2,5,8,4,160]{4,3,2,1,0:T(4,128)S(1)}, f32[2,5,8,4,160]{4,3,2,1,0:T(4,128)}, u32[]{:S(2)}) copy-start(f32[2,5,8,4,160]{4,3,2,1,0:T(4,128)} %param.12) | copy-start | bytes 614404
  6.5 1.2 %copy-start.6 = (f32[297,320]{1,0:T(8,128)S(1)}, f32[297,320]{1,0:T(8,128)}, u32[]{:S(2)}) copy-start(f32[297,320]{1,0:T(8,128)} %constant.25.clone) | copy-start | bytes 1140484
  7.1 1.6 %copy-start.10 = (f32[2,5,8,5,128]{4,2,3,1,0:T(8,128)S(1)}, f32[2,5,8,5,128]{4,2,3,1,0:T(8,128)}, u32[]{:S(2)}) copy-start(f32[2,5,8,5,128]{4,2,3,1,0:T(8,128)} %param.13) | copy-start | bytes 614404
  8.4 0.9 %copy-start.11 = (f32[128,129]{1,0:T(8,128)S(1)}, f32[128,129]{1,0:T(8,128)}, u32[]{:S(2)}) copy-start(f32[128,129]{1,0:T(8,128)} %constant.26.clone) | copy-start | bytes 198148
  8.4 1.3 %copy-start.5 = (f32[297,400]{1,0:T(8,128)S(1)}, f32[297,400]{1,0:T(8,128)}, u32[]{:S(2)}) copy-start(f32[297,400]{1,0:T(8,128)} %constant.27.clone) | copy-start | bytes 1425604
  11.0 6.4 %collective-permute-start = (f32[3,9,33,3]{2,3,1,0:T(4,128)S(1)}, f32[3,9,33,3]{2,3,1,0:T(4,128)S(1)}, u32[]{:S(2)}, u32[]{:S(2)}) collective-permute-start(f32[3,9,33,3]{2,3,1,0:T(4,128)S(1)} %copy.29), channel_id=1, source_target_pairs={{0,1},{1,2},{2,3},{3,4},{4,5},{5,6},{6,7},{7,0},{8,9},{9,10},{10,1... | collective-permute-start | bytes 32084 | tf_op jit(solution)/shard_map/ppermute | solution.py:67
  11.4 4.5 %collective-permute-start.1 = (f32[3,9,33,2]{2,3,1,0:T(2,128)S(1)}, f32[3,9,33,2]{2,3,1,0:T(2,128)S(1)}, u32[]{:S(2)}, u32[]{:S(2)}) collective-permute-start(f32[3,9,33,2]{2,3,1,0:T(2,128)S(1)} %copy.32), channel_id=1, source_target_pairs={{0,7},{1,0},{2,1},{3,2},{4,3},{5,4},{6,5},{7,6},{8,15},{9,8},{10,9... | collective-permute-start | bytes 21392 | tf_op jit(solution)/shard_map/ppermute | solution.py:68
  14.2 3.2 %copy-start = (f32[8,32,2]{2,1,0:T(8,128)}, f32[8,32,2]{2,1,0:T(8,128)S(1)}, u32[]{:S(2)}) copy-start(f32[8,32,2]{2,1,0:T(8,128)S(1)} %collective-permute-done.4) | copy-start | bytes 6148
  14.2 3.5 %copy-start.2 = (f32[8,32,2]{2,1,0:T(8,128)}, f32[8,32,2]{2,1,0:T(8,128)S(1)}, u32[]{:S(2)}) copy-start(f32[8,32,2]{2,1,0:T(8,128)S(1)} %collective-permute-done.5) | copy-start | bytes 6148
  14.4 7.6 %collective-permute-start.6 = (f32[8,4,132]{2,1,0:T(4,128)S(1)}, f32[8,4,132]{2,1,0:T(4,128)S(1)}, u32[]{:S(2)}, u32[]{:S(2)}) collective-permute-start(f32[8,4,132]{2,1,0:T(4,128)S(1)} %fusion.16), channel_id=1, source_target_pairs={{0,8},{8,0},{1,9},{9,1},{2,10},{10,2},{3,11},{11,3},{4,12},{12,4},... | collective-permute-start | bytes 50696 | tf_op jit(solution)/shard_map/ppermute | solution.py:61
  21.1 0.9 %copy-start.1 = (f32[8,32,2]{2,1,0:T(8,128)S(1)}, f32[8,32,2]{2,1,0:T(8,128)}, u32[]{:S(2)}) copy-start(f32[8,32,2]{2,1,0:T(8,128)} %copy-done) | copy-start | bytes 6148
  21.1 1.0 %copy-start.3 = (f32[8,32,2]{2,1,0:T(8,128)S(1)}, f32[8,32,2]{2,1,0:T(8,128)}, u32[]{:S(2)}) copy-start(f32[8,32,2]{2,1,0:T(8,128)} %copy-done.2) | copy-start | bytes 6148
  21.4 8.3 %collective-permute-start.2 = (f32[3,9,5,132]{3,2,1,0:T(8,128)S(1)}, f32[3,9,5,132]{3,2,1,0:T(8,128)S(1)}, u32[]{:S(2)}, u32[]{:S(2)}) collective-permute-start(f32[3,9,5,132]{3,2,1,0:T(8,128)S(1)} %pad_maximum_fusion.2), channel_id=1, source_target_pairs={{0,8},{8,0},{1,9},{9,1},{2,10},{10,2},{3,11},{11,3},{4,12},{12,4},... | collective-permute-start | bytes 213848 | tf_op jit(solution)/shard_map/ppermute | solution.py:61
  22.2 9.9 %collective-permute-start.7 = (f32[4,36,132]{2,1,0:T(8,128)S(1)}, f32[4,36,132]{2,1,0:T(8,128)S(1)}, u32[]{:S(2)}, u32[]{:S(2)}) collective-permute-start(f32[4,36,132]{2,1,0:T(8,128)S(1)} %fusion.13), channel_id=1, source_target_pairs={{0,16},{16,0},{1,17},{17,1},{2,18},{18,2},{3,19},{19,3},{4,20},{20... | collective-permute-start | bytes 228104 | tf_op jit(solution)/shard_map/ppermute | solution.py:61
  31.0 15.9 %collective-permute-start.3 = (f32[3,5,36,132]{3,2,1,0:T(8,128)S(1)}, f32[3,5,36,132]{3,2,1,0:T(8,128)S(1)}, u32[]{:S(2)}, u32[]{:S(2)}) collective-permute-start(f32[3,5,36,132]{3,2,1,0:T(8,128)S(1)} %pad_maximum_fusion), channel_id=1, source_target_pairs={{0,16},{16,0},{1,17},{17,1},{2,18},{18,2},{3,19},{19,3},{4,20},{20... | collective-permute-start | bytes 855368 | tf_op jit(solution)/shard_map/ppermute | solution.py:61

commit v2 on v1

v2 whole, which is shorter than its diff:
```python
import math

import jax
import jax.numpy as jnp
import numpy as np
from jax import lax
from jax.sharding import PartitionSpec as P


def lagrange_table(points, targets):
    table = np.ones((len(targets), len(points)))
    for row_pos in range(len(targets)):
        for col_pos in range(len(points)):
            for other in range(len(points)):
                if other != col_pos:
                    table[row_pos, col_pos] *= (targets[row_pos] - points[other]) / (
                        points[col_pos] - points[other]
                    )
    return table


def basis_tables():
    spread = math.sqrt(3.0 / 7.0)
    targets = [0.0, (1.0 - spread) / 2.0, 0.5, (1.0 + spread) / 2.0, 1.0]
    closed = [0.0, 0.25, 0.5, 0.75, 1.0]
    inner = math.sqrt(3.0 / 7.0 - 2.0 / 7.0 * math.sqrt(6.0 / 5.0))
    outer = math.sqrt(3.0 / 7.0 + 2.0 / 7.0 * math.sqrt(6.0 / 5.0))
    gauss = [(1.0 - outer) / 2.0, (1.0 - inner) / 2.0, (1.0 + inner) / 2.0, (1.0 + outer) / 2.0]
    closed_map = np.asarray(lagrange_table(closed, targets), dtype=np.float32).astype(np.float64)
    open_map = np.asarray(lagrange_table(gauss, targets), dtype=np.float32).astype(np.float64)
    return closed_map, open_map


def assembly_matrix(table, count):
    size = table.shape[1]
    matrix = np.zeros((4 * count + 1, count * size))
    for elem_pos in range(count):
        matrix[4 * elem_pos : 4 * elem_pos + 5, size * elem_pos : size * elem_pos + size] += table
    return matrix


def interpolate(coef, flip, table_x, table_y, table_z):
    ex_count, size_x, ey_count, size_y, merged = coef.shape
    size_z = table_z.shape[1]
    ez_count = merged // size_z
    nx, ny, nz = 4 * ex_count, 4 * ey_count, 4 * ez_count
    precise = lax.Precision.HIGHEST
    orient = jnp.repeat((1 - 2 * flip).astype(jnp.float32), size_z, axis=2)
    signed = (coef * orient[:, None, :, None, :]).reshape(ex_count * size_x * ey_count * size_y, merged)
    plane_map = np.kron(assembly_matrix(table_x, ex_count), assembly_matrix(table_y, ey_count))
    plane_map = plane_map.reshape(nx + 1, ny + 1, -1)
    plane_map = np.concatenate(
        [
            plane_map[:nx, :ny].reshape(nx * ny, -1),
            plane_map[nx, :ny],
            plane_map[:nx, ny],
            plane_map[nx, ny][None],
        ]
    )
    depth_map = assembly_matrix(table_z, ez_count)
    planar = jnp.dot(jnp.asarray(plane_map, jnp.float32), signed, precision=precise)
    body_part = jnp.dot(planar, jnp.asarray(depth_map[:nz].T, jnp.float32), precision=precise)
    top_part = jnp.dot(planar, jnp.asarray(depth_map[nz], jnp.float32), precision=precise)
    return body_part, top_part


def shifted(block, axes, step=1):
    sizes = [lax.axis_size(axis) for axis in axes]
    pairs = []
    for source in np.ndindex(*sizes):
        target = tuple((c + step) % s for c, s in zip(source, sizes))
        pairs.append((int(np.ravel_multi_index(source, sizes)), int(np.ravel_multi_index(target, sizes))))
    if all(a == b for a, b in pairs):
        return block
    return lax.ppermute(block, tuple(axes) if len(axes) > 1 else axes[0], pairs)


def both_ways(up, down, axis):
    count = lax.axis_size(axis)
    if count <= 2:
        both = shifted(jnp.stack([up, down]), [axis])
        return both[0], both[1]
    return shifted(up, [axis]), shifted(down, [axis], -1)


def body(edge_coeffs_x, edge_coeffs_y, edge_coeffs_z, flips, flags):
    closed_map, open_map = basis_tables()
    nx, ny, nz = flags.shape
    parts = [
        interpolate(edge_coeffs_x, flips[0], open_map, closed_map, closed_map),
        interpolate(edge_coeffs_y, flips[1], closed_map, open_map, closed_map),
        interpolate(edge_coeffs_z, flips[2], closed_map, closed_map, open_map),
    ]
    rows = jnp.stack([part[0] for part in parts])
    tops = jnp.stack([part[1] for part in parts])
    own = nx * ny
    main = rows[:, :own].reshape(3, nx, ny, nz)
    x_top = rows[:, own : own + ny]
    y_top = rows[:, own + ny : own + ny + nx]
    xy_top = rows[:, own + ny + nx]
    z_top = tops[:, :own].reshape(3, nx, ny)
    xz_top = tops[:, own : own + ny]
    yz_top = tops[:, own + ny : own + ny + nx]
    xyz_top = tops[:, own + ny + nx]

    x_in = shifted(x_top, ["gx"])
    y_in = shifted(y_top, ["gy"])
    z_in = shifted(z_top, ["gz"])
    xy_in = shifted(xy_top, ["gx", "gy"])
    xz_in = shifted(xz_top, ["gx", "gz"])
    yz_in = shifted(yz_top, ["gy", "gz"])
    xyz_in = shifted(xyz_top, ["gx", "gy", "gz"])

    main = main.at[:, 0].add(x_in)
    main = main.at[:, :, 0].add(y_in)
    main = main.at[:, :, :, 0].add(z_in)
    main = main.at[:, 0, 0].add(xy_in)
    main = main.at[:, 0, :, 0].add(xz_in)
    main = main.at[:, :, 0, 0].add(yz_in)
    main = main.at[:, 0, 0, 0].add(xyz_in)

    masked = main * (1 - flags).astype(jnp.float32)[None]

    lo_x, hi_x = both_ways(masked[:, nx - 2 :], masked[:, :2], "gx")
    up_y = jnp.swapaxes(masked[:, :, ny - 2 :], 1, 2)
    down_y = jnp.swapaxes(masked[:, :, :2], 1, 2)
    lo_y, hi_y = both_ways(up_y, down_y, "gy")
    lo_y, hi_y = jnp.swapaxes(lo_y, 1, 2), jnp.swapaxes(hi_y, 1, 2)
    up_z = jnp.moveaxis(masked[..., nz - 2 :], 3, 1).reshape(3, 2, nx * ny)
    down_z = jnp.moveaxis(masked[..., :2], 3, 1).reshape(3, 2, nx * ny)
    lo_z, hi_z = both_ways(up_z, down_z, "gz")
    lo_z = jnp.moveaxis(lo_z.reshape(3, 2, nx, ny), 1, 3)
    hi_z = jnp.moveaxis(hi_z.reshape(3, 2, nx, ny), 1, 3)

    total = 8.0 * masked
    for lo, hi, dim in ((lo_x, hi_x, 1), (lo_y, hi_y, 2), (lo_z, hi_z, 3)):
        padded = jnp.concatenate([lo, masked, hi], axis=dim)
        length = masked.shape[dim]
        near = lax.slice_in_dim(padded, 1, 1 + length, axis=dim) + lax.slice_in_dim(
            padded, 3, 3 + length, axis=dim
        )
        far = lax.slice_in_dim(padded, 0, length, axis=dim) + lax.slice_in_dim(
            padded, 4, 4 + length, axis=dim
        )
        total = total - 4.0 / 3.0 * near + 1.0 / 12.0 * far
    return 0.25 * total


def solution(mesh):
    in_specs = (
        P("gx", None, "gy", None, "gz"),
        P("gx", None, "gy", None, "gz"),
        P("gx", None, "gy", None, "gz"),
        P(None, "gx", "gy", "gz"),
        P("gx", "gy", "gz"),
    )
    out_specs = P(None, "gx", "gy", "gz")
    return jax.shard_map(body, mesh=mesh, in_specs=in_specs, out_specs=out_specs, check_vma=False)
```

time: 49.5 us -> 53.1 us (1.073)
  the two profiles are of different devices: /device:TPU:8 before, /device:TPU:0 now
where the time goes in v2:
time: 53.1 us; the launch traced here: 52.7 us
  waiting for transfers between devices  20.1 us (38%)
  starting transfers between devices  11.7 us (22%)
  local copies, waits for them, and re-layouts  11.3 us (21%)
  matrix products  5.79 us (11%)
  other arithmetic  3.48 us (7%)
    ppermute x11, waiting for transfers between devices, shifted(): return lax.ppermute(block, tuple(axes) if len(axes) > 1 else axes[0], pairs)  20.1 us
    ppermute x11, starting transfers between devices, shifted(): return lax.ppermute(block, tuple(axes) if len(axes) > 1 else axes[0], pairs)  11.7 us
    scatter-add x1, local copies, waits for them, and re-layouts, body(): main = main.at[:, :, :, 0].add(z_in)  4 us
    dot_general x3, matrix products, interpolate(): jnp.dot(jnp.asarray(plane_map, jnp.float32), signed, precision=precise)  3.28 us
    unnamed x25, local copies, waits for them, and re-layouts  3.24 us
    mul x1, other arithmetic, body(): return 0.25 * total  2.08 us
    dot_general x3, matrix products, interpolate(): jnp.dot(planar, jnp.asarray(depth_map[:nz].T, jnp.float32), precision=pre...  1.73 us
  transfers between devices with their start and end apart: 11, of which 5 were waited for; matrix products, arithmetic and copies ran while one was open for 12% of the time, Pallas kernels for 0%

profile of v2, /device:TPU:0, one launch (start us, length us, event | category | flops | bytes accessed | tf_op | source)
XLA Modules:
  0.0 52.7 jit_solution(10534424421464686554)
XLA Ops:
  0.0 0.8 %convert_bitcast_fusion.2 = (f32[2,8,32]{2,1,0:T(8,128)S(1)}, f32[2,8,32]{2,1,0:T(8,128)S(1)}, f32[2,8,32]{2,1,0:T(8,128)S(1)}) fusion(s32[3,2,8,32]{3,2,1,0:T(8,128)} %param.31), kind=kLoop, calls=%fused_computation.79 | loop fusion | flops 4608 | bytes 12288 | tf_op jit(solution)/shard_map/convert_element_type | solution.py:48
  1.1 0.1 broadcast_in_dim.11
  1.2 0.2 mul.85
  1.4 0.7 %copy-done.3 = f32[2,5,8,4,160]{4,3,2,1,0:T(4,128)S(1)} copy-done((f32[2,5,8,4,160]{4,3,2,1,0:T(4,128)S(1)}, f32[2,5,8,4,160]{4,3,2,1,0:T(4,128)}, u32[]{:S(2)}) %copy-start.3) | copy-done | bytes 204824
  2.2 0.1 reshape.302
  2.3 0.1 broadcast_in_dim.10
  2.4 0.2 mul.81
  2.6 0.7 %copy-done.4 = f32[2,4,8,5,160]{4,2,3,1,0:T(8,128)S(1)} copy-done((f32[2,4,8,5,160]{4,2,3,1,0:T(8,128)S(1)}, f32[2,4,8,5,160]{4,2,3,1,0:T(8,128)}, u32[]{:S(2)}) %copy-start.4) | copy-done | bytes 204824
  3.3 0.1 copy.36
  3.5 0.9 %copy-done.1 = f32[297,320]{1,0:T(8,128)S(1)} copy-done((f32[297,320]{1,0:T(8,128)S(1)}, f32[297,320]{1,0:T(8,128)}, u32[]{:S(2)}) %copy-start.1) | copy-done | bytes 380184
  4.4 1.3 %fusion.36 = f32[160,297]{1,0:T(8,128)S(1)} fusion(f32[320,160]{1,0:T(8,128)S(1)} %reshape.302, f32[297,320]{1,0:T(8,128)S(1)} %copy-done.1), kind=kOutput, calls=%fused_computation.89 | convolution fusion | flops 182476800 | bytes 775040 | tf_op jit(solution)/shard_map/dot_general | solution.py:61
  5.8 0.7 %convolution_bitcast_fusion.1 = f32[1,297,128]{2,1,0:T(8,128)S(1)} fusion(f32[160,297]{1,0:T(8,128)S(1)} %fusion.36, f32[160,128]{1,0:T(8,128)S(1)} %copy-done.5), kind=kOutput, calls=%fused_computation.1 | convolution fusion | flops 72990720 | bytes 424064 | tf_op jit(solution)/shard_map/dot_general | solution.py:62
  6.5 0.3 copy-done.2
  6.8 1.3 %fusion.35 = f32[160,297]{1,0:T(8,128)S(1)} fusion(f32[320,160]{1,0:T(8,128)S(1)} %reshape.301, f32[297,320]{1,0:T(8,128)S(1)} %copy-done.2), kind=kOutput, calls=%fused_computation.88 | convolution fusion | flops 182476800 | bytes 775040 | tf_op jit(solution)/shard_map/dot_general | solution.py:61
  8.1 0.7 %convolution_bitcast_fusion.2 = f32[1,297,128]{2,1,0:T(8,128)S(1)} fusion(f32[160,297]{1,0:T(8,128)S(1)} %fusion.35, f32[160,128]{1,0:T(8,128)S(1)} %copy-done.5), kind=kOutput, calls=%fused_computation.2 | convolution fusion | flops 72990720 | bytes 424064 | tf_op jit(solution)/shard_map/dot_general | solution.py:62
  8.9 0.6 %fusion.37 = f32[128,297]{0,1:T(8,128)S(1)} fusion(f32[400,128]{1,0:T(8,128)S(1)} %reshape.303, f32[297,400]{1,0:T(8,128)S(1)} %copy-done), kind=kOutput, calls=%fused_computation.90 | convolution fusion | flops 182476800 | bytes 832064 | tf_op jit(solution)/shard_map/dot_general | solution.py:61
  9.5 0.2 copy-done.8
  9.7 0.3 convolution_bitcast_fusion
  10.1 3.0 %collective-permute-start = (f32[3,32,128]{2,0,1:T(4,128)S(1)}, f32[3,32,128]{2,0,1:T(4,128)S(1)}, u32[]{:S(2)}, u32[]{:S(2)}) collective-permute-start(f32[3,32,128]{2,0,1:T(4,128)S(1)} %copy.49), channel_id=1, source_target_pairs={{0,16},{16,0},{1,17},{17,1},{2,18},{18,2},{3,19},{19,3},{4,20},{20... | collective-permute-start | bytes 147464 | tf_op jit(solution)/shard_map/ppermute | solution.py:75
  13.1 1.6 %collective-permute-start.1 = (f32[3,8,128]{2,0,1:T(4,128)S(1)}, f32[3,8,128]{2,0,1:T(4,128)S(1)}, u32[]{:S(2)}, u32[]{:S(2)}) collective-permute-start(f32[3,8,128]{2,0,1:T(4,128)S(1)} %copy.50), channel_id=1, source_target_pairs={{0,8},{8,0},{1,9},{9,1},{2,10},{10,2},{3,11},{11,3},{4,12},{12,4},... | collective-permute-start | bytes 36872 | tf_op jit(solution)/shard_map/ppermute | solution.py:75
  14.7 0.3 fusion.25
  14.9 0.3 fusion.27
  15.2 0.4 copy-done.10
  15.6 0.2 fusion.29
  16.0 1.8 %collective-permute-start.4 = (f32[3,32]{1,0:T(4,128)S(1)}, f32[3,32]{1,0:T(4,128)S(1)}, u32[]{:S(2)}, u32[]{:S(2)}) collective-permute-start(f32[3,32]{1,0:T(4,128)S(1)} %slice.354), channel_id=1, source_target_pairs={{0,17},{1,18},{2,19},{3,20},{4,21},{5,22},{6,23},{7,16},{16,1},{17... | collective-permute-start | bytes 1160 | tf_op jit(solution)/shard_map/ppermute | solution.py:75
  17.8 0.2 slice_reduce_fusion
  18.0 1.1 %collective-permute-start.6 = (f32[3]{0:T(128)S(1)}, f32[3]{0:T(128)S(1)}, u32[]{:S(2)}, u32[]{:S(2)}) collective-permute-start(f32[3]{0:T(128)S(1)} %slice_reduce_fusion), channel_id=1, source_target_pairs={{0,25},{1,26},{2,27},{3,28},{4,29},{5,30},{6,31},{7,24},{8,17},{9,... | collective-permute-start | bytes 44 | tf_op jit(solution)/shard_map/ppermute | solution.py:75
  19.3 0.3 copy.40
  19.5 5.1 %collective-permute-done.6 = f32[3]{0:T(128)S(1)} collective-permute-done((f32[3]{0:T(128)S(1)}, f32[3]{0:T(128)S(1)}, u32[]{:S(2)}, u32[]{:S(2)}) %collective-permute-start.6) | collective-permute-done | bytes 44 | tf_op jit(solution)/shard_map/ppermute | solution.py:75
  24.6 0.1 copy.46
  24.7 5.6 %collective-permute-done.5 = f32[3,8]{1,0:T(4,128)S(1)} collective-permute-done((f32[3,8]{1,0:T(4,128)S(1)}, f32[3,8]{1,0:T(4,128)S(1)}, u32[]{:S(2)}, u32[]{:S(2)}) %collective-permute-start.5) | collective-permute-done | bytes 128 | tf_op jit(solution)/shard_map/ppermute | solution.py:75
  30.3 1.5 %collective-permute-start.3 = (f32[3,128]{1,0:T(4,128)S(1)}, f32[3,128]{1,0:T(4,128)S(1)}, u32[]{:S(2)}, u32[]{:S(2)}) collective-permute-start(f32[3,128]{1,0:T(4,128)S(1)} %bitcast.103), channel_id=1, source_target_pairs={{0,24},{8,16},{16,8},{24,0},{1,25},{9,17},{17,9},{25,1},{2,26},{10... | collective-permute-start | bytes 4616 | tf_op jit(solution)/shard_map/ppermute | solution.py:75
  31.8 0.1 copy.45
  31.9 0.1 copy.44
  32.1 0.3 copy.43
  32.4 0.1 slice_add_fusion
  32.6 4.0 %scatter-add.26 = f32[3,8,32,128]{3,0,2,1:T(4,128)S(1)} dynamic-update-slice(f32[3,8,32,128]{3,0,2,1:T(4,128)S(1)} %fusion.32, f32[3,8,32,1]{3,0,2,1:T(4,128)S(1)} %slice_add_fusion, s32[]{:T(128)} %constant.210.clone.1, s32[]{:T(128)} %constant.210.clone.1, s32[]{:T(128)} %constant.210.clone.1, s32[]{:T(128)} %constant.210.clone.1) | dynamic-update-slice | bytes 6148 | tf_op jit(solution)/shard_map/scatter-add | solution.py:116
  36.6 0.2 scatter-add.30
  37.1 0.1 broadcast_multiply_fusion
  37.2 0.4 fusion.34
  37.7 0.5 collective-permute-start.9
  38.2 1.5 %collective-permute-start.8 = (f32[2,3,2,8,128]{4,1,2,3,0:T(4,128)S(1)}, f32[2,3,2,8,128]{4,1,2,3,0:T(4,128)S(1)}, u32[]{:S(2)}, u32[]{:S(2)}) collective-permute-start(f32[2,3,2,8,128]{4,1,2,3,0:T(4,128)S(1)} %pad_maximum_fusion.8), channel_id=1, source_target_pairs={{0,8},{8,0},{1,9},{9,1},{2,10},{10,2},{3,11},{11,3},{4,12},{12,4},... | collective-permute-start | bytes 147464 | tf_op jit(solution)/shard_map/ppermute | solution.py:75
  39.8 0.6 %collective-permute-start.7 = (f32[2,3,2,32,128]{4,1,3,2,0:T(4,128)S(1)}, f32[2,3,2,32,128]{4,1,3,2,0:T(4,128)S(1)}, u32[]{:S(2)}, u32[]{:S(2)}) collective-permute-start(f32[2,3,2,32,128]{4,1,3,2,0:T(4,128)S(1)} %pad_maximum_fusion.7), channel_id=1, source_target_pairs={{0,16},{16,0},{1,17},{17,1},{2,18},{18,2},{3,19},{19,3},{4,20},{20... | collective-permute-start | bytes 589832 | tf_op jit(solution)/shard_map/ppermute | solution.py:75
  40.4 2.2 %collective-permute-done.8 = f32[2,3,2,8,128]{4,1,2,3,0:T(4,128)S(1)} collective-permute-done((f32[2,3,2,8,128]{4,1,2,3,0:T(4,128)S(1)}, f32[2,3,2,8,128]{4,1,2,3,0:T(4,128)S(1)}, u32[]{:S(2)}, u32[]{:S(2)}) %collective-permute-start.8) | collective-permute-done | bytes 49184 | tf_op jit(solution)/shard_map/ppermute | solution.py:75
  42.6 5.2 %collective-permute-done.7 = f32[2,3,2,32,128]{4,1,3,2,0:T(4,128)S(1)} collective-permute-done((f32[2,3,2,32,128]{4,1,3,2,0:T(4,128)S(1)}, f32[2,3,2,32,128]{4,1,3,2,0:T(4,128)S(1)}, u32[]{:S(2)}, u32[]{:S(2)}) %collective-permute-start.7) | collective-permute-done | bytes 196640 | tf_op jit(solution)/shard_map/ppermute | solution.py:75
  47.8 2.0 %collective-permute-done.10 = f32[3,2,256]{1,0,2:T(4,128)S(1)} collective-permute-done((f32[3,2,256]{1,0,2:T(4,128)S(1)}, f32[3,2,256]{1,0,2:T(4,128)S(1)}, u32[]{:S(2)}, u32[]{:S(2)}) %collective-permute-start.10) | collective-permute-done | bytes 6176 | tf_op jit(solution)/shard_map/ppermute | solution.py:75
  49.8 2.1 %fusion.24 = f32[3,8,32,128]{3,0,2,1:T(4,128)S(1)} fusion(f32[3,8,32,2]{3,0,2,1:T(4,128)S(1)} %bitcast.95, f32[3,8,32,128]{3,0,2,1:T(4,128)S(1)} %broadcast_multiply_fusion, f32[3,8,32,2]{3,0,2,1:T(4,128)S(1)} %bitcast.96, f32[3,8,2,128]{3,0,2,1:T(4,128)S(1)} %get-tuple-element.98, f32[3,8,2,128]{3,0,2,1:T(4,128)S(1)} %get-tuple-element.97, ...), kind=kLoop, calls=%fused_computation.46 | loop fusion | flops 3145728 | bytes 1044480 | tf_op jit(solution)/shard_map/mul | solution.py:146
  51.9 0.8 %copy.47 = f32[3,8,32,128]{3,2,1,0:T(8,128)} copy(f32[3,8,32,128]{3,0,2,1:T(4,128)S(1)} %fusion.24) | data formatting | bytes 786432 | tf_op jit(solution)/shard_map/mul | solution.py:146
  (62 shorter events, 1.3 us)
Async XLA Ops:
  0.0 1.0 %copy-start.6 = (f32[2,5,8,5,128]{4,2,3,1,0:T(8,128)S(1)}, f32[2,5,8,5,128]{4,2,3,1,0:T(8,128)}, u32[]{:S(2)}) copy-start(f32[2,5,8,5,128]{4,2,3,1,0:T(8,128)} %param.30) | copy-start | bytes 614404
  1.1 1.0 %copy-start.3 = (f32[2,5,8,4,160]{4,3,2,1,0:T(4,128)S(1)}, f32[2,5,8,4,160]{4,3,2,1,0:T(4,128)}, u32[]{:S(2)}) copy-start(f32[2,5,8,4,160]{4,3,2,1,0:T(4,128)} %param.29) | copy-start | bytes 614404
  2.3 1.0 %copy-start.4 = (f32[2,4,8,5,160]{4,2,3,1,0:T(8,128)S(1)}, f32[2,4,8,5,160]{4,2,3,1,0:T(8,128)}, u32[]{:S(2)}) copy-start(f32[2,4,8,5,160]{4,2,3,1,0:T(8,128)} %param.28) | copy-start | bytes 614404
  3.4 1.0 %copy-start.1 = (f32[297,320]{1,0:T(8,128)S(1)}, f32[297,320]{1,0:T(8,128)}, u32[]{:S(2)}) copy-start(f32[297,320]{1,0:T(8,128)} %constant.218.clone) | copy-start | bytes 1140484
  4.4 1.3 %copy-start.5 = (f32[160,128]{1,0:T(8,128)S(1)}, f32[160,128]{1,0:T(8,128)}, u32[]{:S(2)}) copy-start(f32[160,128]{1,0:T(8,128)} %constant.216.clone) | copy-start | bytes 245764
  5.8 1.0 %copy-start.2 = (f32[297,320]{1,0:T(8,128)S(1)}, f32[297,320]{1,0:T(8,128)}, u32[]{:S(2)}) copy-start(f32[297,320]{1,0:T(8,128)} %constant.215.clone) | copy-start | bytes 1140484
  6.8 2.1 %copy-start = (f32[297,400]{1,0:T(8,128)S(1)}, f32[297,400]{1,0:T(8,128)}, u32[]{:S(2)}) copy-start(f32[297,400]{1,0:T(8,128)} %constant.219.clone) | copy-start | bytes 1425604
  8.9 0.8 %copy-start.8 = (f32[128,128]{1,0:T(8,128)S(1)}, f32[128,128]{1,0:T(8,128)}, u32[]{:S(2)}) copy-start(f32[128,128]{1,0:T(8,128)} %constant.220.clone) | copy-start | bytes 196612
  10.1 22.3 %collective-permute-start = (f32[3,32,128]{2,0,1:T(4,128)S(1)}, f32[3,32,128]{2,0,1:T(4,128)S(1)}, u32[]{:S(2)}, u32[]{:S(2)}) collective-permute-start(f32[3,32,128]{2,0,1:T(4,128)S(1)} %copy.49), channel_id=1, source_target_pairs={{0,16},{16,0},{1,17},{17,1},{2,18},{18,2},{3,19},{19,3},{4,20},{20... | collective-permute-start | bytes 147464 | tf_op jit(solution)/shard_map/ppermute | solution.py:75
  13.1 1.6 %copy-start.9 = (f32[160,1]{0,1:T(1,128)S(1)}, f32[160,1]{0,1:T(1,128)}, u32[]{:S(2)}) copy-start(f32[160,1]{0,1:T(1,128)} %constant.222) | copy-start | bytes 1924
  13.1 19.3 %collective-permute-start.1 = (f32[3,8,128]{2,0,1:T(4,128)S(1)}, f32[3,8,128]{2,0,1:T(4,128)S(1)}, u32[]{:S(2)}, u32[]{:S(2)}) collective-permute-start(f32[3,8,128]{2,0,1:T(4,128)S(1)} %copy.50), channel_id=1, source_target_pairs={{0,8},{8,0},{1,9},{9,1},{2,10},{10,2},{3,11},{11,3},{4,12},{12,4},... | collective-permute-start | bytes 36872 | tf_op jit(solution)/shard_map/ppermute | solution.py:75
  14.9 0.7 %copy-start.10 = (f32[128,1]{0,1:T(1,128)S(1)}, f32[128,1]{0,1:T(1,128)}, u32[]{:S(2)}) copy-start(f32[128,1]{0,1:T(1,128)} %constant.223) | copy-start | bytes 1540
  16.0 16.1 %collective-permute-start.2 = (f32[3,8,32]{2,1,0:T(8,128)S(1)}, f32[3,8,32]{2,1,0:T(8,128)S(1)}, u32[]{:S(2)}, u32[]{:S(2)}) collective-permute-start(f32[3,8,32]{2,1,0:T(8,128)S(1)} %reshape.307), channel_id=1, source_target_pairs={{0,1},{1,2},{2,3},{3,4},{4,5},{5,6},{6,7},{7,0},{8,9},{9,10},{10,1... | collective-permute-start | bytes 9224 | tf_op jit(solution)/shard_map/ppermute | solution.py:75
  16.0 16.0 %collective-permute-start.4 = (f32[3,32]{1,0:T(4,128)S(1)}, f32[3,32]{1,0:T(4,128)S(1)}, u32[]{:S(2)}, u32[]{:S(2)}) collective-permute-start(f32[3,32]{1,0:T(4,128)S(1)} %slice.354), channel_id=1, source_target_pairs={{0,17},{1,18},{2,19},{3,20},{4,21},{5,22},{6,23},{7,16},{16,1},{17... | collective-permute-start | bytes 1160 | tf_op jit(solution)/shard_map/ppermute | solution.py:75
  18.0 1.1 %copy-start.7 = (s32[8,32,128]{2,1,0:T(8,128)S(1)}, s32[8,32,128]{2,1,0:T(8,128)}, u32[]{:S(2)}) copy-start(s32[8,32,128]{2,1,0:T(8,128)} %param.32) | copy-start | bytes 393220
  18.0 6.6 %collective-permute-start.6 = (f32[3]{0:T(128)S(1)}, f32[3]{0:T(128)S(1)}, u32[]{:S(2)}, u32[]{:S(2)}) collective-permute-start(f32[3]{0:T(128)S(1)} %slice_reduce_fusion), channel_id=1, source_target_pairs={{0,25},{1,26},{2,27},{3,28},{4,29},{5,30},{6,31},{7,24},{8,17},{9,... | collective-permute-start | bytes 44 | tf_op jit(solution)/shard_map/ppermute | solution.py:75
  24.6 5.7 %collective-permute-start.5 = (f32[3,8]{1,0:T(4,128)S(1)}, f32[3,8]{1,0:T(4,128)S(1)}, u32[]{:S(2)}, u32[]{:S(2)}) collective-permute-start(f32[3,8]{1,0:T(4,128)S(1)} %slice.356), channel_id=1, source_target_pairs={{0,9},{1,10},{2,11},{3,12},{4,13},{5,14},{6,15},{7,8},{8,1},{9,2},... | collective-permute-start | bytes 296 | tf_op jit(solution)/shard_map/ppermute | solution.py:75
  30.3 6.3 %collective-permute-start.3 = (f32[3,128]{1,0:T(4,128)S(1)}, f32[3,128]{1,0:T(4,128)S(1)}, u32[]{:S(2)}, u32[]{:S(2)}) collective-permute-start(f32[3,128]{1,0:T(4,128)S(1)} %bitcast.103), channel_id=1, source_target_pairs={{0,24},{8,16},{16,8},{24,0},{1,25},{9,17},{17,9},{25,1},{2,26},{10... | collective-permute-start | bytes 4616 | tf_op jit(solution)/shard_map/ppermute | solution.py:75
  37.6 12.2 %collective-permute-start.10 = (f32[3,2,256]{1,0,2:T(4,128)S(1)}, f32[3,2,256]{1,0,2:T(4,128)S(1)}, u32[]{:S(2)}, u32[]{:S(2)}) collective-permute-start(f32[3,2,256]{1,0,2:T(4,128)S(1)} %bitcast.99), channel_id=1, source_target_pairs={{0,7},{1,0},{2,1},{3,2},{4,3},{5,4},{6,5},{7,6},{8,15},{9,8},{10,9... | collective-permute-start | bytes 18440 | tf_op jit(solution)/shard_map/ppermute | solution.py:75
  37.7 12.1 %collective-permute-start.9 = (f32[3,2,256]{1,0,2:T(4,128)S(1)}, f32[3,2,256]{1,0,2:T(4,128)S(1)}, u32[]{:S(2)}, u32[]{:S(2)}) collective-permute-start(f32[3,2,256]{1,0,2:T(4,128)S(1)} %bitcast.98), channel_id=1, source_target_pairs={{0,1},{1,2},{2,3},{3,4},{4,5},{5,6},{6,7},{7,0},{8,9},{9,10},{10,1... | collective-permute-start | bytes 18440 | tf_op jit(solution)/shard_map/ppermute | solution.py:75
  38.2 4.3 %collective-permute-start.8 = (f32[2,3,2,8,128]{4,1,2,3,0:T(4,128)S(1)}, f32[2,3,2,8,128]{4,1,2,3,0:T(4,128)S(1)}, u32[]{:S(2)}, u32[]{:S(2)}) collective-permute-start(f32[2,3,2,8,128]{4,1,2,3,0:T(4,128)S(1)} %pad_maximum_fusion.8), channel_id=1, source_target_pairs={{0,8},{8,0},{1,9},{9,1},{2,10},{10,2},{3,11},{11,3},{4,12},{12,4},... | collective-permute-start | bytes 147464 | tf_op jit(solution)/shard_map/ppermute | solution.py:75
  39.8 8.0 %collective-permute-start.7 = (f32[2,3,2,32,128]{4,1,3,2,0:T(4,128)S(1)}, f32[2,3,2,32,128]{4,1,3,2,0:T(4,128)S(1)}, u32[]{:S(2)}, u32[]{:S(2)}) collective-permute-start(f32[2,3,2,32,128]{4,1,3,2,0:T(4,128)S(1)} %pad_maximum_fusion.7), channel_id=1, source_target_pairs={{0,16},{16,0},{1,17},{17,1},{2,18},{18,2},{3,19},{19,3},{4,20},{20... | collective-permute-start | bytes 589832 | tf_op jit(solution)/shard_map/ppermute | solution.py:75

commit v3 on v1

--- a/solution.py
+++ b/solution.py
@@ -53,27 +53,36 @@
     return nodal.reshape(4 * ex_count + 1, 4 * ey_count + 1, 4 * ez_count + 1)
 
 
-def from_neighbours(up, down, axis, dim):
+def shifted(block, axis, step=1):
     count = lax.axis_size(axis)
     if count == 1:
-        return up, down
-    if count == 2:
-        both = lax.ppermute(jnp.concatenate([up, down], axis=dim), axis, [(0, 1), (1, 0)])
-        rows = up.shape[dim]
-        return (
-            lax.slice_in_dim(both, 0, rows, axis=dim),
-            lax.slice_in_dim(both, rows, both.shape[dim], axis=dim),
-        )
-    from_prev = lax.ppermute(up, axis, [(i, (i + 1) % count) for i in range(count)])
-    from_next = lax.ppermute(down, axis, [(i, (i - 1) % count) for i in range(count)])
-    return from_prev, from_next
+        return block
+    return lax.ppermute(block, axis, [(i, (i + step) % count) for i in range(count)])
+
+
+def both_ways(up, down, axis):
+    if lax.axis_size(axis) <= 2:
+        both = shifted(jnp.concatenate([up, down]), axis)
+        return both[: up.shape[0]], both[up.shape[0] :]
+    return shifted(up, axis), shifted(down, axis, -1)
+
+
+def to_wire(slab, dim):
+    layers = jnp.moveaxis(slab, dim, 0)
+    return layers.reshape(layers.shape[0] * layers.shape[1], -1), layers.shape
+
+
+def from_wire(rows, shape, dim):
+    return jnp.moveaxis(rows.reshape(shape), 0, dim)
 
 
 def fold_and_halo(partial, axis, dim):
     n = partial.shape[dim] - 1
-    up = lax.slice_in_dim(partial, n - 2, n + 1, axis=dim)
-    down = lax.slice_in_dim(partial, 0, 2, axis=dim)
-    from_prev, from_next = from_neighbours(up, down, axis, dim)
+    up, up_shape = to_wire(lax.slice_in_dim(partial, n - 2, n + 1, axis=dim), dim)
+    down, down_shape = to_wire(lax.slice_in_dim(partial, 0, 2, axis=dim), dim)
+    from_prev, from_next = both_ways(up, down, axis)
+    from_prev = from_wire(from_prev, up_shape, dim)
+    from_next = from_wire(from_next, down_shape, dim)
     return jnp.concatenate(
         [
             lax.slice_in_dim(from_prev, 0, 2, axis=dim),
@@ -86,12 +95,67 @@
     )
 
 
-def halo(cells, axis, dim):
-    n = cells.shape[dim]
-    up = lax.slice_in_dim(cells, n - 2, n, axis=dim)
-    down = lax.slice_in_dim(cells, 0, 2, axis=dim)
-    from_prev, from_next = from_neighbours(up, down, axis, dim)
-    return jnp.concatenate([from_prev, cells, from_next], axis=dim)
+def cross_rows(plane, ny, nz):
+    own = plane[:, 2 : ny + 2, 2 : nz + 2]
+    strips_y = jnp.concatenate([plane[:, 0:2, 2 : nz + 2], plane[:, ny + 2 :, 2 : nz + 2]], axis=1)
+    strips_z = jnp.concatenate([plane[:, 2 : ny + 2, 0:2], plane[:, 2 : ny + 2, nz + 2 :]], axis=2)
+    strips_z = jnp.swapaxes(strips_z, 1, 2).reshape(-1)
+    strips_z = jnp.pad(strips_z, (0, -strips_z.shape[0] % nz))
+    return [own.reshape(-1, nz), strips_y.reshape(-1, nz), strips_z.reshape(-1, nz)]
+
+
+def cross_plane(own, strips_y, strips_z):
+    middle = jnp.concatenate([strips_z[..., 0:2], own, strips_z[..., 2:4]], axis=2)
+    widths = ((0, 0), (0, 0), (2, 2))
+    return jnp.concatenate(
+        [jnp.pad(strips_y[:, 0:2], widths), middle, jnp.pad(strips_y[:, 2:4], widths)], axis=1
+    )
+
+
+def fold_and_halo_last(extended, axis, ny, nz):
+    n = extended.shape[1] - 1
+    comps = extended.shape[0] - 1
+    data = extended[:comps]
+    keep = extended[comps]
+
+    def own(block):
+        return block[..., 2 : ny + 2, 2 : nz + 2]
+
+    halo_up = own(data[:, n - 2 : n] * keep[n - 2 : n])
+    halo_down = own(data[:, 1] * keep[1])
+    up_parts = [halo_up.reshape(-1, nz)] + cross_rows(data[:, n], ny, nz)
+    down_parts = [own(data[:, 0]).reshape(-1, nz), own(keep[0]), halo_down.reshape(-1, nz)]
+    up = jnp.concatenate(up_parts)
+    down = jnp.concatenate(down_parts)
+    from_prev, from_next = both_ways(up, down, axis)
+
+    sizes = [part.shape[0] for part in up_parts]
+    marks = np.cumsum([0] + sizes)
+    prev_halo = from_prev[marks[0] : marks[1]].reshape(comps, 2, ny, nz)
+    prev_own = from_prev[marks[1] : marks[2]].reshape(comps, ny, nz)
+    prev_strips_y = from_prev[marks[2] : marks[3]].reshape(comps, 4, nz)
+    prev_strips_z = from_prev[marks[3] : marks[4]].reshape(-1)[: comps * 4 * ny]
+    prev_strips_z = jnp.swapaxes(prev_strips_z.reshape(comps, 4, ny), 1, 2)
+    fold_in = cross_plane(prev_own, prev_strips_y, prev_strips_z)
+
+    plane_rows = comps * ny
+    next_fold = from_next[:plane_rows].reshape(comps, ny, nz)
+    next_keep = from_next[plane_rows : plane_rows + ny]
+    next_halo = from_next[plane_rows + ny :].reshape(comps, ny, nz)
+
+    widths = ((0, 0), (0, 0), (2, 2), (2, 2))
+    first = (data[:, 0] + fold_in) * keep[0]
+    last = (own(data[:, n]) + next_fold) * next_keep
+    return jnp.concatenate(
+        [
+            jnp.pad(prev_halo, widths),
+            first[:, None],
+            data[:, 1:n] * keep[1:n],
+            jnp.pad(last[:, None], widths),
+            jnp.pad(next_halo[:, None], widths),
+        ],
+        axis=1,
+    )
 
 
 def window(padded_array, axis_pos, offset):
@@ -118,16 +182,16 @@
 
 def body(edge_coeffs_x, edge_coeffs_y, edge_coeffs_z, flips, flags):
     closed_map, open_map = basis_tables()
-    keep = (1 - flags).astype(jnp.float32)
-    for axis, dim in (("gz", 2), ("gy", 1), ("gx", 0)):
-        keep = halo(keep, axis, dim)
+    nx, ny, nz = flags.shape
     nodal_x = interpolate(edge_coeffs_x, flips[0], open_map, closed_map, closed_map)
     nodal_y = interpolate(edge_coeffs_y, flips[1], closed_map, open_map, closed_map)
     nodal_z = interpolate(edge_coeffs_z, flips[2], closed_map, closed_map, open_map)
-    extended = jnp.stack([nodal_x, nodal_y, nodal_z])
-    for axis, dim in (("gz", 3), ("gy", 2), ("gx", 1)):
-        extended = fold_and_halo(extended, axis, dim)
-    return stencil_apply(extended * keep[None])
+    keep = jnp.pad((1 - flags).astype(jnp.float32), ((0, 1), (0, 1), (0, 1)))
+    extended = jnp.stack([nodal_x, nodal_y, nodal_z, keep])
+    extended = fold_and_halo(extended, "gz", 3)
+    extended = fold_and_halo(extended, "gy", 2)
+    masked = fold_and_halo_last(extended, "gx", ny, nz)
+    return stencil_apply(masked)
 
 
 def solution(mesh):

time: 49.5 us -> 42.6 us (0.86)
  the two profiles are of different devices: /device:TPU:8 before, /device:TPU:0 now
where the time goes in v3:
time: 42.6 us; the launch traced here: 42.4 us
  local copies, waits for them, and re-layouts  13.3 us (31%)
  waiting for transfers between devices  10 us (23%)
  starting transfers between devices  8.19 us (19%)
  other arithmetic  6.64 us (16%)
  matrix products  3.67 us (9%)
  between operations  0.57 us (1%)
    ppermute x4, waiting for transfers between devices, shifted(): lax.ppermute(block, axis, [(i, (i + step) % count) for i in range(count)])  10 us
    ppermute x4, starting transfers between devices, shifted(): lax.ppermute(block, axis, [(i, (i + step) % count) for i in range(count)])  8.19 us
    concatenate x2, local copies, waits for them, and re-layouts, fold_and_halo(): jnp.concatenate([lax.slice_in_dim(from_prev, 0, 2, axis=dim), lax.slice_i...  4.96 us
    mul x1, other arithmetic, stencil_apply(): return 0.25 * total  2.05 us
    dot_general x3, matrix products, interpolate(): jnp.dot(jnp.asarray(plane_map, jnp.float32), deep, precision=precise)  1.97 us
    add x2, other arithmetic, fold_and_halo(): lax.slice_in_dim(partial, n, n + 1, axis=dim)  1.88 us
    dot_general x3, matrix products, interpolate(): jnp.dot(signed, jnp.asarray(depth_map.T, jnp.float32), precision=precise)  1.7 us
    transpose x8, local copies, waits for them, and re-layouts, to_wire(): layers = jnp.moveaxis(slab, dim, 0)  1.48 us
  transfers between devices with their start and end apart: 4, of which 3 were waited for; matrix products, arithmetic and copies ran while one was open for 6% of the time, Pallas kernels for 0%

profile of v3, /device:TPU:0, one launch (start us, length us, event | category | flops | bytes accessed | tf_op | source)
XLA Modules:
  0.0 42.4 jit_solution(14628145211109622766)
XLA Ops:
  0.0 0.7 %convert_bitcast_fusion.2 = (f32[2,8,32]{2,1,0:T(8,128)S(1)}, f32[2,8,32]{2,1,0:T(8,128)S(1)}, f32[2,8,32]{2,1,0:T(8,128)S(1)}) fusion(s32[3,2,8,32]{3,2,1,0:T(8,128)} %param.14), kind=kLoop, calls=%fused_computation.86 | loop fusion | flops 4608 | bytes 12288 | tf_op jit(solution)/shard_map/convert_element_type | solution.py:47
  0.7 0.1 broadcast_in_dim.16
  0.9 0.2 mul.120
  1.0 1.1 %broadcast_multiply_fusion.1 = f32[2,4,8,5,160]{4,2,3,1,0:T(8,128)S(1)} fusion(f32[2,4,8,5,160]{4,2,3,1,0:T(8,128)} %param.11, f32[2,8,160]{2,1,0:T(8,128)S(1)} %mul.120), kind=kLoop, calls=%fused_computation.62 | loop fusion | flops 51200 | bytes 419840 | tf_op jit(solution)/shard_map/mul | solution.py:48
  2.1 0.1 copy.43
  2.3 0.6 %fusion.36 = f32[320,129]{0,1:T(8,128)S(1)} fusion(f32[320,160]{1,0:T(8,128)S(1)} %reshape.96, f32[160,129]{1,0:T(8,128)S(1)} %copy-done), kind=kOutput, calls=%fused_computation.96 | convolution fusion | flops 79257600 | bytes 452480 | tf_op jit(solution)/shard_map/dot_general | solution.py:51
  3.0 0.7 %fusion.37 = f32[297,129]{1,0:T(8,128)S(1)} fusion(f32[297,320]{1,0:T(8,128)S(1)} %copy-done.3, f32[320,129]{0,1:T(8,128)S(1)} %fusion.36), kind=kOutput, calls=%fused_computation.97 | convolution fusion | flops 147121920 | bytes 698532 | tf_op jit(solution)/shard_map/dot_general | solution.py:52
  4.0 0.5 %copy-done.6 = f32[128,129]{1,0:T(8,128)S(1)} copy-done((f32[128,129]{1,0:T(8,128)S(1)}, f32[128,129]{1,0:T(8,128)}, u32[]{:S(2)}) %copy-start.6) | copy-done | bytes 66072
  4.6 0.4 %fusion.40 = f32[400,129]{0,1:T(8,128)S(1)} fusion(f32[400,128]{1,0:T(8,128)S(1)} %reshape.98, f32[128,129]{1,0:T(8,128)S(1)} %copy-done.6), kind=kOutput, calls=%fused_computation.100 | convolution fusion | flops 79257600 | bytes 477248 | tf_op jit(solution)/shard_map/dot_general | solution.py:51
  5.0 0.7 %fusion.41 = f32[297,129]{1,0:T(8,128)S(1)} fusion(f32[297,400]{1,0:T(8,128)S(1)} %copy-done.1, f32[400,129]{0,1:T(8,128)S(1)} %fusion.40), kind=kOutput, calls=%fused_computation.101 | convolution fusion | flops 183902400 | bytes 834852 | tf_op jit(solution)/shard_map/dot_general | solution.py:52
  5.7 0.1 broadcast_in_dim.17
  5.9 0.2 mul.124
  6.1 0.1 reshape.97
  6.2 0.6 %fusion.38 = f32[320,129]{0,1:T(8,128)S(1)} fusion(f32[320,160]{1,0:T(8,128)S(1)} %reshape.97, f32[160,129]{1,0:T(8,128)S(1)} %copy-done), kind=kOutput, calls=%fused_computation.98 | convolution fusion | flops 79257600 | bytes 452480 | tf_op jit(solution)/shard_map/dot_general | solution.py:51
  6.9 0.7 %fusion.39 = f32[297,129]{1,0:T(8,128)S(1)} fusion(f32[297,320]{1,0:T(8,128)S(1)} %copy-done.2, f32[320,129]{0,1:T(8,128)S(1)} %fusion.38), kind=kOutput, calls=%fused_computation.99 | convolution fusion | flops 147121920 | bytes 698532 | tf_op jit(solution)/shard_map/dot_general | solution.py:52
  7.7 0.1 pad_maximum_fusion
  7.8 0.3 slice_bitcast_fusion.1
  8.1 0.5 %copy.50 = f32[3,4,9,33]{3,2,1,0:T(8,128)S(1)} copy(f32[3,4,9,33]{0,3,2,1:T(8,128)S(1)} %slice_bitcast_fusion.1) | data formatting | bytes 28512 | tf_op jit(solution)/shard_map/transpose | solution.py:71
  8.6 0.1 reshape.99
  8.7 0.5 %collective-permute-start = (f32[12,297]{1,0:T(8,128)S(1)}, f32[12,297]{1,0:T(8,128)S(1)}, u32[]{:S(2)}, u32[]{:S(2)}) collective-permute-start(f32[12,297]{1,0:T(8,128)S(1)} %reshape.99), channel_id=1, source_target_pairs={{0,1},{1,2},{2,3},{3,4},{4,5},{5,6},{6,7},{7,0},{8,9},{9,10},{10,1... | collective-permute-start | bytes 42776 | tf_op jit(solution)/shard_map/ppermute | solution.py:60
  9.3 0.5 %copy.52 = f32[2,4,9,33]{3,2,1,0:T(8,128)S(1)} copy(f32[2,4,9,33]{0,3,2,1:T(8,128)S(1)} %slice_bitcast_fusion) | data formatting | bytes 19008 | tf_op jit(solution)/shard_map/transpose | solution.py:71
  9.9 4.1 %collective-permute-start.1 = (f32[8,297]{1,0:T(8,128)S(1)}, f32[8,297]{1,0:T(8,128)S(1)}, u32[]{:S(2)}, u32[]{:S(2)}) collective-permute-start(f32[8,297]{1,0:T(8,128)S(1)} %reshape.101), channel_id=1, source_target_pairs={{0,7},{1,0},{2,1},{3,2},{4,3},{5,4},{6,5},{7,6},{8,15},{9,8},{10,9... | collective-permute-start | bytes 28520 | tf_op jit(solution)/shard_map/ppermute | solution.py:60
  14.0 1.1 %slice.305 = f32[4,9,33,127]{3,2,1,0:T(8,128)} slice(f32[4,9,33,129]{3,2,1,0:T(8,128)S(1)} %pad_maximum_fusion), slice={[0:4], [0:9], [0:33], [1:128]} | slice | bytes 1207008 | tf_op jit(solution)/shard_map/slice | solution.py:90
  15.1 0.3 collective-permute-done.1
  15.4 0.4 copy.53
  15.9 0.4 copy.51
  16.3 1.8 %slice_add_fusion = (f32[4,9,33,1]{3,2,1,0:T(8,128)}, f32[4,9,33,1]{3,2,1,0:T(8,128)}, f32[4,9,33,1]{3,2,1,0:T(8,128)}) fusion(f32[4,9,33,2]{3,2,1,0:T(8,128)S(1)} %bitcast.81, f32[4,9,33,129]{3,2,1,0:T(8,128)S(1)} %pad_maximum_fusion, f32[4,9,33,3]{3,2,1,0:T(8,128)S(1)} %bitcast.79), kind=kLoop, calls=%fused_computation.21 | loop fusion | flops 2376 | bytes 38016 | tf_op jit(solution)/shard_map/add | solution.py:91
  18.1 3.4 %concatenate.53 = f32[4,9,33,132]{3,2,1,0:T(8,128)S(1)} concatenate(f32[4,9,33,2]{3,2,1,0:T(8,128)S(1)} %bitcast.80, f32[4,9,33,1]{3,2,1,0:T(8,128)} %get-tuple-element.13, f32[4,9,33,127]{3,2,1,0:T(8,128)} %slice.305, f32[4,9,33,1]{3,2,1,0:T(8,128)} %get-tuple-element.12, f32[4,9,33,1]{3,2,1,0:T(8,128)} %get-tuple-element.14), dimensions={3} | concatenate | bytes 1254528 | tf_op jit(solution)/shard_map/concatenate | solution.py:86
  21.6 0.1 reshape.103
  21.7 0.1 reshape.104
  21.9 2.1 %collective-permute-start.2 = (f32[20,1188]{1,0:T(8,128)S(1)}, f32[20,1188]{1,0:T(8,128)S(1)}, u32[]{:S(2)}, u32[]{:S(2)}) collective-permute-start(f32[20,1188]{1,0:T(8,128)S(1)} %pad_maximum_fusion.4), channel_id=1, source_target_pairs={{0,8},{8,0},{1,9},{9,1},{2,10},{10,2},{3,11},{11,3},{4,12},{12,4},... | collective-permute-start | bytes 285128 | tf_op jit(solution)/shard_map/ppermute | solution.py:60
  23.9 0.2 slice.316
  24.1 3.4 %collective-permute-done.2 = f32[20,1188]{1,0:T(8,128)S(1)} collective-permute-done((f32[20,1188]{1,0:T(8,128)S(1)}, f32[20,1188]{1,0:T(8,128)S(1)}, u32[]{:S(2)}, u32[]{:S(2)}) %collective-permute-start.2) | collective-permute-done | bytes 95072 | tf_op jit(solution)/shard_map/ppermute | solution.py:60
  27.5 0.2 reshape.105
  27.8 0.1 reshape.106
  28.0 0.1 slice_add_fusion.2
  28.1 1.6 %concatenate.55 = f32[4,9,36,132]{3,2,1,0:T(8,128)S(1)} concatenate(f32[4,9,2,132]{3,2,1,0:T(2,128)S(1)} %slice.313, f32[4,9,1,132]{3,2,1,0:T(1,128)S(1)} %get-tuple-element.11, f32[4,9,31,132]{3,2,1,0:T(8,128)S(1)} %slice.316, f32[4,9,1,132]{3,2,1,0:T(1,128)S(1)} %get-tuple-element.10, f32[4,9,1,132]{3,2,1,0:T(1,128)S(1)} %get-tuple-element.22), dimensions={2} | concatenate | bytes 1368576 | tf_op jit(solution)/shard_map/concatenate | solution.py:86
  30.2 0.1 copy.60
  30.8 0.1 slice_multiply_fusion.1
  30.9 0.6 %concatenate.58 = f32[527,128]{1,0:T(8,128)S(1)} concatenate(f32[192,128]{1,0:T(8,128)S(1)} %bitcast.87, f32[96,128]{1,0:T(8,128)S(1)} %bitcast.90, f32[12,128]{1,0:T(8,128)S(1)} %reshape.109, f32[3,128]{1,0:T(4,128)S(1)} %reshape.110, f32[96,128]{1,0:T(8,128)S(1)} %bitcast.91, f32[32,128]{1,0:T(8,128)S(1)} %slice.334, f32[96,128]{1,0:T(8,128)S(1)} %bitcast.89), dimensions={0} | concatenate | bytes 539648 | tf_op jit(solution)/shard_map/concatenate | solution.py:65
  31.4 1.5 %collective-permute-start.3 = (f32[527,128]{1,0:T(8,128)S(1)}, f32[527,128]{1,0:T(8,128)S(1)}, u32[]{:S(2)}, u32[]{:S(2)}) collective-permute-start(f32[527,128]{1,0:T(8,128)S(1)} %concatenate.58), channel_id=1, source_target_pairs={{0,16},{16,0},{1,17},{17,1},{2,18},{18,2},{3,19},{19,3},{4,20},{20... | collective-permute-start | bytes 809480 | tf_op jit(solution)/shard_map/ppermute | solution.py:60
  33.0 0.1 slice_multiply_fusion
  33.1 6.3 %collective-permute-done.3 = f32[527,128]{1,0:T(8,128)S(1)} collective-permute-done((f32[527,128]{1,0:T(8,128)S(1)}, f32[527,128]{1,0:T(8,128)S(1)}, u32[]{:S(2)}, u32[]{:S(2)}) %collective-permute-start.3) | collective-permute-done | bytes 269856 | tf_op jit(solution)/shard_map/ppermute | solution.py:60
  39.5 0.1 copy.61
  39.9 0.1 pad.26
  40.0 0.1 maximum_bitcast_fusion
  40.2 0.1 fusion
  40.3 2.0 %fusion.5 = f32[3,8,32,128]{3,2,1,0:T(8,128)} fusion(f32[3,7,36,132]{3,2,1,0:T(8,128)S(1)} %slice_multiply_fusion, f32[3,1,36,132]{3,2,1,0:T(8,128)S(1)} %fusion.30, f32[3,1,32,128]{3,2,1,0:T(8,128)S(1)} %bitcast.94, f32[3,1,36,132]{3,2,1,0:T(8,128)S(1)} %pad.26, f32[3,10,36,132]{3,2,1,0:T(8,128)S(1)} %fusion), kind=kLoop, calls=%fused_computation.29 | loop fusion | flops 3440640 | bytes 1742016 | tf_op jit(solution)/shard_map/mul | solution.py:180
  (73 shorter events, 2.5 us)
Async XLA Ops:
  0.7 1.6 %copy-start = (f32[160,129]{1,0:T(8,128)S(1)}, f32[160,129]{1,0:T(8,128)}, u32[]{:S(2)}) copy-start(f32[160,129]{1,0:T(8,128)} %constant.26.clone) | copy-start | bytes 247684
  1.0 1.9 %copy-start.3 = (f32[297,320]{1,0:T(8,128)S(1)}, f32[297,320]{1,0:T(8,128)}, u32[]{:S(2)}) copy-start(f32[297,320]{1,0:T(8,128)} %constant.27.clone) | copy-start | bytes 1140484
  2.3 1.6 %copy-start.5 = (f32[2,5,8,5,128]{4,2,3,1,0:T(8,128)S(1)}, f32[2,5,8,5,128]{4,2,3,1,0:T(8,128)}, u32[]{:S(2)}) copy-start(f32[2,5,8,5,128]{4,2,3,1,0:T(8,128)} %param.13) | copy-start | bytes 614404
  3.6 0.9 %copy-start.6 = (f32[128,129]{1,0:T(8,128)S(1)}, f32[128,129]{1,0:T(8,128)}, u32[]{:S(2)}) copy-start(f32[128,129]{1,0:T(8,128)} %constant.29.clone) | copy-start | bytes 198148
  3.7 1.3 %copy-start.1 = (f32[297,400]{1,0:T(8,128)S(1)}, f32[297,400]{1,0:T(8,128)}, u32[]{:S(2)}) copy-start(f32[297,400]{1,0:T(8,128)} %constant.30.clone) | copy-start | bytes 1425604
  4.6 1.5 %copy-start.4 = (f32[2,5,8,4,160]{4,3,2,1,0:T(4,128)S(1)}, f32[2,5,8,4,160]{4,3,2,1,0:T(4,128)}, u32[]{:S(2)}) copy-start(f32[2,5,8,4,160]{4,3,2,1,0:T(4,128)} %param.12) | copy-start | bytes 614404
  5.7 1.2 %copy-start.2 = (f32[297,320]{1,0:T(8,128)S(1)}, f32[297,320]{1,0:T(8,128)}, u32[]{:S(2)}) copy-start(f32[297,320]{1,0:T(8,128)} %constant.28.clone) | copy-start | bytes 1140484
  6.1 1.5 %copy-start.7 = (s32[8,32,128]{2,1,0:T(8,128)S(1)}, s32[8,32,128]{2,1,0:T(8,128)}, u32[]{:S(2)}) copy-start(s32[8,32,128]{2,1,0:T(8,128)} %param.15) | copy-start | bytes 393220
  8.7 7.1 %collective-permute-start = (f32[12,297]{1,0:T(8,128)S(1)}, f32[12,297]{1,0:T(8,128)S(1)}, u32[]{:S(2)}, u32[]{:S(2)}) collective-permute-start(f32[12,297]{1,0:T(8,128)S(1)} %reshape.99), channel_id=1, source_target_pairs={{0,1},{1,2},{2,3},{3,4},{4,5},{5,6},{6,7},{7,0},{8,9},{9,10},{10,1... | collective-permute-start | bytes 42776 | tf_op jit(solution)/shard_map/ppermute | solution.py:60
  9.9 5.5 %collective-permute-start.1 = (f32[8,297]{1,0:T(8,128)S(1)}, f32[8,297]{1,0:T(8,128)S(1)}, u32[]{:S(2)}, u32[]{:S(2)}) collective-permute-start(f32[8,297]{1,0:T(8,128)S(1)} %reshape.101), channel_id=1, source_target_pairs={{0,7},{1,0},{2,1},{3,2},{4,3},{5,4},{6,5},{7,6},{8,15},{9,8},{10,9... | collective-permute-start | bytes 28520 | tf_op jit(solution)/shard_map/ppermute | solution.py:60
  21.9 5.6 %collective-permute-start.2 = (f32[20,1188]{1,0:T(8,128)S(1)}, f32[20,1188]{1,0:T(8,128)S(1)}, u32[]{:S(2)}, u32[]{:S(2)}) collective-permute-start(f32[20,1188]{1,0:T(8,128)S(1)} %pad_maximum_fusion.4), channel_id=1, source_target_pairs={{0,8},{8,0},{1,9},{9,1},{2,10},{10,2},{3,11},{11,3},{4,12},{12,4},... | collective-permute-start | bytes 285128 | tf_op jit(solution)/shard_map/ppermute | solution.py:60
  31.4 8.0 %collective-permute-start.3 = (f32[527,128]{1,0:T(8,128)S(1)}, f32[527,128]{1,0:T(8,128)S(1)}, u32[]{:S(2)}, u32[]{:S(2)}) collective-permute-start(f32[527,128]{1,0:T(8,128)S(1)} %concatenate.58), channel_id=1, source_target_pairs={{0,16},{16,0},{1,17},{17,1},{2,18},{18,2},{3,19},{19,3},{4,20},{20... | collective-permute-start | bytes 809480 | tf_op jit(solution)/shard_map/ppermute | solution.py:60

commit v4 on v3

v4 whole, which is shorter than its diff:
```python
import math

import jax
import jax.numpy as jnp
import numpy as np
from jax import lax
from jax.sharding import PartitionSpec as P


def lagrange_table(points, targets):
    table = np.ones((len(targets), len(points)))
    for row_pos in range(len(targets)):
        for col_pos in range(len(points)):
            for other in range(len(points)):
                if other != col_pos:
                    table[row_pos, col_pos] *= (targets[row_pos] - points[other]) / (
                        points[col_pos] - points[other]
                    )
    return table


def basis_tables():
    spread = math.sqrt(3.0 / 7.0)
    targets = [0.0, (1.0 - spread) / 2.0, 0.5, (1.0 + spread) / 2.0, 1.0]
    closed = [0.0, 0.25, 0.5, 0.75, 1.0]
    inner = math.sqrt(3.0 / 7.0 - 2.0 / 7.0 * math.sqrt(6.0 / 5.0))
    outer = math.sqrt(3.0 / 7.0 + 2.0 / 7.0 * math.sqrt(6.0 / 5.0))
    gauss = [(1.0 - outer) / 2.0, (1.0 - inner) / 2.0, (1.0 + inner) / 2.0, (1.0 + outer) / 2.0]
    closed_map = np.asarray(lagrange_table(closed, targets), dtype=np.float32).astype(np.float64)
    open_map = np.asarray(lagrange_table(gauss, targets), dtype=np.float32).astype(np.float64)
    return closed_map, open_map


def assembly_matrix(table, count):
    size = table.shape[1]
    matrix = np.zeros((4 * count + 1, count * size))
    for elem_pos in range(count):
        matrix[4 * elem_pos : 4 * elem_pos + 5, size * elem_pos : size * elem_pos + size] += table
    return matrix


def interpolate(coef, flip, table_x, table_y, table_z):
    ex_count, size_x, ey_count, size_y, merged = coef.shape
    size_z = table_z.shape[1]
    ez_count = merged // size_z
    precise = lax.Precision.HIGHEST
    orient = jnp.repeat((1 - 2 * flip).astype(jnp.float32), size_z, axis=2)
    signed = (coef * orient[:, None, :, None, :]).reshape(ex_count * size_x * ey_count * size_y, merged)
    rows_y = np.pad(assembly_matrix(table_y, ey_count), ((2, 1), (0, 0)))
    plane_map = np.kron(assembly_matrix(table_x, ex_count), rows_y)
    depth_map = np.pad(assembly_matrix(table_z, ez_count), ((2, 1), (0, 0)))
    deep = jnp.dot(signed, jnp.asarray(depth_map.T, jnp.float32), precision=precise)
    nodal = jnp.dot(jnp.asarray(plane_map, jnp.float32), deep, precision=precise)
    return nodal.reshape(4 * ex_count + 1, 4 * ey_count + 4, 4 * ez_count + 4)


def shifted(block, axis, step=1):
    count = lax.axis_size(axis)
    if count == 1:
        return block
    return lax.ppermute(block, axis, [(i, (i + step) % count) for i in range(count)])


def both_ways(up, down, axis):
    if lax.axis_size(axis) <= 2:
        both = shifted(jnp.concatenate([up, down]), axis)
        return both[: up.shape[0]], both[up.shape[0] :]
    return shifted(up, axis), shifted(down, axis, -1)


def to_wire(slab, dim):
    layers = jnp.moveaxis(slab, dim, 0)
    return layers.reshape(layers.shape[0] * layers.shape[1], -1), layers.shape


def from_wire(rows, shape, dim):
    return jnp.moveaxis(rows.reshape(shape), 0, dim)


def fold_and_halo(extended, axis, dim):
    length = extended.shape[dim]
    n = length - 4
    up, up_shape = to_wire(lax.slice_in_dim(extended, n, n + 3, axis=dim), dim)
    down, down_shape = to_wire(lax.slice_in_dim(extended, 2, 4, axis=dim), dim)
    from_prev, from_next = both_ways(up, down, axis)
    widths_prev = [(0, 0)] * extended.ndim
    widths_prev[dim] = (0, length - 3)
    widths_next = [(0, 0)] * extended.ndim
    widths_next[dim] = (n + 2, 0)
    return (
        extended
        + jnp.pad(from_wire(from_prev, up_shape, dim), widths_prev)
        + jnp.pad(from_wire(from_next, down_shape, dim), widths_next)
    )


def pack(parts, width):
    flat = jnp.concatenate([part.reshape(-1) for part in parts])
    flat = jnp.pad(flat, (0, -flat.shape[0] % width))
    return flat.reshape(-1, width)


def unpack(rows, shapes):
    flat = rows.reshape(-1)
    parts = []
    start = 0
    for shape in shapes:
        size = int(np.prod(shape))
        parts.append(flat[start : start + size].reshape(shape))
        start += size
    return parts


def patch(block, row, col):
    at_row = lax.broadcasted_iota(jnp.int32, block.shape, block.ndim - 2) == 0
    at_col = lax.broadcasted_iota(jnp.int32, block.shape, block.ndim - 1) == 0
    return jnp.where(at_col, col[..., None], jnp.where(at_row, row[..., None, :], block))


def cross_plane(own, strips_y, strips_z):
    middle = jnp.concatenate([strips_z[..., 0:2], own, strips_z[..., 2:4]], axis=2)
    widths = ((0, 0), (0, 0), (2, 2))
    return jnp.concatenate(
        [jnp.pad(strips_y[:, 0:2], widths), middle, jnp.pad(strips_y[:, 2:4], widths)], axis=1
    )


def window(padded_array, axis_pos, offset):
    starts = [0, 2, 2, 2]
    limits = [
        padded_array.shape[0],
        padded_array.shape[1] - 2,
        padded_array.shape[2] - 2,
        padded_array.shape[3] - 2,
    ]
    starts[axis_pos] = offset
    limits[axis_pos] = offset + padded_array.shape[axis_pos] - 4
    return lax.slice(padded_array, tuple(starts), tuple(limits))


def stencil_apply(padded_array):
    total = 8.0 * window(padded_array, 1, 2)
    for axis_pos in (1, 2, 3):
        near = window(padded_array, axis_pos, 1) + window(padded_array, axis_pos, 3)
        far = window(padded_array, axis_pos, 0) + window(padded_array, axis_pos, 4)
        total = total - 4.0 / 3.0 * near + 1.0 / 12.0 * far
    return 0.25 * total


def body(edge_coeffs_x, edge_coeffs_y, edge_coeffs_z, flips, flags):
    closed_map, open_map = basis_tables()
    nx, ny, nz = flags.shape
    comps = 3
    nodal_x = interpolate(edge_coeffs_x, flips[0], open_map, closed_map, closed_map)
    nodal_y = interpolate(edge_coeffs_y, flips[1], closed_map, open_map, closed_map)
    nodal_z = interpolate(edge_coeffs_z, flips[2], closed_map, closed_map, open_map)
    keep = jnp.pad((1 - flags).astype(jnp.float32), ((0, 1), (2, 2), (2, 2)))
    extended = jnp.stack([nodal_x, nodal_y, nodal_z, keep])

    def own(block):
        return block[..., 2 : ny + 2, 2 : nz + 2]

    data = extended[:comps]
    up = [
        own(data[:, nx - 2 : nx] * keep[nx - 2 : nx]).reshape(-1, nz),
        own(data[:, nx]).reshape(-1, nz),
    ]
    down = [
        own(data[:, 0]).reshape(-1, nz),
        own(keep[0]),
        own(data[:, 1] * keep[1]).reshape(-1, nz),
    ]
    early_prev, early_next = both_ways(jnp.concatenate(up), jnp.concatenate(down), "gx")

    extended = fold_and_halo(extended, "gz", 3)
    extended = fold_and_halo(extended, "gy", 2)
    data = extended[:comps]
    keep = extended[comps]

    def edges(block):
        return [block[..., 2, 2 : nz + 2], block[..., 2 : ny + 2, 2]]

    top = data[:, nx]
    strips_y = jnp.concatenate([top[:, 0:2, 2 : nz + 2], top[:, ny + 2 :, 2 : nz + 2]], axis=1)
    strips_z = jnp.concatenate([top[:, 2 : ny + 2, 0:2], top[:, 2 : ny + 2, nz + 2 :]], axis=2)
    late_up = edges(data[:, nx - 2 : nx] * keep[nx - 2 : nx]) + edges(top) + [strips_y, strips_z]
    late_down = edges(data[:, 0]) + edges(data[:, 1] * keep[1])
    late_prev, late_next = both_ways(pack(late_up, nz), pack(late_down, nz), "gx")
    halo_row, halo_col, top_row, top_col, in_strips_y, in_strips_z = unpack(
        late_prev,
        [(comps, 2, nz), (comps, 2, ny), (comps, nz), (comps, ny), (comps, 4, nz), (comps, ny, 4)],
    )
    bottom_row, bottom_col, next_row, next_col = unpack(
        late_next, [(comps, nz), (comps, ny), (comps, nz), (comps, ny)]
    )

    plane = comps * ny
    prev_halo = patch(early_prev[: 2 * plane].reshape(comps, 2, ny, nz), halo_row, halo_col)
    prev_top = patch(early_prev[2 * plane :].reshape(comps, ny, nz), top_row, top_col)
    next_bottom = patch(early_next[:plane].reshape(comps, ny, nz), bottom_row, bottom_col)
    next_keep = early_next[plane : plane + ny]
    next_halo = patch(early_next[plane + ny :].reshape(comps, ny, nz), next_row, next_col)

    fold_in = cross_plane(prev_top, in_strips_y, in_strips_z)
    first = (data[:, 0] + fold_in) * keep[0]
    last = (own(data[:, nx]) + next_bottom) * next_keep
    widths = ((0, 0), (0, 0), (2, 2), (2, 2))
    masked = jnp.concatenate(
        [
            jnp.pad(prev_halo, widths),
            first[:, None],
            data[:, 1:nx] * keep[1:nx],
            jnp.pad(last[:, None], widths),
            jnp.pad(next_halo[:, None], widths),
        ],
        axis=1,
    )
    return stencil_apply(masked)


def solution(mesh):
    in_specs = (
        P("gx", None, "gy", None, "gz"),
        P("gx", None, "gy", None, "gz"),
        P("gx", None, "gy", None, "gz"),
        P(None, "gx", "gy", "gz"),
        P("gx", "gy", "gz"),
    )
    out_specs = P(None, "gx", "gy", "gz")
    return jax.shard_map(body, mesh=mesh, in_specs=in_specs, out_specs=out_specs, check_vma=False)
```

time: 42.6 us -> 46.9 us (1.10)
  local copies, waits for them, and re-layouts: 13.3 us -> 16.1 us
  other arithmetic: 6.64 us -> 7.83 us
    concatenate x2 -> x1, local copies, waits for them, and re-layouts: 4.96 us -> 0.08 us  [pack(): flat = jnp.concatenate([part.reshape(-1) for part in parts])]
    unnamed x16 -> x32, local copies, waits for them, and re-layouts: 0.56 us -> 3.61 us
    slice x14 -> x19, local copies, waits for them, and re-layouts: 1.79 us -> 3.85 us  [the longest x1 0.9 us: body(): early_prev[:2 * plane].reshape(comps, 2, ny, nz)]
    reshape x8, local copies, waits for them, and re-layouts: 1.34 us -> 3.08 us  [from_wire(): return jnp.moveaxis(rows.reshape(shape), 0, dim)]
    convert_element_type x1, other arithmetic: 0.01 us -> 0.95 us  [body(): keep = jnp.pad((1 - flags).astype(jnp.float32), ((0, 1), (2, 2), (2, 2)))]
    ppermute x4 -> x5, starting transfers between devices: 8.19 us -> 7.96 us  [shifted(): lax.ppermute(block, axis, [(i, (i + step) % count) for i in range(count)])]
    ppermute x4 -> x5, waiting for transfers between devices: 10 us -> 10.2 us  [shifted(): lax.ppermute(block, axis, [(i, (i + step) % count) for i in range(count)])]
  transfers between devices with their start and end apart: 4 -> 5, of which waited for: 3 -> 4; matrix products, arithmetic and copies ran while one was open for 6% -> 21% of each run, Pallas kernels for 0% -> 0%
where the time goes in v4:
time: 46.9 us; the launch traced here: 46.6 us
  local copies, waits for them, and re-layouts  16.1 us (34%)
  waiting for transfers between devices  10.2 us (22%)
  starting transfers between devices  7.96 us (17%)
  other arithmetic  7.83 us (17%)
  matrix products  3.79 us (8%)
  between operations  0.71 us (2%)
    ppermute x5, waiting for transfers between devices, shifted(): lax.ppermute(block, axis, [(i, (i + step) % count) for i in range(count)])  10.2 us
    ppermute x5, starting transfers between devices, shifted(): lax.ppermute(block, axis, [(i, (i + step) % count) for i in range(count)])  7.96 us
    unnamed x32, local copies, waits for them, and re-layouts  3.61 us
    reshape x8, local copies, waits for them, and re-layouts, from_wire(): return jnp.moveaxis(rows.reshape(shape), 0, dim)  3.08 us
    dot_general x3, matrix products, interpolate(): jnp.dot(jnp.asarray(plane_map, jnp.float32), deep, precision=precise)  2.08 us
    mul x1, other arithmetic, stencil_apply(): return 0.25 * total  2.05 us
    add x2, other arithmetic, fold_and_halo(): extended + jnp.pad(from_wire(from_prev, up_shape, dim), widths_prev)  1.79 us
    dot_general x3, matrix products, interpolate(): jnp.dot(signed, jnp.asarray(depth_map.T, jnp.float32), precision=precise)  1.7 us
  transfers between devices with their start and end apart: 5, of which 4 were waited for; matrix products, arithmetic and copies ran while one was open for 21% of the time, Pallas kernels for 0%

profile of v4, /device:TPU:0, one launch (start us, length us, event | category | flops | bytes accessed | tf_op | source)
XLA Modules:
  0.0 46.6 jit_solution(7115544034351195078)
XLA Ops:
  0.0 1.0 %subtract_convert_fusion = f32[8,32,128]{2,1,0:T(8,128)S(1)} fusion(s32[8,32,128]{2,1,0:T(8,128)} %param.15), kind=kLoop, calls=%fused_computation.69 | loop fusion | flops 65536 | bytes 262144 | tf_op jit(solution)/shard_map/convert_element_type | solution.py:157
  1.1 0.8 %convert_bitcast_fusion.2 = (f32[2,8,32]{2,1,0:T(8,128)S(1)}, f32[2,8,32]{2,1,0:T(8,128)S(1)}, f32[2,8,32]{2,1,0:T(8,128)S(1)}) fusion(s32[3,2,8,32]{3,2,1,0:T(8,128)} %param.14), kind=kLoop, calls=%fused_computation.115 | loop fusion | flops 4608 | bytes 12288 | tf_op jit(solution)/shard_map/convert_element_type | solution.py:47
  2.1 1.0 %broadcast_multiply_fusion.2 = f32[2,5,8,5,128]{4,2,3,1,0:T(8,128)S(1)} fusion(f32[2,5,8,5,128]{4,2,3,1,0:T(8,128)} %param.13, f32[2,8,128]{2,1,0:T(8,128)S(1)} %copy.73), kind=kLoop, calls=%fused_computation.81 | loop fusion | flops 51200 | bytes 417792 | tf_op jit(solution)/shard_map/mul | solution.py:48
  3.2 0.4 fusion.49
  3.6 0.7 %fusion.50 = f32[324,132]{1,0:T(8,128)S(1)} fusion(f32[324,400]{1,0:T(8,128)S(1)} %copy-done.6, f32[400,132]{0,1:T(8,128)S(1)} %fusion.49), kind=kOutput, calls=%fused_computation.150 | convolution fusion | flops 205286400 | bytes 900672 | tf_op jit(solution)/shard_map/dot_general | solution.py:53
  4.4 0.1 broadcast_in_dim.84
  4.5 0.2 mul.140
  4.7 0.1 broadcast_in_dim.85
  4.8 0.2 mul.144
  5.3 0.6 %fusion.47 = f32[320,132]{0,1:T(8,128)S(1)} fusion(f32[320,160]{1,0:T(8,128)S(1)} %reshape.142, f32[160,132]{1,0:T(8,128)S(1)} %copy-done.7), kind=kOutput, calls=%fused_computation.147 | convolution fusion | flops 81100800 | bytes 458240 | tf_op jit(solution)/shard_map/dot_general | solution.py:52
  5.9 0.7 %fusion.48 = f32[324,132]{1,0:T(8,128)S(1)} fusion(f32[324,320]{1,0:T(8,128)S(1)} %copy-done.9, f32[320,132]{0,1:T(8,128)S(1)} %fusion.47), kind=kOutput, calls=%fused_computation.148 | convolution fusion | flops 164229120 | bytes 754752 | tf_op jit(solution)/shard_map/dot_general | solution.py:53
  6.7 0.1 copy.69
  7.0 0.6 %fusion.45 = f32[320,132]{0,1:T(8,128)S(1)} fusion(f32[320,160]{1,0:T(8,128)S(1)} %reshape.141, f32[160,132]{1,0:T(8,128)S(1)} %copy-done.7), kind=kOutput, calls=%fused_computation.145 | convolution fusion | flops 81100800 | bytes 458240 | tf_op jit(solution)/shard_map/dot_general | solution.py:52
  7.6 0.3 copy-done.8
  7.9 0.7 %fusion.46 = f32[324,132]{1,0:T(8,128)S(1)} fusion(f32[324,320]{1,0:T(8,128)S(1)} %copy-done.8, f32[320,132]{0,1:T(8,128)S(1)} %fusion.45), kind=kOutput, calls=%fused_computation.146 | convolution fusion | flops 164229120 | bytes 754752 | tf_op jit(solution)/shard_map/dot_general | solution.py:53
  9.2 0.6 %constant_dynamic-update-slice_fusion.7 = f32[512,128]{1,0:T(8,128)} fusion(f32[192,128]{1,0:T(8,128)S(1)} %bitcast.123), kind=kLoop, calls=%fused_computation.111 | loop fusion | bytes 196608
  9.9 0.6 %constant_dynamic-update-slice_fusion.6 = f32[512,128]{1,0:T(8,128)} fusion(f32[512,128]{1,0:T(8,128)} %constant_dynamic-update-slice_fusion.7, f32[96,128]{1,0:T(8,128)S(1)} %bitcast.128), kind=kLoop, calls=%fused_computation.110 | loop fusion | bytes 98304
  10.6 0.6 %constant_dynamic-update-slice_fusion.5 = f32[512,128]{1,0:T(8,128)} fusion(f32[512,128]{1,0:T(8,128)} %constant_dynamic-update-slice_fusion.6, f32[96,128]{1,0:T(8,128)S(1)} %bitcast.127), kind=kLoop, calls=%fused_computation.109 | loop fusion | bytes 98304
  11.2 0.7 %constant_dynamic-update-slice_fusion.4 = f32[512,128]{1,0:T(8,128)} fusion(f32[512,128]{1,0:T(8,128)} %constant_dynamic-update-slice_fusion.5, f32[36,132]{1,0:T(8,128)S(1)} %get-tuple-element.16), kind=kLoop, calls=%fused_computation.108 | loop fusion | bytes 32768
  11.9 0.6 %constant_dynamic-update-slice_fusion.3 = f32[512,128]{1,0:T(8,128)} fusion(f32[512,128]{1,0:T(8,128)} %constant_dynamic-update-slice_fusion.4, f32[96,128]{1,0:T(8,128)S(1)} %bitcast.126), kind=kLoop, calls=%fused_computation.107 | loop fusion | bytes 98304 | tf_op jit(solution)/shard_map/concatenate | solution.py:66
  12.5 2.9 %collective-permute-start.4 = (f32[512,128]{1,0:T(8,128)}, f32[512,128]{1,0:T(8,128)}, u32[]{:S(2)}, u32[]{:S(2)}) collective-permute-start(f32[512,128]{1,0:T(8,128)} %constant_dynamic-update-slice_fusion.3), channel_id=1, source_target_pairs={{0,16},{16,0},{1,17},{17,1},{2,18},{18,2},{3,19},{19,3},{4,20},{20... | collective-permute-start | bytes 786440 | tf_op jit(solution)/shard_map/ppermute | solution.py:61
  15.4 0.1 pad_bitcast_fusion
  15.6 0.1 pad_maximum_fusion
  15.7 0.6 %copy-done.4 = f32[1,9,36,132]{3,2,1,0:T(8,128)} copy-done((f32[1,9,36,132]{3,2,1,0:T(8,128)}, f32[1,9,36,132]{3,2,1,0:T(8,128)S(1)}, u32[]{:S(2)}) %copy-start.4) | copy-done | bytes 171096
  16.3 0.3 slice_bitcast_fusion
  16.6 0.5 %copy.78 = f32[2,4,9,36]{3,2,1,0:T(8,128)S(1)} copy(f32[2,4,9,36]{0,3,2,1:T(8,128)S(1)} %slice_bitcast_fusion) | data formatting | bytes 20736 | tf_op jit(solution)/shard_map/transpose | solution.py:72
  17.2 2.8 %collective-permute-start.1 = (f32[8,324]{1,0:T(8,128)S(1)}, f32[8,324]{1,0:T(8,128)S(1)}, u32[]{:S(2)}, u32[]{:S(2)}) collective-permute-start(f32[8,324]{1,0:T(8,128)S(1)} %reshape.146), channel_id=1, source_target_pairs={{0,7},{1,0},{2,1},{3,2},{4,3},{5,4},{6,5},{7,6},{8,15},{9,8},{10,9... | collective-permute-start | bytes 31112 | tf_op jit(solution)/shard_map/ppermute | solution.py:61
  20.1 0.5 %copy.76 = f32[3,4,9,36]{3,2,1,0:T(8,128)S(1)} copy(f32[3,4,9,36]{0,3,2,1:T(8,128)S(1)} %slice_bitcast_fusion.1) | data formatting | bytes 31104 | tf_op jit(solution)/shard_map/transpose | solution.py:72
  20.8 0.6 %collective-permute-done.1 = f32[8,324]{1,0:T(8,128)S(1)} collective-permute-done((f32[8,324]{1,0:T(8,128)S(1)}, f32[8,324]{1,0:T(8,128)S(1)}, u32[]{:S(2)}, u32[]{:S(2)}) %collective-permute-start.1) | collective-permute-done | bytes 10400 | tf_op jit(solution)/shard_map/ppermute | solution.py:61
  21.5 1.2 %copy.79 = f32[2,4,9,36]{0,3,2,1:T(8,128)} copy(f32[2,4,9,36]{3,2,1,0:T(8,128)S(1)} %reshape.147) | data formatting | bytes 20736 | tf_op jit(solution)/shard_map/reshape | solution.py:77
  22.7 3.1 %collective-permute-done = f32[12,324]{1,0:T(8,128)S(1)} collective-permute-done((f32[12,324]{1,0:T(8,128)S(1)}, f32[12,324]{1,0:T(8,128)S(1)}, u32[]{:S(2)}, u32[]{:S(2)}) %collective-permute-start) | collective-permute-done | bytes 15584 | tf_op jit(solution)/shard_map/ppermute | solution.py:61
  25.9 1.3 %copy.77 = f32[3,4,9,36]{0,3,2,1:T(8,128)} copy(f32[3,4,9,36]{3,2,1,0:T(8,128)S(1)} %reshape.145) | data formatting | bytes 31104 | tf_op jit(solution)/shard_map/reshape | solution.py:77
  27.2 1.7 %pad_add_fusion.1 = f32[4,9,36,132]{3,2,1,0:T(8,128)S(1)} fusion(f32[4,9,36,2]{3,2,1,0:T(8,128)} %bitcast.118, f32[4,9,36,3]{3,2,1,0:T(8,128)} %bitcast.119, f32[1,9,36,132]{3,2,1,0:T(8,128)S(1)} %copy-done.5, f32[1,9,36,132]{3,2,1,0:T(8,128)S(1)} %stack_reshape.11, f32[1,9,36,132]{3,2,1,0:T(8,128)S(1)} %copy-done.1, f32[1,9,36,132]{3,2,1,0:T(8,128)S(1)} %copy-done.3), kind=kLoop, calls=%fused_computation.10 | loop fusion | flops 855360 | bytes 1394496 | tf_op jit(solution)/shard_map/add | solution.py:91
  29.2 1.6 %collective-permute-start.2 = (f32[20,1188]{1,0:T(8,128)S(1)}, f32[20,1188]{1,0:T(8,128)S(1)}, u32[]{:S(2)}, u32[]{:S(2)}) collective-permute-start(f32[20,1188]{1,0:T(8,128)S(1)} %pad_maximum_fusion.4), channel_id=1, source_target_pairs={{0,8},{8,0},{1,9},{9,1},{2,10},{10,2},{3,11},{11,3},{4,12},{12,4},... | collective-permute-start | bytes 285128 | tf_op jit(solution)/shard_map/ppermute | solution.py:61
  30.8 3.4 %collective-permute-done.2 = f32[20,1188]{1,0:T(8,128)S(1)} collective-permute-done((f32[20,1188]{1,0:T(8,128)S(1)}, f32[20,1188]{1,0:T(8,128)S(1)}, u32[]{:S(2)}, u32[]{:S(2)}) %collective-permute-start.2) | collective-permute-done | bytes 95072 | tf_op jit(solution)/shard_map/ppermute | solution.py:61
  34.1 0.1 reshape.151
  34.4 0.2 reshape.150
  34.6 0.1 pad_add_fusion
  34.8 0.2 slice_reduce_fusion.1
  35.1 0.2 slice_reduce_fusion
  35.4 0.2 slice_reduce_fusion.2
  36.6 0.6 %collective-permute-start.3 = (f32[35,128]{1,0:T(8,128)S(1)}, f32[35,128]{1,0:T(8,128)S(1)}, u32[]{:S(2)}, u32[]{:S(2)}) collective-permute-start(f32[35,128]{1,0:T(8,128)S(1)} %pad_maximum_fusion.6), channel_id=1, source_target_pairs={{0,16},{16,0},{1,17},{17,1},{2,18},{18,2},{3,19},{19,3},{4,20},{20... | collective-permute-start | bytes 53768 | tf_op jit(solution)/shard_map/ppermute | solution.py:61
  37.3 3.1 %collective-permute-done.3 = f32[35,128]{1,0:T(8,128)S(1)} collective-permute-done((f32[35,128]{1,0:T(8,128)S(1)}, f32[35,128]{1,0:T(8,128)S(1)}, u32[]{:S(2)}, u32[]{:S(2)}) %collective-permute-start.3) | collective-permute-done | bytes 17952 | tf_op jit(solution)/shard_map/ppermute | solution.py:61
  41.3 0.7 %slice.424 = f32[32,128]{1,0:T(8,128)S(1)} slice(f32[512,128]{1,0:T(8,128)} %collective-permute-done.4), slice={[384:416], [0:128]} | slice | bytes 32768 | tf_op jit(solution)/shard_map/slice | solution.py:201
  42.1 0.9 %fusion.38 = (f32[96,128]{1,0:T(8,128)S(1)}, f32[96,128]{1,0:T(8,128)S(1)}, f32[96,128]{1,0:T(8,128)S(1)}) fusion(f32[512,128]{1,0:T(8,128)} %collective-permute-done.4), kind=kLoop, calls=%fused_computation.138 | loop fusion | bytes 294912 | tf_op jit(solution)/shard_map/slice | solution.py:200
  43.2 0.9 %slice.417 = f32[192,128]{1,0:T(8,128)S(1)} slice(f32[512,128]{1,0:T(8,128)} %collective-permute-done.4), slice={[0:192], [0:128]} | slice | bytes 196608 | tf_op jit(solution)/shard_map/slice | solution.py:198
  44.4 0.1 fusion
  44.5 2.0 %fusion.5 = f32[3,8,32,128]{3,2,1,0:T(8,128)} fusion(f32[3,7,36,132]{3,2,1,0:T(8,128)S(1)} %slice_multiply_fusion, f32[3,1,36,132]{3,2,1,0:T(8,128)S(1)} %fusion.32, f32[3,1,32,128]{3,2,1,0:T(8,128)S(1)} %select_select_fusion.1, f32[3,1,36,132]{3,2,1,0:T(8,128)S(1)} %pad.56, f32[3,10,36,132]{3,2,1,0:T(8,128)S(1)} %fusion), kind=kLoop, calls=%fused_computation.33 | loop fusion | flops 3440640 | bytes 1742016 | tf_op jit(solution)/shard_map/mul | solution.py:147
  (120 shorter events, 5.2 us)
Async XLA Ops:
  0.0 3.2 %copy-start.12 = (f32[128,132]{1,0:T(8,128)S(1)}, f32[128,132]{1,0:T(8,128)}, u32[]{:S(2)}) copy-start(f32[128,132]{1,0:T(8,128)} %constant.32.clone) | copy-start | bytes 202756
  1.0 2.7 %copy-start.6 = (f32[324,400]{1,0:T(8,128)S(1)}, f32[324,400]{1,0:T(8,128)}, u32[]{:S(2)}) copy-start(f32[324,400]{1,0:T(8,128)} %constant.33.clone) | copy-start | bytes 1555204
  3.6 1.4 %copy-start.10 = (f32[2,5,8,4,160]{4,3,2,1,0:T(4,128)S(1)}, f32[2,5,8,4,160]{4,3,2,1,0:T(4,128)}, u32[]{:S(2)}) copy-start(f32[2,5,8,4,160]{4,3,2,1,0:T(4,128)} %param.12) | copy-start | bytes 614404
  4.3 0.9 %copy-start.7 = (f32[160,132]{1,0:T(8,128)S(1)}, f32[160,132]{1,0:T(8,128)}, u32[]{:S(2)}) copy-start(f32[160,132]{1,0:T(8,128)} %constant.12.clone) | copy-start | bytes 253444
  4.5 1.4 %copy-start.9 = (f32[324,320]{1,0:T(8,128)S(1)}, f32[324,320]{1,0:T(8,128)}, u32[]{:S(2)}) copy-start(f32[324,320]{1,0:T(8,128)} %constant.31.clone) | copy-start | bytes 1244164
  5.1 1.6 %copy-start.11 = (f32[2,4,8,5,160]{4,2,3,1,0:T(8,128)S(1)}, f32[2,4,8,5,160]{4,2,3,1,0:T(8,128)}, u32[]{:S(2)}) copy-start(f32[2,4,8,5,160]{4,2,3,1,0:T(8,128)} %param.11) | copy-start | bytes 614404
  6.7 8.9 %copy-start = (f32[1,9,36,132]{3,2,1,0:T(8,128)}, f32[1,9,36,132]{3,2,1,0:T(8,128)S(1)}, u32[]{:S(2)}) copy-start(f32[1,9,36,132]{3,2,1,0:T(8,128)S(1)} %stack_reshape.10) | copy-start | bytes 513220
  6.7 1.2 %copy-start.8 = (f32[324,320]{1,0:T(8,128)S(1)}, f32[324,320]{1,0:T(8,128)}, u32[]{:S(2)}) copy-start(f32[324,320]{1,0:T(8,128)} %constant.30.clone) | copy-start | bytes 1244164
  8.6 7.0 %copy-start.2 = (f32[1,9,36,132]{3,2,1,0:T(8,128)}, f32[1,9,36,132]{3,2,1,0:T(8,128)S(1)}, u32[]{:S(2)}) copy-start(f32[1,9,36,132]{3,2,1,0:T(8,128)S(1)} %stack_reshape.9) | copy-start | bytes 513220
  12.5 28.9 %collective-permute-start.4 = (f32[512,128]{1,0:T(8,128)}, f32[512,128]{1,0:T(8,128)}, u32[]{:S(2)}, u32[]{:S(2)}) collective-permute-start(f32[512,128]{1,0:T(8,128)} %constant_dynamic-update-slice_fusion.3), channel_id=1, source_target_pairs={{0,16},{16,0},{1,17},{17,1},{2,18},{18,2},{3,19},{19,3},{4,20},{20... | collective-permute-start | bytes 786440 | tf_op jit(solution)/shard_map/ppermute | solution.py:61
  15.6 0.7 %copy-start.4 = (f32[1,9,36,132]{3,2,1,0:T(8,128)}, f32[1,9,36,132]{3,2,1,0:T(8,128)S(1)}, u32[]{:S(2)}) copy-start(f32[1,9,36,132]{3,2,1,0:T(8,128)S(1)} %pad_bitcast_fusion) | copy-start | bytes 513220
  17.2 4.2 %collective-permute-start.1 = (f32[8,324]{1,0:T(8,128)S(1)}, f32[8,324]{1,0:T(8,128)S(1)}, u32[]{:S(2)}, u32[]{:S(2)}) collective-permute-start(f32[8,324]{1,0:T(8,128)S(1)} %reshape.146), channel_id=1, source_target_pairs={{0,7},{1,0},{2,1},{3,2},{4,3},{5,4},{6,5},{7,6},{8,15},{9,8},{10,9... | collective-permute-start | bytes 31112 | tf_op jit(solution)/shard_map/ppermute | solution.py:61
  20.0 7.1 %copy-start.1 = (f32[1,9,36,132]{3,2,1,0:T(8,128)S(1)}, f32[1,9,36,132]{3,2,1,0:T(8,128)}, u32[]{:S(2)}) copy-start(f32[1,9,36,132]{3,2,1,0:T(8,128)} %copy-done) | copy-start | bytes 513220
  20.0 7.1 %copy-start.3 = (f32[1,9,36,132]{3,2,1,0:T(8,128)S(1)}, f32[1,9,36,132]{3,2,1,0:T(8,128)}, u32[]{:S(2)}) copy-start(f32[1,9,36,132]{3,2,1,0:T(8,128)} %copy-done.2) | copy-start | bytes 513220
  20.0 7.1 %copy-start.5 = (f32[1,9,36,132]{3,2,1,0:T(8,128)S(1)}, f32[1,9,36,132]{3,2,1,0:T(8,128)}, u32[]{:S(2)}) copy-start(f32[1,9,36,132]{3,2,1,0:T(8,128)} %copy-done.4) | copy-start | bytes 513220
  20.7 5.1 %collective-permute-start = (f32[12,324]{1,0:T(8,128)S(1)}, f32[12,324]{1,0:T(8,128)S(1)}, u32[]{:S(2)}, u32[]{:S(2)}) collective-permute-start(f32[12,324]{1,0:T(8,128)S(1)} %reshape.144), channel_id=1, source_target_pairs={{0,1},{1,2},{2,3},{3,4},{4,5},{5,6},{6,7},{7,0},{8,9},{9,10},{10,1... | collective-permute-start | bytes 46664 | tf_op jit(solution)/shard_map/ppermute | solution.py:61
  29.2 4.9 %collective-permute-start.2 = (f32[20,1188]{1,0:T(8,128)S(1)}, f32[20,1188]{1,0:T(8,128)S(1)}, u32[]{:S(2)}, u32[]{:S(2)}) collective-permute-start(f32[20,1188]{1,0:T(8,128)S(1)} %pad_maximum_fusion.4), channel_id=1, source_target_pairs={{0,8},{8,0},{1,9},{9,1},{2,10},{10,2},{3,11},{11,3},{4,12},{12,4},... | collective-permute-start | bytes 285128 | tf_op jit(solution)/shard_map/ppermute | solution.py:61
  36.6 3.8 %collective-permute-start.3 = (f32[35,128]{1,0:T(8,128)S(1)}, f32[35,128]{1,0:T(8,128)S(1)}, u32[]{:S(2)}, u32[]{:S(2)}) collective-permute-start(f32[35,128]{1,0:T(8,128)S(1)} %pad_maximum_fusion.6), channel_id=1, source_target_pairs={{0,16},{16,0},{1,17},{17,1},{2,18},{18,2},{3,19},{19,3},{4,20},{20... | collective-permute-start | bytes 53768 | tf_op jit(solution)/shard_map/ppermute | solution.py:61

commit v5 on v3

--- a/solution.py
+++ b/solution.py
@@ -46,11 +46,12 @@
     precise = lax.Precision.HIGHEST
     orient = jnp.repeat((1 - 2 * flip).astype(jnp.float32), size_z, axis=2)
     signed = (coef * orient[:, None, :, None, :]).reshape(ex_count * size_x * ey_count * size_y, merged)
-    plane_map = np.kron(assembly_matrix(table_x, ex_count), assembly_matrix(table_y, ey_count))
-    depth_map = assembly_matrix(table_z, ez_count)
+    rows_y = np.pad(assembly_matrix(table_y, ey_count), ((2, 1), (0, 0)))
+    plane_map = np.kron(assembly_matrix(table_x, ex_count), rows_y)
+    depth_map = np.pad(assembly_matrix(table_z, ez_count), ((2, 1), (0, 0)))
     deep = jnp.dot(signed, jnp.asarray(depth_map.T, jnp.float32), precision=precise)
     nodal = jnp.dot(jnp.asarray(plane_map, jnp.float32), deep, precision=precise)
-    return nodal.reshape(4 * ex_count + 1, 4 * ey_count + 1, 4 * ez_count + 1)
+    return nodal.reshape(4 * ex_count + 1, 4 * ey_count + 4, 4 * ez_count + 4)
 
 
 def shifted(block, axis, step=1):
@@ -76,22 +77,20 @@
     return jnp.moveaxis(rows.reshape(shape), 0, dim)
 
 
-def fold_and_halo(partial, axis, dim):
-    n = partial.shape[dim] - 1
-    up, up_shape = to_wire(lax.slice_in_dim(partial, n - 2, n + 1, axis=dim), dim)
-    down, down_shape = to_wire(lax.slice_in_dim(partial, 0, 2, axis=dim), dim)
+def fold_and_halo(extended, axis, dim):
+    length = extended.shape[dim]
+    n = length - 4
+    up, up_shape = to_wire(lax.slice_in_dim(extended, n, n + 3, axis=dim), dim)
+    down, down_shape = to_wire(lax.slice_in_dim(extended, 2, 4, axis=dim), dim)
     from_prev, from_next = both_ways(up, down, axis)
-    from_prev = from_wire(from_prev, up_shape, dim)
-    from_next = from_wire(from_next, down_shape, dim)
-    return jnp.concatenate(
-        [
-            lax.slice_in_dim(from_prev, 0, 2, axis=dim),
-            lax.slice_in_dim(partial, 0, 1, axis=dim) + lax.slice_in_dim(from_prev, 2, 3, axis=dim),
-            lax.slice_in_dim(partial, 1, n, axis=dim),
-            lax.slice_in_dim(partial, n, n + 1, axis=dim) + lax.slice_in_dim(from_next, 0, 1, axis=dim),
-            lax.slice_in_dim(from_next, 1, 2, axis=dim),
-        ],
-        axis=dim,
+    widths_prev = [(0, 0)] * extended.ndim
+    widths_prev[dim] = (0, length - 3)
+    widths_next = [(0, 0)] * extended.ndim
+    widths_next[dim] = (n + 2, 0)
+    return (
+        extended
+        + jnp.pad(from_wire(from_prev, up_shape, dim), widths_prev)
+        + jnp.pad(from_wire(from_next, down_shape, dim), widths_next)
     )
 
 
@@ -186,7 +185,7 @@
     nodal_x = interpolate(edge_coeffs_x, flips[0], open_map, closed_map, closed_map)
     nodal_y = interpolate(edge_coeffs_y, flips[1], closed_map, open_map, closed_map)
     nodal_z = interpolate(edge_coeffs_z, flips[2], closed_map, closed_map, open_map)
-    keep = jnp.pad((1 - flags).astype(jnp.float32), ((0, 1), (0, 1), (0, 1)))
+    keep = jnp.pad((1 - flags).astype(jnp.float32), ((0, 1), (2, 2), (2, 2)))
     extended = jnp.stack([nodal_x, nodal_y, nodal_z, keep])
     extended = fold_and_halo(extended, "gz", 3)
     extended = fold_and_halo(extended, "gy", 2)

time: 42.6 us -> 40.8 us (0.958)
  local copies, waits for them, and re-layouts: 13.3 us -> 9.23 us
  waiting for transfers between devices: 10 us -> 11.3 us
  other arithmetic: 6.64 us -> 7.43 us
    concatenate x2 -> x0, local copies, waits for them, and re-layouts: 4.96 us -> none  [fold_and_halo(): jnp.concatenate([lax.slice_in_dim(from_prev, 0, 2, axis=dim), lax.slice_i...]
    reshape x8, local copies, waits for them, and re-layouts: 1.34 us -> 3.09 us  [from_wire(): return jnp.moveaxis(rows.reshape(shape), 0, dim)]
    slice x3 -> x0, local copies, waits for them, and re-layouts: 1.32 us -> none  [the longest x2 1.29 us: fold_and_halo(): lax.slice_in_dim(partial, 1, n, axis=dim)]
    ppermute x4, waiting for transfers between devices: 10 us -> 11.3 us  [shifted(): lax.ppermute(block, axis, [(i, (i + step) % count) for i in range(count)])]
    convert_element_type x1, other arithmetic: 0.01 us -> 0.93 us  [body(): keep = jnp.pad((1 - flags).astype(jnp.float32), ((0, 1), (2, 2), (2, 2)))]
    unnamed x16 -> x26, local copies, waits for them, and re-layouts: 0.56 us -> 0.93 us
where the time goes in v5:
time: 40.8 us; the launch traced here: 40.6 us
  waiting for transfers between devices  11.3 us (28%)
  local copies, waits for them, and re-layouts  9.23 us (23%)
  starting transfers between devices  8.2 us (20%)
  other arithmetic  7.43 us (18%)
  matrix products  3.8 us (9%)
  between operations  0.59 us (1%)
    ppermute x4, waiting for transfers between devices, shifted(): lax.ppermute(block, axis, [(i, (i + step) % count) for i in range(count)])  11.3 us
    ppermute x4, starting transfers between devices, shifted(): lax.ppermute(block, axis, [(i, (i + step) % count) for i in range(count)])  8.2 us
    reshape x8, local copies, waits for them, and re-layouts, from_wire(): return jnp.moveaxis(rows.reshape(shape), 0, dim)  3.09 us
    dot_general x3, matrix products, interpolate(): jnp.dot(jnp.asarray(plane_map, jnp.float32), deep, precision=precise)  2.08 us
    mul x1, other arithmetic, stencil_apply(): return 0.25 * total  2.05 us
    add x2, other arithmetic, fold_and_halo(): extended + jnp.pad(from_wire(from_prev, up_shape, dim), widths_prev)  1.77 us
    dot_general x3, matrix products, interpolate(): jnp.dot(signed, jnp.asarray(depth_map.T, jnp.float32), precision=precise)  1.72 us
    transpose x8, local copies, waits for them, and re-layouts, to_wire(): layers = jnp.moveaxis(slab, dim, 0)  1.48 us
  transfers between devices with their start and end apart: 4, of which 3 were waited for; matrix products, arithmetic and copies ran while one was open for 6% of the time, Pallas kernels for 0%

profile of v5, /device:TPU:0, one launch (start us, length us, event | category | flops | bytes accessed | tf_op | source)
XLA Modules:
  0.0 40.6 jit_solution(9650048247933435911)
XLA Ops:
  0.0 0.8 %convert_bitcast_fusion.2 = (f32[2,8,32]{2,1,0:T(8,128)S(1)}, f32[2,8,32]{2,1,0:T(8,128)S(1)}, f32[2,8,32]{2,1,0:T(8,128)S(1)}) fusion(s32[3,2,8,32]{3,2,1,0:T(8,128)} %param.14), kind=kLoop, calls=%fused_computation.84 | loop fusion | flops 4608 | bytes 12288 | tf_op jit(solution)/shard_map/convert_element_type | solution.py:47
  1.0 0.9 %subtract_convert_fusion = f32[8,32,128]{2,1,0:T(8,128)S(1)} fusion(s32[8,32,128]{2,1,0:T(8,128)} %param.15), kind=kLoop, calls=%fused_computation.65 | loop fusion | flops 65536 | bytes 262144 | tf_op jit(solution)/shard_map/convert_element_type | solution.py:188
  1.9 0.9 %broadcast_multiply_fusion.2 = f32[2,5,8,5,128]{4,2,3,1,0:T(8,128)S(1)} fusion(f32[2,5,8,5,128]{4,2,3,1,0:T(8,128)} %param.13, f32[2,8,128]{2,1,0:T(8,128)S(1)} %copy.47), kind=kLoop, calls=%fused_computation.72 | loop fusion | flops 51200 | bytes 417792 | tf_op jit(solution)/shard_map/mul | solution.py:48
  3.0 0.4 %fusion.40 = f32[400,132]{0,1:T(8,128)S(1)} fusion(f32[400,128]{1,0:T(8,128)S(1)} %reshape.98, f32[128,132]{1,0:T(8,128)S(1)} %copy-done.12), kind=kOutput, calls=%fused_computation.98 | convolution fusion | flops 81100800 | bytes 483584 | tf_op jit(solution)/shard_map/dot_general | solution.py:52
  3.5 0.7 %fusion.41 = f32[324,132]{1,0:T(8,128)S(1)} fusion(f32[324,400]{1,0:T(8,128)S(1)} %copy-done.6, f32[400,132]{0,1:T(8,128)S(1)} %fusion.40), kind=kOutput, calls=%fused_computation.99 | convolution fusion | flops 205286400 | bytes 900672 | tf_op jit(solution)/shard_map/dot_general | solution.py:53
  4.2 0.1 pad_bitcast_fusion
  4.4 0.1 broadcast_in_dim.16
  4.5 0.2 mul.120
  4.7 0.1 broadcast_in_dim.17
  4.8 0.2 mul.124
  5.1 0.1 reshape.97
  5.2 0.6 %fusion.38 = f32[320,132]{0,1:T(8,128)S(1)} fusion(f32[320,160]{1,0:T(8,128)S(1)} %reshape.97, f32[160,132]{1,0:T(8,128)S(1)} %copy-done.7), kind=kOutput, calls=%fused_computation.96 | convolution fusion | flops 81100800 | bytes 458240 | tf_op jit(solution)/shard_map/dot_general | solution.py:52
  5.9 0.7 %fusion.39 = f32[324,132]{1,0:T(8,128)S(1)} fusion(f32[324,320]{1,0:T(8,128)S(1)} %copy-done.9, f32[320,132]{0,1:T(8,128)S(1)} %fusion.38), kind=kOutput, calls=%fused_computation.97 | convolution fusion | flops 164229120 | bytes 754752 | tf_op jit(solution)/shard_map/dot_general | solution.py:53
  6.7 0.1 copy.43
  6.9 0.6 %fusion.36 = f32[320,132]{0,1:T(8,128)S(1)} fusion(f32[320,160]{1,0:T(8,128)S(1)} %reshape.96, f32[160,132]{1,0:T(8,128)S(1)} %copy-done.7), kind=kOutput, calls=%fused_computation.94 | convolution fusion | flops 81100800 | bytes 458240 | tf_op jit(solution)/shard_map/dot_general | solution.py:52
  7.5 0.3 copy-done.8
  7.8 0.7 %fusion.37 = f32[324,132]{1,0:T(8,128)S(1)} fusion(f32[324,320]{1,0:T(8,128)S(1)} %copy-done.8, f32[320,132]{0,1:T(8,128)S(1)} %fusion.36), kind=kOutput, calls=%fused_computation.95 | convolution fusion | flops 164229120 | bytes 754752 | tf_op jit(solution)/shard_map/dot_general | solution.py:53
  8.6 0.1 pad_maximum_fusion
  8.7 0.6 %copy-done.4 = f32[1,9,36,132]{3,2,1,0:T(8,128)} copy-done((f32[1,9,36,132]{3,2,1,0:T(8,128)}, f32[1,9,36,132]{3,2,1,0:T(8,128)S(1)}, u32[]{:S(2)}) %copy-start.4) | copy-done | bytes 171096
  9.4 0.5 %copy.50 = f32[3,4,9,36]{3,2,1,0:T(8,128)S(1)} copy(f32[3,4,9,36]{0,3,2,1:T(8,128)S(1)} %slice_bitcast_fusion.1) | data formatting | bytes 31104 | tf_op jit(solution)/shard_map/transpose | solution.py:72
  9.9 0.1 reshape.99
  10.0 0.5 %collective-permute-start = (f32[12,324]{1,0:T(8,128)S(1)}, f32[12,324]{1,0:T(8,128)S(1)}, u32[]{:S(2)}, u32[]{:S(2)}) collective-permute-start(f32[12,324]{1,0:T(8,128)S(1)} %reshape.99), channel_id=1, source_target_pairs={{0,1},{1,2},{2,3},{3,4},{4,5},{5,6},{6,7},{7,0},{8,9},{9,10},{10,1... | collective-permute-start | bytes 46664 | tf_op jit(solution)/shard_map/ppermute | solution.py:61
  10.5 0.3 slice_bitcast_fusion
  10.8 0.5 %copy.52 = f32[2,4,9,36]{3,2,1,0:T(8,128)S(1)} copy(f32[2,4,9,36]{0,3,2,1:T(8,128)S(1)} %slice_bitcast_fusion) | data formatting | bytes 20736 | tf_op jit(solution)/shard_map/transpose | solution.py:72
  11.4 4.1 %collective-permute-start.1 = (f32[8,324]{1,0:T(8,128)S(1)}, f32[8,324]{1,0:T(8,128)S(1)}, u32[]{:S(2)}, u32[]{:S(2)}) collective-permute-start(f32[8,324]{1,0:T(8,128)S(1)} %reshape.101), channel_id=1, source_target_pairs={{0,7},{1,0},{2,1},{3,2},{4,3},{5,4},{6,5},{7,6},{8,15},{9,8},{10,9... | collective-permute-start | bytes 31112 | tf_op jit(solution)/shard_map/ppermute | solution.py:61
  15.5 1.4 %collective-permute-done.1 = f32[8,324]{1,0:T(8,128)S(1)} collective-permute-done((f32[8,324]{1,0:T(8,128)S(1)}, f32[8,324]{1,0:T(8,128)S(1)}, u32[]{:S(2)}, u32[]{:S(2)}) %collective-permute-start.1) | collective-permute-done | bytes 10400 | tf_op jit(solution)/shard_map/ppermute | solution.py:61
  17.0 1.2 %copy.53 = f32[2,4,9,36]{0,3,2,1:T(8,128)} copy(f32[2,4,9,36]{3,2,1,0:T(8,128)S(1)} %reshape.102) | data formatting | bytes 20736 | tf_op jit(solution)/shard_map/reshape | solution.py:77
  18.3 1.3 %copy.51 = f32[3,4,9,36]{0,3,2,1:T(8,128)} copy(f32[3,4,9,36]{3,2,1,0:T(8,128)S(1)} %reshape.100) | data formatting | bytes 31104 | tf_op jit(solution)/shard_map/reshape | solution.py:77
  19.6 1.6 %pad_add_fusion.1 = f32[4,9,36,132]{3,2,1,0:T(8,128)S(1)} fusion(f32[4,9,36,2]{3,2,1,0:T(8,128)} %bitcast.78, f32[4,9,36,3]{3,2,1,0:T(8,128)} %bitcast.79, f32[1,9,36,132]{3,2,1,0:T(8,128)S(1)} %copy-done.1, f32[1,9,36,132]{3,2,1,0:T(8,128)S(1)} %stack_reshape.11, f32[1,9,36,132]{3,2,1,0:T(8,128)S(1)} %copy-done.3, f32[1,9,36,132]{3,2,1,0:T(8,128)S(1)} %copy-done.5), kind=kLoop, calls=%fused_computation.10 | loop fusion | flops 855360 | bytes 1394496 | tf_op jit(solution)/shard_map/add | solution.py:91
  21.3 0.1 reshape.104
  21.5 0.1 reshape.103
  21.6 2.1 %collective-permute-start.2 = (f32[20,1188]{1,0:T(8,128)S(1)}, f32[20,1188]{1,0:T(8,128)S(1)}, u32[]{:S(2)}, u32[]{:S(2)}) collective-permute-start(f32[20,1188]{1,0:T(8,128)S(1)} %pad_maximum_fusion.4), channel_id=1, source_target_pairs={{0,8},{8,0},{1,9},{9,1},{2,10},{10,2},{3,11},{11,3},{4,12},{12,4},... | collective-permute-start | bytes 285128 | tf_op jit(solution)/shard_map/ppermute | solution.py:61
  23.7 3.6 %collective-permute-done.2 = f32[20,1188]{1,0:T(8,128)S(1)} collective-permute-done((f32[20,1188]{1,0:T(8,128)S(1)}, f32[20,1188]{1,0:T(8,128)S(1)}, u32[]{:S(2)}, u32[]{:S(2)}) %collective-permute-start.2) | collective-permute-done | bytes 95072 | tf_op jit(solution)/shard_map/ppermute | solution.py:61
  27.3 0.1 reshape.106
  27.5 0.2 reshape.105
  27.7 0.1 pad_add_fusion
  28.7 0.1 copy.60
  28.8 0.1 slice_multiply_fusion.1
  29.0 0.6 %concatenate.50 = f32[527,128]{1,0:T(8,128)S(1)} concatenate(f32[192,128]{1,0:T(8,128)S(1)} %bitcast.84, f32[96,128]{1,0:T(8,128)S(1)} %bitcast.87, f32[12,128]{1,0:T(8,128)S(1)} %reshape.109, f32[3,128]{1,0:T(4,128)S(1)} %reshape.110, f32[96,128]{1,0:T(8,128)S(1)} %bitcast.88, f32[32,128]{1,0:T(8,128)S(1)} %slice.264, f32[96,128]{1,0:T(8,128)S(1)} %bitcast.86), dimensions={0} | concatenate | bytes 539648 | tf_op jit(solution)/shard_map/concatenate | solution.py:66
  29.6 1.6 %collective-permute-start.3 = (f32[527,128]{1,0:T(8,128)S(1)}, f32[527,128]{1,0:T(8,128)S(1)}, u32[]{:S(2)}, u32[]{:S(2)}) collective-permute-start(f32[527,128]{1,0:T(8,128)S(1)} %concatenate.50), channel_id=1, source_target_pairs={{0,16},{16,0},{1,17},{17,1},{2,18},{18,2},{3,19},{19,3},{4,20},{20... | collective-permute-start | bytes 809480 | tf_op jit(solution)/shard_map/ppermute | solution.py:61
  31.2 0.1 slice_multiply_fusion
  31.3 6.3 %collective-permute-done.3 = f32[527,128]{1,0:T(8,128)S(1)} collective-permute-done((f32[527,128]{1,0:T(8,128)S(1)}, f32[527,128]{1,0:T(8,128)S(1)}, u32[]{:S(2)}, u32[]{:S(2)}) %collective-permute-start.3) | collective-permute-done | bytes 269856 | tf_op jit(solution)/shard_map/ppermute | solution.py:61
  37.6 0.1 reshape_reshape.3
  37.7 0.1 copy.61
  38.1 0.1 pad.46
  38.2 0.1 maximum_bitcast_fusion
  38.4 0.1 fusion
  38.5 2.0 %fusion.5 = f32[3,8,32,128]{3,2,1,0:T(8,128)} fusion(f32[3,7,36,132]{3,2,1,0:T(8,128)S(1)} %slice_multiply_fusion, f32[3,1,36,132]{3,2,1,0:T(8,128)S(1)} %fusion.30, f32[3,1,32,128]{3,2,1,0:T(8,128)S(1)} %bitcast.91, f32[3,1,36,132]{3,2,1,0:T(8,128)S(1)} %pad.46, f32[3,10,36,132]{3,2,1,0:T(8,128)S(1)} %fusion), kind=kLoop, calls=%fused_computation.29 | loop fusion | flops 3440640 | bytes 1742016 | tf_op jit(solution)/shard_map/mul | solution.py:179
  (78 shorter events, 2.4 us)
Async XLA Ops:
  0.0 3.0 %copy-start.12 = (f32[128,132]{1,0:T(8,128)S(1)}, f32[128,132]{1,0:T(8,128)}, u32[]{:S(2)}) copy-start(f32[128,132]{1,0:T(8,128)} %constant.29.clone) | copy-start | bytes 202756
  0.0 3.4 %copy-start.6 = (f32[324,400]{1,0:T(8,128)S(1)}, f32[324,400]{1,0:T(8,128)}, u32[]{:S(2)}) copy-start(f32[324,400]{1,0:T(8,128)} %constant.30.clone) | copy-start | bytes 1555204
  3.4 1.5 %copy-start.10 = (f32[2,5,8,4,160]{4,3,2,1,0:T(4,128)S(1)}, f32[2,5,8,4,160]{4,3,2,1,0:T(4,128)}, u32[]{:S(2)}) copy-start(f32[2,5,8,4,160]{4,3,2,1,0:T(4,128)} %param.12) | copy-start | bytes 614404
  4.2 1.0 %copy-start.7 = (f32[160,132]{1,0:T(8,128)S(1)}, f32[160,132]{1,0:T(8,128)}, u32[]{:S(2)}) copy-start(f32[160,132]{1,0:T(8,128)} %constant.26.clone) | copy-start | bytes 253444
  4.4 4.2 %copy-start = (f32[1,9,36,132]{3,2,1,0:T(8,128)}, f32[1,9,36,132]{3,2,1,0:T(8,128)S(1)}, u32[]{:S(2)}) copy-start(f32[1,9,36,132]{3,2,1,0:T(8,128)S(1)} %pad_bitcast_fusion) | copy-start | bytes 513220
  4.5 1.4 %copy-start.9 = (f32[324,320]{1,0:T(8,128)S(1)}, f32[324,320]{1,0:T(8,128)}, u32[]{:S(2)}) copy-start(f32[324,320]{1,0:T(8,128)} %constant.28.clone) | copy-start | bytes 1244164
  5.1 1.6 %copy-start.11 = (f32[2,4,8,5,160]{4,2,3,1,0:T(8,128)S(1)}, f32[2,4,8,5,160]{4,2,3,1,0:T(8,128)}, u32[]{:S(2)}) copy-start(f32[2,4,8,5,160]{4,2,3,1,0:T(8,128)} %param.11) | copy-start | bytes 614404
  6.6 1.9 %copy-start.2 = (f32[1,9,36,132]{3,2,1,0:T(8,128)}, f32[1,9,36,132]{3,2,1,0:T(8,128)S(1)}, u32[]{:S(2)}) copy-start(f32[1,9,36,132]{3,2,1,0:T(8,128)S(1)} %stack_reshape.10) | copy-start | bytes 513220
  6.6 1.2 %copy-start.8 = (f32[324,320]{1,0:T(8,128)S(1)}, f32[324,320]{1,0:T(8,128)}, u32[]{:S(2)}) copy-start(f32[324,320]{1,0:T(8,128)} %constant.27.clone) | copy-start | bytes 1244164
  8.6 0.8 %copy-start.4 = (f32[1,9,36,132]{3,2,1,0:T(8,128)}, f32[1,9,36,132]{3,2,1,0:T(8,128)S(1)}, u32[]{:S(2)}) copy-start(f32[1,9,36,132]{3,2,1,0:T(8,128)S(1)} %stack_reshape.9) | copy-start | bytes 513220
  10.0 8.2 %collective-permute-start = (f32[12,324]{1,0:T(8,128)S(1)}, f32[12,324]{1,0:T(8,128)S(1)}, u32[]{:S(2)}, u32[]{:S(2)}) collective-permute-start(f32[12,324]{1,0:T(8,128)S(1)} %reshape.99), channel_id=1, source_target_pairs={{0,1},{1,2},{2,3},{3,4},{4,5},{5,6},{6,7},{7,0},{8,9},{9,10},{10,1... | collective-permute-start | bytes 46664 | tf_op jit(solution)/shard_map/ppermute | solution.py:61
  10.8 8.8 %copy-start.1 = (f32[1,9,36,132]{3,2,1,0:T(8,128)S(1)}, f32[1,9,36,132]{3,2,1,0:T(8,128)}, u32[]{:S(2)}) copy-start(f32[1,9,36,132]{3,2,1,0:T(8,128)} %copy-done) | copy-start | bytes 513220
  10.8 8.8 %copy-start.3 = (f32[1,9,36,132]{3,2,1,0:T(8,128)S(1)}, f32[1,9,36,132]{3,2,1,0:T(8,128)}, u32[]{:S(2)}) copy-start(f32[1,9,36,132]{3,2,1,0:T(8,128)} %copy-done.2) | copy-start | bytes 513220
  10.8 8.8 %copy-start.5 = (f32[1,9,36,132]{3,2,1,0:T(8,128)S(1)}, f32[1,9,36,132]{3,2,1,0:T(8,128)}, u32[]{:S(2)}) copy-start(f32[1,9,36,132]{3,2,1,0:T(8,128)} %copy-done.4) | copy-start | bytes 513220
  11.4 5.5 %collective-permute-start.1 = (f32[8,324]{1,0:T(8,128)S(1)}, f32[8,324]{1,0:T(8,128)S(1)}, u32[]{:S(2)}, u32[]{:S(2)}) collective-permute-start(f32[8,324]{1,0:T(8,128)S(1)} %reshape.101), channel_id=1, source_target_pairs={{0,7},{1,0},{2,1},{3,2},{4,3},{5,4},{6,5},{7,6},{8,15},{9,8},{10,9... | collective-permute-start | bytes 31112 | tf_op jit(solution)/shard_map/ppermute | solution.py:61
  21.6 5.7 %collective-permute-start.2 = (f32[20,1188]{1,0:T(8,128)S(1)}, f32[20,1188]{1,0:T(8,128)S(1)}, u32[]{:S(2)}, u32[]{:S(2)}) collective-permute-start(f32[20,1188]{1,0:T(8,128)S(1)} %pad_maximum_fusion.4), channel_id=1, source_target_pairs={{0,8},{8,0},{1,9},{9,1},{2,10},{10,2},{3,11},{11,3},{4,12},{12,4},... | collective-permute-start | bytes 285128 | tf_op jit(solution)/shard_map/ppermute | solution.py:61
  29.6 8.0 %collective-permute-start.3 = (f32[527,128]{1,0:T(8,128)S(1)}, f32[527,128]{1,0:T(8,128)S(1)}, u32[]{:S(2)}, u32[]{:S(2)}) collective-permute-start(f32[527,128]{1,0:T(8,128)S(1)} %concatenate.50), channel_id=1, source_target_pairs={{0,16},{16,0},{1,17},{17,1},{2,18},{18,2},{3,19},{19,3},{4,20},{20... | collective-permute-start | bytes 809480 | tf_op jit(solution)/shard_map/ppermute | solution.py:61

commit v6 on v5

--- a/solution.py
+++ b/solution.py
@@ -39,19 +39,17 @@
     return matrix
 
 
-def interpolate(coef, flip, table_x, table_y, table_z):
+def planar_part(coef, flip, table_x, table_y, size_z):
     ex_count, size_x, ey_count, size_y, merged = coef.shape
-    size_z = table_z.shape[1]
-    ez_count = merged // size_z
-    precise = lax.Precision.HIGHEST
     orient = jnp.repeat((1 - 2 * flip).astype(jnp.float32), size_z, axis=2)
     signed = (coef * orient[:, None, :, None, :]).reshape(ex_count * size_x * ey_count * size_y, merged)
     rows_y = np.pad(assembly_matrix(table_y, ey_count), ((2, 1), (0, 0)))
     plane_map = np.kron(assembly_matrix(table_x, ex_count), rows_y)
-    depth_map = np.pad(assembly_matrix(table_z, ez_count), ((2, 1), (0, 0)))
-    deep = jnp.dot(signed, jnp.asarray(depth_map.T, jnp.float32), precision=precise)
-    nodal = jnp.dot(jnp.asarray(plane_map, jnp.float32), deep, precision=precise)
-    return nodal.reshape(4 * ex_count + 1, 4 * ey_count + 4, 4 * ez_count + 4)
+    return jnp.dot(jnp.asarray(plane_map, jnp.float32), signed, precision=lax.Precision.HIGHEST)
+
+
+def depth_map_of(table_z, merged):
+    return np.pad(assembly_matrix(table_z, merged // table_z.shape[1]), ((2, 1), (0, 0)))
 
 
 def shifted(block, axis, step=1):
@@ -182,12 +180,48 @@
 def body(edge_coeffs_x, edge_coeffs_y, edge_coeffs_z, flips, flags):
     closed_map, open_map = basis_tables()
     nx, ny, nz = flags.shape
-    nodal_x = interpolate(edge_coeffs_x, flips[0], open_map, closed_map, closed_map)
-    nodal_y = interpolate(edge_coeffs_y, flips[1], closed_map, open_map, closed_map)
-    nodal_z = interpolate(edge_coeffs_z, flips[2], closed_map, closed_map, open_map)
+    precise = lax.Precision.HIGHEST
+    inputs = [
+        (edge_coeffs_x, flips[0], open_map, closed_map, closed_map),
+        (edge_coeffs_y, flips[1], closed_map, open_map, closed_map),
+        (edge_coeffs_z, flips[2], closed_map, closed_map, open_map),
+    ]
+    length = nz + 4
+    up_places = [nz, nz + 1, nz + 2]
+    down_places = [2, 3]
+    planars = []
+    depths = []
+    slabs = []
+    for coef, flip, table_x, table_y, table_z in inputs:
+        planar = planar_part(coef, flip, table_x, table_y, table_z.shape[1])
+        depth_map = depth_map_of(table_z, coef.shape[4])
+        edge_map = jnp.asarray(depth_map[up_places + down_places], jnp.float32)
+        planars.append(planar)
+        depths.append(depth_map)
+        slabs.append(lax.dot_general(edge_map, planar, (((1,), (1,)), ((), ())), precision=precise))
     keep = jnp.pad((1 - flags).astype(jnp.float32), ((0, 1), (2, 2), (2, 2)))
-    extended = jnp.stack([nodal_x, nodal_y, nodal_z, keep])
-    extended = fold_and_halo(extended, "gz", 3)
+    slabs.append(jnp.moveaxis(keep[..., up_places + down_places], 2, 0).reshape(5, -1))
+    slabs = jnp.stack(slabs)
+    up = slabs[:, :3].reshape(-1, slabs.shape[2])
+    down = slabs[:, 3:].reshape(-1, slabs.shape[2])
+    from_prev, from_next = both_ways(up, down, "gz")
+    arrived = jnp.concatenate(
+        [from_prev.reshape(4, 3, -1), from_next.reshape(4, 2, -1)], axis=1
+    )
+    place = np.zeros((5, length))
+    for row, col in enumerate([0, 1, 2, nz + 2, nz + 3]):
+        place[row, col] = 1.0
+    place = jnp.asarray(place, jnp.float32)
+    nodal = []
+    for comp in range(3):
+        own_part = jnp.dot(planars[comp], jnp.asarray(depths[comp].T, jnp.float32), precision=precise)
+        folded = lax.dot_general(arrived[comp], place, (((0,), (0,)), ((), ())), precision=precise)
+        nodal.append((own_part + folded).reshape(nx + 1, ny + 4, length))
+    keep_in = jnp.moveaxis(arrived[3].reshape(5, nx + 1, ny + 4), 0, 2)
+    keep = keep + jnp.pad(keep_in[..., :3], ((0, 0), (0, 0), (0, length - 3))) + jnp.pad(
+        keep_in[..., 3:], ((0, 0), (0, 0), (nz + 2, 0))
+    )
+    extended = jnp.stack(nodal + [keep])
     extended = fold_and_halo(extended, "gy", 2)
     masked = fold_and_halo_last(extended, "gx", ny, nz)
     return stencil_apply(masked)

time: 40.8 us -> 41 us (level)
  matrix products: 3.8 us -> 7.02 us
  local copies, waits for them, and re-layouts: 9.23 us -> 6.64 us
  other arithmetic: 7.43 us -> 6.74 us
    dot_general x6 -> x12, matrix products: 3.8 us -> 7.02 us  [the longest x3 3.34 us: planar_part(): jnp.dot(jnp.asarray(plane_map, jnp.float32), signed, precision=lax.Precis...]
    reshape x8 -> x4, local copies, waits for them, and re-layouts: 3.09 us -> 0.42 us  [from_wire(): return jnp.moveaxis(rows.reshape(shape), 0, dim)]
    add x2 -> x1, other arithmetic: 1.77 us -> 0.21 us  [fold_and_halo(): extended + jnp.pad(from_wire(from_prev, up_shape, dim), widths_prev)]
    transpose x8 -> x4, local copies, waits for them, and re-layouts: 1.48 us -> 0.1 us  [to_wire(): layers = jnp.moveaxis(slab, dim, 0)]
    gather x0 -> x1, other arithmetic: none -> 0.66 us  [body(): keep[..., up_places + down_places]]
    gather x0 -> x1, local copies, waits for them, and re-layouts: none -> 0.55 us  [body(): keep[..., up_places + down_places]]
    add x0 -> x3, local copies, waits for them, and re-layouts: none -> 0.45 us  [body(): nodal.append((own_part + folded).reshape(nx + 1, ny + 4, length))]
    unnamed x26 -> x21, local copies, waits for them, and re-layouts: 0.93 us -> 1 us
  transfers between devices with their start and end apart: 4 -> 4, of which waited for: 3 -> 3; matrix products, arithmetic and copies ran while one was open for 6% -> 0% of each run, Pallas kernels for 0% -> 0%
where the time goes in v6:
time: 41 us; the launch traced here: 40.7 us
  waiting for transfers between devices  11.2 us (27%)
  starting transfers between devices  8.46 us (21%)
  matrix products  7.02 us (17%)
  other arithmetic  6.74 us (16%)
  local copies, waits for them, and re-layouts  6.64 us (16%)
  between operations  0.63 us (2%)
    ppermute x4, waiting for transfers between devices, shifted(): lax.ppermute(block, axis, [(i, (i + step) % count) for i in range(count)])  11.2 us
    ppermute x4, starting transfers between devices, shifted(): lax.ppermute(block, axis, [(i, (i + step) % count) for i in range(count)])  8.46 us
    dot_general x3, matrix products, planar_part(): jnp.dot(jnp.asarray(plane_map, jnp.float32), signed, precision=lax.Precis...  3.34 us
    mul x1, other arithmetic, stencil_apply(): return 0.25 * total  2.05 us
    dot_general x3, matrix products, body(): jnp.dot(planars[comp], jnp.asarray(depths[comp].T, jnp.float32), precisio...  1.67 us
    dot_general x3, matrix products, body(): lax.dot_general(arrived[comp], place, (((0,), (0,)), ((), ())), precision...  1.28 us
    mul x3, other arithmetic, planar_part(): coef * orient[:, None, :, None, :]  1.04 us
    unnamed x21, local copies, waits for them, and re-layouts  1 us
  transfers between devices with their start and end apart: 4, of which 3 were waited for; matrix products, arithmetic and copies ran while one was open for 0% of the time, Pallas kernels for 0%

profile of v6, /device:TPU:0, one launch (start us, length us, event | category | flops | bytes accessed | tf_op | source)
XLA Modules:
  0.0 40.7 jit_solution(13902313495789082547)
XLA Ops:
  0.0 0.7 %pad_clamp_fusion = s32[1024]{0:T(1024)S(1)} fusion(s32[5]{0:T(128)} %constant.71), kind=kLoop, calls=%fused_computation.111 | loop fusion | flops 1024 | bytes 4116 | tf_op jit(solution)/shard_map/gather | solution.py:203
  0.7 0.7 %convert_bitcast_fusion.2 = (f32[2,8,32]{2,1,0:T(8,128)S(1)}, f32[2,8,32]{2,1,0:T(8,128)S(1)}, f32[2,8,32]{2,1,0:T(8,128)S(1)}) fusion(s32[3,2,8,32]{3,2,1,0:T(8,128)} %param.19), kind=kLoop, calls=%fused_computation.106 | loop fusion | flops 4608 | bytes 12288 | tf_op jit(solution)/shard_map/convert_element_type | solution.py:44
  1.6 1.0 %subtract_convert_fusion = f32[8,32,128]{2,1,0:T(8,128)S(1)} fusion(s32[8,32,128]{2,1,0:T(8,128)} %param.20), kind=kLoop, calls=%fused_computation.69 | loop fusion | flops 65536 | bytes 262144 | tf_op jit(solution)/shard_map/convert_element_type | solution.py:202
  2.5 0.9 %broadcast_multiply_fusion.2 = f32[2,5,8,5,128]{4,2,3,1,0:T(8,128)S(1)} fusion(f32[2,5,8,5,128]{4,2,3,1,0:T(8,128)} %param.18, f32[2,8,128]{2,1,0:T(8,128)S(1)} %copy.305), kind=kLoop, calls=%fused_computation.76 | loop fusion | flops 51200 | bytes 417792 | tf_op jit(solution)/shard_map/mul | solution.py:45
  3.6 0.1 broadcast_in_dim.19
  3.7 0.2 mul.120
  3.9 0.1 broadcast_in_dim.20
  4.0 0.2 mul.124
  4.3 0.1 reshape.97
  4.4 0.1 copy-done.5
  4.6 0.1 copy.303
  4.8 0.6 %copy-done.3 = f32[324,320]{1,0:T(8,128)S(1)} copy-done((f32[324,320]{1,0:T(8,128)S(1)}, f32[324,320]{1,0:T(8,128)}, u32[]{:S(2)}) %copy-start.3) | copy-done | bytes 414744
  5.4 1.3 %fusion.52 = f32[160,324]{1,0:T(8,128)S(1)} fusion(f32[320,160]{1,0:T(8,128)S(1)} %reshape.97, f32[324,320]{1,0:T(8,128)S(1)} %copy-done.3), kind=kOutput, calls=%fused_computation.121 | convolution fusion | flops 199065600 | bytes 826880 | tf_op jit(solution)/shard_map/dot_general | solution.py:48
  6.7 0.2 convolution_bitcast_fusion.1
  6.9 1.3 %fusion.51 = f32[160,324]{1,0:T(8,128)S(1)} fusion(f32[320,160]{1,0:T(8,128)S(1)} %reshape.96, f32[324,320]{1,0:T(8,128)S(1)} %copy-done.2), kind=kOutput, calls=%fused_computation.120 | convolution fusion | flops 199065600 | bytes 826880 | tf_op jit(solution)/shard_map/dot_general | solution.py:48
  8.3 0.2 convolution_bitcast_fusion.2
  8.6 0.2 copy.327
  8.8 0.2 pad.38.clone
  9.0 0.6 %gather_fusion = f32[5,9,36]{2,1,0:T(8,128)S(1)} fusion(f32[9,36,132]{1,0,2:T(8,128)S(1)} %pad.38.clone, s32[1024]{0:T(1024)S(1)} %pad_clamp_fusion), kind=kCustom, calls=%fused_computation | custom fusion | bytes 12980 | tf_op jit(solution)/shard_map/gather | solution.py:203
  9.7 0.7 %fusion.53 = f32[128,324]{0,1:T(8,128)S(1)} fusion(f32[400,128]{1,0:T(8,128)S(1)} %reshape.98, f32[324,400]{1,0:T(8,128)S(1)} %copy-done), kind=kOutput, calls=%fused_computation.122 | convolution fusion | flops 199065600 | bytes 889088 | tf_op jit(solution)/shard_map/dot_general | solution.py:48
  10.4 0.2 convolution_bitcast_fusion
  10.7 0.5 %collective-permute-start = (f32[12,324]{1,0:T(8,128)S(1)}, f32[12,324]{1,0:T(8,128)S(1)}, u32[]{:S(2)}, u32[]{:S(2)}) collective-permute-start(f32[12,324]{1,0:T(8,128)S(1)} %reshape.99), channel_id=1, source_target_pairs={{0,1},{1,2},{2,3},{3,4},{4,5},{5,6},{6,7},{7,0},{8,9},{9,10},{10,1... | collective-permute-start | bytes 46664 | tf_op jit(solution)/shard_map/ppermute | solution.py:59
  11.3 4.1 %collective-permute-start.1 = (f32[8,324]{1,0:T(8,128)S(1)}, f32[8,324]{1,0:T(8,128)S(1)}, u32[]{:S(2)}, u32[]{:S(2)}) collective-permute-start(f32[8,324]{1,0:T(8,128)S(1)} %reshape.101), channel_id=1, source_target_pairs={{0,7},{1,0},{2,1},{3,2},{4,3},{5,4},{6,5},{7,6},{8,15},{9,8},{10,9... | collective-permute-start | bytes 31112 | tf_op jit(solution)/shard_map/ppermute | solution.py:59
  15.4 1.4 %collective-permute-done.1 = f32[8,324]{1,0:T(8,128)S(1)} collective-permute-done((f32[8,324]{1,0:T(8,128)S(1)}, f32[8,324]{1,0:T(8,128)S(1)}, u32[]{:S(2)}, u32[]{:S(2)}) %collective-permute-start.1) | collective-permute-done | bytes 10400 | tf_op jit(solution)/shard_map/ppermute | solution.py:59
  16.9 0.4 %fusion.37 = f32[324,132]{0,1:T(8,128)S(1)} fusion(f32[5,132]{1,0:T(8,128)S(1)} %copy-done.7, f32[4,3,324]{2,1,0:T(4,128)S(1)} %reshape.100, f32[4,2,324]{2,1,0:T(2,128)S(1)} %reshape.102), kind=kOutput, calls=%fused_computation.98 | convolution fusion | flops 2567700 | bytes 199632 | tf_op jit(solution)/shard_map/dot_general | solution.py:218
  17.3 0.4 %fusion.41 = f32[324,132]{0,1:T(8,128)S(1)} fusion(f32[5,132]{1,0:T(8,128)S(1)} %copy-done.7, f32[4,3,324]{2,1,0:T(4,128)S(1)} %reshape.100, f32[4,2,324]{2,1,0:T(2,128)S(1)} %reshape.102), kind=kOutput, calls=%fused_computation.101 | convolution fusion | flops 2567700 | bytes 199632 | tf_op jit(solution)/shard_map/dot_general | solution.py:218
  17.7 0.4 %fusion.33 = f32[324,132]{0,1:T(8,128)S(1)} fusion(f32[5,132]{1,0:T(8,128)S(1)} %copy-done.7, f32[4,3,324]{2,1,0:T(4,128)S(1)} %reshape.100, f32[4,2,324]{2,1,0:T(2,128)S(1)} %reshape.102), kind=kOutput, calls=%fused_computation.95 | convolution fusion | flops 2567700 | bytes 199632 | tf_op jit(solution)/shard_map/dot_general | solution.py:218
  18.2 0.2 copy.311
  18.5 0.6 %convolution_add_fusion.2 = f32[324,132]{0,1:T(8,128)S(1)} fusion(f32[324,132]{0,1:T(8,128)S(1)} %fusion.37, f32[160,324]{1,0:T(8,128)S(1)} %fusion.51, f32[160,132]{1,0:T(8,128)S(1)} %copy-done.1), kind=kOutput, calls=%fused_computation.16 | convolution fusion | flops 82157328 | bytes 633984 | tf_op jit(solution)/shard_map/dot_general | solution.py:217
  19.2 0.2 copy.308
  19.4 0.6 %convolution_add_fusion.1 = f32[324,132]{0,1:T(8,128)S(1)} fusion(f32[324,132]{0,1:T(8,128)S(1)} %fusion.41, f32[160,324]{1,0:T(8,128)S(1)} %fusion.52, f32[160,132]{1,0:T(8,128)S(1)} %copy-done.1), kind=kOutput, calls=%fused_computation.15 | convolution fusion | flops 82157328 | bytes 633984 | tf_op jit(solution)/shard_map/dot_general | solution.py:217
  20.0 0.2 copy.309
  20.2 0.4 %convolution_add_fusion = f32[324,132]{0,1:T(8,128)S(1)} fusion(f32[324,132]{0,1:T(8,128)S(1)} %fusion.33, f32[128,324]{0,1:T(8,128)S(1)} %fusion.53, f32[128,132]{1,0:T(8,128)S(1)} %copy-done.6), kind=kOutput, calls=%fused_computation.14 | convolution fusion | flops 65734416 | bytes 575616 | tf_op jit(solution)/shard_map/dot_general | solution.py:217
  20.7 0.1 copy.310
  20.9 0.2 add_bitcast_fusion
  21.1 0.1 pad_maximum_fusion
  21.3 0.1 reshape.103
  21.6 2.1 %collective-permute-start.2 = (f32[20,1188]{1,0:T(8,128)S(1)}, f32[20,1188]{1,0:T(8,128)S(1)}, u32[]{:S(2)}, u32[]{:S(2)}) collective-permute-start(f32[20,1188]{1,0:T(8,128)S(1)} %pad_maximum_fusion.4), channel_id=1, source_target_pairs={{0,8},{8,0},{1,9},{9,1},{2,10},{10,2},{3,11},{11,3},{4,12},{12,4},... | collective-permute-start | bytes 285128 | tf_op jit(solution)/shard_map/ppermute | solution.py:59
  23.6 3.6 %collective-permute-done.2 = f32[20,1188]{1,0:T(8,128)S(1)} collective-permute-done((f32[20,1188]{1,0:T(8,128)S(1)}, f32[20,1188]{1,0:T(8,128)S(1)}, u32[]{:S(2)}, u32[]{:S(2)}) %collective-permute-start.2) | collective-permute-done | bytes 95072 | tf_op jit(solution)/shard_map/ppermute | solution.py:59
  27.3 0.1 reshape.106
  27.5 0.2 reshape.105
  27.7 0.2 pad_add_fusion
  29.1 0.6 %concatenate.54 = f32[527,128]{1,0:T(8,128)S(1)} concatenate(f32[192,128]{1,0:T(8,128)S(1)} %bitcast.109, f32[96,128]{1,0:T(8,128)S(1)} %bitcast.112, f32[12,128]{1,0:T(8,128)S(1)} %reshape.109, f32[3,128]{1,0:T(4,128)S(1)} %reshape.110, f32[96,128]{1,0:T(8,128)S(1)} %bitcast.113, f32[32,128]{1,0:T(8,128)S(1)} %slice.297, f32[96,128]{1,0:T(8,128)S(1)} %bitcast.111), dimensions={0} | concatenate | bytes 539648 | tf_op jit(solution)/shard_map/concatenate | solution.py:64
  29.7 1.8 %collective-permute-start.3 = (f32[527,128]{1,0:T(8,128)S(1)}, f32[527,128]{1,0:T(8,128)S(1)}, u32[]{:S(2)}, u32[]{:S(2)}) collective-permute-start(f32[527,128]{1,0:T(8,128)S(1)} %concatenate.54), channel_id=1, source_target_pairs={{0,16},{16,0},{1,17},{17,1},{2,18},{18,2},{3,19},{19,3},{4,20},{20... | collective-permute-start | bytes 809480 | tf_op jit(solution)/shard_map/ppermute | solution.py:59
  31.6 6.2 %collective-permute-done.3 = f32[527,128]{1,0:T(8,128)S(1)} collective-permute-done((f32[527,128]{1,0:T(8,128)S(1)}, f32[527,128]{1,0:T(8,128)S(1)}, u32[]{:S(2)}, u32[]{:S(2)}) %collective-permute-start.3) | collective-permute-done | bytes 269856 | tf_op jit(solution)/shard_map/ppermute | solution.py:59
  38.3 0.1 maximum_bitcast_fusion
  38.5 0.1 fusion
  38.7 2.0 %fusion.5 = f32[3,8,32,128]{3,2,1,0:T(8,128)} fusion(f32[3,7,36,132]{3,2,1,0:T(8,128)S(1)} %slice_multiply_fusion, f32[3,1,36,132]{3,2,1,0:T(8,128)S(1)} %fusion.30, f32[3,1,32,128]{3,2,1,0:T(8,128)S(1)} %bitcast.116, f32[3,1,36,132]{3,2,1,0:T(8,128)S(1)} %pad.46, f32[3,10,36,132]{3,2,1,0:T(8,128)S(1)} %fusion), kind=kLoop, calls=%fused_computation.33 | loop fusion | flops 3440640 | bytes 1742016 | tf_op jit(solution)/shard_map/mul | solution.py:177
  (87 shorter events, 3.2 us)
Async XLA Ops:
  1.5 2.7 %copy-start.4 = (f32[2,5,8,4,160]{4,3,2,1,0:T(4,128)S(1)}, f32[2,5,8,4,160]{4,3,2,1,0:T(4,128)}, u32[]{:S(2)}) copy-start(f32[2,5,8,4,160]{4,3,2,1,0:T(4,128)} %param.17) | copy-start | bytes 614404
  3.6 1.0 %copy-start.5 = (f32[2,4,8,5,160]{4,2,3,1,0:T(8,128)S(1)}, f32[2,4,8,5,160]{4,2,3,1,0:T(8,128)}, u32[]{:S(2)}) copy-start(f32[2,4,8,5,160]{4,2,3,1,0:T(8,128)} %param.16) | copy-start | bytes 614404
  4.3 1.1 %copy-start.3 = (f32[324,320]{1,0:T(8,128)S(1)}, f32[324,320]{1,0:T(8,128)}, u32[]{:S(2)}) copy-start(f32[324,320]{1,0:T(8,128)} %constant.40.clone) | copy-start | bytes 1244164
  4.6 2.1 %copy-start.8 = (f32[5,160]{1,0:T(8,128)S(1)}, f32[5,160]{1,0:T(8,128)}, u32[]{:S(2)}) copy-start(f32[5,160]{1,0:T(8,128)} %constant.39.clone) | copy-start | bytes 9604
  4.6 2.4 %copy-start.2 = (f32[324,320]{1,0:T(8,128)S(1)}, f32[324,320]{1,0:T(8,128)}, u32[]{:S(2)}) copy-start(f32[324,320]{1,0:T(8,128)} %constant.38.clone) | copy-start | bytes 1244164
  8.3 1.4 %copy-start = (f32[324,400]{1,0:T(8,128)S(1)}, f32[324,400]{1,0:T(8,128)}, u32[]{:S(2)}) copy-start(f32[324,400]{1,0:T(8,128)} %constant.41.clone) | copy-start | bytes 1555204
  8.8 1.6 %copy-start.9 = (f32[5,128]{1,0:T(8,128)S(1)}, f32[5,128]{1,0:T(8,128)}, u32[]{:S(2)}) copy-start(f32[5,128]{1,0:T(8,128)} %constant.42.clone) | copy-start | bytes 7684
  8.8 8.0 %copy-start.7 = (f32[5,132]{1,0:T(8,128)S(1)}, f32[5,132]{1,0:T(8,128)}, u32[]{:S(2)}) copy-start(f32[5,132]{1,0:T(8,128)} %constant.44.clone) | copy-start | bytes 7924
  9.7 8.8 %copy-start.1 = (f32[160,132]{1,0:T(8,128)S(1)}, f32[160,132]{1,0:T(8,128)}, u32[]{:S(2)}) copy-start(f32[160,132]{1,0:T(8,128)} %constant.45.clone) | copy-start | bytes 253444
  10.7 6.1 %collective-permute-start = (f32[12,324]{1,0:T(8,128)S(1)}, f32[12,324]{1,0:T(8,128)S(1)}, u32[]{:S(2)}, u32[]{:S(2)}) collective-permute-start(f32[12,324]{1,0:T(8,128)S(1)} %reshape.99), channel_id=1, source_target_pairs={{0,1},{1,2},{2,3},{3,4},{4,5},{5,6},{6,7},{7,0},{8,9},{9,10},{10,1... | collective-permute-start | bytes 46664 | tf_op jit(solution)/shard_map/ppermute | solution.py:59
  11.3 5.5 %collective-permute-start.1 = (f32[8,324]{1,0:T(8,128)S(1)}, f32[8,324]{1,0:T(8,128)S(1)}, u32[]{:S(2)}, u32[]{:S(2)}) collective-permute-start(f32[8,324]{1,0:T(8,128)S(1)} %reshape.101), channel_id=1, source_target_pairs={{0,7},{1,0},{2,1},{3,2},{4,3},{5,4},{6,5},{7,6},{8,15},{9,8},{10,9... | collective-permute-start | bytes 31112 | tf_op jit(solution)/shard_map/ppermute | solution.py:59
  19.3 0.9 %copy-start.6 = (f32[128,132]{1,0:T(8,128)S(1)}, f32[128,132]{1,0:T(8,128)}, u32[]{:S(2)}) copy-start(f32[128,132]{1,0:T(8,128)} %constant.46.clone) | copy-start | bytes 202756
  21.6 5.7 %collective-permute-start.2 = (f32[20,1188]{1,0:T(8,128)S(1)}, f32[20,1188]{1,0:T(8,128)S(1)}, u32[]{:S(2)}, u32[]{:S(2)}) collective-permute-start(f32[20,1188]{1,0:T(8,128)S(1)} %pad_maximum_fusion.4), channel_id=1, source_target_pairs={{0,8},{8,0},{1,9},{9,1},{2,10},{10,2},{3,11},{11,3},{4,12},{12,4},... | collective-permute-start | bytes 285128 | tf_op jit(solution)/shard_map/ppermute | solution.py:59
  29.7 8.0 %collective-permute-start.3 = (f32[527,128]{1,0:T(8,128)S(1)}, f32[527,128]{1,0:T(8,128)S(1)}, u32[]{:S(2)}, u32[]{:S(2)}) collective-permute-start(f32[527,128]{1,0:T(8,128)S(1)} %concatenate.54), channel_id=1, source_target_pairs={{0,16},{16,0},{1,17},{17,1},{2,18},{18,2},{3,19},{19,3},{4,20},{20... | collective-permute-start | bytes 809480 | tf_op jit(solution)/shard_map/ppermute | solution.py:59

commit v7 on v6

--- a/solution.py
+++ b/solution.py
@@ -45,7 +45,7 @@
     signed = (coef * orient[:, None, :, None, :]).reshape(ex_count * size_x * ey_count * size_y, merged)
     rows_y = np.pad(assembly_matrix(table_y, ey_count), ((2, 1), (0, 0)))
     plane_map = np.kron(assembly_matrix(table_x, ex_count), rows_y)
-    return jnp.dot(jnp.asarray(plane_map, jnp.float32), signed, precision=lax.Precision.HIGHEST)
+    return jnp.dot(jnp.asarray(plane_map, jnp.float32), signed, precision=lax.Precision.HIGH)
 
 
 def depth_map_of(table_z, merged):
@@ -198,7 +198,9 @@
         edge_map = jnp.asarray(depth_map[up_places + down_places], jnp.float32)
         planars.append(planar)
         depths.append(depth_map)
-        slabs.append(lax.dot_general(edge_map, planar, (((1,), (1,)), ((), ())), precision=precise))
+        slabs.append(
+            lax.dot_general(edge_map, planar, (((1,), (1,)), ((), ())), precision=lax.Precision.HIGH)
+        )
     keep = jnp.pad((1 - flags).astype(jnp.float32), ((0, 1), (2, 2), (2, 2)))
     slabs.append(jnp.moveaxis(keep[..., up_places + down_places], 2, 0).reshape(5, -1))
     slabs = jnp.stack(slabs)
@@ -214,7 +216,9 @@
     place = jnp.asarray(place, jnp.float32)
     nodal = []
     for comp in range(3):
-        own_part = jnp.dot(planars[comp], jnp.asarray(depths[comp].T, jnp.float32), precision=precise)
+        own_part = jnp.dot(
+            planars[comp], jnp.asarray(depths[comp].T, jnp.float32), precision=lax.Precision.HIGH
+        )
         folded = lax.dot_general(arrived[comp], place, (((0,), (0,)), ((), ())), precision=precise)
         nodal.append((own_part + folded).reshape(nx + 1, ny + 4, length))
     keep_in = jnp.moveaxis(arrived[3].reshape(5, nx + 1, ny + 4), 0, 2)

time: 41 us -> 39 us (0.951)
  matrix products: 7.02 us -> 4.87 us
    dot_general x3, matrix products: 3.34 us -> 1.96 us  [planar_part(): jnp.dot(jnp.asarray(plane_map, jnp.float32), signed, precision=lax.Precis...]
    dot_general x3, matrix products: 1.67 us -> 1.1 us  [body(): jnp.dot(planars[comp], jnp.asarray(depths[comp].T, jnp.float32), precisio...]
where the time goes in v7:
time: 39 us; the launch traced here: 38.7 us
  waiting for transfers between devices  11.2 us (29%)
  starting transfers between devices  8.45 us (22%)
  local copies, waits for them, and re-layouts  6.87 us (18%)
  other arithmetic  6.7 us (17%)
  matrix products  4.87 us (12%)
  between operations  0.63 us (2%)
    ppermute x4, waiting for transfers between devices, shifted(): lax.ppermute(block, axis, [(i, (i + step) % count) for i in range(count)])  11.2 us
    ppermute x4, starting transfers between devices, shifted(): lax.ppermute(block, axis, [(i, (i + step) % count) for i in range(count)])  8.45 us
    mul x1, other arithmetic, stencil_apply(): return 0.25 * total  2.05 us
    dot_general x3, matrix products, planar_part(): jnp.dot(jnp.asarray(plane_map, jnp.float32), signed, precision=lax.Precis...  1.96 us
    dot_general x3, matrix products, body(): lax.dot_general(arrived[comp], place, (((0,), (0,)), ((), ())), precision...  1.28 us
    unnamed x21, local copies, waits for them, and re-layouts  1.23 us
    dot_general x3, matrix products, body(): jnp.dot(planars[comp], jnp.asarray(depths[comp].T, jnp.float32), precisio...  1.1 us
    mul x3, other arithmetic, planar_part(): coef * orient[:, None, :, None, :]  1.04 us
  transfers between devices with their start and end apart: 4, of which 3 were waited for; matrix products, arithmetic and copies ran while one was open for 0% of the time, Pallas kernels for 0%

profile of v7, /device:TPU:0, one launch (start us, length us, event | category | flops | bytes accessed | tf_op | source)
XLA Modules:
  0.0 38.7 jit_solution(5083954170495726085)
XLA Ops:
  0.0 0.7 %pad_clamp_fusion = s32[1024]{0:T(1024)S(1)} fusion(s32[5]{0:T(128)} %constant.71), kind=kLoop, calls=%fused_computation.111 | loop fusion | flops 1024 | bytes 4116 | tf_op jit(solution)/shard_map/gather | solution.py:205
  0.7 0.7 %convert_bitcast_fusion.2 = (f32[2,8,32]{2,1,0:T(8,128)S(1)}, f32[2,8,32]{2,1,0:T(8,128)S(1)}, f32[2,8,32]{2,1,0:T(8,128)S(1)}) fusion(s32[3,2,8,32]{3,2,1,0:T(8,128)} %param.19), kind=kLoop, calls=%fused_computation.106 | loop fusion | flops 4608 | bytes 12288 | tf_op jit(solution)/shard_map/convert_element_type | solution.py:44
  1.6 1.0 %subtract_convert_fusion = f32[8,32,128]{2,1,0:T(8,128)S(1)} fusion(s32[8,32,128]{2,1,0:T(8,128)} %param.20), kind=kLoop, calls=%fused_computation.69 | loop fusion | flops 65536 | bytes 262144 | tf_op jit(solution)/shard_map/convert_element_type | solution.py:204
  2.5 0.9 %broadcast_multiply_fusion.2 = f32[2,5,8,5,128]{4,2,3,1,0:T(8,128)S(1)} fusion(f32[2,5,8,5,128]{4,2,3,1,0:T(8,128)} %param.18, f32[2,8,128]{2,1,0:T(8,128)S(1)} %copy.305), kind=kLoop, calls=%fused_computation.76 | loop fusion | flops 51200 | bytes 417792 | tf_op jit(solution)/shard_map/mul | solution.py:45
  3.6 0.1 broadcast_in_dim.19
  3.7 0.2 mul.120
  3.9 0.1 broadcast_in_dim.20
  4.0 0.2 mul.124
  4.3 0.1 reshape.97
  4.4 0.1 copy-done.5
  4.6 0.1 copy.303
  4.8 0.6 %copy-done.3 = f32[324,320]{1,0:T(8,128)S(1)} copy-done((f32[324,320]{1,0:T(8,128)S(1)}, f32[324,320]{1,0:T(8,128)}, u32[]{:S(2)}) %copy-start.3) | copy-done | bytes 414744
  5.4 0.8 %fusion.52 = f32[160,324]{1,0:T(8,128)S(1)} fusion(f32[320,160]{1,0:T(8,128)S(1)} %reshape.97, f32[324,320]{1,0:T(8,128)S(1)} %copy-done.3), kind=kOutput, calls=%fused_computation.121 | convolution fusion | flops 99532800 | bytes 826880 | tf_op jit(solution)/shard_map/dot_general | solution.py:48
  6.1 0.2 convolution_bitcast_fusion.1
  6.3 0.8 %fusion.51 = f32[160,324]{1,0:T(8,128)S(1)} fusion(f32[320,160]{1,0:T(8,128)S(1)} %reshape.96, f32[324,320]{1,0:T(8,128)S(1)} %copy-done.2), kind=kOutput, calls=%fused_computation.120 | convolution fusion | flops 99532800 | bytes 826880 | tf_op jit(solution)/shard_map/dot_general | solution.py:48
  7.1 0.2 convolution_bitcast_fusion.2
  7.3 0.2 copy.327
  7.5 0.2 pad.38.clone
  7.7 0.6 %gather_fusion = f32[5,9,36]{2,1,0:T(8,128)S(1)} fusion(f32[9,36,132]{1,0,2:T(8,128)S(1)} %pad.38.clone, s32[1024]{0:T(1024)S(1)} %pad_clamp_fusion), kind=kCustom, calls=%fused_computation | custom fusion | bytes 12980 | tf_op jit(solution)/shard_map/gather | solution.py:205
  8.4 0.4 %fusion.53 = f32[128,324]{0,1:T(8,128)S(1)} fusion(f32[400,128]{1,0:T(8,128)S(1)} %reshape.98, f32[324,400]{1,0:T(8,128)S(1)} %copy-done), kind=kOutput, calls=%fused_computation.122 | convolution fusion | flops 99532800 | bytes 889088 | tf_op jit(solution)/shard_map/dot_general | solution.py:48
  8.8 0.2 convolution_bitcast_fusion
  9.1 0.5 %collective-permute-start = (f32[12,324]{1,0:T(8,128)S(1)}, f32[12,324]{1,0:T(8,128)S(1)}, u32[]{:S(2)}, u32[]{:S(2)}) collective-permute-start(f32[12,324]{1,0:T(8,128)S(1)} %reshape.99), channel_id=1, source_target_pairs={{0,1},{1,2},{2,3},{3,4},{4,5},{5,6},{6,7},{7,0},{8,9},{9,10},{10,1... | collective-permute-start | bytes 46664 | tf_op jit(solution)/shard_map/ppermute | solution.py:59
  9.6 4.1 %collective-permute-start.1 = (f32[8,324]{1,0:T(8,128)S(1)}, f32[8,324]{1,0:T(8,128)S(1)}, u32[]{:S(2)}, u32[]{:S(2)}) collective-permute-start(f32[8,324]{1,0:T(8,128)S(1)} %reshape.101), channel_id=1, source_target_pairs={{0,7},{1,0},{2,1},{3,2},{4,3},{5,4},{6,5},{7,6},{8,15},{9,8},{10,9... | collective-permute-start | bytes 31112 | tf_op jit(solution)/shard_map/ppermute | solution.py:59
  13.7 1.4 %collective-permute-done.1 = f32[8,324]{1,0:T(8,128)S(1)} collective-permute-done((f32[8,324]{1,0:T(8,128)S(1)}, f32[8,324]{1,0:T(8,128)S(1)}, u32[]{:S(2)}, u32[]{:S(2)}) %collective-permute-start.1) | collective-permute-done | bytes 10400 | tf_op jit(solution)/shard_map/ppermute | solution.py:59
  15.2 0.4 %fusion.37 = f32[324,132]{0,1:T(8,128)S(1)} fusion(f32[5,132]{1,0:T(8,128)S(1)} %copy-done.7, f32[4,3,324]{2,1,0:T(4,128)S(1)} %reshape.100, f32[4,2,324]{2,1,0:T(2,128)S(1)} %reshape.102), kind=kOutput, calls=%fused_computation.98 | convolution fusion | flops 2567700 | bytes 199632 | tf_op jit(solution)/shard_map/dot_general | solution.py:222
  15.6 0.4 %fusion.41 = f32[324,132]{0,1:T(8,128)S(1)} fusion(f32[5,132]{1,0:T(8,128)S(1)} %copy-done.7, f32[4,3,324]{2,1,0:T(4,128)S(1)} %reshape.100, f32[4,2,324]{2,1,0:T(2,128)S(1)} %reshape.102), kind=kOutput, calls=%fused_computation.101 | convolution fusion | flops 2567700 | bytes 199632 | tf_op jit(solution)/shard_map/dot_general | solution.py:222
  16.1 0.4 %fusion.33 = f32[324,132]{0,1:T(8,128)S(1)} fusion(f32[5,132]{1,0:T(8,128)S(1)} %copy-done.7, f32[4,3,324]{2,1,0:T(4,128)S(1)} %reshape.100, f32[4,2,324]{2,1,0:T(2,128)S(1)} %reshape.102), kind=kOutput, calls=%fused_computation.95 | convolution fusion | flops 2567700 | bytes 199632 | tf_op jit(solution)/shard_map/dot_general | solution.py:222
  16.6 0.2 copy.311
  16.9 0.4 %convolution_add_fusion.2 = f32[324,132]{0,1:T(8,128)S(1)} fusion(f32[324,132]{0,1:T(8,128)S(1)} %fusion.37, f32[160,324]{1,0:T(8,128)S(1)} %fusion.51, f32[160,132]{1,0:T(8,128)S(1)} %copy-done.1), kind=kOutput, calls=%fused_computation.16 | convolution fusion | flops 41100048 | bytes 633984 | tf_op jit(solution)/shard_map/dot_general | solution.py:219
  17.3 0.1 copy.308
  17.5 0.4 %convolution_add_fusion.1 = f32[324,132]{0,1:T(8,128)S(1)} fusion(f32[324,132]{0,1:T(8,128)S(1)} %fusion.41, f32[160,324]{1,0:T(8,128)S(1)} %fusion.52, f32[160,132]{1,0:T(8,128)S(1)} %copy-done.1), kind=kOutput, calls=%fused_computation.15 | convolution fusion | flops 41100048 | bytes 633984 | tf_op jit(solution)/shard_map/dot_general | solution.py:219
  17.9 0.1 copy.309
  18.1 0.3 copy-done.6
  18.4 0.3 convolution_add_fusion
  18.7 0.1 copy.310
  18.9 0.2 add_bitcast_fusion
  19.1 0.1 pad_maximum_fusion
  19.3 0.1 reshape.103
  19.6 2.1 %collective-permute-start.2 = (f32[20,1188]{1,0:T(8,128)S(1)}, f32[20,1188]{1,0:T(8,128)S(1)}, u32[]{:S(2)}, u32[]{:S(2)}) collective-permute-start(f32[20,1188]{1,0:T(8,128)S(1)} %pad_maximum_fusion.4), channel_id=1, source_target_pairs={{0,8},{8,0},{1,9},{9,1},{2,10},{10,2},{3,11},{11,3},{4,12},{12,4},... | collective-permute-start | bytes 285128 | tf_op jit(solution)/shard_map/ppermute | solution.py:59
  21.7 3.6 %collective-permute-done.2 = f32[20,1188]{1,0:T(8,128)S(1)} collective-permute-done((f32[20,1188]{1,0:T(8,128)S(1)}, f32[20,1188]{1,0:T(8,128)S(1)}, u32[]{:S(2)}, u32[]{:S(2)}) %collective-permute-start.2) | collective-permute-done | bytes 95072 | tf_op jit(solution)/shard_map/ppermute | solution.py:59
  25.3 0.1 reshape.106
  25.5 0.2 reshape.105
  25.8 0.2 pad_add_fusion
  27.1 0.6 %concatenate.54 = f32[527,128]{1,0:T(8,128)S(1)} concatenate(f32[192,128]{1,0:T(8,128)S(1)} %bitcast.109, f32[96,128]{1,0:T(8,128)S(1)} %bitcast.112, f32[12,128]{1,0:T(8,128)S(1)} %reshape.109, f32[3,128]{1,0:T(4,128)S(1)} %reshape.110, f32[96,128]{1,0:T(8,128)S(1)} %bitcast.113, f32[32,128]{1,0:T(8,128)S(1)} %slice.297, f32[96,128]{1,0:T(8,128)S(1)} %bitcast.111), dimensions={0} | concatenate | bytes 539648 | tf_op jit(solution)/shard_map/concatenate | solution.py:64
  27.7 1.8 %collective-permute-start.3 = (f32[527,128]{1,0:T(8,128)S(1)}, f32[527,128]{1,0:T(8,128)S(1)}, u32[]{:S(2)}, u32[]{:S(2)}) collective-permute-start(f32[527,128]{1,0:T(8,128)S(1)} %concatenate.54), channel_id=1, source_target_pairs={{0,16},{16,0},{1,17},{17,1},{2,18},{18,2},{3,19},{19,3},{4,20},{20... | collective-permute-start | bytes 809480 | tf_op jit(solution)/shard_map/ppermute | solution.py:59
  29.6 6.2 %collective-permute-done.3 = f32[527,128]{1,0:T(8,128)S(1)} collective-permute-done((f32[527,128]{1,0:T(8,128)S(1)}, f32[527,128]{1,0:T(8,128)S(1)}, u32[]{:S(2)}, u32[]{:S(2)}) %collective-permute-start.3) | collective-permute-done | bytes 269856 | tf_op jit(solution)/shard_map/ppermute | solution.py:59
  36.5 0.1 fusion
  36.7 2.0 %fusion.5 = f32[3,8,32,128]{3,2,1,0:T(8,128)} fusion(f32[3,7,36,132]{3,2,1,0:T(8,128)S(1)} %slice_multiply_fusion, f32[3,1,36,132]{3,2,1,0:T(8,128)S(1)} %fusion.30, f32[3,1,32,128]{3,2,1,0:T(8,128)S(1)} %bitcast.116, f32[3,1,36,132]{3,2,1,0:T(8,128)S(1)} %pad.46, f32[3,10,36,132]{3,2,1,0:T(8,128)S(1)} %fusion), kind=kLoop, calls=%fused_computation.33 | loop fusion | flops 3440640 | bytes 1742016 | tf_op jit(solution)/shard_map/mul | solution.py:177
  (87 shorter events, 3.2 us)
Async XLA Ops:
  1.5 2.7 %copy-start.4 = (f32[2,5,8,4,160]{4,3,2,1,0:T(4,128)S(1)}, f32[2,5,8,4,160]{4,3,2,1,0:T(4,128)}, u32[]{:S(2)}) copy-start(f32[2,5,8,4,160]{4,3,2,1,0:T(4,128)} %param.17) | copy-start | bytes 614404
  3.6 1.0 %copy-start.5 = (f32[2,4,8,5,160]{4,2,3,1,0:T(8,128)S(1)}, f32[2,4,8,5,160]{4,2,3,1,0:T(8,128)}, u32[]{:S(2)}) copy-start(f32[2,4,8,5,160]{4,2,3,1,0:T(8,128)} %param.16) | copy-start | bytes 614404
  4.3 1.1 %copy-start.3 = (f32[324,320]{1,0:T(8,128)S(1)}, f32[324,320]{1,0:T(8,128)}, u32[]{:S(2)}) copy-start(f32[324,320]{1,0:T(8,128)} %constant.40.clone) | copy-start | bytes 1244164
  4.6 1.6 %copy-start.8 = (f32[5,160]{1,0:T(8,128)S(1)}, f32[5,160]{1,0:T(8,128)}, u32[]{:S(2)}) copy-start(f32[5,160]{1,0:T(8,128)} %constant.39.clone) | copy-start | bytes 9604
  4.6 1.7 %copy-start.2 = (f32[324,320]{1,0:T(8,128)S(1)}, f32[324,320]{1,0:T(8,128)}, u32[]{:S(2)}) copy-start(f32[324,320]{1,0:T(8,128)} %constant.38.clone) | copy-start | bytes 1244164
  7.1 1.3 %copy-start = (f32[324,400]{1,0:T(8,128)S(1)}, f32[324,400]{1,0:T(8,128)}, u32[]{:S(2)}) copy-start(f32[324,400]{1,0:T(8,128)} %constant.41.clone) | copy-start | bytes 1555204
  7.5 1.3 %copy-start.9 = (f32[5,128]{1,0:T(8,128)S(1)}, f32[5,128]{1,0:T(8,128)}, u32[]{:S(2)}) copy-start(f32[5,128]{1,0:T(8,128)} %constant.42.clone) | copy-start | bytes 7684
  7.5 7.7 %copy-start.7 = (f32[5,132]{1,0:T(8,128)S(1)}, f32[5,132]{1,0:T(8,128)}, u32[]{:S(2)}) copy-start(f32[5,132]{1,0:T(8,128)} %constant.44.clone) | copy-start | bytes 7924
  8.4 8.5 %copy-start.1 = (f32[160,132]{1,0:T(8,128)S(1)}, f32[160,132]{1,0:T(8,128)}, u32[]{:S(2)}) copy-start(f32[160,132]{1,0:T(8,128)} %constant.45.clone) | copy-start | bytes 253444
  9.1 6.1 %collective-permute-start = (f32[12,324]{1,0:T(8,128)S(1)}, f32[12,324]{1,0:T(8,128)S(1)}, u32[]{:S(2)}, u32[]{:S(2)}) collective-permute-start(f32[12,324]{1,0:T(8,128)S(1)} %reshape.99), channel_id=1, source_target_pairs={{0,1},{1,2},{2,3},{3,4},{4,5},{5,6},{6,7},{7,0},{8,9},{9,10},{10,1... | collective-permute-start | bytes 46664 | tf_op jit(solution)/shard_map/ppermute | solution.py:59
  9.6 5.5 %collective-permute-start.1 = (f32[8,324]{1,0:T(8,128)S(1)}, f32[8,324]{1,0:T(8,128)S(1)}, u32[]{:S(2)}, u32[]{:S(2)}) collective-permute-start(f32[8,324]{1,0:T(8,128)S(1)} %reshape.101), channel_id=1, source_target_pairs={{0,7},{1,0},{2,1},{3,2},{4,3},{5,4},{6,5},{7,6},{8,15},{9,8},{10,9... | collective-permute-start | bytes 31112 | tf_op jit(solution)/shard_map/ppermute | solution.py:59
  17.4 0.9 %copy-start.6 = (f32[128,132]{1,0:T(8,128)S(1)}, f32[128,132]{1,0:T(8,128)}, u32[]{:S(2)}) copy-start(f32[128,132]{1,0:T(8,128)} %constant.46.clone) | copy-start | bytes 202756
  19.6 5.7 %collective-permute-start.2 = (f32[20,1188]{1,0:T(8,128)S(1)}, f32[20,1188]{1,0:T(8,128)S(1)}, u32[]{:S(2)}, u32[]{:S(2)}) collective-permute-start(f32[20,1188]{1,0:T(8,128)S(1)} %pad_maximum_fusion.4), channel_id=1, source_target_pairs={{0,8},{8,0},{1,9},{9,1},{2,10},{10,2},{3,11},{11,3},{4,12},{12,4},... | collective-permute-start | bytes 285128 | tf_op jit(solution)/shard_map/ppermute | solution.py:59
  27.7 8.0 %collective-permute-start.3 = (f32[527,128]{1,0:T(8,128)S(1)}, f32[527,128]{1,0:T(8,128)S(1)}, u32[]{:S(2)}, u32[]{:S(2)}) collective-permute-start(f32[527,128]{1,0:T(8,128)S(1)} %concatenate.54), channel_id=1, source_target_pairs={{0,16},{16,0},{1,17},{17,1},{2,18},{18,2},{3,19},{19,3},{4,20},{20... | collective-permute-start | bytes 809480 | tf_op jit(solution)/shard_map/ppermute | solution.py:59

commit v8 on v7

--- a/solution.py
+++ b/solution.py
@@ -201,8 +201,15 @@
         slabs.append(
             lax.dot_general(edge_map, planar, (((1,), (1,)), ((), ())), precision=lax.Precision.HIGH)
         )
-    keep = jnp.pad((1 - flags).astype(jnp.float32), ((0, 1), (2, 2), (2, 2)))
-    slabs.append(jnp.moveaxis(keep[..., up_places + down_places], 2, 0).reshape(5, -1))
+    keep_own = (1 - flags).astype(jnp.float32)
+    keep = jnp.pad(keep_own, ((0, 1), (2, 2), (2, 2)))
+    keep_layers = [
+        lax.slice_in_dim(keep_own, nz - 2, nz, axis=2),
+        jnp.zeros_like(lax.slice_in_dim(keep_own, 0, 1, axis=2)),
+        lax.slice_in_dim(keep_own, 0, 2, axis=2),
+    ]
+    keep_layers = jnp.moveaxis(jnp.concatenate(keep_layers, axis=2), 2, 0)
+    slabs.append(jnp.pad(keep_layers, ((0, 0), (0, 1), (2, 2))).reshape(5, -1))
     slabs = jnp.stack(slabs)
     up = slabs[:, :3].reshape(-1, slabs.shape[2])
     down = slabs[:, 3:].reshape(-1, slabs.shape[2])

time: 39 us -> 37.8 us (0.969)
  other arithmetic: 6.7 us -> 6.11 us
  local copies, waits for them, and re-layouts: 6.87 us -> 6.29 us
    gather x1 -> x0, other arithmetic: 0.66 us -> none  [body(): keep[..., up_places + down_places]]
    gather x1 -> x0, local copies, waits for them, and re-layouts: 0.55 us -> none  [body(): keep[..., up_places + down_places]]
    unnamed x21 -> x20, local copies, waits for them, and re-layouts: 1.23 us -> 0.94 us
where the time goes in v8:
time: 37.8 us; the launch traced here: 37.6 us
  waiting for transfers between devices  11.2 us (30%)
  starting transfers between devices  8.47 us (22%)
  local copies, waits for them, and re-layouts  6.29 us (17%)
  other arithmetic  6.11 us (16%)
  matrix products  4.88 us (13%)
  between operations  0.61 us (2%)
    ppermute x4, waiting for transfers between devices, shifted(): lax.ppermute(block, axis, [(i, (i + step) % count) for i in range(count)])  11.2 us
    ppermute x4, starting transfers between devices, shifted(): lax.ppermute(block, axis, [(i, (i + step) % count) for i in range(count)])  8.47 us
    mul x1, other arithmetic, stencil_apply(): return 0.25 * total  2.05 us
    dot_general x3, matrix products, planar_part(): jnp.dot(jnp.asarray(plane_map, jnp.float32), signed, precision=lax.Precis...  1.98 us
    dot_general x3, matrix products, body(): lax.dot_general(arrived[comp], place, (((0,), (0,)), ((), ())), precision...  1.28 us
    dot_general x3, matrix products, body(): jnp.dot(planars[comp], jnp.asarray(depths[comp].T, jnp.float32), precisio...  1.1 us
    mul x3, other arithmetic, planar_part(): coef * orient[:, None, :, None, :]  1.04 us
    unnamed x20, local copies, waits for them, and re-layouts  0.94 us
  transfers between devices with their start and end apart: 4, of which 3 were waited for; matrix products, arithmetic and copies ran while one was open for 0% of the time, Pallas kernels for 0%

profile of v8, /device:TPU:0, one launch (start us, length us, event | category | flops | bytes accessed | tf_op | source)
XLA Modules:
  0.0 37.6 jit_solution(5355368752618526250)
XLA Ops:
  0.0 0.7 %convert_bitcast_fusion.2 = (f32[2,8,32]{2,1,0:T(8,128)S(1)}, f32[2,8,32]{2,1,0:T(8,128)S(1)}, f32[2,8,32]{2,1,0:T(8,128)S(1)}) fusion(s32[3,2,8,32]{3,2,1,0:T(8,128)} %param.18), kind=kLoop, calls=%fused_computation.106 | loop fusion | flops 4608 | bytes 12288 | tf_op jit(solution)/shard_map/convert_element_type | solution.py:44
  0.9 0.9 %subtract_convert_fusion = f32[8,32,128]{2,1,0:T(8,128)S(1)} fusion(s32[8,32,128]{2,1,0:T(8,128)} %param.19), kind=kLoop, calls=%fused_computation.68 | loop fusion | flops 65536 | bytes 262144 | tf_op jit(solution)/shard_map/convert_element_type | solution.py:204
  1.8 0.9 %broadcast_multiply_fusion.2 = f32[2,5,8,5,128]{4,2,3,1,0:T(8,128)S(1)} fusion(f32[2,5,8,5,128]{4,2,3,1,0:T(8,128)} %param.17, f32[2,8,128]{2,1,0:T(8,128)S(1)} %copy.50), kind=kLoop, calls=%fused_computation.75 | loop fusion | flops 51200 | bytes 417792 | tf_op jit(solution)/shard_map/mul | solution.py:45
  2.9 0.1 broadcast_in_dim.19
  3.0 0.2 mul.120
  3.2 0.1 broadcast_in_dim.20
  3.4 0.2 mul.124
  3.6 0.1 copy.52
  3.7 0.1 copy.53
  4.3 0.1 reshape.97
  4.5 0.1 copy.48
  4.7 0.6 %copy-done.3 = f32[324,320]{1,0:T(8,128)S(1)} copy-done((f32[324,320]{1,0:T(8,128)S(1)}, f32[324,320]{1,0:T(8,128)}, u32[]{:S(2)}) %copy-start.3) | copy-done | bytes 414744
  5.3 0.8 %fusion.53 = f32[160,324]{1,0:T(8,128)S(1)} fusion(f32[320,160]{1,0:T(8,128)S(1)} %reshape.97, f32[324,320]{1,0:T(8,128)S(1)} %copy-done.3), kind=kOutput, calls=%fused_computation.121 | convolution fusion | flops 99532800 | bytes 826880 | tf_op jit(solution)/shard_map/dot_general | solution.py:48
  6.1 0.2 convolution_bitcast_fusion.1
  6.3 0.8 %fusion.52 = f32[160,324]{1,0:T(8,128)S(1)} fusion(f32[320,160]{1,0:T(8,128)S(1)} %reshape.96, f32[324,320]{1,0:T(8,128)S(1)} %copy-done.2), kind=kOutput, calls=%fused_computation.120 | convolution fusion | flops 99532800 | bytes 826880 | tf_op jit(solution)/shard_map/dot_general | solution.py:48
  7.0 0.2 convolution_bitcast_fusion.2
  7.2 0.4 %fusion.54 = f32[128,324]{0,1:T(8,128)S(1)} fusion(f32[400,128]{1,0:T(8,128)S(1)} %reshape.98, f32[324,400]{1,0:T(8,128)S(1)} %copy-done), kind=kOutput, calls=%fused_computation.122 | convolution fusion | flops 99532800 | bytes 889088 | tf_op jit(solution)/shard_map/dot_general | solution.py:48
  7.7 0.2 convolution_bitcast_fusion
  7.9 0.5 %collective-permute-start = (f32[12,324]{1,0:T(8,128)S(1)}, f32[12,324]{1,0:T(8,128)S(1)}, u32[]{:S(2)}, u32[]{:S(2)}) collective-permute-start(f32[12,324]{1,0:T(8,128)S(1)} %reshape.99), channel_id=1, source_target_pairs={{0,1},{1,2},{2,3},{3,4},{4,5},{5,6},{6,7},{7,0},{8,9},{9,10},{10,1... | collective-permute-start | bytes 46664 | tf_op jit(solution)/shard_map/ppermute | solution.py:59
  8.5 4.1 %collective-permute-start.1 = (f32[8,324]{1,0:T(8,128)S(1)}, f32[8,324]{1,0:T(8,128)S(1)}, u32[]{:S(2)}, u32[]{:S(2)}) collective-permute-start(f32[8,324]{1,0:T(8,128)S(1)} %reshape.101), channel_id=1, source_target_pairs={{0,7},{1,0},{2,1},{3,2},{4,3},{5,4},{6,5},{7,6},{8,15},{9,8},{10,9... | collective-permute-start | bytes 31112 | tf_op jit(solution)/shard_map/ppermute | solution.py:59
  12.6 1.4 %collective-permute-done.1 = f32[8,324]{1,0:T(8,128)S(1)} collective-permute-done((f32[8,324]{1,0:T(8,128)S(1)}, f32[8,324]{1,0:T(8,128)S(1)}, u32[]{:S(2)}, u32[]{:S(2)}) %collective-permute-start.1) | collective-permute-done | bytes 10400 | tf_op jit(solution)/shard_map/ppermute | solution.py:59
  14.0 0.4 %fusion.37 = f32[324,132]{0,1:T(8,128)S(1)} fusion(f32[5,132]{1,0:T(8,128)S(1)} %copy-done.7, f32[4,3,324]{2,1,0:T(4,128)S(1)} %reshape.100, f32[4,2,324]{2,1,0:T(2,128)S(1)} %reshape.102), kind=kOutput, calls=%fused_computation.98 | convolution fusion | flops 2567700 | bytes 199632 | tf_op jit(solution)/shard_map/dot_general | solution.py:229
  14.5 0.4 %fusion.41 = f32[324,132]{0,1:T(8,128)S(1)} fusion(f32[5,132]{1,0:T(8,128)S(1)} %copy-done.7, f32[4,3,324]{2,1,0:T(4,128)S(1)} %reshape.100, f32[4,2,324]{2,1,0:T(2,128)S(1)} %reshape.102), kind=kOutput, calls=%fused_computation.101 | convolution fusion | flops 2567700 | bytes 199632 | tf_op jit(solution)/shard_map/dot_general | solution.py:229
  14.9 0.4 %fusion.33 = f32[324,132]{0,1:T(8,128)S(1)} fusion(f32[5,132]{1,0:T(8,128)S(1)} %copy-done.7, f32[4,3,324]{2,1,0:T(4,128)S(1)} %reshape.100, f32[4,2,324]{2,1,0:T(2,128)S(1)} %reshape.102), kind=kOutput, calls=%fused_computation.95 | convolution fusion | flops 2567700 | bytes 199632 | tf_op jit(solution)/shard_map/dot_general | solution.py:229
  15.4 0.2 copy.57
  15.6 0.1 slice.287
  15.7 0.4 %convolution_add_fusion.2 = f32[324,132]{0,1:T(8,128)S(1)} fusion(f32[324,132]{0,1:T(8,128)S(1)} %fusion.37, f32[160,324]{1,0:T(8,128)S(1)} %fusion.52, f32[160,132]{1,0:T(8,128)S(1)} %copy-done.1), kind=kOutput, calls=%fused_computation.15 | convolution fusion | flops 41100048 | bytes 633984 | tf_op jit(solution)/shard_map/dot_general | solution.py:226
  16.1 0.1 copy.54
  16.3 0.4 %convolution_add_fusion.1 = f32[324,132]{0,1:T(8,128)S(1)} fusion(f32[324,132]{0,1:T(8,128)S(1)} %fusion.41, f32[160,324]{1,0:T(8,128)S(1)} %fusion.53, f32[160,132]{1,0:T(8,128)S(1)} %copy-done.1), kind=kOutput, calls=%fused_computation.14 | convolution fusion | flops 41100048 | bytes 633984 | tf_op jit(solution)/shard_map/dot_general | solution.py:226
  16.7 0.1 copy.55
  16.9 0.3 copy-done.6
  17.2 0.3 convolution_add_fusion
  17.5 0.1 copy.56
  17.7 0.2 add_bitcast_fusion
  17.9 0.1 pad_maximum_fusion
  18.2 0.1 reshape.103
  18.4 2.1 %collective-permute-start.2 = (f32[20,1188]{1,0:T(8,128)S(1)}, f32[20,1188]{1,0:T(8,128)S(1)}, u32[]{:S(2)}, u32[]{:S(2)}) collective-permute-start(f32[20,1188]{1,0:T(8,128)S(1)} %pad_maximum_fusion.4), channel_id=1, source_target_pairs={{0,8},{8,0},{1,9},{9,1},{2,10},{10,2},{3,11},{11,3},{4,12},{12,4},... | collective-permute-start | bytes 285128 | tf_op jit(solution)/shard_map/ppermute | solution.py:59
  20.5 3.6 %collective-permute-done.2 = f32[20,1188]{1,0:T(8,128)S(1)} collective-permute-done((f32[20,1188]{1,0:T(8,128)S(1)}, f32[20,1188]{1,0:T(8,128)S(1)}, u32[]{:S(2)}, u32[]{:S(2)}) %collective-permute-start.2) | collective-permute-done | bytes 95072 | tf_op jit(solution)/shard_map/ppermute | solution.py:59
  24.1 0.1 reshape.106
  24.3 0.2 reshape.105
  24.6 0.2 pad_add_fusion
  26.0 0.6 %concatenate.58 = f32[527,128]{1,0:T(8,128)S(1)} concatenate(f32[192,128]{1,0:T(8,128)S(1)} %bitcast.107, f32[96,128]{1,0:T(8,128)S(1)} %bitcast.110, f32[12,128]{1,0:T(8,128)S(1)} %reshape.109, f32[3,128]{1,0:T(4,128)S(1)} %reshape.110, f32[96,128]{1,0:T(8,128)S(1)} %bitcast.111, f32[32,128]{1,0:T(8,128)S(1)} %slice.305, f32[96,128]{1,0:T(8,128)S(1)} %bitcast.109), dimensions={0} | concatenate | bytes 539648 | tf_op jit(solution)/shard_map/concatenate | solution.py:64
  26.5 1.8 %collective-permute-start.3 = (f32[527,128]{1,0:T(8,128)S(1)}, f32[527,128]{1,0:T(8,128)S(1)}, u32[]{:S(2)}, u32[]{:S(2)}) collective-permute-start(f32[527,128]{1,0:T(8,128)S(1)} %concatenate.58), channel_id=1, source_target_pairs={{0,16},{16,0},{1,17},{17,1},{2,18},{18,2},{3,19},{19,3},{4,20},{20... | collective-permute-start | bytes 809480 | tf_op jit(solution)/shard_map/ppermute | solution.py:59
  28.3 0.1 slice_multiply_fusion
  28.4 6.2 %collective-permute-done.3 = f32[527,128]{1,0:T(8,128)S(1)} collective-permute-done((f32[527,128]{1,0:T(8,128)S(1)}, f32[527,128]{1,0:T(8,128)S(1)}, u32[]{:S(2)}, u32[]{:S(2)}) %collective-permute-start.3) | collective-permute-done | bytes 269856 | tf_op jit(solution)/shard_map/ppermute | solution.py:59
  35.2 0.1 maximum_bitcast_fusion
  35.4 0.1 fusion
  35.5 2.0 %fusion.5 = f32[3,8,32,128]{3,2,1,0:T(8,128)} fusion(f32[3,7,36,132]{3,2,1,0:T(8,128)S(1)} %slice_multiply_fusion, f32[3,1,36,132]{3,2,1,0:T(8,128)S(1)} %fusion.30, f32[3,1,32,128]{3,2,1,0:T(8,128)S(1)} %bitcast.114, f32[3,1,36,132]{3,2,1,0:T(8,128)S(1)} %pad.51, f32[3,10,36,132]{3,2,1,0:T(8,128)S(1)} %fusion), kind=kLoop, calls=%fused_computation.32 | loop fusion | flops 3440640 | bytes 1742016 | tf_op jit(solution)/shard_map/mul | solution.py:177
  (88 shorter events, 3.2 us)
Async XLA Ops:
  2.8 1.4 %copy-start.4 = (f32[2,5,8,4,160]{4,3,2,1,0:T(4,128)S(1)}, f32[2,5,8,4,160]{4,3,2,1,0:T(4,128)}, u32[]{:S(2)}) copy-start(f32[2,5,8,4,160]{4,3,2,1,0:T(4,128)} %param.16) | copy-start | bytes 614404
  3.2 1.2 %copy-start.5 = (f32[2,4,8,5,160]{4,2,3,1,0:T(8,128)S(1)}, f32[2,4,8,5,160]{4,2,3,1,0:T(8,128)}, u32[]{:S(2)}) copy-start(f32[2,4,8,5,160]{4,2,3,1,0:T(8,128)} %param.15) | copy-start | bytes 614404
  4.3 1.0 %copy-start.3 = (f32[324,320]{1,0:T(8,128)S(1)}, f32[324,320]{1,0:T(8,128)}, u32[]{:S(2)}) copy-start(f32[324,320]{1,0:T(8,128)} %constant.35.clone) | copy-start | bytes 1244164
  4.4 1.6 %copy-start.8 = (f32[5,160]{1,0:T(8,128)S(1)}, f32[5,160]{1,0:T(8,128)}, u32[]{:S(2)}) copy-start(f32[5,160]{1,0:T(8,128)} %constant.34.clone) | copy-start | bytes 9604
  4.5 1.8 %copy-start.2 = (f32[324,320]{1,0:T(8,128)S(1)}, f32[324,320]{1,0:T(8,128)}, u32[]{:S(2)}) copy-start(f32[324,320]{1,0:T(8,128)} %constant.14.clone) | copy-start | bytes 1244164
  5.3 1.9 %copy-start = (f32[324,400]{1,0:T(8,128)S(1)}, f32[324,400]{1,0:T(8,128)}, u32[]{:S(2)}) copy-start(f32[324,400]{1,0:T(8,128)} %constant.36.clone) | copy-start | bytes 1555204
  6.1 1.6 %copy-start.9 = (f32[5,128]{1,0:T(8,128)S(1)}, f32[5,128]{1,0:T(8,128)}, u32[]{:S(2)}) copy-start(f32[5,128]{1,0:T(8,128)} %constant.37.clone) | copy-start | bytes 7684
  6.3 7.8 %copy-start.7 = (f32[5,132]{1,0:T(8,128)S(1)}, f32[5,132]{1,0:T(8,128)}, u32[]{:S(2)}) copy-start(f32[5,132]{1,0:T(8,128)} %constant.38.clone) | copy-start | bytes 7924
  7.2 8.5 %copy-start.1 = (f32[160,132]{1,0:T(8,128)S(1)}, f32[160,132]{1,0:T(8,128)}, u32[]{:S(2)}) copy-start(f32[160,132]{1,0:T(8,128)} %constant.39.clone) | copy-start | bytes 253444
  7.9 6.1 %collective-permute-start = (f32[12,324]{1,0:T(8,128)S(1)}, f32[12,324]{1,0:T(8,128)S(1)}, u32[]{:S(2)}, u32[]{:S(2)}) collective-permute-start(f32[12,324]{1,0:T(8,128)S(1)} %reshape.99), channel_id=1, source_target_pairs={{0,1},{1,2},{2,3},{3,4},{4,5},{5,6},{6,7},{7,0},{8,9},{9,10},{10,1... | collective-permute-start | bytes 46664 | tf_op jit(solution)/shard_map/ppermute | solution.py:59
  8.5 5.5 %collective-permute-start.1 = (f32[8,324]{1,0:T(8,128)S(1)}, f32[8,324]{1,0:T(8,128)S(1)}, u32[]{:S(2)}, u32[]{:S(2)}) collective-permute-start(f32[8,324]{1,0:T(8,128)S(1)} %reshape.101), channel_id=1, source_target_pairs={{0,7},{1,0},{2,1},{3,2},{4,3},{5,4},{6,5},{7,6},{8,15},{9,8},{10,9... | collective-permute-start | bytes 31112 | tf_op jit(solution)/shard_map/ppermute | solution.py:59
  16.3 0.9 %copy-start.6 = (f32[128,132]{1,0:T(8,128)S(1)}, f32[128,132]{1,0:T(8,128)}, u32[]{:S(2)}) copy-start(f32[128,132]{1,0:T(8,128)} %constant.40.clone) | copy-start | bytes 202756
  18.4 5.7 %collective-permute-start.2 = (f32[20,1188]{1,0:T(8,128)S(1)}, f32[20,1188]{1,0:T(8,128)S(1)}, u32[]{:S(2)}, u32[]{:S(2)}) collective-permute-start(f32[20,1188]{1,0:T(8,128)S(1)} %pad_maximum_fusion.4), channel_id=1, source_target_pairs={{0,8},{8,0},{1,9},{9,1},{2,10},{10,2},{3,11},{11,3},{4,12},{12,4},... | collective-permute-start | bytes 285128 | tf_op jit(solution)/shard_map/ppermute | solution.py:59
  26.5 8.1 %collective-permute-start.3 = (f32[527,128]{1,0:T(8,128)S(1)}, f32[527,128]{1,0:T(8,128)S(1)}, u32[]{:S(2)}, u32[]{:S(2)}) collective-permute-start(f32[527,128]{1,0:T(8,128)S(1)} %concatenate.58), channel_id=1, source_target_pairs={{0,16},{16,0},{1,17},{17,1},{2,18},{18,2},{3,19},{19,3},{4,20},{20... | collective-permute-start | bytes 809480 | tf_op jit(solution)/shard_map/ppermute | solution.py:59

commit v9 on v5

--- a/solution.py
+++ b/solution.py
@@ -39,19 +39,19 @@
     return matrix
 
 
-def interpolate(coef, flip, table_x, table_y, table_z):
+def signed_coefficients(coef, flip, size_z):
     ex_count, size_x, ey_count, size_y, merged = coef.shape
-    size_z = table_z.shape[1]
-    ez_count = merged // size_z
-    precise = lax.Precision.HIGHEST
     orient = jnp.repeat((1 - 2 * flip).astype(jnp.float32), size_z, axis=2)
-    signed = (coef * orient[:, None, :, None, :]).reshape(ex_count * size_x * ey_count * size_y, merged)
+    return (coef * orient[:, None, :, None, :]).reshape(ex_count * size_x * ey_count * size_y, merged)
+
+
+def plane_map_of(table_x, table_y, ex_count, ey_count):
     rows_y = np.pad(assembly_matrix(table_y, ey_count), ((2, 1), (0, 0)))
-    plane_map = np.kron(assembly_matrix(table_x, ex_count), rows_y)
-    depth_map = np.pad(assembly_matrix(table_z, ez_count), ((2, 1), (0, 0)))
-    deep = jnp.dot(signed, jnp.asarray(depth_map.T, jnp.float32), precision=precise)
-    nodal = jnp.dot(jnp.asarray(plane_map, jnp.float32), deep, precision=precise)
-    return nodal.reshape(4 * ex_count + 1, 4 * ey_count + 4, 4 * ez_count + 4)
+    return np.kron(assembly_matrix(table_x, ex_count), rows_y)
+
+
+def depth_map_of(table_z, merged):
+    return np.pad(assembly_matrix(table_z, merged // table_z.shape[1]), ((2, 1), (0, 0)))
 
 
 def shifted(block, axis, step=1):
@@ -182,15 +182,47 @@
 def body(edge_coeffs_x, edge_coeffs_y, edge_coeffs_z, flips, flags):
     closed_map, open_map = basis_tables()
     nx, ny, nz = flags.shape
-    nodal_x = interpolate(edge_coeffs_x, flips[0], open_map, closed_map, closed_map)
-    nodal_y = interpolate(edge_coeffs_y, flips[1], closed_map, open_map, closed_map)
-    nodal_z = interpolate(edge_coeffs_z, flips[2], closed_map, closed_map, open_map)
+    precise = lax.Precision.HIGH
+    inputs = [
+        (edge_coeffs_x, flips[0], open_map, closed_map, closed_map),
+        (edge_coeffs_y, flips[1], closed_map, open_map, closed_map),
+        (edge_coeffs_z, flips[2], closed_map, closed_map, open_map),
+    ]
     keep = jnp.pad((1 - flags).astype(jnp.float32), ((0, 1), (2, 2), (2, 2)))
-    extended = jnp.stack([nodal_x, nodal_y, nodal_z, keep])
+    boundary = [nx - 2, nx - 1, nx, 0, 1]
+    slabs = []
+    nodal = []
+    for coef, flip, table_x, table_y, table_z in inputs:
+        signed = signed_coefficients(coef, flip, table_z.shape[1])
+        plane_map = plane_map_of(table_x, table_y, coef.shape[0], coef.shape[2])
+        depth_map = jnp.asarray(depth_map_of(table_z, coef.shape[4]).T, jnp.float32)
+        rows = plane_map.reshape(nx + 1, ny + 4, -1)[boundary].reshape(-1, plane_map.shape[1])
+        edge = jnp.dot(jnp.asarray(rows, jnp.float32), signed, precision=precise)
+        slabs.append(jnp.dot(edge, depth_map, precision=precise).reshape(5, ny + 4, nz + 4))
+        planar = jnp.dot(jnp.asarray(plane_map, jnp.float32), signed, precision=precise)
+        nodal.append(jnp.dot(planar, depth_map, precision=precise).reshape(nx + 1, ny + 4, nz + 4))
+    slabs.append(keep[np.array(boundary)])
+    slabs = jnp.stack(slabs)
+    channels = slabs.shape[0]
+    up = slabs[:, :3].reshape(channels * 3, -1)
+    down = slabs[:, 3:].reshape(channels * 2, -1)
+    from_prev, from_next = both_ways(up, down, "gx")
+    from_prev = from_prev.reshape(channels, 3, ny + 4, nz + 4)
+    from_next = from_next.reshape(channels, 2, ny + 4, nz + 4)
+    partial = jnp.stack(nodal + [keep])
+    extended = jnp.concatenate(
+        [
+            from_prev[:, 0:2],
+            partial[:, 0:1] + from_prev[:, 2:3],
+            partial[:, 1:nx],
+            partial[:, nx : nx + 1] + from_next[:, 0:1],
+            from_next[:, 1:2],
+        ],
+        axis=1,
+    )
     extended = fold_and_halo(extended, "gz", 3)
     extended = fold_and_halo(extended, "gy", 2)
-    masked = fold_and_halo_last(extended, "gx", ny, nz)
-    return stencil_apply(masked)
+    return stencil_apply(extended[:3] * extended[3])
 
 
 def solution(mesh):

time: 40.8 us -> 52.6 us (1.29)
  local copies, waits for them, and re-layouts: 9.23 us -> 16.4 us
  matrix products: 3.8 us -> 7.51 us
  other arithmetic: 7.43 us -> 9.06 us
  waiting for transfers between devices: 11.3 us -> 10 us
    dot_general x6 -> x12, matrix products: 3.8 us -> 7.51 us  [the longest x3 4.09 us: body(): jnp.dot(jnp.asarray(plane_map, jnp.float32), signed, precision=precise)]
    reshape x6 -> x7, local copies, waits for them, and re-layouts: 0.31 us -> 3.54 us  [the longest x1 1.84 us: body(): from_next = from_next.reshape(channels, 2, ny + 4, nz + 4)]
    unnamed x26 -> x28, local copies, waits for them, and re-layouts: 0.93 us -> 3.71 us
    slice x2 -> x4, local copies, waits for them, and re-layouts: 0.01 us -> 2.64 us  [both_ways(): return (both[:up.shape[0]], both[up.shape[0]:])]
    ppermute x4, waiting for transfers between devices: 11.3 us -> 10 us  [shifted(): lax.ppermute(block, axis, [(i, (i + step) % count) for i in range(count)])]
    another operation x1 -> x2, other arithmetic: 0.14 us -> 1.36 us  [the longest x1 1.27 us: body(): partial = jnp.stack(nodal + [keep])]
    unnamed x0 -> x2, other arithmetic: none -> 0.97 us
    convert_element_type x1, other arithmetic: 0.93 us -> 0.01 us  [body(): keep = jnp.pad((1 - flags).astype(jnp.float32), ((0, 1), (2, 2), (2, 2)))]
  transfers between devices with their start and end apart: 4 -> 4, of which waited for: 3 -> 3; matrix products, arithmetic and copies ran while one was open for 6% -> 16% of each run, Pallas kernels for 0% -> 0%
where the time goes in v9:
time: 52.6 us; the launch traced here: 52.2 us
  local copies, waits for them, and re-layouts  16.4 us (31%)
  waiting for transfers between devices  10 us (19%)
  other arithmetic  9.06 us (17%)
  starting transfers between devices  8.59 us (16%)
  matrix products  7.51 us (14%)
  between operations  0.6 us (1%)
    ppermute x4, waiting for transfers between devices, shifted(): lax.ppermute(block, axis, [(i, (i + step) % count) for i in range(count)])  10 us
    ppermute x4, starting transfers between devices, shifted(): lax.ppermute(block, axis, [(i, (i + step) % count) for i in range(count)])  8.59 us
    dot_general x3, matrix products, body(): jnp.dot(jnp.asarray(plane_map, jnp.float32), signed, precision=precise)  4.09 us
    unnamed x28, local copies, waits for them, and re-layouts  3.71 us
    slice x4, local copies, waits for them, and re-layouts, both_ways(): return (both[:up.shape[0]], both[up.shape[0]:])  2.64 us
    reshape x8, local copies, waits for them, and re-layouts, from_wire(): return jnp.moveaxis(rows.reshape(shape), 0, dim)  2.56 us
    mul x1, other arithmetic, stencil_apply(): return 0.25 * total  2.03 us
    reshape x1, local copies, waits for them, and re-layouts, body(): from_next = from_next.reshape(channels, 2, ny + 4, nz + 4)  1.84 us
  transfers between devices with their start and end apart: 4, of which 3 were waited for; matrix products, arithmetic and copies ran while one was open for 16% of the time, Pallas kernels for 0%

profile of v9, /device:TPU:0, one launch (start us, length us, event | category | flops | bytes accessed | tf_op | source)
XLA Modules:
  0.0 52.2 jit_solution(14076565931288571292)
XLA Ops:
  0.0 0.8 %convert_bitcast_fusion.2 = (f32[2,8,32]{2,1,0:T(8,128)S(1)}, f32[2,8,32]{2,1,0:T(8,128)S(1)}, f32[2,8,32]{2,1,0:T(8,128)S(1)}) fusion(s32[3,2,8,32]{3,2,1,0:T(8,128)} %param.19), kind=kLoop, calls=%fused_computation.50 | loop fusion | flops 4608 | bytes 12288 | tf_op jit(solution)/shard_map/convert_element_type | solution.py:44
  0.9 0.2 mul.83
  1.1 1.0 %broadcast_multiply_fusion.1 = f32[2,4,8,5,160]{4,2,3,1,0:T(8,128)S(1)} fusion(f32[2,4,8,5,160]{4,2,3,1,0:T(8,128)} %param.16, f32[2,8,160]{2,1,0:T(8,128)S(1)} %mul.83), kind=kLoop, calls=%fused_computation.41 | loop fusion | flops 51200 | bytes 419840 | tf_op jit(solution)/shard_map/mul | solution.py:45
  2.1 0.1 copy.41
  2.3 0.5 fusion.15
  2.8 0.3 fusion.16
  3.4 0.2 mul.87
  3.8 0.5 fusion.17
  4.2 0.3 fusion.18
  5.0 0.3 fusion.19
  5.3 0.2 fusion.20
  5.6 0.1 pad_bitcast_fusion
  5.8 0.6 %gather_fusion = f32[5,36,132]{2,1,0:T(8,128)S(1)} fusion(f32[9,36,132]{2,1,0:T(8,128)S(1)} %get-tuple-element.6, s32[1024]{0:T(1024)S(1)} %pad_clamp_fusion), kind=kCustom, calls=%fused_computation | custom fusion | bytes 190100 | tf_op jit(solution)/shard_map/gather | solution.py:204
  6.5 0.2 reshape.66
  6.7 0.2 reshape.67
  6.9 0.8 %pad_maximum_fusion.2 = f32[20,4752]{1,0:T(8,128)} fusion(f32[8,4752]{1,0:T(8,128)S(1)} %reshape.67, f32[12,4752]{1,0:T(8,128)S(1)} %reshape.66), kind=kLoop, calls=%fused_computation.10 | loop fusion | flops 95040 | bytes 760320 | tf_op jit(solution)/shard_map/concatenate | solution.py:66
  7.7 2.9 %collective-permute-start = (f32[20,4752]{1,0:T(8,128)}, f32[20,4752]{1,0:T(8,128)}, u32[]{:S(2)}, u32[]{:S(2)}) collective-permute-start(f32[20,4752]{1,0:T(8,128)} %pad_maximum_fusion.2), channel_id=1, source_target_pairs={{0,16},{16,0},{1,17},{17,1},{2,18},{18,2},{3,19},{19,3},{4,20},{20... | collective-permute-start | bytes 1140488 | tf_op jit(solution)/shard_map/ppermute | solution.py:61
  10.7 0.8 %fusion.21 = f32[160,324]{1,0:T(8,128)S(1)} fusion(f32[320,160]{1,0:T(8,128)S(1)} %reshape.63, f32[324,320]{1,0:T(8,128)S(1)} %copy-done.5), kind=kOutput, calls=%fused_computation.58 | convolution fusion | flops 99532800 | bytes 826880 | tf_op jit(solution)/shard_map/dot_general | solution.py:202
  11.4 0.5 fusion.22
  12.0 1.8 %fusion.23 = f32[160,324]{1,0:T(8,128)S(1)} fusion(f32[320,160]{1,0:T(8,128)S(1)} %reshape.64, f32[324,320]{1,0:T(8,128)} %constant.42.clone), kind=kOutput, calls=%fused_computation.60 | convolution fusion | flops 99532800 | bytes 826880 | tf_op jit(solution)/shard_map/dot_general | solution.py:202
  13.8 0.5 fusion.24
  14.3 1.5 %fusion.25 = f32[128,324]{0,1:T(8,128)S(1)} fusion(f32[400,128]{1,0:T(8,128)S(1)} %reshape.65, f32[324,400]{1,0:T(8,128)} %constant.45.clone), kind=kOutput, calls=%fused_computation.62 | convolution fusion | flops 99532800 | bytes 889088 | tf_op jit(solution)/shard_map/dot_general | solution.py:202
  15.8 0.3 fusion.26
  16.2 1.3 %pad_maximum_fusion = f32[4,9,36,132]{3,2,1,0:T(8,128)} fusion(f32[1,9,36,132]{3,2,1,0:T(8,128)S(1)} %get-tuple-element.5, f32[1,9,36,132]{3,2,1,0:T(8,128)S(1)} %stack_reshape.23, f32[1,9,36,132]{3,2,1,0:T(8,128)S(1)} %stack_reshape.22, f32[1,9,36,132]{3,2,1,0:T(8,128)S(1)} %stack_reshape.21), kind=kLoop, calls=%fused_computation.4 | loop fusion | flops 513216 | bytes 1368576 | tf_op jit(solution)/shard_map/stack | solution.py:212
  17.4 4.2 %collective-permute-done = f32[20,4752]{1,0:T(8,128)} collective-permute-done((f32[20,4752]{1,0:T(8,128)}, f32[20,4752]{1,0:T(8,128)}, u32[]{:S(2)}, u32[]{:S(2)}) %collective-permute-start) | collective-permute-done | bytes 380192 | tf_op jit(solution)/shard_map/ppermute | solution.py:61
  21.7 1.0 %slice.143 = f32[12,4752]{1,0:T(8,128)S(1)} slice(f32[20,4752]{1,0:T(8,128)} %collective-permute-done), slice={[0:12], [0:4752]} | slice | bytes 456192 | tf_op jit(solution)/shard_map/slice | solution.py:67
  22.7 1.1 %reshape.68 = f32[4,3,36,132]{3,2,1,0:T(8,128)} reshape(f32[12,4752]{1,0:T(8,128)S(1)} %slice.143) | data formatting | bytes 456192 | tf_op jit(solution)/shard_map/reshape | solution.py:210
  23.8 1.0 %slice_dynamic-update-slice_fusion.1 = f32[4,12,36,132]{3,2,1,0:T(8,128)S(1)} fusion(f32[4,3,36,132]{3,2,1,0:T(8,128)} %reshape.68), kind=kLoop, calls=%fused_computation.31 | loop fusion | bytes 479744
  24.7 0.9 %fusion.14 = f32[4,12,36,132]{3,2,1,0:T(8,128)S(1)} fusion(f32[4,12,36,132]{3,2,1,0:T(8,128)S(1)} %slice_dynamic-update-slice_fusion.1, f32[4,3,36,132]{3,2,1,0:T(8,128)} %reshape.68, f32[1,9,36,132]{3,2,1,0:T(8,128)S(1)} %get-tuple-element.5, f32[1,9,36,132]{3,2,1,0:T(8,128)S(1)} %stack_reshape.23, f32[1,9,36,132]{3,2,1,0:T(8,128)S(1)} %stack_reshape.22, ...), kind=kLoop, calls=%fused_computation.39 | loop fusion | flops 76032 | bytes 1714432
  25.7 1.6 %slice.147 = f32[8,4752]{1,0:T(8,128)} slice(f32[20,4752]{1,0:T(8,128)} %collective-permute-done), slice={[12:20], [0:4752]} | slice | bytes 304128 | tf_op jit(solution)/shard_map/slice | solution.py:67
  27.3 1.8 %reshape.69 = f32[4,2,36,132]{3,2,1,0:T(8,128)} reshape(f32[8,4752]{1,0:T(8,128)} %slice.147) | data formatting | bytes 304128 | tf_op jit(solution)/shard_map/reshape | solution.py:211
  29.2 1.4 %slice_dynamic-update-slice_fusion = f32[4,12,36,132]{3,2,1,0:T(8,128)S(1)} fusion(f32[4,12,36,132]{3,2,1,0:T(8,128)S(1)} %fusion.14, f32[4,9,36,132]{3,2,1,0:T(8,128)} %pad_maximum_fusion), kind=kLoop, calls=%fused_computation.5 | loop fusion | bytes 1679104
  30.7 0.5 %copy.51 = f32[3,4,12,36]{3,2,1,0:T(8,128)S(1)} copy(f32[3,4,12,36]{0,3,2,1:T(8,128)S(1)} %slice_bitcast_fusion.1) | data formatting | bytes 41472 | tf_op jit(solution)/shard_map/transpose | solution.py:72
  31.4 0.3 slice_bitcast_fusion
  31.8 0.5 %copy.53 = f32[2,4,12,36]{3,2,1,0:T(8,128)S(1)} copy(f32[2,4,12,36]{0,3,2,1:T(8,128)S(1)} %slice_bitcast_fusion) | data formatting | bytes 27648 | tf_op jit(solution)/shard_map/transpose | solution.py:72
  32.4 3.8 %collective-permute-start.2 = (f32[8,432]{1,0:T(8,128)S(1)}, f32[8,432]{1,0:T(8,128)S(1)}, u32[]{:S(2)}, u32[]{:S(2)}) collective-permute-start(f32[8,432]{1,0:T(8,128)S(1)} %reshape.72), channel_id=1, source_target_pairs={{0,7},{1,0},{2,1},{3,2},{4,3},{5,4},{6,5},{7,6},{8,15},{9,8},{10,9... | collective-permute-start | bytes 41480 | tf_op jit(solution)/shard_map/ppermute | solution.py:61
  36.2 1.4 %collective-permute-done.2 = f32[8,432]{1,0:T(8,128)S(1)} collective-permute-done((f32[8,432]{1,0:T(8,128)S(1)}, f32[8,432]{1,0:T(8,128)S(1)}, u32[]{:S(2)}, u32[]{:S(2)}) %collective-permute-start.2) | collective-permute-done | bytes 13856 | tf_op jit(solution)/shard_map/ppermute | solution.py:61
  37.7 0.5 copy.54
  38.3 1.4 %copy.52 = f32[3,4,12,36]{0,3,2,1:T(8,128)} copy(f32[3,4,12,36]{3,2,1,0:T(8,128)S(1)} %reshape.71) | data formatting | bytes 41472 | tf_op jit(solution)/shard_map/reshape | solution.py:77
  39.7 1.6 %pad_add_fusion.1 = f32[4,12,36,132]{3,2,1,0:T(8,128)S(1)} fusion(f32[4,12,36,2]{3,2,1,0:T(8,128)S(1)} %bitcast.56, f32[4,12,36,132]{3,2,1,0:T(8,128)S(1)} %slice_dynamic-update-slice_fusion.2, f32[4,12,36,3]{3,2,1,0:T(8,128)} %bitcast.57), kind=kLoop, calls=%fused_computation.2 | loop fusion | flops 456192 | bytes 1859328 | tf_op jit(solution)/shard_map/add | solution.py:91
  41.3 1.3 %copy-done = f32[4,12,36,132]{3,2,1,0:T(8,128)} copy-done((f32[4,12,36,132]{3,2,1,0:T(8,128)}, f32[4,12,36,132]{3,2,1,0:T(8,128)S(1)}, u32[]{:S(2)}) %copy-start) | copy-done | bytes 912408
  42.7 0.1 reshape.74
  43.0 1.8 %collective-permute-start.3 = (f32[20,1584]{1,0:T(8,128)S(1)}, f32[20,1584]{1,0:T(8,128)S(1)}, u32[]{:S(2)}, u32[]{:S(2)}) collective-permute-start(f32[20,1584]{1,0:T(8,128)S(1)} %pad_maximum_fusion.4), channel_id=1, source_target_pairs={{0,8},{8,0},{1,9},{9,1},{2,10},{10,2},{3,11},{11,3},{4,12},{12,4},... | collective-permute-start | bytes 380168 | tf_op jit(solution)/shard_map/ppermute | solution.py:61
  44.8 4.4 %collective-permute-done.3 = f32[20,1584]{1,0:T(8,128)S(1)} collective-permute-done((f32[20,1584]{1,0:T(8,128)S(1)}, f32[20,1584]{1,0:T(8,128)S(1)}, u32[]{:S(2)}, u32[]{:S(2)}) %collective-permute-start.3) | collective-permute-done | bytes 126752 | tf_op jit(solution)/shard_map/ppermute | solution.py:61
  49.2 0.2 reshape.76
  49.5 0.1 reshape.77
  49.8 0.2 pad_add_fusion
  50.1 2.0 %fusion.2 = f32[3,8,32,128]{3,2,1,0:T(8,128)} fusion(f32[3,12,36,132]{3,2,1,0:T(8,128)S(1)} %slice_multiply_fusion), kind=kLoop, calls=%fused_computation.14 | loop fusion | flops 1966080 | bytes 5505024 | tf_op jit(solution)/shard_map/mul | solution.py:179
  (68 shorter events, 2.3 us)
Async XLA Ops:
  0.0 2.3 %copy-start.9 = (f32[180,320]{1,0:T(8,128)S(1)}, f32[180,320]{1,0:T(8,128)}, u32[]{:S(2)}) copy-start(f32[180,320]{1,0:T(8,128)} %constant.39.clone) | copy-start | bytes 691204
  0.0 2.8 %copy-start.2 = (f32[160,132]{1,0:T(8,128)S(1)}, f32[160,132]{1,0:T(8,128)}, u32[]{:S(2)}) copy-start(f32[160,132]{1,0:T(8,128)} %constant.38.clone) | copy-start | bytes 253444
  2.1 1.4 %copy-start.7 = (f32[2,5,8,4,160]{4,3,2,1,0:T(4,128)S(1)}, f32[2,5,8,4,160]{4,3,2,1,0:T(4,128)}, u32[]{:S(2)}) copy-start(f32[2,5,8,4,160]{4,3,2,1,0:T(4,128)} %param.17) | copy-start | bytes 614404
  2.3 1.4 %copy-start.8 = (f32[180,320]{1,0:T(8,128)S(1)}, f32[180,320]{1,0:T(8,128)}, u32[]{:S(2)}) copy-start(f32[180,320]{1,0:T(8,128)} %constant.41.clone) | copy-start | bytes 691204
  3.2 1.6 %copy-start.10 = (f32[2,5,8,5,128]{4,2,3,1,0:T(8,128)S(1)}, f32[2,5,8,5,128]{4,2,3,1,0:T(8,128)}, u32[]{:S(2)}) copy-start(f32[2,5,8,5,128]{4,2,3,1,0:T(8,128)} %param.18) | copy-start | bytes 614404
  3.6 1.3 %copy-start.6 = (f32[180,400]{1,0:T(8,128)S(1)}, f32[180,400]{1,0:T(8,128)}, u32[]{:S(2)}) copy-start(f32[180,400]{1,0:T(8,128)} %constant.44.clone) | copy-start | bytes 864004
  3.7 1.5 %copy-start.4 = (f32[128,132]{1,0:T(8,128)S(1)}, f32[128,132]{1,0:T(8,128)}, u32[]{:S(2)}) copy-start(f32[128,132]{1,0:T(8,128)} %constant.43.clone) | copy-start | bytes 202756
  4.6 1.0 %copy-start.11 = (s32[8,32,128]{2,1,0:T(8,128)S(1)}, s32[8,32,128]{2,1,0:T(8,128)}, u32[]{:S(2)}) copy-start(s32[8,32,128]{2,1,0:T(8,128)} %param.20) | copy-start | bytes 393220
  4.8 0.9 %copy-start.12 = (s32[5]{0:T(128)S(1)}, s32[5]{0:T(128)}, u32[]{:S(2)}) copy-start(s32[5]{0:T(128)} %constant.59) | copy-start | bytes 64
  6.4 4.3 %copy-start.5 = (f32[324,320]{1,0:T(8,128)S(1)}, f32[324,320]{1,0:T(8,128)}, u32[]{:S(2)}) copy-start(f32[324,320]{1,0:T(8,128)} %constant.40.clone) | copy-start | bytes 1244164
  7.7 13.9 %collective-permute-start = (f32[20,4752]{1,0:T(8,128)}, f32[20,4752]{1,0:T(8,128)}, u32[]{:S(2)}, u32[]{:S(2)}) collective-permute-start(f32[20,4752]{1,0:T(8,128)} %pad_maximum_fusion.2), channel_id=1, source_target_pairs={{0,16},{16,0},{1,17},{17,1},{2,18},{18,2},{3,19},{19,3},{4,20},{20... | collective-permute-start | bytes 1140488 | tf_op jit(solution)/shard_map/ppermute | solution.py:61
  29.2 1.4 %copy-start.3 = (f32[4,2,36,132]{3,2,1,0:T(8,128)S(1)}, f32[4,2,36,132]{3,2,1,0:T(8,128)}, u32[]{:S(2)}) copy-start(f32[4,2,36,132]{3,2,1,0:T(8,128)} %reshape.69) | copy-start | bytes 456196
  31.4 6.8 %collective-permute-start.1 = (f32[12,432]{1,0:T(8,128)S(1)}, f32[12,432]{1,0:T(8,128)S(1)}, u32[]{:S(2)}, u32[]{:S(2)}) collective-permute-start(f32[12,432]{1,0:T(8,128)S(1)} %reshape.70), channel_id=1, source_target_pairs={{0,1},{1,2},{2,3},{3,4},{4,5},{5,6},{6,7},{7,0},{8,9},{9,10},{10,1... | collective-permute-start | bytes 62216 | tf_op jit(solution)/shard_map/ppermute | solution.py:61
  32.4 5.2 %collective-permute-start.2 = (f32[8,432]{1,0:T(8,128)S(1)}, f32[8,432]{1,0:T(8,128)S(1)}, u32[]{:S(2)}, u32[]{:S(2)}) collective-permute-start(f32[8,432]{1,0:T(8,128)S(1)} %reshape.72), channel_id=1, source_target_pairs={{0,7},{1,0},{2,1},{3,2},{4,3},{5,4},{6,5},{7,6},{8,15},{9,8},{10,9... | collective-permute-start | bytes 41480 | tf_op jit(solution)/shard_map/ppermute | solution.py:61
  41.3 1.3 %copy-start = (f32[4,12,36,132]{3,2,1,0:T(8,128)}, f32[4,12,36,132]{3,2,1,0:T(8,128)S(1)}, u32[]{:S(2)}) copy-start(f32[4,12,36,132]{3,2,1,0:T(8,128)S(1)} %pad_add_fusion.1) | copy-start | bytes 2737156
  42.6 7.1 %copy-start.1 = (f32[4,12,36,132]{3,2,1,0:T(8,128)S(1)}, f32[4,12,36,132]{3,2,1,0:T(8,128)}, u32[]{:S(2)}) copy-start(f32[4,12,36,132]{3,2,1,0:T(8,128)} %copy-done) | copy-start | bytes 2737156
  43.0 6.2 %collective-permute-start.3 = (f32[20,1584]{1,0:T(8,128)S(1)}, f32[20,1584]{1,0:T(8,128)S(1)}, u32[]{:S(2)}, u32[]{:S(2)}) collective-permute-start(f32[20,1584]{1,0:T(8,128)S(1)} %pad_maximum_fusion.4), channel_id=1, source_target_pairs={{0,8},{8,0},{1,9},{9,1},{2,10},{10,2},{3,11},{11,3},{4,12},{12,4},... | collective-permute-start | bytes 380168 | tf_op jit(solution)/shard_map/ppermute | solution.py:61

commit v10 on v8

--- a/solution.py
+++ b/solution.py
@@ -109,7 +109,7 @@
     )
 
 
-def fold_and_halo_last(extended, axis, ny, nz):
+def last_round_and_stencil(extended, axis, ny, nz):
     n = extended.shape[1] - 1
     comps = extended.shape[0] - 1
     data = extended[:comps]
@@ -140,41 +140,25 @@
     next_keep = from_next[plane_rows : plane_rows + ny]
     next_halo = from_next[plane_rows + ny :].reshape(comps, ny, nz)
 
-    widths = ((0, 0), (0, 0), (2, 2), (2, 2))
+    inner = data[:, 1:n] * keep[1:n]
     first = (data[:, 0] + fold_in) * keep[0]
     last = (own(data[:, n]) + next_fold) * next_keep
-    return jnp.concatenate(
-        [
-            jnp.pad(prev_halo, widths),
-            first[:, None],
-            data[:, 1:n] * keep[1:n],
-            jnp.pad(last[:, None], widths),
-            jnp.pad(next_halo[:, None], widths),
-        ],
-        axis=1,
-    )
-
-
-def window(padded_array, axis_pos, offset):
-    starts = [0, 2, 2, 2]
-    limits = [
-        padded_array.shape[0],
-        padded_array.shape[1] - 2,
-        padded_array.shape[2] - 2,
-        padded_array.shape[3] - 2,
-    ]
-    starts[axis_pos] = offset
-    limits[axis_pos] = offset + padded_array.shape[axis_pos] - 4
-    return lax.slice(padded_array, tuple(starts), tuple(limits))
-
-
-def stencil_apply(padded_array):
-    total = 8.0 * window(padded_array, 1, 2)
-    for axis_pos in (1, 2, 3):
-        near = window(padded_array, axis_pos, 1) + window(padded_array, axis_pos, 3)
-        far = window(padded_array, axis_pos, 0) + window(padded_array, axis_pos, 4)
-        total = total - 4.0 / 3.0 * near + 1.0 / 12.0 * far
-    return 0.25 * total
+    across = jnp.concatenate([yz_terms(first[:, None], ny, nz), yz_terms(inner, ny, nz)], axis=1)
+    column = jnp.concatenate(
+        [prev_halo, own(first)[:, None], own(inner), last[:, None], next_halo[:, None]], axis=1
+    )
+    near = column[:, 1 : n + 1] + column[:, 3 : n + 3]
+    far = column[:, 0:n] + column[:, 4 : n + 4]
+    return 0.25 * (across - 4.0 / 3.0 * near + 1.0 / 12.0 * far)
+
+
+def yz_terms(block, ny, nz):
+    def part(dy, dz):
+        return block[..., 2 + dy : ny + 2 + dy, 2 + dz : nz + 2 + dz]
+
+    near = part(-1, 0) + part(1, 0) + part(0, -1) + part(0, 1)
+    far = part(-2, 0) + part(2, 0) + part(0, -2) + part(0, 2)
+    return 8.0 * part(0, 0) - 4.0 / 3.0 * near + 1.0 / 12.0 * far
 
 
 def body(edge_coeffs_x, edge_coeffs_y, edge_coeffs_z, flips, flags):
@@ -234,8 +218,7 @@
     )
     extended = jnp.stack(nodal + [keep])
     extended = fold_and_halo(extended, "gy", 2)
-    masked = fold_and_halo_last(extended, "gx", ny, nz)
-    return stencil_apply(masked)
+    return last_round_and_stencil(extended, "gx", ny, nz)
 
 
 def solution(mesh):

time: 37.8 us -> 36.7 us (0.971)
  waiting for transfers between devices: 11.2 us -> 10.5 us
    mul x5, other arithmetic: 2.38 us -> 1.18 us  [the longest x1 0.89 us: last_round_and_stencil(): return 0.25 * (across - 4.0 / 3.0 * near + 1.0 / 12.0 * far)]
    add x0 -> x2, other arithmetic: none -> 0.95 us  [yz_terms(): return 8.0 * part(0, 0) - 4.0 / 3.0 * near + 1.0 / 12.0 * far]
    ppermute x4, waiting for transfers between devices: 11.2 us -> 10.5 us  [shifted(): lax.ppermute(block, axis, [(i, (i + step) % count) for i in range(count)])]
  transfers between devices with their start and end apart: 4 -> 4, of which waited for: 3 -> 3; matrix products, arithmetic and copies ran while one was open for 0% -> 2% of each run, Pallas kernels for 0% -> 0%
where the time goes in v10:
time: 36.7 us; the launch traced here: 36.5 us
  waiting for transfers between devices  10.5 us (29%)
  starting transfers between devices  8.47 us (23%)
  local copies, waits for them, and re-layouts  6.2 us (17%)
  other arithmetic  5.85 us (16%)
  matrix products  4.88 us (13%)
  between operations  0.63 us (2%)
    ppermute x4, waiting for transfers between devices, shifted(): lax.ppermute(block, axis, [(i, (i + step) % count) for i in range(count)])  10.5 us
    ppermute x4, starting transfers between devices, shifted(): lax.ppermute(block, axis, [(i, (i + step) % count) for i in range(count)])  8.47 us
    dot_general x3, matrix products, planar_part(): jnp.dot(jnp.asarray(plane_map, jnp.float32), signed, precision=lax.Precis...  1.98 us
    dot_general x3, matrix products, body(): lax.dot_general(arrived[comp], place, (((0,), (0,)), ((), ())), precision...  1.28 us
    dot_general x3, matrix products, body(): jnp.dot(planars[comp], jnp.asarray(depths[comp].T, jnp.float32), precisio...  1.1 us
    mul x3, other arithmetic, planar_part(): coef * orient[:, None, :, None, :]  1.04 us
    add x2, other arithmetic, yz_terms(): return 8.0 * part(0, 0) - 4.0 / 3.0 * near + 1.0 / 12.0 * far  0.95 us
    unnamed x20, local copies, waits for them, and re-layouts  0.94 us
  transfers between devices with their start and end apart: 4, of which 3 were waited for; matrix products, arithmetic and copies ran while one was open for 2% of the time, Pallas kernels for 0%

profile of v10, /device:TPU:0, one launch (start us, length us, event | category | flops | bytes accessed | tf_op | source)
XLA Modules:
  0.0 36.5 jit_solution(11921010578732274275)
XLA Ops:
  0.0 0.7 %convert_bitcast_fusion.2 = (f32[2,8,32]{2,1,0:T(8,128)S(1)}, f32[2,8,32]{2,1,0:T(8,128)S(1)}, f32[2,8,32]{2,1,0:T(8,128)S(1)}) fusion(s32[3,2,8,32]{3,2,1,0:T(8,128)} %param.18), kind=kLoop, calls=%fused_computation.92 | loop fusion | flops 4608 | bytes 12288 | tf_op jit(solution)/shard_map/convert_element_type | solution.py:44
  0.9 0.9 %subtract_convert_fusion = f32[8,32,128]{2,1,0:T(8,128)S(1)} fusion(s32[8,32,128]{2,1,0:T(8,128)} %param.19), kind=kLoop, calls=%fused_computation.35 | loop fusion | flops 65536 | bytes 262144 | tf_op jit(solution)/shard_map/convert_element_type | solution.py:188
  1.8 0.9 %broadcast_multiply_fusion.2 = f32[2,5,8,5,128]{4,2,3,1,0:T(8,128)S(1)} fusion(f32[2,5,8,5,128]{4,2,3,1,0:T(8,128)} %param.17, f32[2,8,128]{2,1,0:T(8,128)S(1)} %copy.46), kind=kLoop, calls=%fused_computation.42 | loop fusion | flops 51200 | bytes 417792 | tf_op jit(solution)/shard_map/mul | solution.py:45
  2.9 0.1 broadcast_in_dim.22
  3.0 0.2 mul.148
  3.2 0.1 broadcast_in_dim.23
  3.4 0.2 mul.152
  3.6 0.1 copy.48
  3.7 0.1 copy.49
  4.3 0.1 reshape.97
  4.5 0.1 copy.44
  4.7 0.6 %copy-done.3 = f32[324,320]{1,0:T(8,128)S(1)} copy-done((f32[324,320]{1,0:T(8,128)S(1)}, f32[324,320]{1,0:T(8,128)}, u32[]{:S(2)}) %copy-start.3) | copy-done | bytes 414744
  5.3 0.8 %fusion.41 = f32[160,324]{1,0:T(8,128)S(1)} fusion(f32[320,160]{1,0:T(8,128)S(1)} %reshape.97, f32[324,320]{1,0:T(8,128)S(1)} %copy-done.3), kind=kOutput, calls=%fused_computation.107 | convolution fusion | flops 99532800 | bytes 826880 | tf_op jit(solution)/shard_map/dot_general | solution.py:48
  6.1 0.2 convolution_bitcast_fusion.1
  6.3 0.8 %fusion.40 = f32[160,324]{1,0:T(8,128)S(1)} fusion(f32[320,160]{1,0:T(8,128)S(1)} %reshape.96, f32[324,320]{1,0:T(8,128)S(1)} %copy-done.2), kind=kOutput, calls=%fused_computation.106 | convolution fusion | flops 99532800 | bytes 826880 | tf_op jit(solution)/shard_map/dot_general | solution.py:48
  7.0 0.2 convolution_bitcast_fusion.2
  7.2 0.4 %fusion.42 = f32[128,324]{0,1:T(8,128)S(1)} fusion(f32[400,128]{1,0:T(8,128)S(1)} %reshape.98, f32[324,400]{1,0:T(8,128)S(1)} %copy-done), kind=kOutput, calls=%fused_computation.108 | convolution fusion | flops 99532800 | bytes 889088 | tf_op jit(solution)/shard_map/dot_general | solution.py:48
  7.7 0.2 convolution_bitcast_fusion
  7.9 0.5 %collective-permute-start = (f32[12,324]{1,0:T(8,128)S(1)}, f32[12,324]{1,0:T(8,128)S(1)}, u32[]{:S(2)}, u32[]{:S(2)}) collective-permute-start(f32[12,324]{1,0:T(8,128)S(1)} %reshape.99), channel_id=1, source_target_pairs={{0,1},{1,2},{2,3},{3,4},{4,5},{5,6},{6,7},{7,0},{8,9},{9,10},{10,1... | collective-permute-start | bytes 46664 | tf_op jit(solution)/shard_map/ppermute | solution.py:59
  8.5 4.1 %collective-permute-start.1 = (f32[8,324]{1,0:T(8,128)S(1)}, f32[8,324]{1,0:T(8,128)S(1)}, u32[]{:S(2)}, u32[]{:S(2)}) collective-permute-start(f32[8,324]{1,0:T(8,128)S(1)} %reshape.101), channel_id=1, source_target_pairs={{0,7},{1,0},{2,1},{3,2},{4,3},{5,4},{6,5},{7,6},{8,15},{9,8},{10,9... | collective-permute-start | bytes 31112 | tf_op jit(solution)/shard_map/ppermute | solution.py:59
  12.6 1.4 %collective-permute-done.1 = f32[8,324]{1,0:T(8,128)S(1)} collective-permute-done((f32[8,324]{1,0:T(8,128)S(1)}, f32[8,324]{1,0:T(8,128)S(1)}, u32[]{:S(2)}, u32[]{:S(2)}) %collective-permute-start.1) | collective-permute-done | bytes 10400 | tf_op jit(solution)/shard_map/ppermute | solution.py:59
  14.0 0.4 %fusion.25 = f32[324,132]{0,1:T(8,128)S(1)} fusion(f32[5,132]{1,0:T(8,128)S(1)} %copy-done.7, f32[4,3,324]{2,1,0:T(4,128)S(1)} %reshape.100, f32[4,2,324]{2,1,0:T(2,128)S(1)} %reshape.102), kind=kOutput, calls=%fused_computation.84 | convolution fusion | flops 2567700 | bytes 199632 | tf_op jit(solution)/shard_map/dot_general | solution.py:213
  14.5 0.4 %fusion.29 = f32[324,132]{0,1:T(8,128)S(1)} fusion(f32[5,132]{1,0:T(8,128)S(1)} %copy-done.7, f32[4,3,324]{2,1,0:T(4,128)S(1)} %reshape.100, f32[4,2,324]{2,1,0:T(2,128)S(1)} %reshape.102), kind=kOutput, calls=%fused_computation.87 | convolution fusion | flops 2567700 | bytes 199632 | tf_op jit(solution)/shard_map/dot_general | solution.py:213
  14.9 0.4 %fusion.21 = f32[324,132]{0,1:T(8,128)S(1)} fusion(f32[5,132]{1,0:T(8,128)S(1)} %copy-done.7, f32[4,3,324]{2,1,0:T(4,128)S(1)} %reshape.100, f32[4,2,324]{2,1,0:T(2,128)S(1)} %reshape.102), kind=kOutput, calls=%fused_computation.81 | convolution fusion | flops 2567700 | bytes 199632 | tf_op jit(solution)/shard_map/dot_general | solution.py:213
  15.4 0.2 copy.53
  15.6 0.1 slice.316
  15.7 0.4 %convolution_add_fusion.2 = f32[324,132]{0,1:T(8,128)S(1)} fusion(f32[324,132]{0,1:T(8,128)S(1)} %fusion.25, f32[160,324]{1,0:T(8,128)S(1)} %fusion.40, f32[160,132]{1,0:T(8,128)S(1)} %copy-done.1), kind=kOutput, calls=%fused_computation.4 | convolution fusion | flops 41100048 | bytes 633984 | tf_op jit(solution)/shard_map/dot_general | solution.py:210
  16.1 0.1 copy.50
  16.3 0.4 %convolution_add_fusion.1 = f32[324,132]{0,1:T(8,128)S(1)} fusion(f32[324,132]{0,1:T(8,128)S(1)} %fusion.29, f32[160,324]{1,0:T(8,128)S(1)} %fusion.41, f32[160,132]{1,0:T(8,128)S(1)} %copy-done.1), kind=kOutput, calls=%fused_computation.3 | convolution fusion | flops 41100048 | bytes 633984 | tf_op jit(solution)/shard_map/dot_general | solution.py:210
  16.7 0.1 copy.51
  16.9 0.3 copy-done.6
  17.2 0.3 convolution_add_fusion
  17.5 0.1 copy.52
  17.7 0.2 add_bitcast_fusion
  17.9 0.1 pad_maximum_fusion
  18.2 0.1 reshape.103
  18.4 2.1 %collective-permute-start.2 = (f32[20,1188]{1,0:T(8,128)S(1)}, f32[20,1188]{1,0:T(8,128)S(1)}, u32[]{:S(2)}, u32[]{:S(2)}) collective-permute-start(f32[20,1188]{1,0:T(8,128)S(1)} %pad_maximum_fusion.4), channel_id=1, source_target_pairs={{0,8},{8,0},{1,9},{9,1},{2,10},{10,2},{3,11},{11,3},{4,12},{12,4},... | collective-permute-start | bytes 285128 | tf_op jit(solution)/shard_map/ppermute | solution.py:59
  20.5 3.6 %collective-permute-done.2 = f32[20,1188]{1,0:T(8,128)S(1)} collective-permute-done((f32[20,1188]{1,0:T(8,128)S(1)}, f32[20,1188]{1,0:T(8,128)S(1)}, u32[]{:S(2)}, u32[]{:S(2)}) %collective-permute-start.2) | collective-permute-done | bytes 95072 | tf_op jit(solution)/shard_map/ppermute | solution.py:59
  24.1 0.1 reshape.106
  24.3 0.2 reshape.105
  24.6 0.2 pad_add_fusion
  26.0 0.6 %concatenate.52 = f32[527,128]{1,0:T(8,128)S(1)} concatenate(f32[192,128]{1,0:T(8,128)S(1)} %bitcast.113, f32[96,128]{1,0:T(8,128)S(1)} %bitcast.117, f32[12,128]{1,0:T(8,128)S(1)} %reshape.109, f32[3,128]{1,0:T(4,128)S(1)} %reshape.110, f32[96,128]{1,0:T(8,128)S(1)} %bitcast.118, f32[32,128]{1,0:T(8,128)S(1)} %slice.334, f32[96,128]{1,0:T(8,128)S(1)} %bitcast.116), dimensions={0} | concatenate | bytes 539648 | tf_op jit(solution)/shard_map/concatenate | solution.py:64
  26.5 1.8 %collective-permute-start.3 = (f32[527,128]{1,0:T(8,128)S(1)}, f32[527,128]{1,0:T(8,128)S(1)}, u32[]{:S(2)}, u32[]{:S(2)}) collective-permute-start(f32[527,128]{1,0:T(8,128)S(1)} %concatenate.52), channel_id=1, source_target_pairs={{0,16},{16,0},{1,17},{17,1},{2,18},{18,2},{3,19},{19,3},{4,20},{20... | collective-permute-start | bytes 809480 | tf_op jit(solution)/shard_map/ppermute | solution.py:59
  28.4 0.8 %fusion.7 = (f32[3,7,32,128]{3,2,1,0:T(8,128)S(1)}, f32[3,7,32,128]{3,2,1,0:T(8,128)S(1)}) fusion(f32[3,7,36,132]{3,2,1,0:T(8,128)S(1)} %slice_multiply_fusion), kind=kLoop, calls=%fused_computation.22 | loop fusion | flops 946176 | bytes 3784704 | tf_op jit(solution)/shard_map/add | solution.py:161
  29.2 5.4 %collective-permute-done.3 = f32[527,128]{1,0:T(8,128)S(1)} collective-permute-done((f32[527,128]{1,0:T(8,128)S(1)}, f32[527,128]{1,0:T(8,128)S(1)}, u32[]{:S(2)}, u32[]{:S(2)}) %collective-permute-start.3) | collective-permute-done | bytes 269856 | tf_op jit(solution)/shard_map/ppermute | solution.py:59
  35.0 0.1 maximum_bitcast_fusion
  35.2 0.2 fusion.16
  35.6 0.9 %fusion.3 = f32[3,8,32,128]{3,2,1,0:T(8,128)} fusion(f32[3,1,32,128]{3,2,1,0:T(8,128)S(1)} %bitcast.120, f32[3,1,32,128]{3,2,1,0:T(8,128)S(1)} %multiply_bitcast_fusion, f32[3,7,32,128]{3,2,1,0:T(8,128)S(1)} %get-tuple-element.11, f32[3,10,32,128]{3,2,1,0:T(8,128)S(1)} %pad_maximum_fusion.1, f32[3,7,32,128]{3,2,1,0:T(8,128)S(1)} %get-tuple-element.10, ...), kind=kLoop, calls=%fused_computation.14 | loop fusion | flops 1081344 | bytes 2015232 | tf_op jit(solution)/shard_map/mul | solution.py:152
  (90 shorter events, 3.3 us)
Async XLA Ops:
  2.8 1.4 %copy-start.4 = (f32[2,5,8,4,160]{4,3,2,1,0:T(4,128)S(1)}, f32[2,5,8,4,160]{4,3,2,1,0:T(4,128)}, u32[]{:S(2)}) copy-start(f32[2,5,8,4,160]{4,3,2,1,0:T(4,128)} %param.16) | copy-start | bytes 614404
  3.2 1.2 %copy-start.5 = (f32[2,4,8,5,160]{4,2,3,1,0:T(8,128)S(1)}, f32[2,4,8,5,160]{4,2,3,1,0:T(8,128)}, u32[]{:S(2)}) copy-start(f32[2,4,8,5,160]{4,2,3,1,0:T(8,128)} %param.15) | copy-start | bytes 614404
  4.3 1.0 %copy-start.3 = (f32[324,320]{1,0:T(8,128)S(1)}, f32[324,320]{1,0:T(8,128)}, u32[]{:S(2)}) copy-start(f32[324,320]{1,0:T(8,128)} %constant.11.clone) | copy-start | bytes 1244164
  4.4 1.6 %copy-start.8 = (f32[5,160]{1,0:T(8,128)S(1)}, f32[5,160]{1,0:T(8,128)}, u32[]{:S(2)}) copy-start(f32[5,160]{1,0:T(8,128)} %constant.10.clone) | copy-start | bytes 9604
  4.5 1.8 %copy-start.2 = (f32[324,320]{1,0:T(8,128)S(1)}, f32[324,320]{1,0:T(8,128)}, u32[]{:S(2)}) copy-start(f32[324,320]{1,0:T(8,128)} %constant.9.clone) | copy-start | bytes 1244164
  5.3 1.9 %copy-start = (f32[324,400]{1,0:T(8,128)S(1)}, f32[324,400]{1,0:T(8,128)}, u32[]{:S(2)}) copy-start(f32[324,400]{1,0:T(8,128)} %constant.12.clone) | copy-start | bytes 1555204
  6.1 1.6 %copy-start.9 = (f32[5,128]{1,0:T(8,128)S(1)}, f32[5,128]{1,0:T(8,128)}, u32[]{:S(2)}) copy-start(f32[5,128]{1,0:T(8,128)} %constant.13.clone) | copy-start | bytes 7684
  6.3 7.8 %copy-start.7 = (f32[5,132]{1,0:T(8,128)S(1)}, f32[5,132]{1,0:T(8,128)}, u32[]{:S(2)}) copy-start(f32[5,132]{1,0:T(8,128)} %constant.14.clone) | copy-start | bytes 7924
  7.2 8.5 %copy-start.1 = (f32[160,132]{1,0:T(8,128)S(1)}, f32[160,132]{1,0:T(8,128)}, u32[]{:S(2)}) copy-start(f32[160,132]{1,0:T(8,128)} %constant.44.clone) | copy-start | bytes 253444
  7.9 6.1 %collective-permute-start = (f32[12,324]{1,0:T(8,128)S(1)}, f32[12,324]{1,0:T(8,128)S(1)}, u32[]{:S(2)}, u32[]{:S(2)}) collective-permute-start(f32[12,324]{1,0:T(8,128)S(1)} %reshape.99), channel_id=1, source_target_pairs={{0,1},{1,2},{2,3},{3,4},{4,5},{5,6},{6,7},{7,0},{8,9},{9,10},{10,1... | collective-permute-start | bytes 46664 | tf_op jit(solution)/shard_map/ppermute | solution.py:59
  8.5 5.5 %collective-permute-start.1 = (f32[8,324]{1,0:T(8,128)S(1)}, f32[8,324]{1,0:T(8,128)S(1)}, u32[]{:S(2)}, u32[]{:S(2)}) collective-permute-start(f32[8,324]{1,0:T(8,128)S(1)} %reshape.101), channel_id=1, source_target_pairs={{0,7},{1,0},{2,1},{3,2},{4,3},{5,4},{6,5},{7,6},{8,15},{9,8},{10,9... | collective-permute-start | bytes 31112 | tf_op jit(solution)/shard_map/ppermute | solution.py:59
  16.3 0.9 %copy-start.6 = (f32[128,132]{1,0:T(8,128)S(1)}, f32[128,132]{1,0:T(8,128)}, u32[]{:S(2)}) copy-start(f32[128,132]{1,0:T(8,128)} %constant.45.clone) | copy-start | bytes 202756
  18.4 5.7 %collective-permute-start.2 = (f32[20,1188]{1,0:T(8,128)S(1)}, f32[20,1188]{1,0:T(8,128)S(1)}, u32[]{:S(2)}, u32[]{:S(2)}) collective-permute-start(f32[20,1188]{1,0:T(8,128)S(1)} %pad_maximum_fusion.4), channel_id=1, source_target_pairs={{0,8},{8,0},{1,9},{9,1},{2,10},{10,2},{3,11},{11,3},{4,12},{12,4},... | collective-permute-start | bytes 285128 | tf_op jit(solution)/shard_map/ppermute | solution.py:59
  26.5 8.1 %collective-permute-start.3 = (f32[527,128]{1,0:T(8,128)S(1)}, f32[527,128]{1,0:T(8,128)S(1)}, u32[]{:S(2)}, u32[]{:S(2)}) collective-permute-start(f32[527,128]{1,0:T(8,128)S(1)} %concatenate.52), channel_id=1, source_target_pairs={{0,16},{16,0},{1,17},{17,1},{2,18},{18,2},{3,19},{19,3},{4,20},{20... | collective-permute-start | bytes 809480 | tf_op jit(solution)/shard_map/ppermute | solution.py:59

commit v11 on v10

--- a/solution.py
+++ b/solution.py
@@ -198,6 +198,12 @@
     up = slabs[:, :3].reshape(-1, slabs.shape[2])
     down = slabs[:, 3:].reshape(-1, slabs.shape[2])
     from_prev, from_next = both_ways(up, down, "gz")
+    own_parts = lax.optimization_barrier(
+        [
+            jnp.dot(planar, jnp.asarray(depth.T, jnp.float32), precision=lax.Precision.HIGH)
+            for planar, depth in zip(planars, depths)
+        ]
+    )
     arrived = jnp.concatenate(
         [from_prev.reshape(4, 3, -1), from_next.reshape(4, 2, -1)], axis=1
     )
@@ -207,11 +213,8 @@
     place = jnp.asarray(place, jnp.float32)
     nodal = []
     for comp in range(3):
-        own_part = jnp.dot(
-            planars[comp], jnp.asarray(depths[comp].T, jnp.float32), precision=lax.Precision.HIGH
-        )
         folded = lax.dot_general(arrived[comp], place, (((0,), (0,)), ((), ())), precision=precise)
-        nodal.append((own_part + folded).reshape(nx + 1, ny + 4, length))
+        nodal.append((own_parts[comp] + folded).reshape(nx + 1, ny + 4, length))
     keep_in = jnp.moveaxis(arrived[3].reshape(5, nx + 1, ny + 4), 0, 2)
     keep = keep + jnp.pad(keep_in[..., :3], ((0, 0), (0, 0), (0, length - 3))) + jnp.pad(
         keep_in[..., 3:], ((0, 0), (0, 0), (nz + 2, 0))

time: 36.7 us -> 36.7 us (level)
  waiting for transfers between devices: 10.5 us -> 11.4 us
  starting transfers between devices: 8.47 us -> 7.73 us
    ppermute x4, waiting for transfers between devices: 10.5 us -> 11.4 us  [shifted(): lax.ppermute(block, axis, [(i, (i + step) % count) for i in range(count)])]
    ppermute x4, starting transfers between devices: 8.47 us -> 7.73 us  [shifted(): lax.ppermute(block, axis, [(i, (i + step) % count) for i in range(count)])]
  transfers between devices with their start and end apart: 4 -> 4, of which waited for: 3 -> 4; matrix products, arithmetic and copies ran while one was open for 2% -> 5% of each run, Pallas kernels for 0% -> 0%
where the time goes in v11:
time: 36.7 us; the launch traced here: 36.4 us
  waiting for transfers between devices  11.4 us (31%)
  starting transfers between devices  7.73 us (21%)
  local copies, waits for them, and re-layouts  5.93 us (16%)
  other arithmetic  5.89 us (16%)
  matrix products  4.88 us (13%)
  between operations  0.63 us (2%)
    ppermute x4, waiting for transfers between devices, shifted(): lax.ppermute(block, axis, [(i, (i + step) % count) for i in range(count)])  11.4 us
    ppermute x4, starting transfers between devices, shifted(): lax.ppermute(block, axis, [(i, (i + step) % count) for i in range(count)])  7.73 us
    dot_general x3, matrix products, planar_part(): jnp.dot(jnp.asarray(plane_map, jnp.float32), signed, precision=lax.Precis...  1.98 us
    dot_general x3, matrix products, body(): lax.dot_general(arrived[comp], place, (((0,), (0,)), ((), ())), precision...  1.29 us
    dot_general x3, matrix products, body(): jnp.dot(planar, jnp.asarray(depth.T, jnp.float32), precision=lax.Precisio...  1.09 us
    mul x3, other arithmetic, planar_part(): coef * orient[:, None, :, None, :]  1.04 us
    add x2, other arithmetic, yz_terms(): return 8.0 * part(0, 0) - 4.0 / 3.0 * near + 1.0 / 12.0 * far  0.95 us
    convert_element_type x1, other arithmetic, body(): keep_own = (1 - flags).astype(jnp.float32)  0.93 us
  transfers between devices with their start and end apart: 4, of which 4 were waited for; matrix products, arithmetic and copies ran while one was open for 5% of the time, Pallas kernels for 0%

profile of v11, /device:TPU:0, one launch (start us, length us, event | category | flops | bytes accessed | tf_op | source)
XLA Modules:
  0.0 36.4 jit_solution(253938899644030048)
XLA Ops:
  0.0 0.7 %convert_bitcast_fusion.2 = (f32[2,8,32]{2,1,0:T(8,128)S(1)}, f32[2,8,32]{2,1,0:T(8,128)S(1)}, f32[2,8,32]{2,1,0:T(8,128)S(1)}) fusion(s32[3,2,8,32]{3,2,1,0:T(8,128)} %param.18), kind=kLoop, calls=%fused_computation.89 | loop fusion | flops 4608 | bytes 12288 | tf_op jit(solution)/shard_map/convert_element_type | solution.py:44
  0.9 0.9 %subtract_convert_fusion = f32[8,32,128]{2,1,0:T(8,128)S(1)} fusion(s32[8,32,128]{2,1,0:T(8,128)} %param.19), kind=kLoop, calls=%fused_computation.35 | loop fusion | flops 65536 | bytes 262144 | tf_op jit(solution)/shard_map/convert_element_type | solution.py:188
  1.8 0.9 %broadcast_multiply_fusion.2 = f32[2,5,8,5,128]{4,2,3,1,0:T(8,128)S(1)} fusion(f32[2,5,8,5,128]{4,2,3,1,0:T(8,128)} %param.17, f32[2,8,128]{2,1,0:T(8,128)S(1)} %copy.46), kind=kLoop, calls=%fused_computation.42 | loop fusion | flops 51200 | bytes 417792 | tf_op jit(solution)/shard_map/mul | solution.py:45
  2.9 0.1 broadcast_in_dim.22
  3.0 0.2 mul.148
  3.2 0.1 broadcast_in_dim.23
  3.4 0.2 mul.152
  3.6 0.1 copy.48
  3.7 0.1 copy.49
  4.3 0.1 reshape.97
  4.5 0.1 copy.44
  4.7 0.6 %copy-done.3 = f32[324,320]{1,0:T(8,128)S(1)} copy-done((f32[324,320]{1,0:T(8,128)S(1)}, f32[324,320]{1,0:T(8,128)}, u32[]{:S(2)}) %copy-start.3) | copy-done | bytes 414744
  5.3 0.8 %fusion.39 = f32[160,324]{1,0:T(8,128)S(1)} fusion(f32[320,160]{1,0:T(8,128)S(1)} %reshape.97, f32[324,320]{1,0:T(8,128)S(1)} %copy-done.3), kind=kOutput, calls=%fused_computation.105 | convolution fusion | flops 99532800 | bytes 826880 | tf_op jit(solution)/shard_map/dot_general | solution.py:48
  6.1 0.2 convolution_bitcast_fusion.1
  6.3 0.8 %fusion.37 = f32[160,324]{1,0:T(8,128)S(1)} fusion(f32[320,160]{1,0:T(8,128)S(1)} %reshape.96, f32[324,320]{1,0:T(8,128)S(1)} %copy-done.2), kind=kOutput, calls=%fused_computation.103 | convolution fusion | flops 99532800 | bytes 826880 | tf_op jit(solution)/shard_map/dot_general | solution.py:48
  7.0 0.2 convolution_bitcast_fusion.2
  7.2 0.4 %fusion.41 = f32[128,324]{0,1:T(8,128)S(1)} fusion(f32[400,128]{1,0:T(8,128)S(1)} %reshape.98, f32[324,400]{1,0:T(8,128)S(1)} %copy-done), kind=kOutput, calls=%fused_computation.107 | convolution fusion | flops 99532800 | bytes 889088 | tf_op jit(solution)/shard_map/dot_general | solution.py:48
  7.7 0.2 convolution_bitcast_fusion
  7.9 4.5 %collective-permute-start.1 = (f32[8,324]{1,0:T(8,128)S(1)}, f32[8,324]{1,0:T(8,128)S(1)}, u32[]{:S(2)}, u32[]{:S(2)}) collective-permute-start(f32[8,324]{1,0:T(8,128)S(1)} %reshape.101), channel_id=1, source_target_pairs={{0,7},{1,0},{2,1},{3,2},{4,3},{5,4},{6,5},{7,6},{8,15},{9,8},{10,9... | collective-permute-start | bytes 31112 | tf_op jit(solution)/shard_map/ppermute | solution.py:59
  12.6 0.4 %fusion.40 = f32[324,132]{0,1:T(8,128)S(1)} fusion(f32[160,324]{1,0:T(8,128)S(1)} %fusion.39, f32[160,132]{1,0:T(8,128)S(1)} %copy-done.1), kind=kOutput, calls=%fused_computation.106 | convolution fusion | flops 41057280 | bytes 462912 | tf_op jit(solution)/shard_map/dot_general | solution.py:203
  13.0 0.4 %fusion.38 = f32[324,132]{0,1:T(8,128)S(1)} fusion(f32[160,324]{1,0:T(8,128)S(1)} %fusion.37, f32[160,132]{1,0:T(8,128)S(1)} %copy-done.1), kind=kOutput, calls=%fused_computation.104 | convolution fusion | flops 41057280 | bytes 462912 | tf_op jit(solution)/shard_map/dot_general | solution.py:203
  13.4 0.3 fusion.42
  13.7 0.2 collective-permute-done.1
  13.9 3.7 %collective-permute-done = f32[12,324]{1,0:T(8,128)S(1)} collective-permute-done((f32[12,324]{1,0:T(8,128)S(1)}, f32[12,324]{1,0:T(8,128)S(1)}, u32[]{:S(2)}, u32[]{:S(2)}) %collective-permute-start) | collective-permute-done | bytes 15584 | tf_op jit(solution)/shard_map/ppermute | solution.py:59
  17.6 0.4 %convolution_add_fusion.2 = f32[324,132]{0,1:T(8,128)S(1)} fusion(f32[324,132]{0,1:T(8,128)S(1)} %fusion.38, f32[5,132]{1,0:T(8,128)S(1)} %copy-done.7, f32[4,3,324]{2,1,0:T(4,128)S(1)} %reshape.100, f32[4,2,324]{2,1,0:T(2,128)S(1)} %reshape.102), kind=kOutput, calls=%fused_computation.4 | convolution fusion | flops 2610468 | bytes 370704 | tf_op jit(solution)/shard_map/dot_general | solution.py:216
  18.1 0.4 %convolution_add_fusion.1 = f32[324,132]{0,1:T(8,128)S(1)} fusion(f32[324,132]{0,1:T(8,128)S(1)} %fusion.40, f32[5,132]{1,0:T(8,128)S(1)} %copy-done.7, f32[4,3,324]{2,1,0:T(4,128)S(1)} %reshape.100, f32[4,2,324]{2,1,0:T(2,128)S(1)} %reshape.102), kind=kOutput, calls=%fused_computation.3 | convolution fusion | flops 2610468 | bytes 370704 | tf_op jit(solution)/shard_map/dot_general | solution.py:216
  18.5 0.4 %convolution_add_fusion = f32[324,132]{0,1:T(8,128)S(1)} fusion(f32[324,132]{0,1:T(8,128)S(1)} %fusion.42, f32[5,132]{1,0:T(8,128)S(1)} %copy-done.7, f32[4,3,324]{2,1,0:T(4,128)S(1)} %reshape.100, f32[4,2,324]{2,1,0:T(2,128)S(1)} %reshape.102), kind=kOutput, calls=%fused_computation.2 | convolution fusion | flops 2610468 | bytes 370704 | tf_op jit(solution)/shard_map/dot_general | solution.py:216
  19.0 0.1 copy.52
  19.2 0.1 copy.51
  19.4 0.1 copy.50
  19.6 0.2 copy.53
  19.8 0.1 slice.316
  19.9 0.2 add_bitcast_fusion
  20.1 0.2 pad_maximum_fusion
  20.4 0.1 reshape.103
  20.6 1.6 %collective-permute-start.2 = (f32[20,1188]{1,0:T(8,128)S(1)}, f32[20,1188]{1,0:T(8,128)S(1)}, u32[]{:S(2)}, u32[]{:S(2)}) collective-permute-start(f32[20,1188]{1,0:T(8,128)S(1)} %pad_maximum_fusion.4), channel_id=1, source_target_pairs={{0,8},{8,0},{1,9},{9,1},{2,10},{10,2},{3,11},{11,3},{4,12},{12,4},... | collective-permute-start | bytes 285128 | tf_op jit(solution)/shard_map/ppermute | solution.py:59
  22.2 3.4 %collective-permute-done.2 = f32[20,1188]{1,0:T(8,128)S(1)} collective-permute-done((f32[20,1188]{1,0:T(8,128)S(1)}, f32[20,1188]{1,0:T(8,128)S(1)}, u32[]{:S(2)}, u32[]{:S(2)}) %collective-permute-start.2) | collective-permute-done | bytes 95072 | tf_op jit(solution)/shard_map/ppermute | solution.py:59
  25.6 0.1 reshape.106
  25.8 0.2 reshape.105
  26.1 0.2 pad_add_fusion
  27.3 0.1 slice_multiply_fusion.1
  27.5 0.6 %concatenate.52 = f32[527,128]{1,0:T(8,128)S(1)} concatenate(f32[192,128]{1,0:T(8,128)S(1)} %bitcast.113, f32[96,128]{1,0:T(8,128)S(1)} %bitcast.117, f32[12,128]{1,0:T(8,128)S(1)} %reshape.109, f32[3,128]{1,0:T(4,128)S(1)} %reshape.110, f32[96,128]{1,0:T(8,128)S(1)} %bitcast.118, f32[32,128]{1,0:T(8,128)S(1)} %slice.334, f32[96,128]{1,0:T(8,128)S(1)} %bitcast.116), dimensions={0} | concatenate | bytes 539648 | tf_op jit(solution)/shard_map/concatenate | solution.py:64
  28.0 1.6 %collective-permute-start.3 = (f32[527,128]{1,0:T(8,128)S(1)}, f32[527,128]{1,0:T(8,128)S(1)}, u32[]{:S(2)}, u32[]{:S(2)}) collective-permute-start(f32[527,128]{1,0:T(8,128)S(1)} %concatenate.52), channel_id=1, source_target_pairs={{0,16},{16,0},{1,17},{17,1},{2,18},{18,2},{3,19},{19,3},{4,20},{20... | collective-permute-start | bytes 809480 | tf_op jit(solution)/shard_map/ppermute | solution.py:59
  29.7 0.8 %fusion.7 = (f32[3,7,32,128]{3,2,1,0:T(8,128)S(1)}, f32[3,7,32,128]{3,2,1,0:T(8,128)S(1)}) fusion(f32[3,7,36,132]{3,2,1,0:T(8,128)S(1)} %slice_multiply_fusion), kind=kLoop, calls=%fused_computation.22 | loop fusion | flops 946176 | bytes 3784704 | tf_op jit(solution)/shard_map/add | solution.py:161
  30.4 4.1 %collective-permute-done.3 = f32[527,128]{1,0:T(8,128)S(1)} collective-permute-done((f32[527,128]{1,0:T(8,128)S(1)}, f32[527,128]{1,0:T(8,128)S(1)}, u32[]{:S(2)}, u32[]{:S(2)}) %collective-permute-start.3) | collective-permute-done | bytes 269856 | tf_op jit(solution)/shard_map/ppermute | solution.py:59
  34.9 0.1 maximum_bitcast_fusion
  35.1 0.2 fusion.16
  35.5 0.9 %fusion.3 = f32[3,8,32,128]{3,2,1,0:T(8,128)} fusion(f32[3,1,32,128]{3,2,1,0:T(8,128)S(1)} %bitcast.120, f32[3,1,32,128]{3,2,1,0:T(8,128)S(1)} %multiply_bitcast_fusion, f32[3,7,32,128]{3,2,1,0:T(8,128)S(1)} %get-tuple-element.17, f32[3,10,32,128]{3,2,1,0:T(8,128)S(1)} %pad_maximum_fusion.1, f32[3,7,32,128]{3,2,1,0:T(8,128)S(1)} %get-tuple-element.16, ...), kind=kLoop, calls=%fused_computation.14 | loop fusion | flops 1081344 | bytes 2015232 | tf_op jit(solution)/shard_map/mul | solution.py:152
  (90 shorter events, 3.3 us)
Async XLA Ops:
  2.8 1.4 %copy-start.4 = (f32[2,5,8,4,160]{4,3,2,1,0:T(4,128)S(1)}, f32[2,5,8,4,160]{4,3,2,1,0:T(4,128)}, u32[]{:S(2)}) copy-start(f32[2,5,8,4,160]{4,3,2,1,0:T(4,128)} %param.16) | copy-start | bytes 614404
  3.2 1.2 %copy-start.5 = (f32[2,4,8,5,160]{4,2,3,1,0:T(8,128)S(1)}, f32[2,4,8,5,160]{4,2,3,1,0:T(8,128)}, u32[]{:S(2)}) copy-start(f32[2,4,8,5,160]{4,2,3,1,0:T(8,128)} %param.15) | copy-start | bytes 614404
  4.3 1.0 %copy-start.3 = (f32[324,320]{1,0:T(8,128)S(1)}, f32[324,320]{1,0:T(8,128)}, u32[]{:S(2)}) copy-start(f32[324,320]{1,0:T(8,128)} %constant.11.clone) | copy-start | bytes 1244164
  4.4 1.6 %copy-start.8 = (f32[5,160]{1,0:T(8,128)S(1)}, f32[5,160]{1,0:T(8,128)}, u32[]{:S(2)}) copy-start(f32[5,160]{1,0:T(8,128)} %constant.10.clone) | copy-start | bytes 9604
  4.5 1.8 %copy-start.2 = (f32[324,320]{1,0:T(8,128)S(1)}, f32[324,320]{1,0:T(8,128)}, u32[]{:S(2)}) copy-start(f32[324,320]{1,0:T(8,128)} %constant.9.clone) | copy-start | bytes 1244164
  5.3 1.9 %copy-start = (f32[324,400]{1,0:T(8,128)S(1)}, f32[324,400]{1,0:T(8,128)}, u32[]{:S(2)}) copy-start(f32[324,400]{1,0:T(8,128)} %constant.12.clone) | copy-start | bytes 1555204
  6.1 1.6 %copy-start.9 = (f32[5,128]{1,0:T(8,128)S(1)}, f32[5,128]{1,0:T(8,128)}, u32[]{:S(2)}) copy-start(f32[5,128]{1,0:T(8,128)} %constant.13.clone) | copy-start | bytes 7684
  6.3 6.3 %copy-start.1 = (f32[160,132]{1,0:T(8,128)S(1)}, f32[160,132]{1,0:T(8,128)}, u32[]{:S(2)}) copy-start(f32[160,132]{1,0:T(8,128)} %constant.14.clone) | copy-start | bytes 253444
  7.0 6.3 %copy-start.6 = (f32[128,132]{1,0:T(8,128)S(1)}, f32[128,132]{1,0:T(8,128)}, u32[]{:S(2)}) copy-start(f32[128,132]{1,0:T(8,128)} %constant.44.clone) | copy-start | bytes 202756
  7.2 10.4 %copy-start.7 = (f32[5,132]{1,0:T(8,128)S(1)}, f32[5,132]{1,0:T(8,128)}, u32[]{:S(2)}) copy-start(f32[5,132]{1,0:T(8,128)} %constant.45.clone) | copy-start | bytes 7924
  7.9 5.9 %collective-permute-start.1 = (f32[8,324]{1,0:T(8,128)S(1)}, f32[8,324]{1,0:T(8,128)S(1)}, u32[]{:S(2)}, u32[]{:S(2)}) collective-permute-start(f32[8,324]{1,0:T(8,128)S(1)} %reshape.101), channel_id=1, source_target_pairs={{0,7},{1,0},{2,1},{3,2},{4,3},{5,4},{6,5},{7,6},{8,15},{9,8},{10,9... | collective-permute-start | bytes 31112 | tf_op jit(solution)/shard_map/ppermute | solution.py:59
  12.5 5.1 %collective-permute-start = (f32[12,324]{1,0:T(8,128)S(1)}, f32[12,324]{1,0:T(8,128)S(1)}, u32[]{:S(2)}, u32[]{:S(2)}) collective-permute-start(f32[12,324]{1,0:T(8,128)S(1)} %reshape.99), channel_id=1, source_target_pairs={{0,1},{1,2},{2,3},{3,4},{4,5},{5,6},{6,7},{7,0},{8,9},{9,10},{10,1... | collective-permute-start | bytes 46664 | tf_op jit(solution)/shard_map/ppermute | solution.py:59
  20.6 4.9 %collective-permute-start.2 = (f32[20,1188]{1,0:T(8,128)S(1)}, f32[20,1188]{1,0:T(8,128)S(1)}, u32[]{:S(2)}, u32[]{:S(2)}) collective-permute-start(f32[20,1188]{1,0:T(8,128)S(1)} %pad_maximum_fusion.4), channel_id=1, source_target_pairs={{0,8},{8,0},{1,9},{9,1},{2,10},{10,2},{3,11},{11,3},{4,12},{12,4},... | collective-permute-start | bytes 285128 | tf_op jit(solution)/shard_map/ppermute | solution.py:59
  28.0 6.5 %collective-permute-start.3 = (f32[527,128]{1,0:T(8,128)S(1)}, f32[527,128]{1,0:T(8,128)S(1)}, u32[]{:S(2)}, u32[]{:S(2)}) collective-permute-start(f32[527,128]{1,0:T(8,128)S(1)} %concatenate.52), channel_id=1, source_target_pairs={{0,16},{16,0},{1,17},{17,1},{2,18},{18,2},{3,19},{19,3},{4,20},{20... | collective-permute-start | bytes 809480 | tf_op jit(solution)/shard_map/ppermute | solution.py:59

commit v12 on v11

--- a/solution.py
+++ b/solution.py
@@ -159,6 +159,92 @@
     near = part(-1, 0) + part(1, 0) + part(0, -1) + part(0, 1)
     far = part(-2, 0) + part(2, 0) + part(0, -2) + part(0, 2)
     return 8.0 * part(0, 0) - 4.0 / 3.0 * near + 1.0 / 12.0 * far
+
+
+def window(padded_array, axis_pos, offset):
+    starts = [0, 2, 2, 2]
+    limits = [
+        padded_array.shape[0],
+        padded_array.shape[1] - 2,
+        padded_array.shape[2] - 2,
+        padded_array.shape[3] - 2,
+    ]
+    starts[axis_pos] = offset
+    limits[axis_pos] = offset + padded_array.shape[axis_pos] - 4
+    return lax.slice(padded_array, tuple(starts), tuple(limits))
+
+
+def stencil_apply(padded_array):
+    total = 8.0 * window(padded_array, 1, 2)
+    for axis_pos in (1, 2, 3):
+        near = window(padded_array, axis_pos, 1) + window(padded_array, axis_pos, 3)
+        far = window(padded_array, axis_pos, 0) + window(padded_array, axis_pos, 4)
+        total = total - 4.0 / 3.0 * near + 1.0 / 12.0 * far
+    return 0.25 * total
+
+
+def exchange(payloads, axes):
+    sizes = [lax.axis_size(axis) for axis in axes]
+    groups = {}
+    for offset in payloads:
+        key = tuple(o % s for o, s in zip(offset, sizes))
+        groups.setdefault(key, []).append(offset)
+    arrived = {}
+    for key, offsets in groups.items():
+        flat = jnp.concatenate([payloads[offset].reshape(-1) for offset in offsets])
+        length = flat.shape[0]
+        rows = jnp.pad(flat, (0, -length % 128)).reshape(-1, 128)
+        if any(key):
+            pairs = []
+            for source in np.ndindex(*sizes):
+                target = tuple((c + k) % s for c, k, s in zip(source, key, sizes))
+                pairs.append((int(np.ravel_multi_index(source, sizes)), int(np.ravel_multi_index(target, sizes))))
+            rows = lax.ppermute(rows, tuple(axes), pairs)
+        flat = rows.reshape(-1)
+        start = 0
+        for offset in offsets:
+            shape = payloads[offset].shape
+            size = int(np.prod(shape))
+            arrived[offset] = flat[start : start + size].reshape(shape)
+            start += size
+    return arrived
+
+
+def placed(block, starts, shape):
+    return jnp.pad(block, [(b, s - b - d) for b, d, s in zip(starts, block.shape, shape)])
+
+
+def plane_round_and_stencil(extended, nx, ny):
+    e = extended
+    payloads = {
+        (1, 0): e[:, nx - 2 : nx + 1, 2 : ny + 3],
+        (-1, 0): e[:, 0:2, 2 : ny + 2],
+        (0, 1): e[:, :, ny : ny + 3],
+        (0, -1): e[:, 0:nx, 2:4],
+        (1, 1): jnp.concatenate([e[:, nx - 2 : nx + 1, ny + 2], e[:, nx, ny : ny + 2]], axis=1),
+        (-1, 1): e[:, 0:2, ny + 2],
+        (1, -1): e[:, nx, 2:4],
+    }
+    got = exchange(payloads, ("gx", "gy"))
+    channels, _, _, depth = e.shape
+    shape = (channels, nx + 4, ny + 4, depth)
+
+    def at(block, layer, row):
+        return placed(block, (0, layer, row, 0), shape)
+
+    corner = got[(1, 1)]
+    total = (
+        at(e, 2, 0)
+        + at(got[(1, 0)], 0, 2)
+        + at(got[(-1, 0)], nx + 2, 2)
+        + at(got[(0, 1)], 2, 0)
+        + at(got[(0, -1)], 2, ny + 2)
+        + at(corner[:, 0:3, None], 0, 2)
+        + at(corner[:, 3:5, :][:, None], 2, 0)
+        + at(got[(-1, 1)][:, :, None], nx + 2, 2)
+        + at(got[(1, -1)][:, None], 2, ny + 2)
+    )
+    return stencil_apply(total[:-1] * total[-1])
 
 
 def body(edge_coeffs_x, edge_coeffs_y, edge_coeffs_z, flips, flags):
@@ -220,8 +306,7 @@
         keep_in[..., 3:], ((0, 0), (0, 0), (nz + 2, 0))
     )
     extended = jnp.stack(nodal + [keep])
-    extended = fold_and_halo(extended, "gy", 2)
-    return last_round_and_stencil(extended, "gx", ny, nz)
+    return plane_round_and_stencil(extended, nx, ny)
 
 
 def solution(mesh):

time: 36.7 us -> 36.2 us (0.986)
  waiting for transfers between devices: 11.4 us -> 9.78 us
  matrix products: 4.88 us -> 5.97 us
  starting transfers between devices: 7.73 us -> 8.23 us
  local copies, waits for them, and re-layouts: 5.93 us -> 5.54 us
    ppermute x4 -> x2, waiting for transfers between devices: 11.4 us -> 3.89 us  [shifted(): lax.ppermute(block, axis, [(i, (i + step) % count) for i in range(count)])]
    ppermute x0 -> x3, waiting for transfers between devices: none -> 5.89 us  [exchange(): rows = lax.ppermute(rows, tuple(axes), pairs)]
    ppermute x0 -> x3, starting transfers between devices: none -> 3.63 us  [exchange(): rows = lax.ppermute(rows, tuple(axes), pairs)]
    ppermute x4 -> x2, starting transfers between devices: 7.73 us -> 4.6 us  [shifted(): lax.ppermute(block, axis, [(i, (i + step) % count) for i in range(count)])]
    reshape x9 -> x11, local copies, waits for them, and re-layouts: 0.74 us -> 1.86 us  [the longest x5 1.09 us: exchange(): arrived[offset] = flat[start:start + size].reshape(shape)]
    dot_general x3, matrix products: 1.98 us -> 3.07 us  [planar_part(): jnp.dot(jnp.asarray(plane_map, jnp.float32), signed, precision=lax.Precis...]
    mul x5 -> x2, other arithmetic: 1.18 us -> 2.19 us  [the longest x1 2.03 us: stencil_apply(): return 0.25 * total]
    add x3 -> x1, other arithmetic: 1.16 us -> 0.27 us  [plane_round_and_stencil(): at(e, 2, 0) + at(got[1, 0], 0, 2) + at(got[-1, 0], nx + 2, 2)]
  transfers between devices with their start and end apart: 4 -> 5, of which waited for: 4 -> 5; matrix products, arithmetic and copies ran while one was open for 5% -> 8% of each run, Pallas kernels for 0% -> 0%
where the time goes in v12:
time: 36.2 us; the launch traced here: 36 us
  waiting for transfers between devices  9.78 us (27%)
  starting transfers between devices  8.23 us (23%)
  matrix products  5.97 us (16%)
  other arithmetic  5.86 us (16%)
  local copies, waits for them, and re-layouts  5.54 us (15%)
  between operations  0.63 us (2%)
    ppermute x3, waiting for transfers between devices, exchange(): rows = lax.ppermute(rows, tuple(axes), pairs)  5.89 us
    ppermute x2, starting transfers between devices, shifted(): lax.ppermute(block, axis, [(i, (i + step) % count) for i in range(count)])  4.6 us
    ppermute x2, waiting for transfers between devices, shifted(): lax.ppermute(block, axis, [(i, (i + step) % count) for i in range(count)])  3.89 us
    ppermute x3, starting transfers between devices, exchange(): rows = lax.ppermute(rows, tuple(axes), pairs)  3.63 us
    dot_general x3, matrix products, planar_part(): jnp.dot(jnp.asarray(plane_map, jnp.float32), signed, precision=lax.Precis...  3.07 us
    mul x1, other arithmetic, stencil_apply(): return 0.25 * total  2.03 us
    dot_general x3, matrix products, body(): lax.dot_general(arrived[comp], place, (((0,), (0,)), ((), ())), precision...  1.28 us
    dot_general x3, matrix products, body(): jnp.dot(planar, jnp.asarray(depth.T, jnp.float32), precision=lax.Precisio...  1.09 us
  transfers between devices with their start and end apart: 5, of which 5 were waited for; matrix products, arithmetic and copies ran while one was open for 8% of the time, Pallas kernels for 0%

profile of v12, /device:TPU:0, one launch (start us, length us, event | category | flops | bytes accessed | tf_op | source)
XLA Modules:
  0.0 36.0 jit_solution(4815075855542491929)
XLA Ops:
  0.0 0.7 %convert_bitcast_fusion.2 = (f32[2,8,32]{2,1,0:T(8,128)S(1)}, f32[2,8,32]{2,1,0:T(8,128)S(1)}, f32[2,8,32]{2,1,0:T(8,128)S(1)}) fusion(s32[3,2,8,32]{3,2,1,0:T(8,128)} %param.18), kind=kLoop, calls=%fused_computation.66 | loop fusion | flops 4608 | bytes 12288 | tf_op jit(solution)/shard_map/convert_element_type | solution.py:44
  0.9 1.0 %subtract_convert_fusion = f32[8,32,128]{2,1,0:T(8,128)S(1)} fusion(s32[8,32,128]{2,1,0:T(8,128)} %param.19), kind=kLoop, calls=%fused_computation.36 | loop fusion | flops 65536 | bytes 262144 | tf_op jit(solution)/shard_map/convert_element_type | solution.py:274
  1.9 0.9 %broadcast_multiply_fusion.2 = f32[2,5,8,5,128]{4,2,3,1,0:T(8,128)S(1)} fusion(f32[2,5,8,5,128]{4,2,3,1,0:T(8,128)} %param.17, f32[2,8,128]{2,1,0:T(8,128)S(1)} %copy.52), kind=kLoop, calls=%fused_computation.37 | loop fusion | flops 51200 | bytes 417792 | tf_op jit(solution)/shard_map/mul | solution.py:45
  3.0 0.1 broadcast_in_dim.18
  3.1 0.2 mul.83
  3.3 0.1 broadcast_in_dim.19
  3.4 0.2 mul.87
  3.8 0.1 copy.55
  4.3 0.1 reshape.88
  4.5 0.1 copy.50
  4.7 1.9 %fusion.32 = f32[160,324]{1,0:T(8,128)S(1)} fusion(f32[320,160]{1,0:T(8,128)S(1)} %reshape.88, f32[324,320]{1,0:T(8,128)} %constant.35.clone), kind=kOutput, calls=%fused_computation.75 | convolution fusion | flops 99532800 | bytes 826880 | tf_op jit(solution)/shard_map/dot_general | solution.py:48
  6.6 0.2 convolution_bitcast_fusion.1
  6.8 0.8 %fusion.30 = f32[160,324]{1,0:T(8,128)S(1)} fusion(f32[320,160]{1,0:T(8,128)S(1)} %reshape.87, f32[324,320]{1,0:T(8,128)S(1)} %copy-done.2), kind=kOutput, calls=%fused_computation.73 | convolution fusion | flops 99532800 | bytes 826880 | tf_op jit(solution)/shard_map/dot_general | solution.py:48
  7.6 0.2 convolution_bitcast_fusion.2
  7.7 0.4 %fusion.34 = f32[128,324]{0,1:T(8,128)S(1)} fusion(f32[400,128]{1,0:T(8,128)S(1)} %reshape.89, f32[324,400]{1,0:T(8,128)S(1)} %copy-done), kind=kOutput, calls=%fused_computation.77 | convolution fusion | flops 99532800 | bytes 889088 | tf_op jit(solution)/shard_map/dot_general | solution.py:48
  8.2 0.2 convolution_bitcast_fusion
  8.4 4.5 %collective-permute-start.1 = (f32[8,324]{1,0:T(8,128)S(1)}, f32[8,324]{1,0:T(8,128)S(1)}, u32[]{:S(2)}, u32[]{:S(2)}) collective-permute-start(f32[8,324]{1,0:T(8,128)S(1)} %reshape.92), channel_id=1, source_target_pairs={{0,7},{1,0},{2,1},{3,2},{4,3},{5,4},{6,5},{7,6},{8,15},{9,8},{10,9... | collective-permute-start | bytes 31112 | tf_op jit(solution)/shard_map/ppermute | solution.py:59
  13.1 0.4 %fusion.33 = f32[324,132]{0,1:T(8,128)S(1)} fusion(f32[160,324]{1,0:T(8,128)S(1)} %fusion.32, f32[160,132]{1,0:T(8,128)S(1)} %copy-done.1), kind=kOutput, calls=%fused_computation.76 | convolution fusion | flops 41057280 | bytes 462912 | tf_op jit(solution)/shard_map/dot_general | solution.py:289
  13.5 0.4 %fusion.31 = f32[324,132]{0,1:T(8,128)S(1)} fusion(f32[160,324]{1,0:T(8,128)S(1)} %fusion.30, f32[160,132]{1,0:T(8,128)S(1)} %copy-done.1), kind=kOutput, calls=%fused_computation.74 | convolution fusion | flops 41057280 | bytes 462912 | tf_op jit(solution)/shard_map/dot_general | solution.py:289
  13.9 0.3 fusion.35
  14.2 0.2 collective-permute-done.1
  14.4 3.7 %collective-permute-done = f32[12,324]{1,0:T(8,128)S(1)} collective-permute-done((f32[12,324]{1,0:T(8,128)S(1)}, f32[12,324]{1,0:T(8,128)S(1)}, u32[]{:S(2)}, u32[]{:S(2)}) %collective-permute-start) | collective-permute-done | bytes 15584 | tf_op jit(solution)/shard_map/ppermute | solution.py:59
  18.2 0.4 %convolution_add_fusion.2 = f32[324,132]{0,1:T(8,128)S(1)} fusion(f32[324,132]{0,1:T(8,128)S(1)} %fusion.31, f32[5,132]{1,0:T(8,128)S(1)} %copy-done.6, f32[4,3,324]{2,1,0:T(4,128)S(1)} %reshape.91, f32[4,2,324]{2,1,0:T(2,128)S(1)} %reshape.93), kind=kOutput, calls=%fused_computation.5 | convolution fusion | flops 2610468 | bytes 370704 | tf_op jit(solution)/shard_map/dot_general | solution.py:302
  18.6 0.4 %convolution_add_fusion.1 = f32[324,132]{0,1:T(8,128)S(1)} fusion(f32[324,132]{0,1:T(8,128)S(1)} %fusion.33, f32[5,132]{1,0:T(8,128)S(1)} %copy-done.6, f32[4,3,324]{2,1,0:T(4,128)S(1)} %reshape.91, f32[4,2,324]{2,1,0:T(2,128)S(1)} %reshape.93), kind=kOutput, calls=%fused_computation.4 | convolution fusion | flops 2610468 | bytes 370704 | tf_op jit(solution)/shard_map/dot_general | solution.py:302
  19.0 0.4 %convolution_add_fusion = f32[324,132]{0,1:T(8,128)S(1)} fusion(f32[324,132]{0,1:T(8,128)S(1)} %fusion.35, f32[5,132]{1,0:T(8,128)S(1)} %copy-done.6, f32[4,3,324]{2,1,0:T(4,128)S(1)} %reshape.91, f32[4,2,324]{2,1,0:T(2,128)S(1)} %reshape.93), kind=kOutput, calls=%fused_computation.3 | convolution fusion | flops 2610468 | bytes 370704 | tf_op jit(solution)/shard_map/dot_general | solution.py:302
  19.5 0.1 copy.58
  19.7 0.1 copy.57
  19.9 0.1 copy.56
  20.1 0.2 copy.59
  20.4 0.2 add_bitcast_fusion
  20.6 0.1 pad_maximum_fusion
  21.4 2.5 %collective-permute-start.4 = (f32[38,128]{1,0:T(8,128)S(1)}, f32[38,128]{1,0:T(8,128)S(1)}, u32[]{:S(2)}, u32[]{:S(2)}) collective-permute-start(f32[38,128]{1,0:T(8,128)S(1)} %pad_bitcast_fusion), channel_id=1, source_target_pairs={{0,24},{8,16},{16,8},{24,0},{1,25},{9,17},{17,9},{25,1},{2,26},{10... | collective-permute-start | bytes 58376 | tf_op jit(solution)/shard_map/ppermute | solution.py:202
  24.0 0.1 reshape.101
  24.1 0.1 reshape.100
  24.3 0.5 %collective-permute-start.3 = (f32[178,128]{1,0:T(8,128)S(1)}, f32[178,128]{1,0:T(8,128)S(1)}, u32[]{:S(2)}, u32[]{:S(2)}) collective-permute-start(f32[178,128]{1,0:T(8,128)S(1)} %fusion.14), channel_id=1, source_target_pairs={{0,8},{8,0},{16,24},{24,16},{1,9},{9,1},{17,25},{25,17},{2,10},{10... | collective-permute-start | bytes 273416 | tf_op jit(solution)/shard_map/ppermute | solution.py:202
  24.8 0.2 reshape.95
  25.0 0.2 reshape.94
  25.3 0.6 %collective-permute-start.2 = (f32[673,128]{1,0:T(8,128)S(1)}, f32[673,128]{1,0:T(8,128)S(1)}, u32[]{:S(2)}, u32[]{:S(2)}) collective-permute-start(f32[673,128]{1,0:T(8,128)S(1)} %fusion.13), channel_id=1, source_target_pairs={{0,16},{8,24},{16,0},{24,8},{1,17},{9,25},{17,1},{25,9},{2,18},{10... | collective-permute-start | bytes 1033736 | tf_op jit(solution)/shard_map/ppermute | solution.py:202
  26.0 0.5 %collective-permute-done.4 = f32[38,128]{1,0:T(8,128)S(1)} collective-permute-done((f32[38,128]{1,0:T(8,128)S(1)}, f32[38,128]{1,0:T(8,128)S(1)}, u32[]{:S(2)}, u32[]{:S(2)}) %collective-permute-start.4) | collective-permute-done | bytes 19488 | tf_op jit(solution)/shard_map/ppermute | solution.py:202
  26.9 2.0 %collective-permute-done.3 = f32[178,128]{1,0:T(8,128)S(1)} collective-permute-done((f32[178,128]{1,0:T(8,128)S(1)}, f32[178,128]{1,0:T(8,128)S(1)}, u32[]{:S(2)}, u32[]{:S(2)}) %collective-permute-start.3) | collective-permute-done | bytes 91168 | tf_op jit(solution)/shard_map/ppermute | solution.py:202
  29.0 0.2 reshape.105
  29.2 0.2 reshape.104
  29.4 3.4 %collective-permute-done.2 = f32[673,128]{1,0:T(8,128)S(1)} collective-permute-done((f32[673,128]{1,0:T(8,128)S(1)}, f32[673,128]{1,0:T(8,128)S(1)}, u32[]{:S(2)}, u32[]{:S(2)}) %collective-permute-start.2) | collective-permute-done | bytes 344608 | tf_op jit(solution)/shard_map/ppermute | solution.py:202
  32.8 0.3 reshape.99
  33.2 0.3 reshape.98
  33.5 0.3 pad_add_fusion
  33.8 0.2 slice_multiply_fusion
  34.0 2.0 %fusion.2 = f32[3,8,32,128]{3,2,1,0:T(8,128)} fusion(f32[3,12,36,132]{3,2,1,0:T(8,128)S(1)} %slice_multiply_fusion), kind=kLoop, calls=%fused_computation.13 | loop fusion | flops 1966080 | bytes 5505024 | tf_op jit(solution)/shard_map/mul | solution.py:183
  (77 shorter events, 2.8 us)
Async XLA Ops:
  0.8 3.4 %copy-start.3 = (f32[2,5,8,4,160]{4,3,2,1,0:T(4,128)S(1)}, f32[2,5,8,4,160]{4,3,2,1,0:T(4,128)}, u32[]{:S(2)}) copy-start(f32[2,5,8,4,160]{4,3,2,1,0:T(4,128)} %param.16) | copy-start | bytes 614404
  2.9 1.5 %copy-start.4 = (f32[2,4,8,5,160]{4,2,3,1,0:T(8,128)S(1)}, f32[2,4,8,5,160]{4,2,3,1,0:T(8,128)}, u32[]{:S(2)}) copy-start(f32[2,4,8,5,160]{4,2,3,1,0:T(8,128)} %param.15) | copy-start | bytes 614404
  4.3 2.3 %copy-start.7 = (f32[5,160]{1,0:T(8,128)S(1)}, f32[5,160]{1,0:T(8,128)}, u32[]{:S(2)}) copy-start(f32[5,160]{1,0:T(8,128)} %constant.34.clone) | copy-start | bytes 9604
  4.4 2.3 %copy-start.2 = (f32[324,320]{1,0:T(8,128)S(1)}, f32[324,320]{1,0:T(8,128)}, u32[]{:S(2)}) copy-start(f32[324,320]{1,0:T(8,128)} %constant.14.clone) | copy-start | bytes 1244164
  4.6 3.1 %copy-start = (f32[324,400]{1,0:T(8,128)S(1)}, f32[324,400]{1,0:T(8,128)}, u32[]{:S(2)}) copy-start(f32[324,400]{1,0:T(8,128)} %constant.36.clone) | copy-start | bytes 1555204
  4.7 3.5 %copy-start.8 = (f32[5,128]{1,0:T(8,128)S(1)}, f32[5,128]{1,0:T(8,128)}, u32[]{:S(2)}) copy-start(f32[5,128]{1,0:T(8,128)} %constant.37.clone) | copy-start | bytes 7684
  4.7 8.4 %copy-start.1 = (f32[160,132]{1,0:T(8,128)S(1)}, f32[160,132]{1,0:T(8,128)}, u32[]{:S(2)}) copy-start(f32[160,132]{1,0:T(8,128)} %constant.38.clone) | copy-start | bytes 253444
  6.8 7.1 %copy-start.5 = (f32[128,132]{1,0:T(8,128)S(1)}, f32[128,132]{1,0:T(8,128)}, u32[]{:S(2)}) copy-start(f32[128,132]{1,0:T(8,128)} %constant.39.clone) | copy-start | bytes 202756
  7.6 10.6 %copy-start.6 = (f32[5,132]{1,0:T(8,128)S(1)}, f32[5,132]{1,0:T(8,128)}, u32[]{:S(2)}) copy-start(f32[5,132]{1,0:T(8,128)} %constant.40.clone) | copy-start | bytes 7924
  8.4 6.0 %collective-permute-start.1 = (f32[8,324]{1,0:T(8,128)S(1)}, f32[8,324]{1,0:T(8,128)S(1)}, u32[]{:S(2)}, u32[]{:S(2)}) collective-permute-start(f32[8,324]{1,0:T(8,128)S(1)} %reshape.92), channel_id=1, source_target_pairs={{0,7},{1,0},{2,1},{3,2},{4,3},{5,4},{6,5},{7,6},{8,15},{9,8},{10,9... | collective-permute-start | bytes 31112 | tf_op jit(solution)/shard_map/ppermute | solution.py:59
  13.0 5.1 %collective-permute-start = (f32[12,324]{1,0:T(8,128)S(1)}, f32[12,324]{1,0:T(8,128)S(1)}, u32[]{:S(2)}, u32[]{:S(2)}) collective-permute-start(f32[12,324]{1,0:T(8,128)S(1)} %reshape.90), channel_id=1, source_target_pairs={{0,1},{1,2},{2,3},{3,4},{4,5},{5,6},{6,7},{7,0},{8,9},{9,10},{10,1... | collective-permute-start | bytes 46664 | tf_op jit(solution)/shard_map/ppermute | solution.py:59
  21.4 5.0 %collective-permute-start.4 = (f32[38,128]{1,0:T(8,128)S(1)}, f32[38,128]{1,0:T(8,128)S(1)}, u32[]{:S(2)}, u32[]{:S(2)}) collective-permute-start(f32[38,128]{1,0:T(8,128)S(1)} %pad_bitcast_fusion), channel_id=1, source_target_pairs={{0,24},{8,16},{16,8},{24,0},{1,25},{9,17},{17,9},{25,1},{2,26},{10... | collective-permute-start | bytes 58376 | tf_op jit(solution)/shard_map/ppermute | solution.py:202
  24.3 4.6 %collective-permute-start.3 = (f32[178,128]{1,0:T(8,128)S(1)}, f32[178,128]{1,0:T(8,128)S(1)}, u32[]{:S(2)}, u32[]{:S(2)}) collective-permute-start(f32[178,128]{1,0:T(8,128)S(1)} %fusion.14), channel_id=1, source_target_pairs={{0,8},{8,0},{16,24},{24,16},{1,9},{9,1},{17,25},{25,17},{2,10},{10... | collective-permute-start | bytes 273416 | tf_op jit(solution)/shard_map/ppermute | solution.py:202
  25.3 7.4 %collective-permute-start.2 = (f32[673,128]{1,0:T(8,128)S(1)}, f32[673,128]{1,0:T(8,128)S(1)}, u32[]{:S(2)}, u32[]{:S(2)}) collective-permute-start(f32[673,128]{1,0:T(8,128)S(1)} %fusion.13), channel_id=1, source_target_pairs={{0,16},{8,24},{16,0},{24,8},{1,17},{9,25},{17,1},{25,9},{2,18},{10... | collective-permute-start | bytes 1033736 | tf_op jit(solution)/shard_map/ppermute | solution.py:202

commit v13 on v12

--- a/solution.py
+++ b/solution.py
@@ -191,7 +191,7 @@
         groups.setdefault(key, []).append(offset)
     arrived = {}
     for key, offsets in groups.items():
-        flat = jnp.concatenate([payloads[offset].reshape(-1) for offset in offsets])
+        flat = jnp.concatenate([part.reshape(-1) for offset in offsets for part in payloads[offset]])
         length = flat.shape[0]
         rows = jnp.pad(flat, (0, -length % 128)).reshape(-1, 128)
         if any(key):
@@ -203,10 +203,12 @@
         flat = rows.reshape(-1)
         start = 0
         for offset in offsets:
-            shape = payloads[offset].shape
-            size = int(np.prod(shape))
-            arrived[offset] = flat[start : start + size].reshape(shape)
-            start += size
+            parts = []
+            for part in payloads[offset]:
+                size = int(np.prod(part.shape))
+                parts.append(flat[start : start + size].reshape(part.shape))
+                start += size
+            arrived[offset] = parts
     return arrived
 
 
@@ -217,32 +219,34 @@
 def plane_round_and_stencil(extended, nx, ny):
     e = extended
     payloads = {
-        (1, 0): e[:, nx - 2 : nx + 1, 2 : ny + 3],
-        (-1, 0): e[:, 0:2, 2 : ny + 2],
-        (0, 1): e[:, :, ny : ny + 3],
-        (0, -1): e[:, 0:nx, 2:4],
-        (1, 1): jnp.concatenate([e[:, nx - 2 : nx + 1, ny + 2], e[:, nx, ny : ny + 2]], axis=1),
-        (-1, 1): e[:, 0:2, ny + 2],
-        (1, -1): e[:, nx, 2:4],
+        (1, 0): (e[:, nx - 2 : nx, 2 : ny + 2, 2:-2], e[:-1, nx : nx + 1, 2 : ny + 3]),
+        (-1, 0): (e[:, 0:2, 2 : ny + 2, 2:-2],),
+        (0, 1): (e[:, :, ny : ny + 3],),
+        (0, -1): (e[:, 0:nx, 2:4],),
+        (1, 1): (e[:, nx - 2 : nx + 1, ny + 2], e[:, nx, ny : ny + 2]),
+        (-1, 1): (e[:, 0:2, ny + 2],),
+        (1, -1): (e[:, nx, 2:4],),
     }
     got = exchange(payloads, ("gx", "gy"))
     channels, _, _, depth = e.shape
     shape = (channels, nx + 4, ny + 4, depth)
 
-    def at(block, layer, row):
-        return placed(block, (0, layer, row, 0), shape)
-
-    corner = got[(1, 1)]
+    def at(block, layer, row, col=0):
+        return placed(block, (0, layer, row, col), shape)
+
+    halo_x, fold_x = got[(1, 0)]
+    corner_x, corner_y = got[(1, 1)]
     total = (
         at(e, 2, 0)
-        + at(got[(1, 0)], 0, 2)
-        + at(got[(-1, 0)], nx + 2, 2)
-        + at(got[(0, 1)], 2, 0)
-        + at(got[(0, -1)], 2, ny + 2)
-        + at(corner[:, 0:3, None], 0, 2)
-        + at(corner[:, 3:5, :][:, None], 2, 0)
-        + at(got[(-1, 1)][:, :, None], nx + 2, 2)
-        + at(got[(1, -1)][:, None], 2, ny + 2)
+        + at(halo_x, 0, 2, 2)
+        + at(fold_x, 2, 2)
+        + at(got[(-1, 0)][0], nx + 2, 2, 2)
+        + at(got[(0, 1)][0], 2, 0)
+        + at(got[(0, -1)][0], 2, ny + 2)
+        + at(corner_x[:, :, None], 0, 2)
+        + at(corner_y[:, None], 2, 0)
+        + at(got[(-1, 1)][0][:, :, None], nx + 2, 2)
+        + at(got[(1, -1)][0][:, None], 2, ny + 2)
     )
     return stencil_apply(total[:-1] * total[-1])
 

time: 36.2 us -> 35.6 us (0.983)
  waiting for transfers between devices: 9.78 us -> 8.79 us
  local copies, waits for them, and re-layouts: 5.54 us -> 5.93 us
    ppermute x3, waiting for transfers between devices: 5.89 us -> 4.9 us  [exchange(): rows = lax.ppermute(rows, tuple(axes), pairs)]
    reshape x10 -> x6, local copies, waits for them, and re-layouts: 1.86 us -> 0.88 us  [the longest x3 0.47 us: exchange(): parts.append(flat[start:start + size].reshape(part.shape))]
    concatenate x2, local copies, waits for them, and re-layouts: 0.09 us -> 0.99 us  [exchange(): jnp.concatenate([part.reshape(-1) for offset in offsets for part in paylo...]
    another operation x4 -> x8, local copies, waits for them, and re-layouts: 0.35 us -> 0.72 us  [the longest x4 0.35 us: exchange(): part.reshape(-1)]
  transfers between devices with their start and end apart: 5 -> 5, of which waited for: 5 -> 5; matrix products, arithmetic and copies ran while one was open for 8% -> 9% of each run, Pallas kernels for 0% -> 0%
where the time goes in v13:
time: 35.6 us; the launch traced here: 35.3 us
  waiting for transfers between devices  8.79 us (25%)
  starting transfers between devices  8.23 us (23%)
  matrix products  5.97 us (17%)
  local copies, waits for them, and re-layouts  5.93 us (17%)
  other arithmetic  5.84 us (16%)
  between operations  0.59 us (2%)
    ppermute x3, waiting for transfers between devices, exchange(): rows = lax.ppermute(rows, tuple(axes), pairs)  4.9 us
    ppermute x2, starting transfers between devices, shifted(): lax.ppermute(block, axis, [(i, (i + step) % count) for i in range(count)])  4.6 us
    ppermute x2, waiting for transfers between devices, shifted(): lax.ppermute(block, axis, [(i, (i + step) % count) for i in range(count)])  3.89 us
    ppermute x3, starting transfers between devices, exchange(): rows = lax.ppermute(rows, tuple(axes), pairs)  3.62 us
    dot_general x3, matrix products, planar_part(): jnp.dot(jnp.asarray(plane_map, jnp.float32), signed, precision=lax.Precis...  3.07 us
    mul x1, other arithmetic, stencil_apply(): return 0.25 * total  2.03 us
    dot_general x3, matrix products, body(): lax.dot_general(arrived[comp], place, (((0,), (0,)), ((), ())), precision...  1.28 us
    dot_general x3, matrix products, body(): jnp.dot(planar, jnp.asarray(depth.T, jnp.float32), precision=lax.Precisio...  1.09 us
  transfers between devices with their start and end apart: 5, of which 5 were waited for; matrix products, arithmetic and copies ran while one was open for 9% of the time, Pallas kernels for 0%

profile of v13, /device:TPU:0, one launch (start us, length us, event | category | flops | bytes accessed | tf_op | source)
XLA Modules:
  0.0 35.3 jit_solution(11138286229440910593)
XLA Ops:
  0.0 0.7 %convert_bitcast_fusion.2 = (f32[2,8,32]{2,1,0:T(8,128)S(1)}, f32[2,8,32]{2,1,0:T(8,128)S(1)}, f32[2,8,32]{2,1,0:T(8,128)S(1)}) fusion(s32[3,2,8,32]{3,2,1,0:T(8,128)} %param.18), kind=kLoop, calls=%fused_computation.62 | loop fusion | flops 4608 | bytes 12288 | tf_op jit(solution)/shard_map/convert_element_type | solution.py:44
  0.9 1.0 %subtract_convert_fusion = f32[8,32,128]{2,1,0:T(8,128)S(1)} fusion(s32[8,32,128]{2,1,0:T(8,128)} %param.19), kind=kLoop, calls=%fused_computation.34 | loop fusion | flops 65536 | bytes 262144 | tf_op jit(solution)/shard_map/convert_element_type | solution.py:278
  1.9 0.9 %broadcast_multiply_fusion.2 = f32[2,5,8,5,128]{4,2,3,1,0:T(8,128)S(1)} fusion(f32[2,5,8,5,128]{4,2,3,1,0:T(8,128)} %param.17, f32[2,8,128]{2,1,0:T(8,128)S(1)} %copy.51), kind=kLoop, calls=%fused_computation.37 | loop fusion | flops 51200 | bytes 417792 | tf_op jit(solution)/shard_map/mul | solution.py:45
  3.0 0.1 broadcast_in_dim.12
  3.1 0.2 mul.83
  3.3 0.1 broadcast_in_dim.13
  3.4 0.2 mul.87
  3.7 0.1 copy.53
  3.8 0.1 copy.54
  4.3 0.1 reshape.90
  4.5 0.1 copy.49
  4.7 1.9 %fusion.32 = f32[160,324]{1,0:T(8,128)S(1)} fusion(f32[320,160]{1,0:T(8,128)S(1)} %reshape.90, f32[324,320]{1,0:T(8,128)} %constant.35.clone), kind=kOutput, calls=%fused_computation.72 | convolution fusion | flops 99532800 | bytes 826880 | tf_op jit(solution)/shard_map/dot_general | solution.py:48
  6.6 0.2 convolution_bitcast_fusion.1
  6.8 0.8 %fusion.30 = f32[160,324]{1,0:T(8,128)S(1)} fusion(f32[320,160]{1,0:T(8,128)S(1)} %reshape.89, f32[324,320]{1,0:T(8,128)S(1)} %copy-done.2), kind=kOutput, calls=%fused_computation.70 | convolution fusion | flops 99532800 | bytes 826880 | tf_op jit(solution)/shard_map/dot_general | solution.py:48
  7.6 0.2 convolution_bitcast_fusion.2
  7.7 0.4 %fusion.34 = f32[128,324]{0,1:T(8,128)S(1)} fusion(f32[400,128]{1,0:T(8,128)S(1)} %reshape.91, f32[324,400]{1,0:T(8,128)S(1)} %copy-done), kind=kOutput, calls=%fused_computation.74 | convolution fusion | flops 99532800 | bytes 889088 | tf_op jit(solution)/shard_map/dot_general | solution.py:48
  8.2 0.2 convolution_bitcast_fusion
  8.4 4.5 %collective-permute-start.1 = (f32[8,324]{1,0:T(8,128)S(1)}, f32[8,324]{1,0:T(8,128)S(1)}, u32[]{:S(2)}, u32[]{:S(2)}) collective-permute-start(f32[8,324]{1,0:T(8,128)S(1)} %reshape.94), channel_id=1, source_target_pairs={{0,7},{1,0},{2,1},{3,2},{4,3},{5,4},{6,5},{7,6},{8,15},{9,8},{10,9... | collective-permute-start | bytes 31112 | tf_op jit(solution)/shard_map/ppermute | solution.py:59
  13.1 0.4 %fusion.33 = f32[324,132]{0,1:T(8,128)S(1)} fusion(f32[160,324]{1,0:T(8,128)S(1)} %fusion.32, f32[160,132]{1,0:T(8,128)S(1)} %copy-done.1), kind=kOutput, calls=%fused_computation.73 | convolution fusion | flops 41057280 | bytes 462912 | tf_op jit(solution)/shard_map/dot_general | solution.py:293
  13.5 0.4 %fusion.31 = f32[324,132]{0,1:T(8,128)S(1)} fusion(f32[160,324]{1,0:T(8,128)S(1)} %fusion.30, f32[160,132]{1,0:T(8,128)S(1)} %copy-done.1), kind=kOutput, calls=%fused_computation.71 | convolution fusion | flops 41057280 | bytes 462912 | tf_op jit(solution)/shard_map/dot_general | solution.py:293
  13.9 0.3 fusion.35
  14.2 0.2 collective-permute-done.1
  14.4 3.7 %collective-permute-done = f32[12,324]{1,0:T(8,128)S(1)} collective-permute-done((f32[12,324]{1,0:T(8,128)S(1)}, f32[12,324]{1,0:T(8,128)S(1)}, u32[]{:S(2)}, u32[]{:S(2)}) %collective-permute-start) | collective-permute-done | bytes 15584 | tf_op jit(solution)/shard_map/ppermute | solution.py:59
  18.2 0.4 %convolution_add_fusion.2 = f32[324,132]{0,1:T(8,128)S(1)} fusion(f32[324,132]{0,1:T(8,128)S(1)} %fusion.31, f32[5,132]{1,0:T(8,128)S(1)} %copy-done.6, f32[4,3,324]{2,1,0:T(4,128)S(1)} %reshape.93, f32[4,2,324]{2,1,0:T(2,128)S(1)} %reshape.95), kind=kOutput, calls=%fused_computation.5 | convolution fusion | flops 2610468 | bytes 370704 | tf_op jit(solution)/shard_map/dot_general | solution.py:306
  18.6 0.4 %convolution_add_fusion.1 = f32[324,132]{0,1:T(8,128)S(1)} fusion(f32[324,132]{0,1:T(8,128)S(1)} %fusion.33, f32[5,132]{1,0:T(8,128)S(1)} %copy-done.6, f32[4,3,324]{2,1,0:T(4,128)S(1)} %reshape.93, f32[4,2,324]{2,1,0:T(2,128)S(1)} %reshape.95), kind=kOutput, calls=%fused_computation.4 | convolution fusion | flops 2610468 | bytes 370704 | tf_op jit(solution)/shard_map/dot_general | solution.py:306
  19.0 0.4 %convolution_add_fusion = f32[324,132]{0,1:T(8,128)S(1)} fusion(f32[324,132]{0,1:T(8,128)S(1)} %fusion.35, f32[5,132]{1,0:T(8,128)S(1)} %copy-done.6, f32[4,3,324]{2,1,0:T(4,128)S(1)} %reshape.93, f32[4,2,324]{2,1,0:T(2,128)S(1)} %reshape.95), kind=kOutput, calls=%fused_computation.3 | convolution fusion | flops 2610468 | bytes 370704 | tf_op jit(solution)/shard_map/dot_general | solution.py:306
  19.5 0.1 copy.57
  19.7 0.1 copy.56
  19.9 0.1 copy.55
  20.1 0.2 copy.58
  20.4 0.2 add_bitcast_fusion
  20.7 0.1 pad_maximum_fusion
  21.0 0.1 fusion.26
  21.1 0.1 reshape.97
  21.7 2.5 %collective-permute-start.4 = (f32[38,128]{1,0:T(8,128)S(1)}, f32[38,128]{1,0:T(8,128)S(1)}, u32[]{:S(2)}, u32[]{:S(2)}) collective-permute-start(f32[38,128]{1,0:T(8,128)S(1)} %pad_bitcast_fusion.1), channel_id=1, source_target_pairs={{0,24},{8,16},{16,8},{24,0},{1,25},{9,17},{17,9},{25,1},{2,26},{10... | collective-permute-start | bytes 58376 | tf_op jit(solution)/shard_map/ppermute | solution.py:202
  24.2 0.1 reshape.105
  24.4 0.1 reshape.104
  24.5 0.9 %concatenate.18 = f32[78604]{0:T(1024)S(1)} concatenate(f32[32768]{0:T(1024)S(1)} %bitcast.78, f32[13068]{0:T(1024)S(1)} %reshape.97, f32[32768]{0:T(1024)S(1)} %bitcast.77), dimensions={0} | concatenate | bytes 628832 | tf_op jit(solution)/shard_map/concatenate | solution.py:194
  25.5 0.6 %collective-permute-start.2 = (f32[615,128]{1,0:T(8,128)S(1)}, f32[615,128]{1,0:T(8,128)S(1)}, u32[]{:S(2)}, u32[]{:S(2)}) collective-permute-start(f32[615,128]{1,0:T(8,128)S(1)} %pad_bitcast_fusion), channel_id=1, source_target_pairs={{0,16},{8,24},{16,0},{24,8},{1,17},{9,25},{17,1},{25,9},{2,18},{10... | collective-permute-start | bytes 944648 | tf_op jit(solution)/shard_map/ppermute | solution.py:202
  26.2 0.5 %collective-permute-start.3 = (f32[178,128]{1,0:T(8,128)S(1)}, f32[178,128]{1,0:T(8,128)S(1)}, u32[]{:S(2)}, u32[]{:S(2)}) collective-permute-start(f32[178,128]{1,0:T(8,128)S(1)} %fusion.13), channel_id=1, source_target_pairs={{0,8},{8,0},{16,24},{24,16},{1,9},{9,1},{17,25},{25,17},{2,10},{10... | collective-permute-start | bytes 273416 | tf_op jit(solution)/shard_map/ppermute | solution.py:202
  27.2 3.5 %collective-permute-done.3 = f32[178,128]{1,0:T(8,128)S(1)} collective-permute-done((f32[178,128]{1,0:T(8,128)S(1)}, f32[178,128]{1,0:T(8,128)S(1)}, u32[]{:S(2)}, u32[]{:S(2)}) %collective-permute-start.3) | collective-permute-done | bytes 91168 | tf_op jit(solution)/shard_map/ppermute | solution.py:202
  30.8 0.2 reshape.109
  31.0 0.2 reshape.108
  31.2 1.3 %collective-permute-done.2 = f32[615,128]{1,0:T(8,128)S(1)} collective-permute-done((f32[615,128]{1,0:T(8,128)S(1)}, f32[615,128]{1,0:T(8,128)S(1)}, u32[]{:S(2)}, u32[]{:S(2)}) %collective-permute-start.2) | collective-permute-done | bytes 314912 | tf_op jit(solution)/shard_map/ppermute | solution.py:202
  32.6 0.1 reshape.102
  32.8 0.4 %pad_add_fusion = f32[4,12,36,132]{3,2,1,0:T(8,128)S(1)} fusion(f32[4,1,2,132]{3,2,1,0:T(2,128)S(1)} %bitcast.87, f32[4,2,1,132]{3,2,1,0:T(1,128)S(1)} %broadcast_in_dim_reshape.20, f32[4,1,2,132]{3,2,1,0:T(2,128)S(1)} %bitcast.86, f32[4,3,1,132]{3,2,1,0:T(1,128)S(1)} %broadcast_in_dim_reshape.19, f32[4,8,2,132]{3,2,1,0:T(2,128)S(1)} %reshape.109, ...), kind=kLoop, calls=%fused_computation | loop fusion | flops 2052864 | bytes 2020912 | tf_op jit(solution)/shard_map/add | solution.py:240
  33.2 0.1 slice_multiply_fusion
  33.3 2.0 %fusion.2 = f32[3,8,32,128]{3,2,1,0:T(8,128)} fusion(f32[3,12,36,132]{3,2,1,0:T(8,128)S(1)} %slice_multiply_fusion), kind=kLoop, calls=%fused_computation.13 | loop fusion | flops 1966080 | bytes 5505024 | tf_op jit(solution)/shard_map/mul | solution.py:183
  (72 shorter events, 2.8 us)
Async XLA Ops:
  0.8 3.4 %copy-start.3 = (f32[2,5,8,4,160]{4,3,2,1,0:T(4,128)S(1)}, f32[2,5,8,4,160]{4,3,2,1,0:T(4,128)}, u32[]{:S(2)}) copy-start(f32[2,5,8,4,160]{4,3,2,1,0:T(4,128)} %param.16) | copy-start | bytes 614404
  2.9 1.5 %copy-start.4 = (f32[2,4,8,5,160]{4,2,3,1,0:T(8,128)S(1)}, f32[2,4,8,5,160]{4,2,3,1,0:T(8,128)}, u32[]{:S(2)}) copy-start(f32[2,4,8,5,160]{4,2,3,1,0:T(8,128)} %param.15) | copy-start | bytes 614404
  4.3 2.3 %copy-start.7 = (f32[5,160]{1,0:T(8,128)S(1)}, f32[5,160]{1,0:T(8,128)}, u32[]{:S(2)}) copy-start(f32[5,160]{1,0:T(8,128)} %constant.34.clone) | copy-start | bytes 9604
  4.4 2.3 %copy-start.2 = (f32[324,320]{1,0:T(8,128)S(1)}, f32[324,320]{1,0:T(8,128)}, u32[]{:S(2)}) copy-start(f32[324,320]{1,0:T(8,128)} %constant.14.clone) | copy-start | bytes 1244164
  4.6 3.1 %copy-start = (f32[324,400]{1,0:T(8,128)S(1)}, f32[324,400]{1,0:T(8,128)}, u32[]{:S(2)}) copy-start(f32[324,400]{1,0:T(8,128)} %constant.36.clone) | copy-start | bytes 1555204
  4.7 3.5 %copy-start.8 = (f32[5,128]{1,0:T(8,128)S(1)}, f32[5,128]{1,0:T(8,128)}, u32[]{:S(2)}) copy-start(f32[5,128]{1,0:T(8,128)} %constant.37.clone) | copy-start | bytes 7684
  4.7 8.4 %copy-start.1 = (f32[160,132]{1,0:T(8,128)S(1)}, f32[160,132]{1,0:T(8,128)}, u32[]{:S(2)}) copy-start(f32[160,132]{1,0:T(8,128)} %constant.38.clone) | copy-start | bytes 253444
  6.8 7.1 %copy-start.5 = (f32[128,132]{1,0:T(8,128)S(1)}, f32[128,132]{1,0:T(8,128)}, u32[]{:S(2)}) copy-start(f32[128,132]{1,0:T(8,128)} %constant.39.clone) | copy-start | bytes 202756
  7.6 10.6 %copy-start.6 = (f32[5,132]{1,0:T(8,128)S(1)}, f32[5,132]{1,0:T(8,128)}, u32[]{:S(2)}) copy-start(f32[5,132]{1,0:T(8,128)} %constant.40.clone) | copy-start | bytes 7924
  8.4 6.0 %collective-permute-start.1 = (f32[8,324]{1,0:T(8,128)S(1)}, f32[8,324]{1,0:T(8,128)S(1)}, u32[]{:S(2)}, u32[]{:S(2)}) collective-permute-start(f32[8,324]{1,0:T(8,128)S(1)} %reshape.94), channel_id=1, source_target_pairs={{0,7},{1,0},{2,1},{3,2},{4,3},{5,4},{6,5},{7,6},{8,15},{9,8},{10,9... | collective-permute-start | bytes 31112 | tf_op jit(solution)/shard_map/ppermute | solution.py:59
  13.0 5.1 %collective-permute-start = (f32[12,324]{1,0:T(8,128)S(1)}, f32[12,324]{1,0:T(8,128)S(1)}, u32[]{:S(2)}, u32[]{:S(2)}) collective-permute-start(f32[12,324]{1,0:T(8,128)S(1)} %reshape.92), channel_id=1, source_target_pairs={{0,1},{1,2},{2,3},{3,4},{4,5},{5,6},{6,7},{7,0},{8,9},{9,10},{10,1... | collective-permute-start | bytes 46664 | tf_op jit(solution)/shard_map/ppermute | solution.py:59
  21.7 5.0 %collective-permute-start.4 = (f32[38,128]{1,0:T(8,128)S(1)}, f32[38,128]{1,0:T(8,128)S(1)}, u32[]{:S(2)}, u32[]{:S(2)}) collective-permute-start(f32[38,128]{1,0:T(8,128)S(1)} %pad_bitcast_fusion.1), channel_id=1, source_target_pairs={{0,24},{8,16},{16,8},{24,0},{1,25},{9,17},{17,9},{25,1},{2,26},{10... | collective-permute-start | bytes 58376 | tf_op jit(solution)/shard_map/ppermute | solution.py:202
  25.5 7.0 %collective-permute-start.2 = (f32[615,128]{1,0:T(8,128)S(1)}, f32[615,128]{1,0:T(8,128)S(1)}, u32[]{:S(2)}, u32[]{:S(2)}) collective-permute-start(f32[615,128]{1,0:T(8,128)S(1)} %pad_bitcast_fusion), channel_id=1, source_target_pairs={{0,16},{8,24},{16,0},{24,8},{1,17},{9,25},{17,1},{25,9},{2,18},{10... | collective-permute-start | bytes 944648 | tf_op jit(solution)/shard_map/ppermute | solution.py:202
  26.2 4.6 %collective-permute-start.3 = (f32[178,128]{1,0:T(8,128)S(1)}, f32[178,128]{1,0:T(8,128)S(1)}, u32[]{:S(2)}, u32[]{:S(2)}) collective-permute-start(f32[178,128]{1,0:T(8,128)S(1)} %fusion.13), channel_id=1, source_target_pairs={{0,8},{8,0},{16,24},{24,16},{1,9},{9,1},{17,25},{25,17},{2,10},{10... | collective-permute-start | bytes 273416 | tf_op jit(solution)/shard_map/ppermute | solution.py:202

commit v14 on v13

--- a/solution.py
+++ b/solution.py
@@ -190,10 +190,15 @@
         key = tuple(o % s for o, s in zip(offset, sizes))
         groups.setdefault(key, []).append(offset)
     arrived = {}
+    previous = None
     for key, offsets in groups.items():
-        flat = jnp.concatenate([part.reshape(-1) for offset in offsets for part in payloads[offset]])
+        parts = [part for offset in offsets for part in payloads[offset]]
+        if previous is not None:
+            previous, parts = lax.optimization_barrier((previous, parts))
+        flat = jnp.concatenate([part.reshape(-1) for part in parts])
         length = flat.shape[0]
         rows = jnp.pad(flat, (0, -length % 128)).reshape(-1, 128)
+        previous = rows
         if any(key):
             pairs = []
             for source in np.ndindex(*sizes):

time: 35.6 us -> 34.5 us (0.969)
  waiting for transfers between devices: 8.79 us -> 7.7 us
    ppermute x3, waiting for transfers between devices: 4.9 us -> 3.81 us  [exchange(): rows = lax.ppermute(rows, tuple(axes), pairs)]
    reshape x3 -> x7, local copies, waits for them, and re-layouts: 0.41 us -> 0.76 us  [exchange(): flat = jnp.concatenate([part.reshape(-1) for part in parts])]
  transfers between devices with their start and end apart: 5 -> 5, of which waited for: 5 -> 3; matrix products, arithmetic and copies ran while one was open for 9% -> 8% of each run, Pallas kernels for 0% -> 0%
where the time goes in v14:
time: 34.5 us; the launch traced here: 34.3 us
  starting transfers between devices  8.22 us (24%)
  waiting for transfers between devices  7.7 us (22%)
  matrix products  5.97 us (17%)
  local copies, waits for them, and re-layouts  5.89 us (17%)
  other arithmetic  5.84 us (17%)
  between operations  0.65 us (2%)
    ppermute x2, starting transfers between devices, shifted(): lax.ppermute(block, axis, [(i, (i + step) % count) for i in range(count)])  4.6 us
    ppermute x2, waiting for transfers between devices, shifted(): lax.ppermute(block, axis, [(i, (i + step) % count) for i in range(count)])  3.89 us
    ppermute x3, waiting for transfers between devices, exchange(): rows = lax.ppermute(rows, tuple(axes), pairs)  3.81 us
    ppermute x3, starting transfers between devices, exchange(): rows = lax.ppermute(rows, tuple(axes), pairs)  3.62 us
    dot_general x3, matrix products, planar_part(): jnp.dot(jnp.asarray(plane_map, jnp.float32), signed, precision=lax.Precis...  3.07 us
    mul x1, other arithmetic, stencil_apply(): return 0.25 * total  2.03 us
    dot_general x3, matrix products, body(): lax.dot_general(arrived[comp], place, (((0,), (0,)), ((), ())), precision...  1.28 us
    dot_general x3, matrix products, body(): jnp.dot(planar, jnp.asarray(depth.T, jnp.float32), precision=lax.Precisio...  1.09 us
  transfers between devices with their start and end apart: 5, of which 3 were waited for; matrix products, arithmetic and copies ran while one was open for 8% of the time, Pallas kernels for 0%

profile of v14, /device:TPU:0, one launch (start us, length us, event | category | flops | bytes accessed | tf_op | source)
XLA Modules:
  0.0 34.3 jit_solution(5908619420955796606)
XLA Ops:
  0.0 0.7 %convert_bitcast_fusion.2 = (f32[2,8,32]{2,1,0:T(8,128)S(1)}, f32[2,8,32]{2,1,0:T(8,128)S(1)}, f32[2,8,32]{2,1,0:T(8,128)S(1)}) fusion(s32[3,2,8,32]{3,2,1,0:T(8,128)} %param.18), kind=kLoop, calls=%fused_computation.64 | loop fusion | flops 4608 | bytes 12288 | tf_op jit(solution)/shard_map/convert_element_type | solution.py:44
  0.9 1.0 %subtract_convert_fusion = f32[8,32,128]{2,1,0:T(8,128)S(1)} fusion(s32[8,32,128]{2,1,0:T(8,128)} %param.19), kind=kLoop, calls=%fused_computation.34 | loop fusion | flops 65536 | bytes 262144 | tf_op jit(solution)/shard_map/convert_element_type | solution.py:283
  1.9 0.9 %broadcast_multiply_fusion.2 = f32[2,5,8,5,128]{4,2,3,1,0:T(8,128)S(1)} fusion(f32[2,5,8,5,128]{4,2,3,1,0:T(8,128)} %param.17, f32[2,8,128]{2,1,0:T(8,128)S(1)} %copy.55), kind=kLoop, calls=%fused_computation.37 | loop fusion | flops 51200 | bytes 417792 | tf_op jit(solution)/shard_map/mul | solution.py:45
  3.0 0.1 broadcast_in_dim.12
  3.1 0.2 mul.83
  3.3 0.1 broadcast_in_dim.13
  3.4 0.2 mul.87
  3.7 0.1 copy.57
  3.8 0.1 copy.58
  4.3 0.1 reshape.102
  4.5 0.1 copy.53
  4.7 1.9 %fusion.31 = f32[160,324]{1,0:T(8,128)S(1)} fusion(f32[320,160]{1,0:T(8,128)S(1)} %reshape.102, f32[324,320]{1,0:T(8,128)} %constant.35.clone), kind=kOutput, calls=%fused_computation.73 | convolution fusion | flops 99532800 | bytes 826880 | tf_op jit(solution)/shard_map/dot_general | solution.py:48
  6.6 0.2 convolution_bitcast_fusion.1
  6.8 0.8 %fusion.29 = f32[160,324]{1,0:T(8,128)S(1)} fusion(f32[320,160]{1,0:T(8,128)S(1)} %reshape.101, f32[324,320]{1,0:T(8,128)S(1)} %copy-done.2), kind=kOutput, calls=%fused_computation.71 | convolution fusion | flops 99532800 | bytes 826880 | tf_op jit(solution)/shard_map/dot_general | solution.py:48
  7.6 0.2 convolution_bitcast_fusion.2
  7.7 0.4 %fusion.33 = f32[128,324]{0,1:T(8,128)S(1)} fusion(f32[400,128]{1,0:T(8,128)S(1)} %reshape.103, f32[324,400]{1,0:T(8,128)S(1)} %copy-done), kind=kOutput, calls=%fused_computation.75 | convolution fusion | flops 99532800 | bytes 889088 | tf_op jit(solution)/shard_map/dot_general | solution.py:48
  8.2 0.2 convolution_bitcast_fusion
  8.4 4.5 %collective-permute-start.1 = (f32[8,324]{1,0:T(8,128)S(1)}, f32[8,324]{1,0:T(8,128)S(1)}, u32[]{:S(2)}, u32[]{:S(2)}) collective-permute-start(f32[8,324]{1,0:T(8,128)S(1)} %reshape.106), channel_id=1, source_target_pairs={{0,7},{1,0},{2,1},{3,2},{4,3},{5,4},{6,5},{7,6},{8,15},{9,8},{10,9... | collective-permute-start | bytes 31112 | tf_op jit(solution)/shard_map/ppermute | solution.py:59
  13.1 0.4 %fusion.32 = f32[324,132]{0,1:T(8,128)S(1)} fusion(f32[160,324]{1,0:T(8,128)S(1)} %fusion.31, f32[160,132]{1,0:T(8,128)S(1)} %copy-done.1), kind=kOutput, calls=%fused_computation.74 | convolution fusion | flops 41057280 | bytes 462912 | tf_op jit(solution)/shard_map/dot_general | solution.py:298
  13.5 0.4 %fusion.30 = f32[324,132]{0,1:T(8,128)S(1)} fusion(f32[160,324]{1,0:T(8,128)S(1)} %fusion.29, f32[160,132]{1,0:T(8,128)S(1)} %copy-done.1), kind=kOutput, calls=%fused_computation.72 | convolution fusion | flops 41057280 | bytes 462912 | tf_op jit(solution)/shard_map/dot_general | solution.py:298
  13.9 0.3 fusion.34
  14.2 0.2 collective-permute-done.1
  14.4 3.7 %collective-permute-done = f32[12,324]{1,0:T(8,128)S(1)} collective-permute-done((f32[12,324]{1,0:T(8,128)S(1)}, f32[12,324]{1,0:T(8,128)S(1)}, u32[]{:S(2)}, u32[]{:S(2)}) %collective-permute-start) | collective-permute-done | bytes 15584 | tf_op jit(solution)/shard_map/ppermute | solution.py:59
  18.2 0.4 %convolution_add_fusion.2 = f32[324,132]{0,1:T(8,128)S(1)} fusion(f32[324,132]{0,1:T(8,128)S(1)} %fusion.30, f32[5,132]{1,0:T(8,128)S(1)} %copy-done.6, f32[4,3,324]{2,1,0:T(4,128)S(1)} %reshape.105, f32[4,2,324]{2,1,0:T(2,128)S(1)} %reshape.107), kind=kOutput, calls=%fused_computation.5 | convolution fusion | flops 2610468 | bytes 370704 | tf_op jit(solution)/shard_map/dot_general | solution.py:311
  18.6 0.4 %convolution_add_fusion.1 = f32[324,132]{0,1:T(8,128)S(1)} fusion(f32[324,132]{0,1:T(8,128)S(1)} %fusion.32, f32[5,132]{1,0:T(8,128)S(1)} %copy-done.6, f32[4,3,324]{2,1,0:T(4,128)S(1)} %reshape.105, f32[4,2,324]{2,1,0:T(2,128)S(1)} %reshape.107), kind=kOutput, calls=%fused_computation.4 | convolution fusion | flops 2610468 | bytes 370704 | tf_op jit(solution)/shard_map/dot_general | solution.py:311
  19.0 0.4 %convolution_add_fusion = f32[324,132]{0,1:T(8,128)S(1)} fusion(f32[324,132]{0,1:T(8,128)S(1)} %fusion.34, f32[5,132]{1,0:T(8,128)S(1)} %copy-done.6, f32[4,3,324]{2,1,0:T(4,128)S(1)} %reshape.105, f32[4,2,324]{2,1,0:T(2,128)S(1)} %reshape.107), kind=kOutput, calls=%fused_computation.3 | convolution fusion | flops 2610468 | bytes 370704 | tf_op jit(solution)/shard_map/dot_general | solution.py:311
  19.5 0.1 copy.61
  19.7 0.1 copy.60
  19.9 0.1 copy.59
  20.1 0.2 copy.62
  20.3 0.1 slice.196
  20.4 0.2 add_bitcast_fusion
  20.7 0.1 pad_maximum_fusion
  20.9 0.1 fusion.26
  21.1 0.1 reshape.109
  21.2 0.9 %concatenate.18 = f32[78604]{0:T(1024)S(1)} concatenate(f32[32768]{0:T(1024)S(1)} %bitcast.88, f32[13068]{0:T(1024)S(1)} %reshape.109, f32[32768]{0:T(1024)S(1)} %bitcast.87), dimensions={0} | concatenate | bytes 628832 | tf_op jit(solution)/shard_map/concatenate | solution.py:198
  22.2 1.6 %collective-permute-start.2 = (f32[615,128]{1,0:T(8,128)S(1)}, f32[615,128]{1,0:T(8,128)S(1)}, u32[]{:S(2)}, u32[]{:S(2)}) collective-permute-start(f32[615,128]{1,0:T(8,128)S(1)} %pad_bitcast_fusion), channel_id=1, source_target_pairs={{0,16},{8,24},{16,0},{24,8},{1,17},{9,25},{17,1},{25,9},{2,18},{10... | collective-permute-start | bytes 944648 | tf_op jit(solution)/shard_map/ppermute | solution.py:207
  23.7 0.1 reshape.116
  23.9 0.1 reshape.117
  24.6 1.5 %collective-permute-start.4 = (f32[38,128]{1,0:T(8,128)S(1)}, f32[38,128]{1,0:T(8,128)S(1)}, u32[]{:S(2)}, u32[]{:S(2)}) collective-permute-start(f32[38,128]{1,0:T(8,128)S(1)} %pad_bitcast_fusion.1), channel_id=1, source_target_pairs={{0,24},{8,16},{16,8},{24,0},{1,25},{9,17},{17,9},{25,1},{2,26},{10... | collective-permute-start | bytes 58376 | tf_op jit(solution)/shard_map/ppermute | solution.py:207
  26.1 0.5 %collective-permute-start.3 = (f32[178,128]{1,0:T(8,128)S(1)}, f32[178,128]{1,0:T(8,128)S(1)}, u32[]{:S(2)}, u32[]{:S(2)}) collective-permute-start(f32[178,128]{1,0:T(8,128)S(1)} %fusion.13), channel_id=1, source_target_pairs={{0,8},{8,0},{16,24},{24,16},{1,9},{9,1},{17,25},{25,17},{2,10},{10... | collective-permute-start | bytes 273416 | tf_op jit(solution)/shard_map/ppermute | solution.py:207
  26.7 3.8 %collective-permute-done.4 = f32[38,128]{1,0:T(8,128)S(1)} collective-permute-done((f32[38,128]{1,0:T(8,128)S(1)}, f32[38,128]{1,0:T(8,128)S(1)}, u32[]{:S(2)}, u32[]{:S(2)}) %collective-permute-start.4) | collective-permute-done | bytes 19488 | tf_op jit(solution)/shard_map/ppermute | solution.py:207
  31.0 0.2 reshape.121
  31.2 0.2 reshape.120
  31.5 0.1 reshape.114
  31.7 0.4 %pad_add_fusion = f32[4,12,36,132]{3,2,1,0:T(8,128)S(1)} fusion(f32[4,1,2,132]{3,2,1,0:T(2,128)S(1)} %bitcast.98, f32[4,2,1,132]{3,2,1,0:T(1,128)S(1)} %broadcast_in_dim_reshape.20, f32[4,1,2,132]{3,2,1,0:T(2,128)S(1)} %bitcast.97, f32[4,3,1,132]{3,2,1,0:T(1,128)S(1)} %broadcast_in_dim_reshape.19, f32[4,8,2,132]{3,2,1,0:T(2,128)S(1)} %reshape.121, ...), kind=kLoop, calls=%fused_computation | loop fusion | flops 2052864 | bytes 2020912 | tf_op jit(solution)/shard_map/add | solution.py:245
  32.1 0.1 slice_multiply_fusion
  32.2 2.0 %fusion.2 = f32[3,8,32,128]{3,2,1,0:T(8,128)} fusion(f32[3,12,36,132]{3,2,1,0:T(8,128)S(1)} %slice_multiply_fusion), kind=kLoop, calls=%fused_computation.13 | loop fusion | flops 1966080 | bytes 5505024 | tf_op jit(solution)/shard_map/mul | solution.py:183
  (75 shorter events, 2.6 us)
Async XLA Ops:
  0.8 3.4 %copy-start.3 = (f32[2,5,8,4,160]{4,3,2,1,0:T(4,128)S(1)}, f32[2,5,8,4,160]{4,3,2,1,0:T(4,128)}, u32[]{:S(2)}) copy-start(f32[2,5,8,4,160]{4,3,2,1,0:T(4,128)} %param.16) | copy-start | bytes 614404
  2.9 1.5 %copy-start.4 = (f32[2,4,8,5,160]{4,2,3,1,0:T(8,128)S(1)}, f32[2,4,8,5,160]{4,2,3,1,0:T(8,128)}, u32[]{:S(2)}) copy-start(f32[2,4,8,5,160]{4,2,3,1,0:T(8,128)} %param.15) | copy-start | bytes 614404
  4.3 2.3 %copy-start.7 = (f32[5,160]{1,0:T(8,128)S(1)}, f32[5,160]{1,0:T(8,128)}, u32[]{:S(2)}) copy-start(f32[5,160]{1,0:T(8,128)} %constant.34.clone) | copy-start | bytes 9604
  4.4 2.3 %copy-start.2 = (f32[324,320]{1,0:T(8,128)S(1)}, f32[324,320]{1,0:T(8,128)}, u32[]{:S(2)}) copy-start(f32[324,320]{1,0:T(8,128)} %constant.14.clone) | copy-start | bytes 1244164
  4.6 3.1 %copy-start = (f32[324,400]{1,0:T(8,128)S(1)}, f32[324,400]{1,0:T(8,128)}, u32[]{:S(2)}) copy-start(f32[324,400]{1,0:T(8,128)} %constant.36.clone) | copy-start | bytes 1555204
  4.7 3.5 %copy-start.8 = (f32[5,128]{1,0:T(8,128)S(1)}, f32[5,128]{1,0:T(8,128)}, u32[]{:S(2)}) copy-start(f32[5,128]{1,0:T(8,128)} %constant.37.clone) | copy-start | bytes 7684
  4.7 8.4 %copy-start.1 = (f32[160,132]{1,0:T(8,128)S(1)}, f32[160,132]{1,0:T(8,128)}, u32[]{:S(2)}) copy-start(f32[160,132]{1,0:T(8,128)} %constant.38.clone) | copy-start | bytes 253444
  6.8 7.1 %copy-start.5 = (f32[128,132]{1,0:T(8,128)S(1)}, f32[128,132]{1,0:T(8,128)}, u32[]{:S(2)}) copy-start(f32[128,132]{1,0:T(8,128)} %constant.39.clone) | copy-start | bytes 202756
  7.6 10.6 %copy-start.6 = (f32[5,132]{1,0:T(8,128)S(1)}, f32[5,132]{1,0:T(8,128)}, u32[]{:S(2)}) copy-start(f32[5,132]{1,0:T(8,128)} %constant.40.clone) | copy-start | bytes 7924
  8.4 6.0 %collective-permute-start.1 = (f32[8,324]{1,0:T(8,128)S(1)}, f32[8,324]{1,0:T(8,128)S(1)}, u32[]{:S(2)}, u32[]{:S(2)}) collective-permute-start(f32[8,324]{1,0:T(8,128)S(1)} %reshape.106), channel_id=1, source_target_pairs={{0,7},{1,0},{2,1},{3,2},{4,3},{5,4},{6,5},{7,6},{8,15},{9,8},{10,9... | collective-permute-start | bytes 31112 | tf_op jit(solution)/shard_map/ppermute | solution.py:59
  13.0 5.1 %collective-permute-start = (f32[12,324]{1,0:T(8,128)S(1)}, f32[12,324]{1,0:T(8,128)S(1)}, u32[]{:S(2)}, u32[]{:S(2)}) collective-permute-start(f32[12,324]{1,0:T(8,128)S(1)} %reshape.104), channel_id=1, source_target_pairs={{0,1},{1,2},{2,3},{3,4},{4,5},{5,6},{6,7},{7,0},{8,9},{9,10},{10,1... | collective-permute-start | bytes 46664 | tf_op jit(solution)/shard_map/ppermute | solution.py:59
  22.2 9.2 %collective-permute-start.2 = (f32[615,128]{1,0:T(8,128)S(1)}, f32[615,128]{1,0:T(8,128)S(1)}, u32[]{:S(2)}, u32[]{:S(2)}) collective-permute-start(f32[615,128]{1,0:T(8,128)S(1)} %pad_bitcast_fusion), channel_id=1, source_target_pairs={{0,16},{8,24},{16,0},{24,8},{1,17},{9,25},{17,1},{25,9},{2,18},{10... | collective-permute-start | bytes 944648 | tf_op jit(solution)/shard_map/ppermute | solution.py:207
  24.6 5.9 %collective-permute-start.4 = (f32[38,128]{1,0:T(8,128)S(1)}, f32[38,128]{1,0:T(8,128)S(1)}, u32[]{:S(2)}, u32[]{:S(2)}) collective-permute-start(f32[38,128]{1,0:T(8,128)S(1)} %pad_bitcast_fusion.1), channel_id=1, source_target_pairs={{0,24},{8,16},{16,8},{24,0},{1,25},{9,17},{17,9},{25,1},{2,26},{10... | collective-permute-start | bytes 58376 | tf_op jit(solution)/shard_map/ppermute | solution.py:207
  26.1 4.8 %collective-permute-start.3 = (f32[178,128]{1,0:T(8,128)S(1)}, f32[178,128]{1,0:T(8,128)S(1)}, u32[]{:S(2)}, u32[]{:S(2)}) collective-permute-start(f32[178,128]{1,0:T(8,128)S(1)} %fusion.13), channel_id=1, source_target_pairs={{0,8},{8,0},{16,24},{24,16},{1,9},{9,1},{17,25},{25,17},{2,10},{10... | collective-permute-start | bytes 273416 | tf_op jit(solution)/shard_map/ppermute | solution.py:207

commit v15 on v14

--- a/solution.py
+++ b/solution.py
@@ -253,7 +253,24 @@
         + at(got[(-1, 1)][0][:, :, None], nx + 2, 2)
         + at(got[(1, -1)][0][:, None], 2, ny + 2)
     )
-    return stencil_apply(total[:-1] * total[-1])
+    masked = total[:-1] * total[-1]
+    inner = z_terms(e[:-1, 1:nx, 3 : ny + 2] * e[-1, 1:nx, 3 : ny + 2])
+    rows = jnp.concatenate([z_terms(masked[:, 3 : nx + 2, 2:3]), inner], axis=2)
+    result = jnp.concatenate([z_terms(masked[:, 2:3, 2 : ny + 2]), rows], axis=1)
+    for axis_pos in (1, 2):
+        near = window(masked, axis_pos, 1) + window(masked, axis_pos, 3)
+        far = window(masked, axis_pos, 0) + window(masked, axis_pos, 4)
+        result = result - 4.0 / 3.0 * near + 1.0 / 12.0 * far
+    return 0.25 * result
+
+
+def z_terms(block):
+    nz = block.shape[-1] - 4
+
+    def part(dz):
+        return block[..., 2 + dz : nz + 2 + dz]
+
+    return 8.0 * part(0) - 4.0 / 3.0 * (part(-1) + part(1)) + 1.0 / 12.0 * (part(-2) + part(2))
 
 
 def body(edge_coeffs_x, edge_coeffs_y, edge_coeffs_z, flips, flags):

time: 34.5 us -> 34.1 us (0.988)
  local copies, waits for them, and re-layouts: 5.89 us -> 8.04 us
  matrix products: 5.97 us -> 4.88 us
  waiting for transfers between devices: 7.7 us -> 6.74 us
  other arithmetic: 5.84 us -> 5.27 us
    ppermute x2, waiting for transfers between devices: 3.89 us -> 0.28 us  [shifted(): lax.ppermute(block, axis, [(i, (i + step) % count) for i in range(count)])]
    ppermute x3, waiting for transfers between devices: 3.81 us -> 6.46 us  [exchange(): rows = lax.ppermute(rows, tuple(axes), pairs)]
    unnamed x19 -> x27, local copies, waits for them, and re-layouts: 0.07 us -> 2.14 us
    dot_general x3, matrix products: 3.07 us -> 1.97 us  [planar_part(): jnp.dot(jnp.asarray(plane_map, jnp.float32), signed, precision=lax.Precis...]
    mul x3, other arithmetic: 1.04 us -> 0.12 us  [planar_part(): coef * orient[:, None, :, None, :]]
    add x0 -> x3, other arithmetic: none -> 0.7 us  [z_terms(): 8.0 * part(0) - 4.0 / 3.0 * (part(-1) + part(1))]
    mul x2 -> x3, other arithmetic: 2.17 us -> 1.87 us  [the longest x1 1.63 us: plane_round_and_stencil(): return 0.25 * result]
  transfers between devices with their start and end apart: 5 -> 5, of which waited for: 3 -> 2; matrix products, arithmetic and copies ran while one was open for 8% -> 10% of each run, Pallas kernels for 0% -> 0%
where the time goes in v15:
time: 34.1 us; the launch traced here: 33.9 us
  starting transfers between devices  8.26 us (24%)
  local copies, waits for them, and re-layouts  8.04 us (24%)
  waiting for transfers between devices  6.74 us (20%)
  other arithmetic  5.27 us (15%)
  matrix products  4.88 us (14%)
  between operations  0.69 us (2%)
    ppermute x3, waiting for transfers between devices, exchange(): rows = lax.ppermute(rows, tuple(axes), pairs)  6.46 us
    ppermute x2, starting transfers between devices, shifted(): lax.ppermute(block, axis, [(i, (i + step) % count) for i in range(count)])  4.61 us
    ppermute x3, starting transfers between devices, exchange(): rows = lax.ppermute(rows, tuple(axes), pairs)  3.64 us
    unnamed x27, local copies, waits for them, and re-layouts  2.14 us
    dot_general x3, matrix products, planar_part(): jnp.dot(jnp.asarray(plane_map, jnp.float32), signed, precision=lax.Precis...  1.97 us
    mul x1, other arithmetic, plane_round_and_stencil(): return 0.25 * result  1.63 us
    dot_general x3, matrix products, body(): lax.dot_general(arrived[comp], place, (((0,), (0,)), ((), ())), precision...  1.29 us
    dot_general x3, matrix products, body(): jnp.dot(planar, jnp.asarray(depth.T, jnp.float32), precision=lax.Precisio...  1.1 us
  transfers between devices with their start and end apart: 5, of which 2 were waited for; matrix products, arithmetic and copies ran while one was open for 10% of the time, Pallas kernels for 0%

profile of v15, /device:TPU:0, one launch (start us, length us, event | category | flops | bytes accessed | tf_op | source)
XLA Modules:
  0.0 33.9 jit_solution(7621953941434620881)
XLA Ops:
  0.0 1.0 %subtract_convert_fusion = f32[8,32,128]{2,1,0:T(8,128)S(1)} fusion(s32[8,32,128]{2,1,0:T(8,128)} %param.19), kind=kLoop, calls=%fused_computation.36 | loop fusion | flops 65536 | bytes 262144 | tf_op jit(solution)/shard_map/convert_element_type | solution.py:300
  1.2 0.1 copy.61
  1.6 0.7 %convert_bitcast_fusion.2 = (f32[2,8,32]{2,1,0:T(8,128)S(1)}, f32[2,8,32]{2,1,0:T(8,128)S(1)}, f32[2,8,32]{2,1,0:T(8,128)S(1)}) fusion(s32[3,2,8,32]{3,2,1,0:T(8,128)} %param.18), kind=kLoop, calls=%fused_computation.81 | loop fusion | flops 4608 | bytes 12288 | tf_op jit(solution)/shard_map/convert_element_type | solution.py:44
  2.4 0.1 broadcast_in_dim.12
  2.5 0.2 mul.135
  2.7 0.1 copy.56
  3.0 0.1 broadcast_in_dim.13
  3.1 0.2 mul.139
  3.3 0.4 %copy-done.6 = f32[2,5,8,4,160]{4,3,2,1,0:T(4,128)S(1)} copy-done((f32[2,5,8,4,160]{4,3,2,1,0:T(4,128)S(1)}, f32[2,5,8,4,160]{4,3,2,1,0:T(4,128)}, u32[]{:S(2)}) %copy-start.6) | copy-done | bytes 204824
  3.9 0.8 %fusion.37 = f32[160,324]{1,0:T(8,128)S(1)} fusion(f32[320,160]{1,0:T(8,128)S(1)} %reshape.101, f32[324,320]{1,0:T(8,128)S(1)} %copy-done.4), kind=kOutput, calls=%fused_computation.88 | convolution fusion | flops 99532800 | bytes 826880 | tf_op jit(solution)/shard_map/dot_general | solution.py:48
  4.7 0.2 convolution_bitcast_fusion.2
  4.9 0.8 %fusion.39 = f32[160,324]{1,0:T(8,128)S(1)} fusion(f32[320,160]{1,0:T(8,128)S(1)} %reshape.102, f32[324,320]{1,0:T(8,128)S(1)} %copy-done.3), kind=kOutput, calls=%fused_computation.90 | convolution fusion | flops 99532800 | bytes 826880 | tf_op jit(solution)/shard_map/dot_general | solution.py:48
  5.7 0.2 convolution_bitcast_fusion.1
  6.2 0.4 %fusion.41 = f32[128,324]{0,1:T(8,128)S(1)} fusion(f32[400,128]{1,0:T(8,128)S(1)} %reshape.103, f32[324,400]{1,0:T(8,128)S(1)} %copy-done.1), kind=kOutput, calls=%fused_computation.92 | convolution fusion | flops 99532800 | bytes 889088 | tf_op jit(solution)/shard_map/dot_general | solution.py:48
  6.6 0.2 convolution_bitcast_fusion
  6.9 0.5 %collective-permute-start = (f32[12,324]{1,0:T(8,128)S(1)}, f32[12,324]{1,0:T(8,128)S(1)}, u32[]{:S(2)}, u32[]{:S(2)}) collective-permute-start(f32[12,324]{1,0:T(8,128)S(1)} %reshape.104), channel_id=1, source_target_pairs={{0,1},{1,2},{2,3},{3,4},{4,5},{5,6},{6,7},{7,0},{8,9},{9,10},{10,1... | collective-permute-start | bytes 46664 | tf_op jit(solution)/shard_map/ppermute | solution.py:59
  7.4 4.1 %collective-permute-start.1 = (f32[8,324]{1,0:T(8,128)S(1)}, f32[8,324]{1,0:T(8,128)S(1)}, u32[]{:S(2)}, u32[]{:S(2)}) collective-permute-start(f32[8,324]{1,0:T(8,128)S(1)} %reshape.106), channel_id=1, source_target_pairs={{0,7},{1,0},{2,1},{3,2},{4,3},{5,4},{6,5},{7,6},{8,15},{9,8},{10,9... | collective-permute-start | bytes 31112 | tf_op jit(solution)/shard_map/ppermute | solution.py:59
  11.5 0.4 %fusion.38 = f32[324,132]{0,1:T(8,128)S(1)} fusion(f32[160,324]{1,0:T(8,128)S(1)} %fusion.37, f32[160,132]{1,0:T(8,128)S(1)} %copy-done.2), kind=kOutput, calls=%fused_computation.89 | convolution fusion | flops 41057280 | bytes 462912 | tf_op jit(solution)/shard_map/dot_general | solution.py:315
  11.9 0.4 %fusion.40 = f32[324,132]{0,1:T(8,128)S(1)} fusion(f32[160,324]{1,0:T(8,128)S(1)} %fusion.39, f32[160,132]{1,0:T(8,128)S(1)} %copy-done.2), kind=kOutput, calls=%fused_computation.91 | convolution fusion | flops 41057280 | bytes 462912 | tf_op jit(solution)/shard_map/dot_general | solution.py:315
  12.3 0.3 fusion.42
  12.7 0.3 collective-permute-done.1
  13.0 0.4 %convolution_add_fusion.2 = f32[324,132]{0,1:T(8,128)S(1)} fusion(f32[324,132]{0,1:T(8,128)S(1)} %fusion.38, f32[5,132]{1,0:T(8,128)S(1)} %copy-done.9, f32[4,3,324]{2,1,0:T(4,128)S(1)} %reshape.105, f32[4,2,324]{2,1,0:T(2,128)S(1)} %reshape.107), kind=kOutput, calls=%fused_computation.5 | convolution fusion | flops 2610468 | bytes 370704 | tf_op jit(solution)/shard_map/dot_general | solution.py:328
  13.4 0.1 copy.62
  13.6 0.8 %constant_dynamic-update-slice_fusion.2 = f32[3,9,36,132]{3,2,1,0:T(8,128)} fusion(f32[1,9,36,132]{3,2,1,0:T(8,128)S(1)} %stack_reshape.13), kind=kLoop, calls=%fused_computation.77 | loop fusion | bytes 539712
  14.4 0.4 %convolution_add_fusion.1 = f32[324,132]{0,1:T(8,128)S(1)} fusion(f32[324,132]{0,1:T(8,128)S(1)} %fusion.40, f32[5,132]{1,0:T(8,128)S(1)} %copy-done.9, f32[4,3,324]{2,1,0:T(4,128)S(1)} %reshape.105, f32[4,2,324]{2,1,0:T(2,128)S(1)} %reshape.107), kind=kOutput, calls=%fused_computation.4 | convolution fusion | flops 2610468 | bytes 370704 | tf_op jit(solution)/shard_map/dot_general | solution.py:328
  14.8 0.1 copy.63
  15.0 0.4 %convolution_add_fusion = f32[324,132]{0,1:T(8,128)S(1)} fusion(f32[324,132]{0,1:T(8,128)S(1)} %fusion.42, f32[5,132]{1,0:T(8,128)S(1)} %copy-done.9, f32[4,3,324]{2,1,0:T(4,128)S(1)} %reshape.105, f32[4,2,324]{2,1,0:T(2,128)S(1)} %reshape.107), kind=kOutput, calls=%fused_computation.3 | convolution fusion | flops 2610468 | bytes 370704 | tf_op jit(solution)/shard_map/dot_general | solution.py:328
  15.5 0.1 copy.64
  15.7 0.2 copy.65
  16.0 0.2 add_bitcast_fusion
  16.3 0.1 pad_maximum_fusion
  16.4 0.1 fusion.34
  16.7 0.8 %copy-done = f32[3,9,36,132]{3,2,1,0:T(8,128)S(1)} copy-done((f32[3,9,36,132]{3,2,1,0:T(8,128)S(1)}, f32[3,9,36,132]{3,2,1,0:T(8,128)}, u32[]{:S(2)}) %copy-start) | copy-done | bytes 513240
  17.7 0.1 reshape.109
  17.8 0.9 %concatenate.25 = f32[78604]{0:T(1024)S(1)} concatenate(f32[32768]{0:T(1024)S(1)} %bitcast.90, f32[13068]{0:T(1024)S(1)} %reshape.109, f32[32768]{0:T(1024)S(1)} %bitcast.89), dimensions={0} | concatenate | bytes 628832 | tf_op jit(solution)/shard_map/concatenate | solution.py:198
  18.8 2.0 %collective-permute-start.2 = (f32[615,128]{1,0:T(8,128)S(1)}, f32[615,128]{1,0:T(8,128)S(1)}, u32[]{:S(2)}, u32[]{:S(2)}) collective-permute-start(f32[615,128]{1,0:T(8,128)S(1)} %pad_bitcast_fusion), channel_id=1, source_target_pairs={{0,16},{8,24},{16,0},{24,8},{1,17},{9,25},{17,1},{25,9},{2,18},{10... | collective-permute-start | bytes 944648 | tf_op jit(solution)/shard_map/ppermute | solution.py:207
  20.8 0.1 reshape.116
  21.0 0.1 reshape.117
  21.2 1.5 %collective-permute-start.3 = (f32[178,128]{1,0:T(8,128)S(1)}, f32[178,128]{1,0:T(8,128)S(1)}, u32[]{:S(2)}, u32[]{:S(2)}) collective-permute-start(f32[178,128]{1,0:T(8,128)S(1)} %fusion.13), channel_id=1, source_target_pairs={{0,8},{8,0},{16,24},{24,16},{1,9},{9,1},{17,25},{25,17},{2,10},{10... | collective-permute-start | bytes 273416 | tf_op jit(solution)/shard_map/ppermute | solution.py:207
  23.3 0.4 %fusion.10 = f32[3,7,31,128]{3,2,1,0:T(8,128)S(1)} fusion(f32[3,7,31,132]{3,2,1,0:T(8,128)S(1)} %slice_multiply_fusion.1), kind=kLoop, calls=%fused_computation.27 | loop fusion | flops 583296 | bytes 1999872 | tf_op jit(solution)/shard_map/add | solution.py:273
  23.7 6.5 %collective-permute-done.4 = f32[38,128]{1,0:T(8,128)S(1)} collective-permute-done((f32[38,128]{1,0:T(8,128)S(1)}, f32[38,128]{1,0:T(8,128)S(1)}, u32[]{:S(2)}, u32[]{:S(2)}) %collective-permute-start.4) | collective-permute-done | bytes 19488 | tf_op jit(solution)/shard_map/ppermute | solution.py:207
  30.8 0.2 reshape.120
  31.0 0.2 reshape.121
  31.3 0.1 reshape.114
  31.4 0.4 %pad_add_fusion = f32[4,12,36,132]{3,2,1,0:T(8,128)S(1)} fusion(f32[4,1,2,132]{3,2,1,0:T(2,128)S(1)} %bitcast.100, f32[4,2,1,132]{3,2,1,0:T(1,128)S(1)} %broadcast_in_dim_reshape.20, f32[4,1,2,132]{3,2,1,0:T(2,128)S(1)} %bitcast.99, f32[4,3,1,132]{3,2,1,0:T(1,128)S(1)} %broadcast_in_dim_reshape.19, f32[4,8,2,132]{3,2,1,0:T(2,128)S(1)} %reshape.121, ...), kind=kLoop, calls=%fused_computation | loop fusion | flops 2052864 | bytes 2020912 | tf_op jit(solution)/shard_map/add | solution.py:245
  31.8 0.1 slice_multiply_fusion
  32.1 0.2 fusion.28
  32.2 1.6 %fusion.2 = f32[3,8,32,128]{3,2,1,0:T(8,128)} fusion(f32[3,12,36,132]{3,2,1,0:T(8,128)S(1)} %slice_multiply_fusion, f32[3,7,31,128]{3,2,1,0:T(8,128)S(1)} %fusion.10, f32[3,7,1,128]{3,2,1,0:T(1,128)S(1)} %fusion.28, f32[3,1,32,128]{3,2,1,0:T(8,128)S(1)} %fusion.15), kind=kLoop, calls=%fused_computation.14 | loop fusion | flops 1474560 | bytes 3932160 | tf_op jit(solution)/shard_map/mul | solution.py:264
  (89 shorter events, 3.3 us)
Async XLA Ops:
  0.0 2.7 %copy-start.5 = (f32[2,4,8,5,160]{4,2,3,1,0:T(8,128)S(1)}, f32[2,4,8,5,160]{4,2,3,1,0:T(8,128)}, u32[]{:S(2)}) copy-start(f32[2,4,8,5,160]{4,2,3,1,0:T(8,128)} %param.15) | copy-start | bytes 614404
  2.7 1.0 %copy-start.6 = (f32[2,5,8,4,160]{4,3,2,1,0:T(4,128)S(1)}, f32[2,5,8,4,160]{4,3,2,1,0:T(4,128)}, u32[]{:S(2)}) copy-start(f32[2,5,8,4,160]{4,3,2,1,0:T(4,128)} %param.16) | copy-start | bytes 614404
  2.9 1.1 %copy-start.4 = (f32[324,320]{1,0:T(8,128)S(1)}, f32[324,320]{1,0:T(8,128)}, u32[]{:S(2)}) copy-start(f32[324,320]{1,0:T(8,128)} %constant.22.clone) | copy-start | bytes 1244164
  2.9 1.7 %copy-start.10 = (f32[5,160]{1,0:T(8,128)S(1)}, f32[5,160]{1,0:T(8,128)}, u32[]{:S(2)}) copy-start(f32[5,160]{1,0:T(8,128)} %constant.23.clone) | copy-start | bytes 9604
  3.1 1.8 %copy-start.3 = (f32[324,320]{1,0:T(8,128)S(1)}, f32[324,320]{1,0:T(8,128)}, u32[]{:S(2)}) copy-start(f32[324,320]{1,0:T(8,128)} %constant.24.clone) | copy-start | bytes 1244164
  3.9 2.1 %copy-start.7 = (f32[2,5,8,5,128]{4,2,3,1,0:T(8,128)S(1)}, f32[2,5,8,5,128]{4,2,3,1,0:T(8,128)}, u32[]{:S(2)}) copy-start(f32[2,5,8,5,128]{4,2,3,1,0:T(8,128)} %param.17) | copy-start | bytes 614404
  4.9 1.3 %copy-start.1 = (f32[324,400]{1,0:T(8,128)S(1)}, f32[324,400]{1,0:T(8,128)}, u32[]{:S(2)}) copy-start(f32[324,400]{1,0:T(8,128)} %constant.9.clone) | copy-start | bytes 1555204
  5.8 0.8 %copy-start.11 = (f32[5,128]{1,0:T(8,128)S(1)}, f32[5,128]{1,0:T(8,128)}, u32[]{:S(2)}) copy-start(f32[5,128]{1,0:T(8,128)} %constant.10.clone) | copy-start | bytes 7684
  6.0 5.5 %copy-start.2 = (f32[160,132]{1,0:T(8,128)S(1)}, f32[160,132]{1,0:T(8,128)}, u32[]{:S(2)}) copy-start(f32[160,132]{1,0:T(8,128)} %constant.11.clone) | copy-start | bytes 253444
  6.2 6.1 %copy-start.8 = (f32[128,132]{1,0:T(8,128)S(1)}, f32[128,132]{1,0:T(8,128)}, u32[]{:S(2)}) copy-start(f32[128,132]{1,0:T(8,128)} %constant.12.clone) | copy-start | bytes 202756
  6.2 6.8 %copy-start.9 = (f32[5,132]{1,0:T(8,128)S(1)}, f32[5,132]{1,0:T(8,128)}, u32[]{:S(2)}) copy-start(f32[5,132]{1,0:T(8,128)} %constant.13.clone) | copy-start | bytes 7924
  6.9 6.1 %collective-permute-start = (f32[12,324]{1,0:T(8,128)S(1)}, f32[12,324]{1,0:T(8,128)S(1)}, u32[]{:S(2)}, u32[]{:S(2)}) collective-permute-start(f32[12,324]{1,0:T(8,128)S(1)} %reshape.104), channel_id=1, source_target_pairs={{0,1},{1,2},{2,3},{3,4},{4,5},{5,6},{6,7},{7,0},{8,9},{9,10},{10,1... | collective-permute-start | bytes 46664 | tf_op jit(solution)/shard_map/ppermute | solution.py:59
  7.4 5.5 %collective-permute-start.1 = (f32[8,324]{1,0:T(8,128)S(1)}, f32[8,324]{1,0:T(8,128)S(1)}, u32[]{:S(2)}, u32[]{:S(2)}) collective-permute-start(f32[8,324]{1,0:T(8,128)S(1)} %reshape.106), channel_id=1, source_target_pairs={{0,7},{1,0},{2,1},{3,2},{4,3},{5,4},{6,5},{7,6},{8,15},{9,8},{10,9... | collective-permute-start | bytes 31112 | tf_op jit(solution)/shard_map/ppermute | solution.py:59
  16.3 1.2 %copy-start = (f32[3,9,36,132]{3,2,1,0:T(8,128)S(1)}, f32[3,9,36,132]{3,2,1,0:T(8,128)}, u32[]{:S(2)}) copy-start(f32[3,9,36,132]{3,2,1,0:T(8,128)} %constant_dynamic-update-slice_fusion.2) | copy-start | bytes 1539652
  18.8 12.3 %collective-permute-start.2 = (f32[615,128]{1,0:T(8,128)S(1)}, f32[615,128]{1,0:T(8,128)S(1)}, u32[]{:S(2)}, u32[]{:S(2)}) collective-permute-start(f32[615,128]{1,0:T(8,128)S(1)} %pad_bitcast_fusion), channel_id=1, source_target_pairs={{0,16},{8,24},{16,0},{24,8},{1,17},{9,25},{17,1},{25,9},{2,18},{10... | collective-permute-start | bytes 944648 | tf_op jit(solution)/shard_map/ppermute | solution.py:207
  21.2 9.4 %collective-permute-start.3 = (f32[178,128]{1,0:T(8,128)S(1)}, f32[178,128]{1,0:T(8,128)S(1)}, u32[]{:S(2)}, u32[]{:S(2)}) collective-permute-start(f32[178,128]{1,0:T(8,128)S(1)} %fusion.13), channel_id=1, source_target_pairs={{0,8},{8,0},{16,24},{24,16},{1,9},{9,1},{17,25},{25,17},{2,10},{10... | collective-permute-start | bytes 273416 | tf_op jit(solution)/shard_map/ppermute | solution.py:207
  23.2 7.0 %collective-permute-start.4 = (f32[38,128]{1,0:T(8,128)S(1)}, f32[38,128]{1,0:T(8,128)S(1)}, u32[]{:S(2)}, u32[]{:S(2)}) collective-permute-start(f32[38,128]{1,0:T(8,128)S(1)} %pad_bitcast_fusion.1), channel_id=1, source_target_pairs={{0,24},{8,16},{16,8},{24,0},{1,25},{9,17},{17,9},{25,1},{2,26},{10... | collective-permute-start | bytes 58376 | tf_op jit(solution)/shard_map/ppermute | solution.py:207

commit v16 on v15

--- a/solution.py
+++ b/solution.py
@@ -224,8 +224,16 @@
 def plane_round_and_stencil(extended, nx, ny):
     e = extended
     payloads = {
-        (1, 0): (e[:, nx - 2 : nx, 2 : ny + 2, 2:-2], e[:-1, nx : nx + 1, 2 : ny + 3]),
-        (-1, 0): (e[:, 0:2, 2 : ny + 2, 2:-2],),
+        (1, 0): (
+            e[:-1, nx - 2 : nx, 2 : ny + 2, 2:-2] * e[-1, nx - 2 : nx, 2 : ny + 2, 2:-2],
+            e[-1:, nx - 2 : nx, 2:3, 2:-2],
+            e[:-1, nx : nx + 1, 2 : ny + 3],
+        ),
+        (-1, 0): (
+            e[:, 0:1, 2 : ny + 2, 2:-2],
+            e[:-1, 1:2, 2 : ny + 2, 2:-2] * e[-1, 1:2, 2 : ny + 2, 2:-2],
+            e[-1:, 1:2, 2:3, 2:-2],
+        ),
         (0, 1): (e[:, :, ny : ny + 3],),
         (0, -1): (e[:, 0:nx, 2:4],),
         (1, 1): (e[:, nx - 2 : nx + 1, ny + 2], e[:, nx, ny : ny + 2]),
@@ -239,13 +247,17 @@
     def at(block, layer, row, col=0):
         return placed(block, (0, layer, row, col), shape)
 
-    halo_x, fold_x = got[(1, 0)]
+    halo_x, halo_keep, fold_x = got[(1, 0)]
+    bottom, next_halo, next_keep = got[(-1, 0)]
     corner_x, corner_y = got[(1, 1)]
+    data_shape = (channels - 1,) + shape[1:]
+    premasked = placed(halo_x, (0, 0, 2, 2), data_shape) + placed(next_halo, (0, nx + 3, 2, 2), data_shape)
     total = (
         at(e, 2, 0)
-        + at(halo_x, 0, 2, 2)
+        + placed(halo_keep, (channels - 1, 0, 2, 2), shape)
+        + placed(next_keep, (channels - 1, nx + 3, 2, 2), shape)
         + at(fold_x, 2, 2)
-        + at(got[(-1, 0)][0], nx + 2, 2, 2)
+        + at(bottom, nx + 2, 2, 2)
         + at(got[(0, 1)][0], 2, 0)
         + at(got[(0, -1)][0], 2, ny + 2)
         + at(corner_x[:, :, None], 0, 2)
@@ -253,7 +265,7 @@
         + at(got[(-1, 1)][0][:, :, None], nx + 2, 2)
         + at(got[(1, -1)][0][:, None], 2, ny + 2)
     )
-    masked = total[:-1] * total[-1]
+    masked = total[:-1] * total[-1] + premasked
     inner = z_terms(e[:-1, 1:nx, 3 : ny + 2] * e[-1, 1:nx, 3 : ny + 2])
     rows = jnp.concatenate([z_terms(masked[:, 3 : nx + 2, 2:3]), inner], axis=2)
     result = jnp.concatenate([z_terms(masked[:, 2:3, 2 : ny + 2]), rows], axis=1)

time: 34.1 us -> 36.8 us (1.079)
  local copies, waits for them, and re-layouts: 8.04 us -> 11.5 us
  waiting for transfers between devices: 6.74 us -> 5.75 us
    ppermute x3, waiting for transfers between devices: 6.46 us -> 5.48 us  [exchange(): rows = lax.ppermute(rows, tuple(axes), pairs)]
    concatenate x2, local copies, waits for them, and re-layouts: 0.99 us -> 1.81 us  [exchange(): flat = jnp.concatenate([part.reshape(-1) for part in parts])]
    unnamed x27 -> x39, local copies, waits for them, and re-layouts: 2.14 us -> 1.45 us
    reshape x7 -> x8, local copies, waits for them, and re-layouts: 0.76 us -> 1.41 us  [exchange(): flat = jnp.concatenate([part.reshape(-1) for part in parts])]
    slice x1, local copies, waits for them, and re-layouts: 0.03 us -> 0.66 us  [plane_round_and_stencil(): e[:, 0:nx, 2:4]]
    squeeze x1, local copies, waits for them, and re-layouts: 0.01 us -> 0.61 us  [plane_round_and_stencil(): e[:, nx, 2:4]]
    slice x2, local copies, waits for them, and re-layouts: 0.02 us -> 0.61 us  [plane_round_and_stencil(): e[:, nx - 2:nx + 1, ny + 2]]
    slice x1 -> x2, local copies, waits for them, and re-layouts: 0.13 us -> 0.72 us  [the longest x1 0.64 us: plane_round_and_stencil(): e[-1:, nx - 2:nx, 2:3, 2:-2]]
  transfers between devices with their start and end apart: 5 -> 5, of which waited for: 2 -> 2; matrix products, arithmetic and copies ran while one was open for 10% -> 9% of each run, Pallas kernels for 0% -> 0%
where the time goes in v16:
time: 36.8 us; the launch traced here: 36.6 us
  local copies, waits for them, and re-layouts  11.5 us (31%)
  starting transfers between devices  8.25 us (22%)
  waiting for transfers between devices  5.75 us (16%)
  other arithmetic  5.45 us (15%)
  matrix products  4.88 us (13%)
  between operations  0.75 us (2%)
    ppermute x3, waiting for transfers between devices, exchange(): rows = lax.ppermute(rows, tuple(axes), pairs)  5.48 us
    ppermute x2, starting transfers between devices, shifted(): lax.ppermute(block, axis, [(i, (i + step) % count) for i in range(count)])  4.61 us
    ppermute x3, starting transfers between devices, exchange(): rows = lax.ppermute(rows, tuple(axes), pairs)  3.64 us
    dot_general x3, matrix products, planar_part(): jnp.dot(jnp.asarray(plane_map, jnp.float32), signed, precision=lax.Precis...  1.97 us
    concatenate x2, local copies, waits for them, and re-layouts, exchange(): flat = jnp.concatenate([part.reshape(-1) for part in parts])  1.81 us
    mul x1, other arithmetic, plane_round_and_stencil(): return 0.25 * result  1.63 us
    unnamed x39, local copies, waits for them, and re-layouts  1.45 us
    reshape x8, local copies, waits for them, and re-layouts, exchange(): flat = jnp.concatenate([part.reshape(-1) for part in parts])  1.41 us
  transfers between devices with their start and end apart: 5, of which 2 were waited for; matrix products, arithmetic and copies ran while one was open for 9% of the time, Pallas kernels for 0%

profile of v16, /device:TPU:0, one launch (start us, length us, event | category | flops | bytes accessed | tf_op | source)
XLA Modules:
  0.0 36.6 jit_solution(13701289490493379762)
XLA Ops:
  0.0 1.0 %subtract_convert_fusion = f32[8,32,128]{2,1,0:T(8,128)S(1)} fusion(s32[8,32,128]{2,1,0:T(8,128)} %param.19), kind=kLoop, calls=%fused_computation.37 | loop fusion | flops 65536 | bytes 262144 | tf_op jit(solution)/shard_map/convert_element_type | solution.py:312
  1.6 0.7 %convert_bitcast_fusion = (f32[2,8,32]{2,1,0:T(8,128)S(1)}, f32[2,8,32]{2,1,0:T(8,128)S(1)}, f32[2,8,32]{2,1,0:T(8,128)S(1)}) fusion(s32[3,2,8,32]{3,2,1,0:T(8,128)} %param.18), kind=kLoop, calls=%fused_computation.84 | loop fusion | flops 4608 | bytes 12288 | tf_op jit(solution)/shard_map/convert_element_type | solution.py:44
  2.5 0.2 mul.155
  2.7 0.1 copy.37
  3.1 0.2 mul.159
  3.3 0.4 %copy-done.6 = f32[2,5,8,4,160]{4,3,2,1,0:T(4,128)S(1)} copy-done((f32[2,5,8,4,160]{4,3,2,1,0:T(4,128)S(1)}, f32[2,5,8,4,160]{4,3,2,1,0:T(4,128)}, u32[]{:S(2)}) %copy-start.6) | copy-done | bytes 204824
  3.9 0.8 %fusion.37 = f32[160,324]{1,0:T(8,128)S(1)} fusion(f32[320,160]{1,0:T(8,128)S(1)} %reshape.123, f32[324,320]{1,0:T(8,128)S(1)} %copy-done.4), kind=kOutput, calls=%fused_computation.94 | convolution fusion | flops 99532800 | bytes 826880 | tf_op jit(solution)/shard_map/dot_general | solution.py:48
  4.7 0.2 convolution_bitcast_fusion.2
  4.9 0.8 %fusion.39 = f32[160,324]{1,0:T(8,128)S(1)} fusion(f32[320,160]{1,0:T(8,128)S(1)} %reshape.124, f32[324,320]{1,0:T(8,128)S(1)} %copy-done.3), kind=kOutput, calls=%fused_computation.96 | convolution fusion | flops 99532800 | bytes 826880 | tf_op jit(solution)/shard_map/dot_general | solution.py:48
  5.7 0.2 convolution_bitcast_fusion.1
  6.2 0.4 %fusion.41 = f32[128,324]{0,1:T(8,128)S(1)} fusion(f32[400,128]{1,0:T(8,128)S(1)} %reshape.125, f32[324,400]{1,0:T(8,128)S(1)} %copy-done.1), kind=kOutput, calls=%fused_computation.98 | convolution fusion | flops 99532800 | bytes 889088 | tf_op jit(solution)/shard_map/dot_general | solution.py:48
  6.6 0.2 convolution_bitcast_fusion
  6.9 0.5 %collective-permute-start = (f32[12,324]{1,0:T(8,128)S(1)}, f32[12,324]{1,0:T(8,128)S(1)}, u32[]{:S(2)}, u32[]{:S(2)}) collective-permute-start(f32[12,324]{1,0:T(8,128)S(1)} %reshape.126), channel_id=1, source_target_pairs={{0,1},{1,2},{2,3},{3,4},{4,5},{5,6},{6,7},{7,0},{8,9},{9,10},{10,1... | collective-permute-start | bytes 46664 | tf_op jit(solution)/shard_map/ppermute | solution.py:59
  7.4 4.1 %collective-permute-start.1 = (f32[8,324]{1,0:T(8,128)S(1)}, f32[8,324]{1,0:T(8,128)S(1)}, u32[]{:S(2)}, u32[]{:S(2)}) collective-permute-start(f32[8,324]{1,0:T(8,128)S(1)} %reshape.128), channel_id=1, source_target_pairs={{0,7},{1,0},{2,1},{3,2},{4,3},{5,4},{6,5},{7,6},{8,15},{9,8},{10,9... | collective-permute-start | bytes 31112 | tf_op jit(solution)/shard_map/ppermute | solution.py:59
  11.5 0.4 %fusion.38 = f32[324,132]{0,1:T(8,128)S(1)} fusion(f32[160,324]{1,0:T(8,128)S(1)} %fusion.37, f32[160,132]{1,0:T(8,128)S(1)} %copy-done.2), kind=kOutput, calls=%fused_computation.95 | convolution fusion | flops 41057280 | bytes 462912 | tf_op jit(solution)/shard_map/dot_general | solution.py:327
  11.9 0.4 %fusion.40 = f32[324,132]{0,1:T(8,128)S(1)} fusion(f32[160,324]{1,0:T(8,128)S(1)} %fusion.39, f32[160,132]{1,0:T(8,128)S(1)} %copy-done.2), kind=kOutput, calls=%fused_computation.97 | convolution fusion | flops 41057280 | bytes 462912 | tf_op jit(solution)/shard_map/dot_general | solution.py:327
  12.3 0.3 fusion.42
  12.7 0.3 collective-permute-done.1
  13.1 0.2 copy.46
  13.3 0.2 add_bitcast_fusion
  13.7 0.6 %slice.295 = f32[1,2,1,128]{3,2,1,0:T(1,128)} slice(f32[1,9,36,132]{3,2,1,0:T(8,128)S(1)} %add_bitcast_fusion), slice={[0:1], [6:8], [2:3], [2:130]} | slice | bytes 2048 | tf_op jit(solution)/shard_map/slice | solution.py:229
  14.4 0.6 %slice_bitcast_fusion.7 = f32[128]{0:T(128)} fusion(f32[1,9,36,132]{3,2,1,0:T(8,128)S(1)} %add_bitcast_fusion), kind=kLoop, calls=%fused_computation.88 | loop fusion | bytes 1024 | tf_op jit(solution)/shard_map/reshape | solution.py:198
  15.0 0.4 %convolution_add_fusion.1 = f32[324,132]{0,1:T(8,128)S(1)} fusion(f32[324,132]{0,1:T(8,128)S(1)} %fusion.40, f32[5,132]{1,0:T(8,128)S(1)} %copy-done.10, f32[4,3,324]{2,1,0:T(4,128)S(1)} %reshape.127, f32[4,2,324]{2,1,0:T(2,128)S(1)} %reshape.129), kind=kOutput, calls=%fused_computation.5 | convolution fusion | flops 2610468 | bytes 370704 | tf_op jit(solution)/shard_map/dot_general | solution.py:340
  15.4 0.1 copy.44
  15.6 0.4 %convolution_add_fusion.2 = f32[324,132]{0,1:T(8,128)S(1)} fusion(f32[324,132]{0,1:T(8,128)S(1)} %fusion.38, f32[5,132]{1,0:T(8,128)S(1)} %copy-done.10, f32[4,3,324]{2,1,0:T(4,128)S(1)} %reshape.127, f32[4,2,324]{2,1,0:T(2,128)S(1)} %reshape.129), kind=kOutput, calls=%fused_computation.6 | convolution fusion | flops 2610468 | bytes 370704 | tf_op jit(solution)/shard_map/dot_general | solution.py:340
  16.1 0.1 copy.43
  16.3 0.8 %constant_dynamic-update-slice_fusion.2 = f32[3,9,36,132]{3,2,1,0:T(8,128)} fusion(f32[1,9,36,132]{3,2,1,0:T(8,128)S(1)} %stack_reshape.13), kind=kLoop, calls=%fused_computation.82 | loop fusion | bytes 539712
  17.0 0.4 %convolution_add_fusion = f32[324,132]{0,1:T(8,128)S(1)} fusion(f32[324,132]{0,1:T(8,128)S(1)} %fusion.42, f32[5,132]{1,0:T(8,128)S(1)} %copy-done.10, f32[4,3,324]{2,1,0:T(4,128)S(1)} %reshape.127, f32[4,2,324]{2,1,0:T(2,128)S(1)} %reshape.129), kind=kOutput, calls=%fused_computation.4 | convolution fusion | flops 2610468 | bytes 370704 | tf_op jit(solution)/shard_map/dot_general | solution.py:340
  17.5 0.1 copy.45
  17.7 0.1 pad_maximum_fusion
  17.9 0.7 %slice.306 = f32[4,8,2,132]{3,2,1,0:T(2,128)} slice(f32[4,9,36,132]{3,2,1,0:T(8,128)S(1)} %pad_maximum_fusion), slice={[0:4], [0:8], [2:4], [0:132]} | slice | bytes 67584 | tf_op jit(solution)/shard_map/slice | solution.py:238
  18.6 0.6 %slice.309 = f32[4,3,1,132]{3,2,1,0:T(1,128)} slice(f32[4,9,36,132]{3,2,1,0:T(8,128)S(1)} %pad_maximum_fusion), slice={[0:4], [6:9], [34:35], [0:132]} | slice | bytes 12672 | tf_op jit(solution)/shard_map/slice | solution.py:239
  19.2 0.6 %slice_bitcast_fusion.4 = (f32[4,2,132]{2,1,0:T(2,128)}, f32[4,2,132]{2,1,0:T(2,128)}) fusion(f32[4,9,36,132]{3,2,1,0:T(8,128)S(1)} %pad_maximum_fusion), kind=kLoop, calls=%fused_computation.78 | loop fusion | bytes 16896 | tf_op jit(solution)/shard_map/squeeze | solution.py:241
  20.3 0.1 reshape.132
  20.6 1.7 %concatenate.27 = f32[66700]{0:T(1024)S(1)} concatenate(f32[24576]{0:T(1024)S(1)} %bitcast.99, f32[256]{0:T(256)S(1)} %bitcast.114, f32[13068]{0:T(1024)S(1)} %reshape.132, f32[16384]{0:T(1024)S(1)} %bitcast.105, f32[12288]{0:T(1024)S(1)} %bitcast.107, f32[128]{0:T(128)S(1)} %copy-done.17), dimensions={0} | concatenate | bytes 533600 | tf_op jit(solution)/shard_map/concatenate | solution.py:198
  22.3 2.0 %collective-permute-start.2 = (f32[522,128]{1,0:T(8,128)S(1)}, f32[522,128]{1,0:T(8,128)S(1)}, u32[]{:S(2)}, u32[]{:S(2)}) collective-permute-start(f32[522,128]{1,0:T(8,128)S(1)} %pad_bitcast_fusion), channel_id=1, source_target_pairs={{0,16},{8,24},{16,0},{24,8},{1,17},{9,25},{17,1},{25,9},{2,18},{10... | collective-permute-start | bytes 801800 | tf_op jit(solution)/shard_map/ppermute | solution.py:207
  24.3 0.1 reshape.142
  24.5 0.1 reshape.143
  24.7 1.5 %collective-permute-start.3 = (f32[178,128]{1,0:T(8,128)S(1)}, f32[178,128]{1,0:T(8,128)S(1)}, u32[]{:S(2)}, u32[]{:S(2)}) collective-permute-start(f32[178,128]{1,0:T(8,128)S(1)} %fusion.14), channel_id=1, source_target_pairs={{0,8},{8,0},{16,24},{24,16},{1,9},{9,1},{17,25},{25,17},{2,10},{10... | collective-permute-start | bytes 273416 | tf_op jit(solution)/shard_map/ppermute | solution.py:207
  26.9 0.4 %fusion.11 = f32[3,7,31,128]{3,2,1,0:T(8,128)S(1)} fusion(f32[3,7,31,132]{3,2,1,0:T(8,128)S(1)} %slice_multiply_fusion.1), kind=kLoop, calls=%fused_computation.28 | loop fusion | flops 583296 | bytes 1999872 | tf_op jit(solution)/shard_map/add | solution.py:285
  27.3 5.5 %collective-permute-done.4 = f32[38,128]{1,0:T(8,128)S(1)} collective-permute-done((f32[38,128]{1,0:T(8,128)S(1)}, f32[38,128]{1,0:T(8,128)S(1)}, u32[]{:S(2)}, u32[]{:S(2)}) %collective-permute-start.4) | collective-permute-done | bytes 19488 | tf_op jit(solution)/shard_map/ppermute | solution.py:207
  33.3 0.2 reshape.146
  33.5 0.2 reshape.147
  33.9 0.1 reshape.140
  34.1 0.3 pad_add_fusion
  34.4 0.2 fusion
  34.8 0.2 fusion.29
  34.9 1.6 %fusion.3 = f32[3,8,32,128]{3,2,1,0:T(8,128)} fusion(f32[3,12,36,132]{3,2,1,0:T(8,128)S(1)} %fusion, f32[3,7,31,128]{3,2,1,0:T(8,128)S(1)} %fusion.11, f32[3,7,1,128]{3,2,1,0:T(1,128)S(1)} %fusion.29, f32[3,1,32,128]{3,2,1,0:T(8,128)S(1)} %fusion.16), kind=kLoop, calls=%fused_computation.15 | loop fusion | flops 1474560 | bytes 3932160 | tf_op jit(solution)/shard_map/mul | solution.py:276
  (110 shorter events, 4.3 us)
Async XLA Ops:
  0.0 2.7 %copy-start.5 = (f32[2,4,8,5,160]{4,2,3,1,0:T(8,128)S(1)}, f32[2,4,8,5,160]{4,2,3,1,0:T(8,128)}, u32[]{:S(2)}) copy-start(f32[2,4,8,5,160]{4,2,3,1,0:T(8,128)} %param.15) | copy-start | bytes 614404
  2.7 1.0 %copy-start.6 = (f32[2,5,8,4,160]{4,3,2,1,0:T(4,128)S(1)}, f32[2,5,8,4,160]{4,3,2,1,0:T(4,128)}, u32[]{:S(2)}) copy-start(f32[2,5,8,4,160]{4,3,2,1,0:T(4,128)} %param.16) | copy-start | bytes 614404
  2.9 1.1 %copy-start.4 = (f32[324,320]{1,0:T(8,128)S(1)}, f32[324,320]{1,0:T(8,128)}, u32[]{:S(2)}) copy-start(f32[324,320]{1,0:T(8,128)} %constant.22.clone) | copy-start | bytes 1244164
  2.9 1.7 %copy-start.12 = (f32[5,160]{1,0:T(8,128)S(1)}, f32[5,160]{1,0:T(8,128)}, u32[]{:S(2)}) copy-start(f32[5,160]{1,0:T(8,128)} %constant.23.clone) | copy-start | bytes 9604
  3.1 1.8 %copy-start.3 = (f32[324,320]{1,0:T(8,128)S(1)}, f32[324,320]{1,0:T(8,128)}, u32[]{:S(2)}) copy-start(f32[324,320]{1,0:T(8,128)} %constant.24.clone) | copy-start | bytes 1244164
  3.9 2.1 %copy-start.8 = (f32[2,5,8,5,128]{4,2,3,1,0:T(8,128)S(1)}, f32[2,5,8,5,128]{4,2,3,1,0:T(8,128)}, u32[]{:S(2)}) copy-start(f32[2,5,8,5,128]{4,2,3,1,0:T(8,128)} %param.17) | copy-start | bytes 614404
  4.9 1.3 %copy-start.1 = (f32[324,400]{1,0:T(8,128)S(1)}, f32[324,400]{1,0:T(8,128)}, u32[]{:S(2)}) copy-start(f32[324,400]{1,0:T(8,128)} %constant.9.clone) | copy-start | bytes 1555204
  5.8 0.8 %copy-start.16 = (f32[5,128]{1,0:T(8,128)S(1)}, f32[5,128]{1,0:T(8,128)}, u32[]{:S(2)}) copy-start(f32[5,128]{1,0:T(8,128)} %constant.10.clone) | copy-start | bytes 7684
  6.0 5.5 %copy-start.2 = (f32[160,132]{1,0:T(8,128)S(1)}, f32[160,132]{1,0:T(8,128)}, u32[]{:S(2)}) copy-start(f32[160,132]{1,0:T(8,128)} %constant.11.clone) | copy-start | bytes 253444
  6.2 6.1 %copy-start.9 = (f32[128,132]{1,0:T(8,128)S(1)}, f32[128,132]{1,0:T(8,128)}, u32[]{:S(2)}) copy-start(f32[128,132]{1,0:T(8,128)} %constant.12.clone) | copy-start | bytes 202756
  6.9 6.1 %collective-permute-start = (f32[12,324]{1,0:T(8,128)S(1)}, f32[12,324]{1,0:T(8,128)S(1)}, u32[]{:S(2)}, u32[]{:S(2)}) collective-permute-start(f32[12,324]{1,0:T(8,128)S(1)} %reshape.126), channel_id=1, source_target_pairs={{0,1},{1,2},{2,3},{3,4},{4,5},{5,6},{6,7},{7,0},{8,9},{9,10},{10,1... | collective-permute-start | bytes 46664 | tf_op jit(solution)/shard_map/ppermute | solution.py:59
  7.4 5.5 %collective-permute-start.1 = (f32[8,324]{1,0:T(8,128)S(1)}, f32[8,324]{1,0:T(8,128)S(1)}, u32[]{:S(2)}, u32[]{:S(2)}) collective-permute-start(f32[8,324]{1,0:T(8,128)S(1)} %reshape.128), channel_id=1, source_target_pairs={{0,7},{1,0},{2,1},{3,2},{4,3},{5,4},{6,5},{7,6},{8,15},{9,8},{10,9... | collective-permute-start | bytes 31112 | tf_op jit(solution)/shard_map/ppermute | solution.py:59
  12.3 2.7 %copy-start.10 = (f32[5,132]{1,0:T(8,128)S(1)}, f32[5,132]{1,0:T(8,128)}, u32[]{:S(2)}) copy-start(f32[5,132]{1,0:T(8,128)} %constant.13.clone) | copy-start | bytes 7924
  17.7 2.2 %copy-start = (f32[3,9,36,132]{3,2,1,0:T(8,128)S(1)}, f32[3,9,36,132]{3,2,1,0:T(8,128)}, u32[]{:S(2)}) copy-start(f32[3,9,36,132]{3,2,1,0:T(8,128)} %constant_dynamic-update-slice_fusion.2) | copy-start | bytes 1539652
  19.9 0.7 %copy-start.15 = (f32[1,2,1,128]{3,2,1,0:T(1,128)S(1)}, f32[1,2,1,128]{3,2,1,0:T(1,128)}, u32[]{:S(2)}) copy-start(f32[1,2,1,128]{3,2,1,0:T(1,128)} %slice.295) | copy-start | bytes 3076
  19.9 0.7 %copy-start.17 = (f32[128]{0:T(128)S(1)}, f32[128]{0:T(128)}, u32[]{:S(2)}) copy-start(f32[128]{0:T(128)} %slice_bitcast_fusion.7) | copy-start | bytes 1540
  20.1 4.4 %copy-start.7 = (f32[4,8,2,132]{3,2,1,0:T(2,128)S(1)}, f32[4,8,2,132]{3,2,1,0:T(2,128)}, u32[]{:S(2)}) copy-start(f32[4,8,2,132]{3,2,1,0:T(2,128)} %slice.306) | copy-start | bytes 101380
  20.1 6.2 %copy-start.11 = (f32[4,3,1,132]{3,2,1,0:T(1,128)S(1)}, f32[4,3,1,132]{3,2,1,0:T(1,128)}, u32[]{:S(2)}) copy-start(f32[4,3,1,132]{3,2,1,0:T(1,128)} %slice.309) | copy-start | bytes 19012
  20.1 6.3 %copy-start.14 = (f32[4,2,132]{2,1,0:T(2,128)S(1)}, f32[4,2,132]{2,1,0:T(2,128)}, u32[]{:S(2)}) copy-start(f32[4,2,132]{2,1,0:T(2,128)} %get-tuple-element.20) | copy-start | bytes 12676
  20.1 6.5 %copy-start.13 = (f32[4,2,132]{2,1,0:T(2,128)S(1)}, f32[4,2,132]{2,1,0:T(2,128)}, u32[]{:S(2)}) copy-start(f32[4,2,132]{2,1,0:T(2,128)} %get-tuple-element.22) | copy-start | bytes 12676
  22.3 11.4 %collective-permute-start.2 = (f32[522,128]{1,0:T(8,128)S(1)}, f32[522,128]{1,0:T(8,128)S(1)}, u32[]{:S(2)}, u32[]{:S(2)}) collective-permute-start(f32[522,128]{1,0:T(8,128)S(1)} %pad_bitcast_fusion), channel_id=1, source_target_pairs={{0,16},{8,24},{16,0},{24,8},{1,17},{9,25},{17,1},{25,9},{2,18},{10... | collective-permute-start | bytes 801800 | tf_op jit(solution)/shard_map/ppermute | solution.py:207
  24.7 8.5 %collective-permute-start.3 = (f32[178,128]{1,0:T(8,128)S(1)}, f32[178,128]{1,0:T(8,128)S(1)}, u32[]{:S(2)}, u32[]{:S(2)}) collective-permute-start(f32[178,128]{1,0:T(8,128)S(1)} %fusion.14), channel_id=1, source_target_pairs={{0,8},{8,0},{16,24},{24,16},{1,9},{9,1},{17,25},{25,17},{2,10},{10... | collective-permute-start | bytes 273416 | tf_op jit(solution)/shard_map/ppermute | solution.py:207
  26.8 6.0 %collective-permute-start.4 = (f32[38,128]{1,0:T(8,128)S(1)}, f32[38,128]{1,0:T(8,128)S(1)}, u32[]{:S(2)}, u32[]{:S(2)}) collective-permute-start(f32[38,128]{1,0:T(8,128)S(1)} %pad_bitcast_fusion.1), channel_id=1, source_target_pairs={{0,24},{8,16},{16,8},{24,0},{1,25},{9,17},{17,9},{25,1},{2,26},{10... | collective-permute-start | bytes 58376 | tf_op jit(solution)/shard_map/ppermute | solution.py:207

commit v17 on v15

--- a/solution.py
+++ b/solution.py
@@ -224,8 +224,8 @@
 def plane_round_and_stencil(extended, nx, ny):
     e = extended
     payloads = {
+        (-1, 0): (e[:, 0:2, 2 : ny + 2, 2:-2],),
         (1, 0): (e[:, nx - 2 : nx, 2 : ny + 2, 2:-2], e[:-1, nx : nx + 1, 2 : ny + 3]),
-        (-1, 0): (e[:, 0:2, 2 : ny + 2, 2:-2],),
         (0, 1): (e[:, :, ny : ny + 3],),
         (0, -1): (e[:, 0:nx, 2:4],),
         (1, 1): (e[:, nx - 2 : nx + 1, ny + 2], e[:, nx, ny : ny + 2]),

time: 34.1 us -> 35 us (1.026)
  local copies, waits for them, and re-layouts: 8.04 us -> 8.8 us
    slice x7 -> x6, local copies, waits for them, and re-layouts: 0.27 us -> 1.96 us  [exchange(): parts.append(flat[start:start + size].reshape(part.shape))]
    concatenate x2 -> x1, local copies, waits for them, and re-layouts: 0.99 us -> 0.08 us  [exchange(): flat = jnp.concatenate([part.reshape(-1) for part in parts])]
  transfers between devices with their start and end apart: 5 -> 5, of which waited for: 2 -> 2; matrix products, arithmetic and copies ran while one was open for 10% -> 9% of each run, Pallas kernels for 0% -> 0%
where the time goes in v17:
time: 35 us; the launch traced here: 34.7 us
  local copies, waits for them, and re-layouts  8.8 us (25%)
  starting transfers between devices  8.26 us (24%)
  waiting for transfers between devices  6.76 us (19%)
  other arithmetic  5.3 us (15%)
  matrix products  4.88 us (14%)
  between operations  0.67 us (2%)
    ppermute x3, waiting for transfers between devices, exchange(): rows = lax.ppermute(rows, tuple(axes), pairs)  6.49 us
    ppermute x2, starting transfers between devices, shifted(): lax.ppermute(block, axis, [(i, (i + step) % count) for i in range(count)])  4.61 us
    ppermute x3, starting transfers between devices, exchange(): rows = lax.ppermute(rows, tuple(axes), pairs)  3.64 us
    unnamed x27, local copies, waits for them, and re-layouts  2.15 us
    dot_general x3, matrix products, planar_part(): jnp.dot(jnp.asarray(plane_map, jnp.float32), signed, precision=lax.Precis...  1.97 us
    slice x6, local copies, waits for them, and re-layouts, exchange(): parts.append(flat[start:start + size].reshape(part.shape))  1.96 us
    mul x1, other arithmetic, plane_round_and_stencil(): return 0.25 * result  1.63 us
    dot_general x3, matrix products, body(): lax.dot_general(arrived[comp], place, (((0,), (0,)), ((), ())), precision...  1.29 us
  transfers between devices with their start and end apart: 5, of which 2 were waited for; matrix products, arithmetic and copies ran while one was open for 9% of the time, Pallas kernels for 0%

profile of v17, /device:TPU:0, one launch (start us, length us, event | category | flops | bytes accessed | tf_op | source)
XLA Modules:
  0.0 34.7 jit_solution(9102012852953402934)
XLA Ops:
  0.0 1.0 %subtract_convert_fusion = f32[8,32,128]{2,1,0:T(8,128)S(1)} fusion(s32[8,32,128]{2,1,0:T(8,128)} %param.19), kind=kLoop, calls=%fused_computation.39 | loop fusion | flops 65536 | bytes 262144 | tf_op jit(solution)/shard_map/convert_element_type | solution.py:300
  1.6 0.7 %convert_bitcast_fusion = (f32[2,8,32]{2,1,0:T(8,128)S(1)}, f32[2,8,32]{2,1,0:T(8,128)S(1)}, f32[2,8,32]{2,1,0:T(8,128)S(1)}) fusion(s32[3,2,8,32]{3,2,1,0:T(8,128)} %param.18), kind=kLoop, calls=%fused_computation.82 | loop fusion | flops 4608 | bytes 12288 | tf_op jit(solution)/shard_map/convert_element_type | solution.py:44
  2.4 0.1 broadcast_in_dim.12
  2.5 0.2 mul.135
  2.7 0.1 copy.56
  3.0 0.1 broadcast_in_dim.13
  3.1 0.2 mul.139
  3.3 0.4 %copy-done.6 = f32[2,5,8,4,160]{4,3,2,1,0:T(4,128)S(1)} copy-done((f32[2,5,8,4,160]{4,3,2,1,0:T(4,128)S(1)}, f32[2,5,8,4,160]{4,3,2,1,0:T(4,128)}, u32[]{:S(2)}) %copy-start.6) | copy-done | bytes 204824
  3.9 0.8 %fusion.39 = f32[160,324]{1,0:T(8,128)S(1)} fusion(f32[320,160]{1,0:T(8,128)S(1)} %reshape.103, f32[324,320]{1,0:T(8,128)S(1)} %copy-done.4), kind=kOutput, calls=%fused_computation.92 | convolution fusion | flops 99532800 | bytes 826880 | tf_op jit(solution)/shard_map/dot_general | solution.py:48
  4.7 0.2 convolution_bitcast_fusion.2
  4.9 0.8 %fusion.41 = f32[160,324]{1,0:T(8,128)S(1)} fusion(f32[320,160]{1,0:T(8,128)S(1)} %reshape.104, f32[324,320]{1,0:T(8,128)S(1)} %copy-done.3), kind=kOutput, calls=%fused_computation.94 | convolution fusion | flops 99532800 | bytes 826880 | tf_op jit(solution)/shard_map/dot_general | solution.py:48
  5.7 0.2 convolution_bitcast_fusion.1
  6.2 0.4 %fusion.43 = f32[128,324]{0,1:T(8,128)S(1)} fusion(f32[400,128]{1,0:T(8,128)S(1)} %reshape.105, f32[324,400]{1,0:T(8,128)S(1)} %copy-done.1), kind=kOutput, calls=%fused_computation.96 | convolution fusion | flops 99532800 | bytes 889088 | tf_op jit(solution)/shard_map/dot_general | solution.py:48
  6.6 0.2 convolution_bitcast_fusion
  6.9 0.5 %collective-permute-start = (f32[12,324]{1,0:T(8,128)S(1)}, f32[12,324]{1,0:T(8,128)S(1)}, u32[]{:S(2)}, u32[]{:S(2)}) collective-permute-start(f32[12,324]{1,0:T(8,128)S(1)} %reshape.106), channel_id=1, source_target_pairs={{0,1},{1,2},{2,3},{3,4},{4,5},{5,6},{6,7},{7,0},{8,9},{9,10},{10,1... | collective-permute-start | bytes 46664 | tf_op jit(solution)/shard_map/ppermute | solution.py:59
  7.4 4.1 %collective-permute-start.1 = (f32[8,324]{1,0:T(8,128)S(1)}, f32[8,324]{1,0:T(8,128)S(1)}, u32[]{:S(2)}, u32[]{:S(2)}) collective-permute-start(f32[8,324]{1,0:T(8,128)S(1)} %reshape.108), channel_id=1, source_target_pairs={{0,7},{1,0},{2,1},{3,2},{4,3},{5,4},{6,5},{7,6},{8,15},{9,8},{10,9... | collective-permute-start | bytes 31112 | tf_op jit(solution)/shard_map/ppermute | solution.py:59
  11.5 0.4 %fusion.40 = f32[324,132]{0,1:T(8,128)S(1)} fusion(f32[160,324]{1,0:T(8,128)S(1)} %fusion.39, f32[160,132]{1,0:T(8,128)S(1)} %copy-done.2), kind=kOutput, calls=%fused_computation.93 | convolution fusion | flops 41057280 | bytes 462912 | tf_op jit(solution)/shard_map/dot_general | solution.py:315
  11.9 0.4 %fusion.42 = f32[324,132]{0,1:T(8,128)S(1)} fusion(f32[160,324]{1,0:T(8,128)S(1)} %fusion.41, f32[160,132]{1,0:T(8,128)S(1)} %copy-done.2), kind=kOutput, calls=%fused_computation.95 | convolution fusion | flops 41057280 | bytes 462912 | tf_op jit(solution)/shard_map/dot_general | solution.py:315
  12.3 0.3 fusion.44
  12.7 0.3 collective-permute-done.1
  13.0 0.4 %convolution_add_fusion.1 = f32[324,132]{0,1:T(8,128)S(1)} fusion(f32[324,132]{0,1:T(8,128)S(1)} %fusion.42, f32[5,132]{1,0:T(8,128)S(1)} %copy-done.9, f32[4,3,324]{2,1,0:T(4,128)S(1)} %reshape.107, f32[4,2,324]{2,1,0:T(2,128)S(1)} %reshape.109), kind=kOutput, calls=%fused_computation.4 | convolution fusion | flops 2610468 | bytes 370704 | tf_op jit(solution)/shard_map/dot_general | solution.py:328
  13.4 0.1 copy.63
  13.6 0.4 %convolution_add_fusion.2 = f32[324,132]{0,1:T(8,128)S(1)} fusion(f32[324,132]{0,1:T(8,128)S(1)} %fusion.40, f32[5,132]{1,0:T(8,128)S(1)} %copy-done.9, f32[4,3,324]{2,1,0:T(4,128)S(1)} %reshape.107, f32[4,2,324]{2,1,0:T(2,128)S(1)} %reshape.109), kind=kOutput, calls=%fused_computation.5 | convolution fusion | flops 2610468 | bytes 370704 | tf_op jit(solution)/shard_map/dot_general | solution.py:328
  14.1 0.1 copy.62
  14.3 0.8 %constant_dynamic-update-slice_fusion.2 = f32[3,9,36,132]{3,2,1,0:T(8,128)} fusion(f32[1,9,36,132]{3,2,1,0:T(8,128)S(1)} %stack_reshape.13), kind=kLoop, calls=%fused_computation.80 | loop fusion | bytes 539712
  15.0 0.4 %convolution_add_fusion = f32[324,132]{0,1:T(8,128)S(1)} fusion(f32[324,132]{0,1:T(8,128)S(1)} %fusion.44, f32[5,132]{1,0:T(8,128)S(1)} %copy-done.9, f32[4,3,324]{2,1,0:T(4,128)S(1)} %reshape.107, f32[4,2,324]{2,1,0:T(2,128)S(1)} %reshape.109), kind=kOutput, calls=%fused_computation.3 | convolution fusion | flops 2610468 | bytes 370704 | tf_op jit(solution)/shard_map/dot_general | solution.py:328
  15.5 0.1 copy.64
  15.8 0.2 copy.65
  16.0 0.2 add_bitcast_fusion
  16.3 0.1 pad_maximum_fusion
  16.4 0.1 fusion.35
  16.7 0.8 %copy-done = f32[3,9,36,132]{3,2,1,0:T(8,128)S(1)} copy-done((f32[3,9,36,132]{3,2,1,0:T(8,128)S(1)}, f32[3,9,36,132]{3,2,1,0:T(8,128)}, u32[]{:S(2)}) %copy-start) | copy-done | bytes 513240
  17.7 0.1 reshape.112
  17.9 2.0 %collective-permute-start.2 = (f32[615,128]{1,0:T(8,128)S(1)}, f32[615,128]{1,0:T(8,128)}, u32[]{:S(2)}, u32[]{:S(2)}) collective-permute-start(f32[615,128]{1,0:T(8,128)S(1)} %fusion.13), channel_id=1, source_target_pairs={{0,16},{8,24},{16,0},{24,8},{1,17},{9,25},{17,1},{25,9},{2,18},{10... | collective-permute-start | bytes 944648 | tf_op jit(solution)/shard_map/ppermute | solution.py:207
  19.9 0.1 reshape.118
  20.1 0.1 reshape.119
  20.3 1.5 %collective-permute-start.3 = (f32[178,128]{1,0:T(8,128)S(1)}, f32[178,128]{1,0:T(8,128)S(1)}, u32[]{:S(2)}, u32[]{:S(2)}) collective-permute-start(f32[178,128]{1,0:T(8,128)S(1)} %fusion.14), channel_id=1, source_target_pairs={{0,8},{8,0},{16,24},{24,16},{1,9},{9,1},{17,25},{25,17},{2,10},{10... | collective-permute-start | bytes 273416 | tf_op jit(solution)/shard_map/ppermute | solution.py:207
  22.4 0.4 %fusion.10 = f32[3,7,31,128]{3,2,1,0:T(8,128)S(1)} fusion(f32[3,7,31,132]{3,2,1,0:T(8,128)S(1)} %slice_multiply_fusion.1), kind=kLoop, calls=%fused_computation.27 | loop fusion | flops 583296 | bytes 1999872 | tf_op jit(solution)/shard_map/add | solution.py:273
  22.8 6.5 %collective-permute-done.4 = f32[38,128]{1,0:T(8,128)S(1)} collective-permute-done((f32[38,128]{1,0:T(8,128)S(1)}, f32[38,128]{1,0:T(8,128)S(1)}, u32[]{:S(2)}, u32[]{:S(2)}) %collective-permute-start.4) | collective-permute-done | bytes 19488 | tf_op jit(solution)/shard_map/ppermute | solution.py:207
  29.9 0.2 reshape.122
  30.1 0.2 reshape.123
  30.3 0.8 %slice.263 = f32[13068]{0:T(1024)S(1)} slice(f32[78720]{0:T(1024)} %bitcast.17), slice={[65536:78604]} | slice | bytes 104544 | tf_op jit(solution)/shard_map/slice | solution.py:214
  31.1 0.1 reshape.116
  31.2 1.0 %fusion.36 = (f32[256,128]{1,0:T(8,128)S(1)}, f32[256,128]{1,0:T(8,128)S(1)}) fusion(f32[615,128]{1,0:T(8,128)} %collective-permute-done.2), kind=kLoop, calls=%fused_computation.89 | loop fusion | bytes 524288 | tf_op jit(solution)/shard_map/slice | solution.py:214
  32.2 0.4 %pad_add_fusion = f32[4,12,36,132]{3,2,1,0:T(8,128)S(1)} fusion(f32[4,1,2,132]{3,2,1,0:T(2,128)S(1)} %bitcast.98, f32[4,2,1,132]{3,2,1,0:T(1,128)S(1)} %broadcast_in_dim_reshape.20, f32[4,1,2,132]{3,2,1,0:T(2,128)S(1)} %bitcast.97, f32[4,3,1,132]{3,2,1,0:T(1,128)S(1)} %broadcast_in_dim_reshape.19, f32[4,8,2,132]{3,2,1,0:T(2,128)S(1)} %reshape.123, ...), kind=kLoop, calls=%fused_computation | loop fusion | flops 2052864 | bytes 2020912 | tf_op jit(solution)/shard_map/add | solution.py:245
  32.6 0.1 slice_multiply_fusion
  32.9 0.2 fusion.29
  33.0 1.6 %fusion.2 = f32[3,8,32,128]{3,2,1,0:T(8,128)} fusion(f32[3,12,36,132]{3,2,1,0:T(8,128)S(1)} %slice_multiply_fusion, f32[3,7,31,128]{3,2,1,0:T(8,128)S(1)} %fusion.10, f32[3,7,1,128]{3,2,1,0:T(1,128)S(1)} %fusion.29, f32[3,1,32,128]{3,2,1,0:T(8,128)S(1)} %fusion.16), kind=kLoop, calls=%fused_computation.14 | loop fusion | flops 1474560 | bytes 3932160 | tf_op jit(solution)/shard_map/mul | solution.py:264
  (87 shorter events, 3.3 us)
Async XLA Ops:
  0.0 2.7 %copy-start.5 = (f32[2,4,8,5,160]{4,2,3,1,0:T(8,128)S(1)}, f32[2,4,8,5,160]{4,2,3,1,0:T(8,128)}, u32[]{:S(2)}) copy-start(f32[2,4,8,5,160]{4,2,3,1,0:T(8,128)} %param.15) | copy-start | bytes 614404
  2.7 1.0 %copy-start.6 = (f32[2,5,8,4,160]{4,3,2,1,0:T(4,128)S(1)}, f32[2,5,8,4,160]{4,3,2,1,0:T(4,128)}, u32[]{:S(2)}) copy-start(f32[2,5,8,4,160]{4,3,2,1,0:T(4,128)} %param.16) | copy-start | bytes 614404
  2.9 1.1 %copy-start.4 = (f32[324,320]{1,0:T(8,128)S(1)}, f32[324,320]{1,0:T(8,128)}, u32[]{:S(2)}) copy-start(f32[324,320]{1,0:T(8,128)} %constant.22.clone) | copy-start | bytes 1244164
  2.9 1.7 %copy-start.10 = (f32[5,160]{1,0:T(8,128)S(1)}, f32[5,160]{1,0:T(8,128)}, u32[]{:S(2)}) copy-start(f32[5,160]{1,0:T(8,128)} %constant.23.clone) | copy-start | bytes 9604
  3.1 1.8 %copy-start.3 = (f32[324,320]{1,0:T(8,128)S(1)}, f32[324,320]{1,0:T(8,128)}, u32[]{:S(2)}) copy-start(f32[324,320]{1,0:T(8,128)} %constant.24.clone) | copy-start | bytes 1244164
  3.9 2.1 %copy-start.7 = (f32[2,5,8,5,128]{4,2,3,1,0:T(8,128)S(1)}, f32[2,5,8,5,128]{4,2,3,1,0:T(8,128)}, u32[]{:S(2)}) copy-start(f32[2,5,8,5,128]{4,2,3,1,0:T(8,128)} %param.17) | copy-start | bytes 614404
  4.9 1.3 %copy-start.1 = (f32[324,400]{1,0:T(8,128)S(1)}, f32[324,400]{1,0:T(8,128)}, u32[]{:S(2)}) copy-start(f32[324,400]{1,0:T(8,128)} %constant.9.clone) | copy-start | bytes 1555204
  5.8 0.8 %copy-start.11 = (f32[5,128]{1,0:T(8,128)S(1)}, f32[5,128]{1,0:T(8,128)}, u32[]{:S(2)}) copy-start(f32[5,128]{1,0:T(8,128)} %constant.10.clone) | copy-start | bytes 7684
  6.0 5.5 %copy-start.2 = (f32[160,132]{1,0:T(8,128)S(1)}, f32[160,132]{1,0:T(8,128)}, u32[]{:S(2)}) copy-start(f32[160,132]{1,0:T(8,128)} %constant.11.clone) | copy-start | bytes 253444
  6.2 6.1 %copy-start.8 = (f32[128,132]{1,0:T(8,128)S(1)}, f32[128,132]{1,0:T(8,128)}, u32[]{:S(2)}) copy-start(f32[128,132]{1,0:T(8,128)} %constant.12.clone) | copy-start | bytes 202756
  6.2 6.8 %copy-start.9 = (f32[5,132]{1,0:T(8,128)S(1)}, f32[5,132]{1,0:T(8,128)}, u32[]{:S(2)}) copy-start(f32[5,132]{1,0:T(8,128)} %constant.13.clone) | copy-start | bytes 7924
  6.9 6.1 %collective-permute-start = (f32[12,324]{1,0:T(8,128)S(1)}, f32[12,324]{1,0:T(8,128)S(1)}, u32[]{:S(2)}, u32[]{:S(2)}) collective-permute-start(f32[12,324]{1,0:T(8,128)S(1)} %reshape.106), channel_id=1, source_target_pairs={{0,1},{1,2},{2,3},{3,4},{4,5},{5,6},{6,7},{7,0},{8,9},{9,10},{10,1... | collective-permute-start | bytes 46664 | tf_op jit(solution)/shard_map/ppermute | solution.py:59
  7.4 5.5 %collective-permute-start.1 = (f32[8,324]{1,0:T(8,128)S(1)}, f32[8,324]{1,0:T(8,128)S(1)}, u32[]{:S(2)}, u32[]{:S(2)}) collective-permute-start(f32[8,324]{1,0:T(8,128)S(1)} %reshape.108), channel_id=1, source_target_pairs={{0,7},{1,0},{2,1},{3,2},{4,3},{5,4},{6,5},{7,6},{8,15},{9,8},{10,9... | collective-permute-start | bytes 31112 | tf_op jit(solution)/shard_map/ppermute | solution.py:59
  16.3 1.2 %copy-start = (f32[3,9,36,132]{3,2,1,0:T(8,128)S(1)}, f32[3,9,36,132]{3,2,1,0:T(8,128)}, u32[]{:S(2)}) copy-start(f32[3,9,36,132]{3,2,1,0:T(8,128)} %constant_dynamic-update-slice_fusion.2) | copy-start | bytes 1539652
  17.9 12.4 %collective-permute-start.2 = (f32[615,128]{1,0:T(8,128)S(1)}, f32[615,128]{1,0:T(8,128)}, u32[]{:S(2)}, u32[]{:S(2)}) collective-permute-start(f32[615,128]{1,0:T(8,128)S(1)} %fusion.13), channel_id=1, source_target_pairs={{0,16},{8,24},{16,0},{24,8},{1,17},{9,25},{17,1},{25,9},{2,18},{10... | collective-permute-start | bytes 944648 | tf_op jit(solution)/shard_map/ppermute | solution.py:207
  20.3 9.5 %collective-permute-start.3 = (f32[178,128]{1,0:T(8,128)S(1)}, f32[178,128]{1,0:T(8,128)S(1)}, u32[]{:S(2)}, u32[]{:S(2)}) collective-permute-start(f32[178,128]{1,0:T(8,128)S(1)} %fusion.14), channel_id=1, source_target_pairs={{0,8},{8,0},{16,24},{24,16},{1,9},{9,1},{17,25},{25,17},{2,10},{10... | collective-permute-start | bytes 273416 | tf_op jit(solution)/shard_map/ppermute | solution.py:207
  22.3 7.0 %collective-permute-start.4 = (f32[38,128]{1,0:T(8,128)S(1)}, f32[38,128]{1,0:T(8,128)S(1)}, u32[]{:S(2)}, u32[]{:S(2)}) collective-permute-start(f32[38,128]{1,0:T(8,128)S(1)} %pad_bitcast_fusion), channel_id=1, source_target_pairs={{0,24},{8,16},{16,8},{24,0},{1,25},{9,17},{17,9},{25,1},{2,26},{10... | collective-permute-start | bytes 58376 | tf_op jit(solution)/shard_map/ppermute | solution.py:207

commit v18 on v15

--- a/solution.py
+++ b/solution.py
@@ -221,6 +221,18 @@
     return jnp.pad(block, [(b, s - b - d) for b, d, s in zip(starts, block.shape, shape)])
 
 
+class Channels:
+    def __init__(self, parts):
+        self.parts = parts
+        self.shape = (len(parts),) + parts[0].shape
+
+    def __getitem__(self, index):
+        picked = self.parts[index[0]]
+        if isinstance(index[0], int):
+            return picked[index[1:]]
+        return jnp.stack([part[index[1:]] for part in picked])
+
+
 def plane_round_and_stencil(extended, nx, ny):
     e = extended
     payloads = {
@@ -242,7 +254,7 @@
     halo_x, fold_x = got[(1, 0)]
     corner_x, corner_y = got[(1, 1)]
     total = (
-        at(e, 2, 0)
+        at(jnp.stack(e.parts), 2, 0)
         + at(halo_x, 0, 2, 2)
         + at(fold_x, 2, 2)
         + at(got[(-1, 0)][0], nx + 2, 2, 2)
@@ -331,7 +343,7 @@
     keep = keep + jnp.pad(keep_in[..., :3], ((0, 0), (0, 0), (0, length - 3))) + jnp.pad(
         keep_in[..., 3:], ((0, 0), (0, 0), (nz + 2, 0))
     )
-    extended = jnp.stack(nodal + [keep])
+    extended = Channels(nodal + [keep])
     return plane_round_and_stencil(extended, nx, ny)
 
 

time: 34.1 us -> 42.9 us (1.26)
  local copies, waits for them, and re-layouts: 8.04 us -> 11.7 us
  other arithmetic: 5.27 us -> 8.2 us
  matrix products: 4.88 us -> 5.99 us
  waiting for transfers between devices: 6.74 us -> 7.48 us
    ppermute x2, waiting for transfers between devices: 0.28 us -> 3.89 us  [shifted(): lax.ppermute(block, axis, [(i, (i + step) % count) for i in range(count)])]
    another operation x4 -> x19, local copies, waits for them, and re-layouts: 0.13 us -> 3.58 us  [the longest x16 3.47 us: __getitem__(): return jnp.stack([part[index[1:]] for part in picked])]
    ppermute x3, waiting for transfers between devices: 6.46 us -> 3.59 us  [exchange(): rows = lax.ppermute(rows, tuple(axes), pairs)]
    add x1 -> x2, other arithmetic: 0.36 us -> 2.56 us  [the longest x1 2.36 us: plane_round_and_stencil(): at(jnp.stack(e.parts), 2, 0) + at(halo_x, 0, 2, 2) + at(fold_x, 2, 2)]
    slice x7 -> x5, local copies, waits for them, and re-layouts: 0.22 us -> 2.38 us  [the longest x4 2.36 us: __getitem__(): return jnp.stack([part[index[1:]] for part in picked])]
    unnamed x27 -> x52, local copies, waits for them, and re-layouts: 2.14 us -> 0.14 us
    dot_general x3, matrix products: 1.97 us -> 3.07 us  [planar_part(): jnp.dot(jnp.asarray(plane_map, jnp.float32), signed, precision=lax.Precis...]
    mul x3, other arithmetic: 0.12 us -> 1.04 us  [planar_part(): coef * orient[:, None, :, None, :]]
  transfers between devices with their start and end apart: 5 -> 5, of which waited for: 2 -> 4; matrix products, arithmetic and copies ran while one was open for 10% -> 8% of each run, Pallas kernels for 0% -> 0%
where the time goes in v18:
time: 42.9 us; the launch traced here: 42.6 us
  local copies, waits for them, and re-layouts  11.7 us (27%)
  starting transfers between devices  8.28 us (19%)
  other arithmetic  8.2 us (19%)
  waiting for transfers between devices  7.48 us (17%)
  matrix products  5.99 us (14%)
  between operations  0.97 us (2%)
    ppermute x2, starting transfers between devices, shifted(): lax.ppermute(block, axis, [(i, (i + step) % count) for i in range(count)])  4.6 us
    ppermute x2, waiting for transfers between devices, shifted(): lax.ppermute(block, axis, [(i, (i + step) % count) for i in range(count)])  3.89 us
    ppermute x3, starting transfers between devices, exchange(): rows = lax.ppermute(rows, tuple(axes), pairs)  3.68 us
    ppermute x3, waiting for transfers between devices, exchange(): rows = lax.ppermute(rows, tuple(axes), pairs)  3.59 us
    another operation x16, local copies, waits for them, and re-layouts, __getitem__(): return jnp.stack([part[index[1:]] for part in picked])  3.47 us
    dot_general x3, matrix products, planar_part(): jnp.dot(jnp.asarray(plane_map, jnp.float32), signed, precision=lax.Precis...  3.07 us
    slice x4, local copies, waits for them, and re-layouts, __getitem__(): return jnp.stack([part[index[1:]] for part in picked])  2.36 us
    add x1, other arithmetic, plane_round_and_stencil(): at(jnp.stack(e.parts), 2, 0) + at(halo_x, 0, 2, 2) + at(fold_x, 2, 2)  2.36 us
  transfers between devices with their start and end apart: 5, of which 4 were waited for; matrix products, arithmetic and copies ran while one was open for 8% of the time, Pallas kernels for 0%

profile of v18, /device:TPU:0, one launch (start us, length us, event | category | flops | bytes accessed | tf_op | source)
XLA Modules:
  0.0 42.6 jit_solution(16182936674710740405)
XLA Ops:
  0.0 0.7 %convert_bitcast_fusion.2 = (f32[2,8,32]{2,1,0:T(8,128)S(1)}, f32[2,8,32]{2,1,0:T(8,128)S(1)}, f32[2,8,32]{2,1,0:T(8,128)S(1)}) fusion(s32[3,2,8,32]{3,2,1,0:T(8,128)} %param.18), kind=kLoop, calls=%fused_computation.117 | loop fusion | flops 4608 | bytes 12288 | tf_op jit(solution)/shard_map/convert_element_type | solution.py:44
  0.9 1.0 %subtract_convert_fusion = f32[8,32,128]{2,1,0:T(8,128)S(1)} fusion(s32[8,32,128]{2,1,0:T(8,128)} %param.19), kind=kLoop, calls=%fused_computation.54 | loop fusion | flops 65536 | bytes 262144 | tf_op jit(solution)/shard_map/convert_element_type | solution.py:312
  1.9 0.9 %broadcast_multiply_fusion.2 = f32[2,5,8,5,128]{4,2,3,1,0:T(8,128)S(1)} fusion(f32[2,5,8,5,128]{4,2,3,1,0:T(8,128)} %param.17, f32[2,8,128]{2,1,0:T(8,128)S(1)} %copy.88), kind=kLoop, calls=%fused_computation.56 | loop fusion | flops 51200 | bytes 417792 | tf_op jit(solution)/shard_map/mul | solution.py:45
  3.1 0.2 mul.133
  3.4 0.2 mul.137
  4.7 1.9 %fusion.52 = f32[160,324]{1,0:T(8,128)S(1)} fusion(f32[320,160]{1,0:T(8,128)S(1)} %reshape.112, f32[324,320]{1,0:T(8,128)} %constant.24.clone), kind=kOutput, calls=%fused_computation.137 | convolution fusion | flops 99532800 | bytes 826880 | tf_op jit(solution)/shard_map/dot_general | solution.py:48
  6.6 0.2 convolution_bitcast_fusion.1
  6.8 0.8 %fusion.50 = f32[160,324]{1,0:T(8,128)S(1)} fusion(f32[320,160]{1,0:T(8,128)S(1)} %reshape.111, f32[324,320]{1,0:T(8,128)S(1)} %copy-done.2), kind=kOutput, calls=%fused_computation.135 | convolution fusion | flops 99532800 | bytes 826880 | tf_op jit(solution)/shard_map/dot_general | solution.py:48
  7.6 0.2 convolution_bitcast_fusion.2
  7.7 0.4 %fusion.54 = f32[128,324]{0,1:T(8,128)S(1)} fusion(f32[400,128]{1,0:T(8,128)S(1)} %reshape.113, f32[324,400]{1,0:T(8,128)S(1)} %copy-done), kind=kOutput, calls=%fused_computation.139 | convolution fusion | flops 99532800 | bytes 889088 | tf_op jit(solution)/shard_map/dot_general | solution.py:48
  8.2 0.2 convolution_bitcast_fusion
  8.4 4.5 %collective-permute-start.1 = (f32[8,324]{1,0:T(8,128)S(1)}, f32[8,324]{1,0:T(8,128)S(1)}, u32[]{:S(2)}, u32[]{:S(2)}) collective-permute-start(f32[8,324]{1,0:T(8,128)S(1)} %reshape.116), channel_id=1, source_target_pairs={{0,7},{1,0},{2,1},{3,2},{4,3},{5,4},{6,5},{7,6},{8,15},{9,8},{10,9... | collective-permute-start | bytes 31112 | tf_op jit(solution)/shard_map/ppermute | solution.py:59
  13.1 0.4 fusion.53
  13.5 0.4 fusion.51
  13.9 0.3 fusion.55
  14.2 0.2 collective-permute-done.1
  14.4 3.7 %collective-permute-done = f32[12,324]{1,0:T(8,128)S(1)} collective-permute-done((f32[12,324]{1,0:T(8,128)S(1)}, f32[12,324]{1,0:T(8,128)S(1)}, u32[]{:S(2)}, u32[]{:S(2)}) %collective-permute-start) | collective-permute-done | bytes 15584 | tf_op jit(solution)/shard_map/ppermute | solution.py:59
  18.2 0.2 copy.95
  18.5 0.2 pad_add_fusion
  18.7 0.6 %fusion.47 = (f32[1,2,132]{2,1,0:T(2,128)}, f32[1,2,132]{2,1,0:T(2,128)}) fusion(f32[9,36,132]{2,1,0:T(8,128)S(1)} %pad_add_fusion), kind=kLoop, calls=%fused_computation.132 | loop fusion | bytes 4224 | tf_op jit(solution)/shard_map/slice | solution.py:233
  19.4 0.4 %convolution_add_fusion.2 = f32[324,132]{0,1:T(8,128)S(1)} fusion(f32[324,132]{0,1:T(8,128)S(1)} %fusion.51, f32[5,132]{1,0:T(8,128)S(1)} %copy-done.6, f32[4,3,324]{2,1,0:T(4,128)S(1)} %reshape.115, f32[4,2,324]{2,1,0:T(2,128)S(1)} %reshape.117), kind=kOutput, calls=%fused_computation.18 | convolution fusion | flops 2610468 | bytes 370704 | tf_op jit(solution)/shard_map/dot_general | solution.py:340
  19.9 0.1 copy.92
  20.1 0.6 %fusion.44 = (f32[1,2,132]{2,1,0:T(2,128)}, f32[1,2,132]{2,1,0:T(2,128)}) fusion(f32[9,36,132]{2,1,0:T(8,128)S(1)} %reshape.118), kind=kLoop, calls=%fused_computation.129 | loop fusion | bytes 4224 | tf_op jit(solution)/shard_map/slice | solution.py:233
  20.8 0.4 %convolution_add_fusion.1 = f32[324,132]{0,1:T(8,128)S(1)} fusion(f32[324,132]{0,1:T(8,128)S(1)} %fusion.53, f32[5,132]{1,0:T(8,128)S(1)} %copy-done.6, f32[4,3,324]{2,1,0:T(4,128)S(1)} %reshape.115, f32[4,2,324]{2,1,0:T(2,128)S(1)} %reshape.117), kind=kOutput, calls=%fused_computation.17 | convolution fusion | flops 2610468 | bytes 370704 | tf_op jit(solution)/shard_map/dot_general | solution.py:340
  21.2 0.1 copy.93
  21.4 0.6 %slice_bitcast_fusion.29 = (f32[1,2,132]{2,0,1:T(1,128)}, f32[1,2,132]{2,0,1:T(1,128)}) fusion(f32[9,36,132]{2,1,0:T(8,128)S(1)} %reshape.119, f32[9,36,132]{2,1,0:T(8,128)S(1)} %reshape.118), kind=kLoop, calls=%fused_computation.124 | loop fusion | bytes 4224 | tf_op jit(solution)/shard_map/stack;squeeze | solution.py:233
  22.0 0.6 %fusion.45 = (f32[1,2,132]{2,1,0:T(2,128)}, f32[1,2,132]{2,1,0:T(2,128)}) fusion(f32[9,36,132]{2,1,0:T(8,128)S(1)} %reshape.119), kind=kLoop, calls=%fused_computation.130 | loop fusion | bytes 4224 | tf_op jit(solution)/shard_map/slice | solution.py:233
  22.6 0.6 %slice_bitcast_fusion.25 = (f32[1,3,132]{2,0,1:T(1,128)}, f32[1,3,132]{2,0,1:T(1,128)}) fusion(f32[9,36,132]{2,1,0:T(8,128)S(1)} %reshape.119, f32[9,36,132]{2,1,0:T(8,128)S(1)} %reshape.118), kind=kLoop, calls=%fused_computation.120 | loop fusion | bytes 6336 | tf_op jit(solution)/shard_map/stack;squeeze | solution.py:233
  23.3 0.4 %convolution_add_fusion = f32[324,132]{0,1:T(8,128)S(1)} fusion(f32[324,132]{0,1:T(8,128)S(1)} %fusion.55, f32[5,132]{1,0:T(8,128)S(1)} %copy-done.6, f32[4,3,324]{2,1,0:T(4,128)S(1)} %reshape.115, f32[4,2,324]{2,1,0:T(2,128)S(1)} %reshape.117), kind=kOutput, calls=%fused_computation.16 | convolution fusion | flops 2610468 | bytes 370704 | tf_op jit(solution)/shard_map/dot_general | solution.py:340
  23.8 0.1 copy.94
  24.0 0.6 %slice_bitcast_fusion.27 = (f32[1,2,132]{2,0,1:T(1,128)}, f32[1,2,132]{2,0,1:T(1,128)}) fusion(f32[9,36,132]{2,1,0:T(8,128)S(1)} %pad_add_fusion, f32[9,36,132]{2,1,0:T(8,128)S(1)} %reshape.120), kind=kLoop, calls=%fused_computation.122 | loop fusion | bytes 4224 | tf_op jit(solution)/shard_map/stack;squeeze | solution.py:233
  24.6 0.6 %fusion.46 = (f32[1,2,132]{2,1,0:T(2,128)}, f32[1,2,132]{2,1,0:T(2,128)}) fusion(f32[9,36,132]{2,1,0:T(8,128)S(1)} %reshape.120), kind=kLoop, calls=%fused_computation.131 | loop fusion | bytes 4224 | tf_op jit(solution)/shard_map/slice | solution.py:233
  25.2 0.6 %slice_bitcast_fusion.23 = (f32[1,3,132]{2,0,1:T(1,128)}, f32[1,3,132]{2,0,1:T(1,128)}) fusion(f32[9,36,132]{2,1,0:T(8,128)S(1)} %pad_add_fusion, f32[9,36,132]{2,1,0:T(8,128)S(1)} %reshape.120), kind=kLoop, calls=%fused_computation.118 | loop fusion | bytes 6336 | tf_op jit(solution)/shard_map/stack;squeeze | solution.py:233
  25.8 0.6 %slice_bitcast_fusion.19 = (f32[1,8,2,132]{3,2,1,0:T(2,128)S(1)}, f32[1,8,2,132]{3,2,1,0:T(2,128)}) fusion(f32[9,36,132]{2,1,0:T(8,128)S(1)} %pad_add_fusion, f32[9,36,132]{2,1,0:T(8,128)S(1)} %reshape.120), kind=kLoop, calls=%fused_computation.92 | loop fusion | bytes 33792 | tf_op jit(solution)/shard_map/stack | solution.py:233
  26.9 0.9 %concatenate.23 = f32[78604]{0:T(1024)S(1)} concatenate(f32[32768]{0:T(1024)S(1)} %bitcast.137, f32[13068]{0:T(1024)S(1)} %reshape.122, f32[32768]{0:T(1024)S(1)} %bitcast.138), dimensions={0} | concatenate | bytes 628832 | tf_op jit(solution)/shard_map/concatenate | solution.py:198
  27.9 1.6 %collective-permute-start.2 = (f32[615,128]{1,0:T(8,128)S(1)}, f32[615,128]{1,0:T(8,128)S(1)}, u32[]{:S(2)}, u32[]{:S(2)}) collective-permute-start(f32[615,128]{1,0:T(8,128)S(1)} %pad_bitcast_fusion), channel_id=1, source_target_pairs={{0,16},{8,24},{16,0},{24,8},{1,17},{9,25},{17,1},{25,9},{2,18},{10... | collective-permute-start | bytes 944648 | tf_op jit(solution)/shard_map/ppermute | solution.py:207
  29.5 0.1 reshape.129
  29.7 0.1 reshape.130
  30.6 1.5 %collective-permute-start.4 = (f32[38,128]{1,0:T(8,128)S(1)}, f32[38,128]{1,0:T(8,128)S(1)}, u32[]{:S(2)}, u32[]{:S(2)}) collective-permute-start(f32[38,128]{1,0:T(8,128)S(1)} %pad_bitcast_fusion.1), channel_id=1, source_target_pairs={{0,24},{8,16},{16,8},{24,0},{1,25},{9,17},{17,9},{25,1},{2,26},{10... | collective-permute-start | bytes 58376 | tf_op jit(solution)/shard_map/ppermute | solution.py:207
  32.2 0.4 fusion.20
  32.8 0.6 %collective-permute-start.3 = (f32[178,128]{1,0:T(8,128)S(1)}, f32[178,128]{1,0:T(8,128)S(1)}, u32[]{:S(2)}, u32[]{:S(2)}) collective-permute-start(f32[178,128]{1,0:T(8,128)S(1)} %fusion.23), channel_id=1, source_target_pairs={{0,8},{8,0},{16,24},{24,16},{1,9},{9,1},{17,25},{25,17},{2,10},{10... | collective-permute-start | bytes 273416 | tf_op jit(solution)/shard_map/ppermute | solution.py:207
  33.4 2.7 %collective-permute-done.4 = f32[38,128]{1,0:T(8,128)S(1)} collective-permute-done((f32[38,128]{1,0:T(8,128)S(1)}, f32[38,128]{1,0:T(8,128)S(1)}, u32[]{:S(2)}, u32[]{:S(2)}) %collective-permute-start.4) | collective-permute-done | bytes 19488 | tf_op jit(solution)/shard_map/ppermute | solution.py:207
  36.5 0.9 %collective-permute-done.3 = f32[178,128]{1,0:T(8,128)S(1)} collective-permute-done((f32[178,128]{1,0:T(8,128)S(1)}, f32[178,128]{1,0:T(8,128)S(1)}, u32[]{:S(2)}, u32[]{:S(2)}) %collective-permute-start.3) | collective-permute-done | bytes 91168 | tf_op jit(solution)/shard_map/ppermute | solution.py:207
  37.5 0.2 reshape.134
  37.7 0.2 reshape.133
  38.2 2.4 %fusion.8 = f32[4,12,36,132]{3,2,1,0:T(8,128)S(1)} fusion(f32[1,9,36,132]{3,2,1,0:T(8,128)S(1)} %bitcast.131, f32[1,9,36,132]{3,2,1,0:T(8,128)S(1)} %stack_reshape.15, f32[1,9,36,132]{3,2,1,0:T(8,128)S(1)} %stack_reshape.14, f32[1,9,36,132]{3,2,1,0:T(8,128)S(1)} %stack_reshape.13, f32[4,1,2,132]{3,2,1,0:T(2,128)S(1)} %bitcast.147, ...), kind=kLoop, calls=%fused_computation.11 | loop fusion | flops 4333824 | bytes 2020912 | tf_op jit(solution)/shard_map/add | solution.py:257
  40.7 0.2 fusion.38
  41.0 1.6 %fusion.12 = f32[3,8,32,128]{3,2,1,0:T(8,128)} fusion(f32[3,12,36,132]{3,2,1,0:T(8,128)S(1)} %slice_multiply_fusion, f32[3,7,31,128]{3,2,1,0:T(8,128)S(1)} %fusion.20, f32[3,7,1,128]{3,2,1,0:T(1,128)S(1)} %fusion.38, f32[3,1,32,128]{3,2,1,0:T(8,128)S(1)} %fusion.25), kind=kLoop, calls=%fused_computation.27 | loop fusion | flops 1474560 | bytes 3932160 | tf_op jit(solution)/shard_map/mul | solution.py:276
  (135 shorter events, 4.7 us)
Async XLA Ops:
  0.8 3.4 %copy-start.3 = (f32[2,5,8,4,160]{4,3,2,1,0:T(4,128)S(1)}, f32[2,5,8,4,160]{4,3,2,1,0:T(4,128)}, u32[]{:S(2)}) copy-start(f32[2,5,8,4,160]{4,3,2,1,0:T(4,128)} %param.16) | copy-start | bytes 614404
  2.9 1.5 %copy-start.4 = (f32[2,4,8,5,160]{4,2,3,1,0:T(8,128)S(1)}, f32[2,4,8,5,160]{4,2,3,1,0:T(8,128)}, u32[]{:S(2)}) copy-start(f32[2,4,8,5,160]{4,2,3,1,0:T(8,128)} %param.15) | copy-start | bytes 614404
  4.3 2.3 %copy-start.8 = (f32[5,160]{1,0:T(8,128)S(1)}, f32[5,160]{1,0:T(8,128)}, u32[]{:S(2)}) copy-start(f32[5,160]{1,0:T(8,128)} %constant.23.clone) | copy-start | bytes 9604
  4.4 2.3 %copy-start.2 = (f32[324,320]{1,0:T(8,128)S(1)}, f32[324,320]{1,0:T(8,128)}, u32[]{:S(2)}) copy-start(f32[324,320]{1,0:T(8,128)} %constant.22.clone) | copy-start | bytes 1244164
  4.6 3.1 %copy-start = (f32[324,400]{1,0:T(8,128)S(1)}, f32[324,400]{1,0:T(8,128)}, u32[]{:S(2)}) copy-start(f32[324,400]{1,0:T(8,128)} %constant.9.clone) | copy-start | bytes 1555204
  4.7 3.5 %copy-start.25 = (f32[5,128]{1,0:T(8,128)S(1)}, f32[5,128]{1,0:T(8,128)}, u32[]{:S(2)}) copy-start(f32[5,128]{1,0:T(8,128)} %constant.10.clone) | copy-start | bytes 7684
  4.7 8.4 %copy-start.1 = (f32[160,132]{1,0:T(8,128)S(1)}, f32[160,132]{1,0:T(8,128)}, u32[]{:S(2)}) copy-start(f32[160,132]{1,0:T(8,128)} %constant.11.clone) | copy-start | bytes 253444
  6.8 7.1 %copy-start.5 = (f32[128,132]{1,0:T(8,128)S(1)}, f32[128,132]{1,0:T(8,128)}, u32[]{:S(2)}) copy-start(f32[128,132]{1,0:T(8,128)} %constant.12.clone) | copy-start | bytes 202756
  8.4 5.9 %collective-permute-start.1 = (f32[8,324]{1,0:T(8,128)S(1)}, f32[8,324]{1,0:T(8,128)S(1)}, u32[]{:S(2)}, u32[]{:S(2)}) collective-permute-start(f32[8,324]{1,0:T(8,128)S(1)} %reshape.116), channel_id=1, source_target_pairs={{0,7},{1,0},{2,1},{3,2},{4,3},{5,4},{6,5},{7,6},{8,15},{9,8},{10,9... | collective-permute-start | bytes 31112 | tf_op jit(solution)/shard_map/ppermute | solution.py:59
  13.0 6.4 %copy-start.6 = (f32[5,132]{1,0:T(8,128)S(1)}, f32[5,132]{1,0:T(8,128)}, u32[]{:S(2)}) copy-start(f32[5,132]{1,0:T(8,128)} %constant.13.clone) | copy-start | bytes 7924
  13.0 5.1 %collective-permute-start = (f32[12,324]{1,0:T(8,128)S(1)}, f32[12,324]{1,0:T(8,128)S(1)}, u32[]{:S(2)}, u32[]{:S(2)}) collective-permute-start(f32[12,324]{1,0:T(8,128)S(1)} %reshape.114), channel_id=1, source_target_pairs={{0,1},{1,2},{2,3},{3,4},{4,5},{5,6},{6,7},{7,0},{8,9},{9,10},{10,1... | collective-permute-start | bytes 46664 | tf_op jit(solution)/shard_map/ppermute | solution.py:59
  26.6 2.9 %copy-start.7 = (f32[1,8,2,132]{3,2,1,0:T(2,128)S(1)}, f32[1,8,2,132]{3,2,1,0:T(2,128)}, u32[]{:S(2)}) copy-start(f32[1,8,2,132]{3,2,1,0:T(2,128)} %get-tuple-element.56) | copy-start | bytes 25348
  26.6 3.3 %copy-start.21 = (f32[1,2,132]{2,0,1:T(1,128)S(1)}, f32[1,2,132]{2,0,1:T(1,128)}, u32[]{:S(2)}) copy-start(f32[1,2,132]{2,0,1:T(1,128)} %get-tuple-element.67) | copy-start | bytes 3172
  26.6 3.3 %copy-start.22 = (f32[1,2,132]{2,0,1:T(1,128)S(1)}, f32[1,2,132]{2,0,1:T(1,128)}, u32[]{:S(2)}) copy-start(f32[1,2,132]{2,0,1:T(1,128)} %get-tuple-element.68) | copy-start | bytes 3172
  26.6 3.3 %copy-start.23 = (f32[1,2,132]{2,0,1:T(1,128)S(1)}, f32[1,2,132]{2,0,1:T(1,128)}, u32[]{:S(2)}) copy-start(f32[1,2,132]{2,0,1:T(1,128)} %get-tuple-element.65) | copy-start | bytes 3172
  26.6 3.3 %copy-start.24 = (f32[1,2,132]{2,0,1:T(1,128)S(1)}, f32[1,2,132]{2,0,1:T(1,128)}, u32[]{:S(2)}) copy-start(f32[1,2,132]{2,0,1:T(1,128)} %get-tuple-element.66) | copy-start | bytes 3172
  26.6 3.3 %copy-start.9 = (f32[1,3,132]{2,0,1:T(1,128)S(1)}, f32[1,3,132]{2,0,1:T(1,128)}, u32[]{:S(2)}) copy-start(f32[1,3,132]{2,0,1:T(1,128)} %get-tuple-element.61) | copy-start | bytes 4756
  26.6 3.3 %copy-start.10 = (f32[1,3,132]{2,0,1:T(1,128)S(1)}, f32[1,3,132]{2,0,1:T(1,128)}, u32[]{:S(2)}) copy-start(f32[1,3,132]{2,0,1:T(1,128)} %get-tuple-element.62) | copy-start | bytes 4756
  26.6 3.3 %copy-start.11 = (f32[1,3,132]{2,0,1:T(1,128)S(1)}, f32[1,3,132]{2,0,1:T(1,128)}, u32[]{:S(2)}) copy-start(f32[1,3,132]{2,0,1:T(1,128)} %get-tuple-element.59) | copy-start | bytes 4756
  26.6 3.3 %copy-start.12 = (f32[1,3,132]{2,0,1:T(1,128)S(1)}, f32[1,3,132]{2,0,1:T(1,128)}, u32[]{:S(2)}) copy-start(f32[1,3,132]{2,0,1:T(1,128)} %get-tuple-element.60) | copy-start | bytes 4756
  26.7 3.4 %copy-start.13 = (f32[1,2,132]{2,1,0:T(2,128)S(1)}, f32[1,2,132]{2,1,0:T(2,128)}, u32[]{:S(2)}) copy-start(f32[1,2,132]{2,1,0:T(2,128)} %get-tuple-element.29) | copy-start | bytes 3172
  26.7 3.4 %copy-start.14 = (f32[1,2,132]{2,1,0:T(2,128)S(1)}, f32[1,2,132]{2,1,0:T(2,128)}, u32[]{:S(2)}) copy-start(f32[1,2,132]{2,1,0:T(2,128)} %get-tuple-element.30) | copy-start | bytes 3172
  26.7 3.4 %copy-start.15 = (f32[1,2,132]{2,1,0:T(2,128)S(1)}, f32[1,2,132]{2,1,0:T(2,128)}, u32[]{:S(2)}) copy-start(f32[1,2,132]{2,1,0:T(2,128)} %get-tuple-element.23) | copy-start | bytes 3172
  26.7 3.4 %copy-start.16 = (f32[1,2,132]{2,1,0:T(2,128)S(1)}, f32[1,2,132]{2,1,0:T(2,128)}, u32[]{:S(2)}) copy-start(f32[1,2,132]{2,1,0:T(2,128)} %get-tuple-element.24) | copy-start | bytes 3172
  26.7 3.4 %copy-start.17 = (f32[1,2,132]{2,1,0:T(2,128)S(1)}, f32[1,2,132]{2,1,0:T(2,128)}, u32[]{:S(2)}) copy-start(f32[1,2,132]{2,1,0:T(2,128)} %get-tuple-element.25) | copy-start | bytes 3172
  26.7 3.4 %copy-start.18 = (f32[1,2,132]{2,1,0:T(2,128)S(1)}, f32[1,2,132]{2,1,0:T(2,128)}, u32[]{:S(2)}) copy-start(f32[1,2,132]{2,1,0:T(2,128)} %get-tuple-element.26) | copy-start | bytes 3172
  26.7 3.4 %copy-start.19 = (f32[1,2,132]{2,1,0:T(2,128)S(1)}, f32[1,2,132]{2,1,0:T(2,128)}, u32[]{:S(2)}) copy-start(f32[1,2,132]{2,1,0:T(2,128)} %get-tuple-element.27) | copy-start | bytes 3172
  26.7 3.4 %copy-start.20 = (f32[1,2,132]{2,1,0:T(2,128)S(1)}, f32[1,2,132]{2,1,0:T(2,128)}, u32[]{:S(2)}) copy-start(f32[1,2,132]{2,1,0:T(2,128)} %get-tuple-element.28) | copy-start | bytes 3172
  27.9 10.0 %collective-permute-start.2 = (f32[615,128]{1,0:T(8,128)S(1)}, f32[615,128]{1,0:T(8,128)S(1)}, u32[]{:S(2)}, u32[]{:S(2)}) collective-permute-start(f32[615,128]{1,0:T(8,128)S(1)} %pad_bitcast_fusion), channel_id=1, source_target_pairs={{0,16},{8,24},{16,0},{24,8},{1,17},{9,25},{17,1},{25,9},{2,18},{10... | collective-permute-start | bytes 944648 | tf_op jit(solution)/shard_map/ppermute | solution.py:207
  30.6 5.4 %collective-permute-start.4 = (f32[38,128]{1,0:T(8,128)S(1)}, f32[38,128]{1,0:T(8,128)S(1)}, u32[]{:S(2)}, u32[]{:S(2)}) collective-permute-start(f32[38,128]{1,0:T(8,128)S(1)} %pad_bitcast_fusion.1), channel_id=1, source_target_pairs={{0,24},{8,16},{16,8},{24,0},{1,25},{9,17},{17,9},{25,1},{2,26},{10... | collective-permute-start | bytes 58376 | tf_op jit(solution)/shard_map/ppermute | solution.py:207
  32.8 4.6 %collective-permute-start.3 = (f32[178,128]{1,0:T(8,128)S(1)}, f32[178,128]{1,0:T(8,128)S(1)}, u32[]{:S(2)}, u32[]{:S(2)}) collective-permute-start(f32[178,128]{1,0:T(8,128)S(1)} %fusion.23), channel_id=1, source_target_pairs={{0,8},{8,0},{16,24},{24,16},{1,9},{9,1},{17,25},{25,17},{2,10},{10... | collective-permute-start | bytes 273416 | tf_op jit(solution)/shard_map/ppermute | solution.py:207

commit v19 on v15

--- a/solution.py
+++ b/solution.py
@@ -297,14 +297,12 @@
         slabs.append(
             lax.dot_general(edge_map, planar, (((1,), (1,)), ((), ())), precision=lax.Precision.HIGH)
         )
-    keep_own = (1 - flags).astype(jnp.float32)
-    keep = jnp.pad(keep_own, ((0, 1), (2, 2), (2, 2)))
     keep_layers = [
-        lax.slice_in_dim(keep_own, nz - 2, nz, axis=2),
-        jnp.zeros_like(lax.slice_in_dim(keep_own, 0, 1, axis=2)),
-        lax.slice_in_dim(keep_own, 0, 2, axis=2),
+        lax.slice_in_dim(flags, nz - 2, nz, axis=2),
+        jnp.ones_like(lax.slice_in_dim(flags, 0, 1, axis=2)),
+        lax.slice_in_dim(flags, 0, 2, axis=2),
     ]
-    keep_layers = jnp.moveaxis(jnp.concatenate(keep_layers, axis=2), 2, 0)
+    keep_layers = (1 - jnp.moveaxis(jnp.concatenate(keep_layers, axis=2), 2, 0)).astype(jnp.float32)
     slabs.append(jnp.pad(keep_layers, ((0, 0), (0, 1), (2, 2))).reshape(5, -1))
     slabs = jnp.stack(slabs)
     up = slabs[:, :3].reshape(-1, slabs.shape[2])
@@ -327,6 +325,7 @@
     for comp in range(3):
         folded = lax.dot_general(arrived[comp], place, (((0,), (0,)), ((), ())), precision=precise)
         nodal.append((own_parts[comp] + folded).reshape(nx + 1, ny + 4, length))
+    keep = jnp.pad((1 - flags).astype(jnp.float32), ((0, 1), (2, 2), (2, 2)))
     keep_in = jnp.moveaxis(arrived[3].reshape(5, nx + 1, ny + 4), 0, 2)
     keep = keep + jnp.pad(keep_in[..., :3], ((0, 0), (0, 0), (0, length - 3))) + jnp.pad(
         keep_in[..., 3:], ((0, 0), (0, 0), (nz + 2, 0))

time: 34.1 us -> 34.2 us (level)
    mul x3, other arithmetic: 0.12 us -> 1.14 us  [planar_part(): coef * orient[:, None, :, None, :]]
    convert_element_type x1 -> x2, other arithmetic: 0.96 us -> 0.09 us  [the longest x1 0.08 us: body(): (1 - jnp.moveaxis(jnp.concatenate(keep_layers, axis=2), 2, 0)).astype(jnp...]
    unnamed x27 -> x29, local copies, waits for them, and re-layouts: 2.14 us -> 2.35 us
where the time goes in v19:
time: 34.2 us; the launch traced here: 33.9 us
  starting transfers between devices  8.25 us (24%)
  local copies, waits for them, and re-layouts  8.01 us (23%)
  waiting for transfers between devices  6.76 us (20%)
  other arithmetic  5.34 us (16%)
  matrix products  4.85 us (14%)
  between operations  0.71 us (2%)
    ppermute x3, waiting for transfers between devices, exchange(): rows = lax.ppermute(rows, tuple(axes), pairs)  6.49 us
    ppermute x2, starting transfers between devices, shifted(): lax.ppermute(block, axis, [(i, (i + step) % count) for i in range(count)])  4.61 us
    ppermute x3, starting transfers between devices, exchange(): rows = lax.ppermute(rows, tuple(axes), pairs)  3.64 us
    unnamed x29, local copies, waits for them, and re-layouts  2.35 us
    dot_general x3, matrix products, planar_part(): jnp.dot(jnp.asarray(plane_map, jnp.float32), signed, precision=lax.Precis...  1.95 us
    mul x1, other arithmetic, plane_round_and_stencil(): return 0.25 * result  1.63 us
    dot_general x3, matrix products, body(): lax.dot_general(arrived[comp], place, (((0,), (0,)), ((), ())), precision...  1.28 us
    mul x3, other arithmetic, planar_part(): coef * orient[:, None, :, None, :]  1.14 us
  transfers between devices with their start and end apart: 5, of which 2 were waited for; matrix products, arithmetic and copies ran while one was open for 10% of the time, Pallas kernels for 0%

profile of v19, /device:TPU:0, one launch (start us, length us, event | category | flops | bytes accessed | tf_op | source)
XLA Modules:
  0.0 33.9 jit_solution(909809882954114093)
XLA Ops:
  0.0 0.7 %convert_bitcast_fusion.2 = (f32[2,8,32]{2,1,0:T(8,128)S(1)}, f32[2,8,32]{2,1,0:T(8,128)S(1)}, f32[2,8,32]{2,1,0:T(8,128)S(1)}) fusion(s32[3,2,8,32]{3,2,1,0:T(8,128)} %param.18), kind=kLoop, calls=%fused_computation.83 | loop fusion | flops 4608 | bytes 12288 | tf_op jit(solution)/shard_map/convert_element_type | solution.py:44
  0.7 0.1 broadcast_in_dim.12
  0.9 0.2 mul.135
  1.0 1.0 %broadcast_multiply_fusion.1 = f32[2,4,8,5,160]{4,2,3,1,0:T(8,128)S(1)} fusion(f32[2,4,8,5,160]{4,2,3,1,0:T(8,128)} %param.15, f32[2,8,160]{2,1,0:T(8,128)S(1)} %mul.135), kind=kLoop, calls=%fused_computation.35 | loop fusion | flops 51200 | bytes 419840 | tf_op jit(solution)/shard_map/mul | solution.py:45
  2.1 0.1 copy.56
  2.3 0.1 broadcast_in_dim.13
  2.5 0.2 mul.139
  2.8 0.4 %copy-done.4 = f32[324,320]{1,0:T(8,128)S(1)} copy-done((f32[324,320]{1,0:T(8,128)S(1)}, f32[324,320]{1,0:T(8,128)}, u32[]{:S(2)}) %copy-start.4) | copy-done | bytes 414744
  3.3 0.8 %fusion.39 = f32[160,324]{1,0:T(8,128)S(1)} fusion(f32[320,160]{1,0:T(8,128)S(1)} %reshape.101, f32[324,320]{1,0:T(8,128)S(1)} %copy-done.4), kind=kOutput, calls=%fused_computation.90 | convolution fusion | flops 99532800 | bytes 826880 | tf_op jit(solution)/shard_map/dot_general | solution.py:48
  4.0 0.2 convolution_bitcast_fusion.2
  4.2 0.8 %fusion.41 = f32[160,324]{1,0:T(8,128)S(1)} fusion(f32[320,160]{1,0:T(8,128)S(1)} %reshape.102, f32[324,320]{1,0:T(8,128)S(1)} %copy-done.5), kind=kOutput, calls=%fused_computation.92 | convolution fusion | flops 99532800 | bytes 826880 | tf_op jit(solution)/shard_map/dot_general | solution.py:48
  5.0 0.2 convolution_bitcast_fusion.1
  5.7 0.1 copy.75
  6.2 0.4 %fusion.43 = f32[128,324]{0,1:T(8,128)S(1)} fusion(f32[400,128]{1,0:T(8,128)S(1)} %reshape.103, f32[324,400]{1,0:T(8,128)S(1)} %copy-done.2), kind=kOutput, calls=%fused_computation.94 | convolution fusion | flops 99532800 | bytes 889088 | tf_op jit(solution)/shard_map/dot_general | solution.py:48
  6.7 0.2 convolution_bitcast_fusion
  6.9 0.5 %collective-permute-start = (f32[12,324]{1,0:T(8,128)S(1)}, f32[12,324]{1,0:T(8,128)S(1)}, u32[]{:S(2)}, u32[]{:S(2)}) collective-permute-start(f32[12,324]{1,0:T(8,128)S(1)} %reshape.104), channel_id=1, source_target_pairs={{0,1},{1,2},{2,3},{3,4},{4,5},{5,6},{6,7},{7,0},{8,9},{9,10},{10,1... | collective-permute-start | bytes 46664 | tf_op jit(solution)/shard_map/ppermute | solution.py:59
  7.4 4.1 %collective-permute-start.1 = (f32[8,324]{1,0:T(8,128)S(1)}, f32[8,324]{1,0:T(8,128)S(1)}, u32[]{:S(2)}, u32[]{:S(2)}) collective-permute-start(f32[8,324]{1,0:T(8,128)S(1)} %reshape.106), channel_id=1, source_target_pairs={{0,7},{1,0},{2,1},{3,2},{4,3},{5,4},{6,5},{7,6},{8,15},{9,8},{10,9... | collective-permute-start | bytes 31112 | tf_op jit(solution)/shard_map/ppermute | solution.py:59
  11.6 0.4 %fusion.40 = f32[324,132]{0,1:T(8,128)S(1)} fusion(f32[160,324]{1,0:T(8,128)S(1)} %fusion.39, f32[160,132]{1,0:T(8,128)S(1)} %copy-done.3), kind=kOutput, calls=%fused_computation.91 | convolution fusion | flops 41057280 | bytes 462912 | tf_op jit(solution)/shard_map/dot_general | solution.py:313
  11.9 0.4 %fusion.42 = f32[324,132]{0,1:T(8,128)S(1)} fusion(f32[160,324]{1,0:T(8,128)S(1)} %fusion.41, f32[160,132]{1,0:T(8,128)S(1)} %copy-done.3), kind=kOutput, calls=%fused_computation.93 | convolution fusion | flops 41057280 | bytes 462912 | tf_op jit(solution)/shard_map/dot_general | solution.py:313
  12.3 0.3 fusion.44
  12.7 0.3 collective-permute-done.1
  13.0 0.4 %convolution_add_fusion.2 = f32[324,132]{0,1:T(8,128)S(1)} fusion(f32[324,132]{0,1:T(8,128)S(1)} %fusion.40, f32[5,132]{1,0:T(8,128)S(1)} %copy-done.9, f32[4,3,324]{2,1,0:T(4,128)S(1)} %reshape.105, f32[4,2,324]{2,1,0:T(2,128)S(1)} %reshape.107), kind=kOutput, calls=%fused_computation.5 | convolution fusion | flops 2610468 | bytes 370704 | tf_op jit(solution)/shard_map/dot_general | solution.py:326
  13.5 0.1 copy.62
  13.7 0.8 %constant_dynamic-update-slice_fusion.2 = f32[3,9,36,132]{3,2,1,0:T(8,128)} fusion(f32[1,9,36,132]{3,2,1,0:T(8,128)S(1)} %stack_reshape.13), kind=kLoop, calls=%fused_computation.79 | loop fusion | bytes 539712
  14.4 0.4 %convolution_add_fusion.1 = f32[324,132]{0,1:T(8,128)S(1)} fusion(f32[324,132]{0,1:T(8,128)S(1)} %fusion.42, f32[5,132]{1,0:T(8,128)S(1)} %copy-done.9, f32[4,3,324]{2,1,0:T(4,128)S(1)} %reshape.105, f32[4,2,324]{2,1,0:T(2,128)S(1)} %reshape.107), kind=kOutput, calls=%fused_computation.4 | convolution fusion | flops 2610468 | bytes 370704 | tf_op jit(solution)/shard_map/dot_general | solution.py:326
  14.9 0.1 copy.63
  15.1 0.4 %convolution_add_fusion = f32[324,132]{0,1:T(8,128)S(1)} fusion(f32[324,132]{0,1:T(8,128)S(1)} %fusion.44, f32[5,132]{1,0:T(8,128)S(1)} %copy-done.9, f32[4,3,324]{2,1,0:T(4,128)S(1)} %reshape.105, f32[4,2,324]{2,1,0:T(2,128)S(1)} %reshape.107), kind=kOutput, calls=%fused_computation.3 | convolution fusion | flops 2610468 | bytes 370704 | tf_op jit(solution)/shard_map/dot_general | solution.py:326
  15.5 0.1 copy.64
  15.8 0.2 copy.65
  16.0 0.2 add_bitcast_fusion
  16.3 0.1 pad_maximum_fusion
  16.4 0.1 fusion.36
  16.7 0.8 %copy-done = f32[3,9,36,132]{3,2,1,0:T(8,128)S(1)} copy-done((f32[3,9,36,132]{3,2,1,0:T(8,128)S(1)}, f32[3,9,36,132]{3,2,1,0:T(8,128)}, u32[]{:S(2)}) %copy-start) | copy-done | bytes 513240
  17.7 0.1 reshape.109
  17.9 0.9 %concatenate.25 = f32[78604]{0:T(1024)S(1)} concatenate(f32[32768]{0:T(1024)S(1)} %bitcast.90, f32[13068]{0:T(1024)S(1)} %reshape.109, f32[32768]{0:T(1024)S(1)} %bitcast.89), dimensions={0} | concatenate | bytes 628832 | tf_op jit(solution)/shard_map/concatenate | solution.py:198
  18.8 2.0 %collective-permute-start.2 = (f32[615,128]{1,0:T(8,128)S(1)}, f32[615,128]{1,0:T(8,128)S(1)}, u32[]{:S(2)}, u32[]{:S(2)}) collective-permute-start(f32[615,128]{1,0:T(8,128)S(1)} %pad_bitcast_fusion), channel_id=1, source_target_pairs={{0,16},{8,24},{16,0},{24,8},{1,17},{9,25},{17,1},{25,9},{2,18},{10... | collective-permute-start | bytes 944648 | tf_op jit(solution)/shard_map/ppermute | solution.py:207
  20.9 0.1 reshape.116
  21.0 0.1 reshape.117
  21.2 1.5 %collective-permute-start.3 = (f32[178,128]{1,0:T(8,128)S(1)}, f32[178,128]{1,0:T(8,128)S(1)}, u32[]{:S(2)}, u32[]{:S(2)}) collective-permute-start(f32[178,128]{1,0:T(8,128)S(1)} %fusion.13), channel_id=1, source_target_pairs={{0,8},{8,0},{16,24},{24,16},{1,9},{9,1},{17,25},{25,17},{2,10},{10... | collective-permute-start | bytes 273416 | tf_op jit(solution)/shard_map/ppermute | solution.py:207
  23.3 0.4 %fusion.10 = f32[3,7,31,128]{3,2,1,0:T(8,128)S(1)} fusion(f32[3,7,31,132]{3,2,1,0:T(8,128)S(1)} %slice_multiply_fusion.1), kind=kLoop, calls=%fused_computation.27 | loop fusion | flops 583296 | bytes 1999872 | tf_op jit(solution)/shard_map/add | solution.py:273
  23.8 6.5 %collective-permute-done.4 = f32[38,128]{1,0:T(8,128)S(1)} collective-permute-done((f32[38,128]{1,0:T(8,128)S(1)}, f32[38,128]{1,0:T(8,128)S(1)}, u32[]{:S(2)}, u32[]{:S(2)}) %collective-permute-start.4) | collective-permute-done | bytes 19488 | tf_op jit(solution)/shard_map/ppermute | solution.py:207
  30.8 0.2 reshape.120
  31.0 0.2 reshape.121
  31.3 0.1 reshape.114
  31.5 0.4 %pad_add_fusion = f32[4,12,36,132]{3,2,1,0:T(8,128)S(1)} fusion(f32[4,1,2,132]{3,2,1,0:T(2,128)S(1)} %bitcast.100, f32[4,2,1,132]{3,2,1,0:T(1,128)S(1)} %broadcast_in_dim_reshape.20, f32[4,1,2,132]{3,2,1,0:T(2,128)S(1)} %bitcast.99, f32[4,3,1,132]{3,2,1,0:T(1,128)S(1)} %broadcast_in_dim_reshape.19, f32[4,8,2,132]{3,2,1,0:T(2,128)S(1)} %reshape.121, ...), kind=kLoop, calls=%fused_computation | loop fusion | flops 2052864 | bytes 2020912 | tf_op jit(solution)/shard_map/add | solution.py:245
  31.9 0.1 slice_multiply_fusion
  32.1 0.2 fusion.30
  32.3 1.6 %fusion.2 = f32[3,8,32,128]{3,2,1,0:T(8,128)} fusion(f32[3,12,36,132]{3,2,1,0:T(8,128)S(1)} %slice_multiply_fusion, f32[3,7,31,128]{3,2,1,0:T(8,128)S(1)} %fusion.10, f32[3,7,1,128]{3,2,1,0:T(1,128)S(1)} %fusion.30, f32[3,1,32,128]{3,2,1,0:T(8,128)S(1)} %fusion.15), kind=kLoop, calls=%fused_computation.14 | loop fusion | flops 1474560 | bytes 3932160 | tf_op jit(solution)/shard_map/mul | solution.py:264
  (89 shorter events, 3.2 us)
Async XLA Ops:
  1.0 1.6 %copy-start.6 = (f32[2,5,8,4,160]{4,3,2,1,0:T(4,128)S(1)}, f32[2,5,8,4,160]{4,3,2,1,0:T(4,128)}, u32[]{:S(2)}) copy-start(f32[2,5,8,4,160]{4,3,2,1,0:T(4,128)} %param.16) | copy-start | bytes 614404
  2.2 1.0 %copy-start.4 = (f32[324,320]{1,0:T(8,128)S(1)}, f32[324,320]{1,0:T(8,128)}, u32[]{:S(2)}) copy-start(f32[324,320]{1,0:T(8,128)} %constant.22.clone) | copy-start | bytes 1244164
  2.3 1.7 %copy-start.10 = (f32[5,160]{1,0:T(8,128)S(1)}, f32[5,160]{1,0:T(8,128)}, u32[]{:S(2)}) copy-start(f32[5,160]{1,0:T(8,128)} %constant.23.clone) | copy-start | bytes 9604
  2.5 1.8 %copy-start.5 = (f32[324,320]{1,0:T(8,128)S(1)}, f32[324,320]{1,0:T(8,128)}, u32[]{:S(2)}) copy-start(f32[324,320]{1,0:T(8,128)} %constant.24.clone) | copy-start | bytes 1244164
  3.3 2.1 %copy-start.7 = (f32[2,5,8,5,128]{4,2,3,1,0:T(8,128)S(1)}, f32[2,5,8,5,128]{4,2,3,1,0:T(8,128)}, u32[]{:S(2)}) copy-start(f32[2,5,8,5,128]{4,2,3,1,0:T(8,128)} %param.17) | copy-start | bytes 614404
  4.2 1.3 %copy-start.1 = (s32[8,32,128]{2,1,0:T(8,128)S(1)}, s32[8,32,128]{2,1,0:T(8,128)}, u32[]{:S(2)}) copy-start(s32[8,32,128]{2,1,0:T(8,128)} %param.19) | copy-start | bytes 393220
  5.0 1.2 %copy-start.2 = (f32[324,400]{1,0:T(8,128)S(1)}, f32[324,400]{1,0:T(8,128)}, u32[]{:S(2)}) copy-start(f32[324,400]{1,0:T(8,128)} %constant.25.clone) | copy-start | bytes 1555204
  5.4 1.2 %copy-start.11 = (f32[5,128]{1,0:T(8,128)S(1)}, f32[5,128]{1,0:T(8,128)}, u32[]{:S(2)}) copy-start(f32[5,128]{1,0:T(8,128)} %constant.9.clone) | copy-start | bytes 7684
  5.5 6.1 %copy-start.3 = (f32[160,132]{1,0:T(8,128)S(1)}, f32[160,132]{1,0:T(8,128)}, u32[]{:S(2)}) copy-start(f32[160,132]{1,0:T(8,128)} %constant.10.clone) | copy-start | bytes 253444
  5.9 6.5 %copy-start.8 = (f32[128,132]{1,0:T(8,128)S(1)}, f32[128,132]{1,0:T(8,128)}, u32[]{:S(2)}) copy-start(f32[128,132]{1,0:T(8,128)} %constant.11.clone) | copy-start | bytes 202756
  6.6 6.4 %copy-start.9 = (f32[5,132]{1,0:T(8,128)S(1)}, f32[5,132]{1,0:T(8,128)}, u32[]{:S(2)}) copy-start(f32[5,132]{1,0:T(8,128)} %constant.12.clone) | copy-start | bytes 7924
  6.9 6.1 %collective-permute-start = (f32[12,324]{1,0:T(8,128)S(1)}, f32[12,324]{1,0:T(8,128)S(1)}, u32[]{:S(2)}, u32[]{:S(2)}) collective-permute-start(f32[12,324]{1,0:T(8,128)S(1)} %reshape.104), channel_id=1, source_target_pairs={{0,1},{1,2},{2,3},{3,4},{4,5},{5,6},{6,7},{7,0},{8,9},{9,10},{10,1... | collective-permute-start | bytes 46664 | tf_op jit(solution)/shard_map/ppermute | solution.py:59
  7.4 5.5 %collective-permute-start.1 = (f32[8,324]{1,0:T(8,128)S(1)}, f32[8,324]{1,0:T(8,128)S(1)}, u32[]{:S(2)}, u32[]{:S(2)}) collective-permute-start(f32[8,324]{1,0:T(8,128)S(1)} %reshape.106), channel_id=1, source_target_pairs={{0,7},{1,0},{2,1},{3,2},{4,3},{5,4},{6,5},{7,6},{8,15},{9,8},{10,9... | collective-permute-start | bytes 31112 | tf_op jit(solution)/shard_map/ppermute | solution.py:59
  16.3 1.2 %copy-start = (f32[3,9,36,132]{3,2,1,0:T(8,128)S(1)}, f32[3,9,36,132]{3,2,1,0:T(8,128)}, u32[]{:S(2)}) copy-start(f32[3,9,36,132]{3,2,1,0:T(8,128)} %constant_dynamic-update-slice_fusion.2) | copy-start | bytes 1539652
  18.8 12.4 %collective-permute-start.2 = (f32[615,128]{1,0:T(8,128)S(1)}, f32[615,128]{1,0:T(8,128)S(1)}, u32[]{:S(2)}, u32[]{:S(2)}) collective-permute-start(f32[615,128]{1,0:T(8,128)S(1)} %pad_bitcast_fusion), channel_id=1, source_target_pairs={{0,16},{8,24},{16,0},{24,8},{1,17},{9,25},{17,1},{25,9},{2,18},{10... | collective-permute-start | bytes 944648 | tf_op jit(solution)/shard_map/ppermute | solution.py:207
  21.2 9.5 %collective-permute-start.3 = (f32[178,128]{1,0:T(8,128)S(1)}, f32[178,128]{1,0:T(8,128)S(1)}, u32[]{:S(2)}, u32[]{:S(2)}) collective-permute-start(f32[178,128]{1,0:T(8,128)S(1)} %fusion.13), channel_id=1, source_target_pairs={{0,8},{8,0},{16,24},{24,16},{1,9},{9,1},{17,25},{25,17},{2,10},{10... | collective-permute-start | bytes 273416 | tf_op jit(solution)/shard_map/ppermute | solution.py:207
  23.3 7.0 %collective-permute-start.4 = (f32[38,128]{1,0:T(8,128)S(1)}, f32[38,128]{1,0:T(8,128)S(1)}, u32[]{:S(2)}, u32[]{:S(2)}) collective-permute-start(f32[38,128]{1,0:T(8,128)S(1)} %pad_bitcast_fusion.1), channel_id=1, source_target_pairs={{0,24},{8,16},{16,8},{24,0},{1,25},{9,17},{17,9},{25,1},{2,26},{10... | collective-permute-start | bytes 58376 | tf_op jit(solution)/shard_map/ppermute | solution.py:207

commit v20 on v15

--- a/solution.py
+++ b/solution.py
@@ -195,7 +195,7 @@
         parts = [part for offset in offsets for part in payloads[offset]]
         if previous is not None:
             previous, parts = lax.optimization_barrier((previous, parts))
-        flat = jnp.concatenate([part.reshape(-1) for part in parts])
+        flat = jnp.concatenate([jnp.pad(part.reshape(-1), (0, -part.size % 1024)) for part in parts])
         length = flat.shape[0]
         rows = jnp.pad(flat, (0, -length % 128)).reshape(-1, 128)
         previous = rows
@@ -212,7 +212,7 @@
             for part in payloads[offset]:
                 size = int(np.prod(part.shape))
                 parts.append(flat[start : start + size].reshape(part.shape))
-                start += size
+                start += size + (-size % 1024)
             arrived[offset] = parts
     return arrived
 

time: 34.1 us -> 35.1 us (1.029)
  local copies, waits for them, and re-layouts: 8.04 us -> 8.58 us
    slice x7 -> x6, local copies, waits for them, and re-layouts: 0.27 us -> 1.82 us  [exchange(): parts.append(flat[start:start + size].reshape(part.shape))]
    concatenate x2, local copies, waits for them, and re-layouts: 0.99 us -> 0.01 us  [exchange(): jnp.concatenate([jnp.pad(part.reshape(-1), (0, -part.size % 1024)) for pa...]
    reshape x9 -> x7, local copies, waits for them, and re-layouts: 0.79 us -> 0.76 us  [exchange(): part.reshape(-1)]
  transfers between devices with their start and end apart: 5 -> 5, of which waited for: 2 -> 2; matrix products, arithmetic and copies ran while one was open for 10% -> 8% of each run, Pallas kernels for 0% -> 0%
where the time goes in v20:
time: 35.1 us; the launch traced here: 34.8 us
  local copies, waits for them, and re-layouts  8.58 us (24%)
  starting transfers between devices  8.32 us (24%)
  waiting for transfers between devices  7.08 us (20%)
  other arithmetic  5.23 us (15%)
  matrix products  4.87 us (14%)
  between operations  0.7 us (2%)
    ppermute x3, waiting for transfers between devices, exchange(): rows = lax.ppermute(rows, tuple(axes), pairs)  6.81 us
    ppermute x2, starting transfers between devices, shifted(): lax.ppermute(block, axis, [(i, (i + step) % count) for i in range(count)])  4.61 us
    ppermute x3, starting transfers between devices, exchange(): rows = lax.ppermute(rows, tuple(axes), pairs)  3.71 us
    unnamed x27, local copies, waits for them, and re-layouts  2.15 us
    dot_general x3, matrix products, planar_part(): jnp.dot(jnp.asarray(plane_map, jnp.float32), signed, precision=lax.Precis...  1.97 us
    slice x6, local copies, waits for them, and re-layouts, exchange(): parts.append(flat[start:start + size].reshape(part.shape))  1.82 us
    mul x1, other arithmetic, plane_round_and_stencil(): return 0.25 * result  1.63 us
    dot_general x3, matrix products, body(): lax.dot_general(arrived[comp], place, (((0,), (0,)), ((), ())), precision...  1.27 us
  transfers between devices with their start and end apart: 5, of which 2 were waited for; matrix products, arithmetic and copies ran while one was open for 8% of the time, Pallas kernels for 0%

profile of v20, /device:TPU:0, one launch (start us, length us, event | category | flops | bytes accessed | tf_op | source)
XLA Modules:
  0.0 34.8 jit_solution(16473341776492331416)
XLA Ops:
  0.0 1.0 %subtract_convert_fusion = f32[8,32,128]{2,1,0:T(8,128)S(1)} fusion(s32[8,32,128]{2,1,0:T(8,128)} %param.19), kind=kLoop, calls=%fused_computation.41 | loop fusion | flops 65536 | bytes 262144 | tf_op jit(solution)/shard_map/convert_element_type | solution.py:300
  1.6 0.7 %convert_bitcast_fusion = (f32[2,8,32]{2,1,0:T(8,128)S(1)}, f32[2,8,32]{2,1,0:T(8,128)S(1)}, f32[2,8,32]{2,1,0:T(8,128)S(1)}) fusion(s32[3,2,8,32]{3,2,1,0:T(8,128)} %param.18), kind=kLoop, calls=%fused_computation.89 | loop fusion | flops 4608 | bytes 12288 | tf_op jit(solution)/shard_map/convert_element_type | solution.py:44
  2.4 0.1 broadcast_in_dim.12
  2.5 0.2 mul.135
  2.7 0.1 copy.56
  3.0 0.1 broadcast_in_dim.13
  3.1 0.2 mul.139
  3.3 0.4 %copy-done.6 = f32[2,5,8,4,160]{4,3,2,1,0:T(4,128)S(1)} copy-done((f32[2,5,8,4,160]{4,3,2,1,0:T(4,128)S(1)}, f32[2,5,8,4,160]{4,3,2,1,0:T(4,128)}, u32[]{:S(2)}) %copy-start.6) | copy-done | bytes 204824
  3.9 0.8 %fusion.41 = f32[160,324]{1,0:T(8,128)S(1)} fusion(f32[320,160]{1,0:T(8,128)S(1)} %reshape.107, f32[324,320]{1,0:T(8,128)S(1)} %copy-done.4), kind=kOutput, calls=%fused_computation.99 | convolution fusion | flops 99532800 | bytes 826880 | tf_op jit(solution)/shard_map/dot_general | solution.py:48
  4.7 0.2 convolution_bitcast_fusion.2
  4.9 0.8 %fusion.43 = f32[160,324]{1,0:T(8,128)S(1)} fusion(f32[320,160]{1,0:T(8,128)S(1)} %reshape.108, f32[324,320]{1,0:T(8,128)S(1)} %copy-done.3), kind=kOutput, calls=%fused_computation.101 | convolution fusion | flops 99532800 | bytes 826880 | tf_op jit(solution)/shard_map/dot_general | solution.py:48
  5.7 0.2 convolution_bitcast_fusion.1
  6.2 0.4 %fusion.45 = f32[128,324]{0,1:T(8,128)S(1)} fusion(f32[400,128]{1,0:T(8,128)S(1)} %reshape.109, f32[324,400]{1,0:T(8,128)S(1)} %copy-done.1), kind=kOutput, calls=%fused_computation.103 | convolution fusion | flops 99532800 | bytes 889088 | tf_op jit(solution)/shard_map/dot_general | solution.py:48
  6.6 0.2 convolution_bitcast_fusion
  6.9 0.5 %collective-permute-start = (f32[12,324]{1,0:T(8,128)S(1)}, f32[12,324]{1,0:T(8,128)S(1)}, u32[]{:S(2)}, u32[]{:S(2)}) collective-permute-start(f32[12,324]{1,0:T(8,128)S(1)} %reshape.110), channel_id=1, source_target_pairs={{0,1},{1,2},{2,3},{3,4},{4,5},{5,6},{6,7},{7,0},{8,9},{9,10},{10,1... | collective-permute-start | bytes 46664 | tf_op jit(solution)/shard_map/ppermute | solution.py:59
  7.4 4.1 %collective-permute-start.1 = (f32[8,324]{1,0:T(8,128)S(1)}, f32[8,324]{1,0:T(8,128)S(1)}, u32[]{:S(2)}, u32[]{:S(2)}) collective-permute-start(f32[8,324]{1,0:T(8,128)S(1)} %reshape.112), channel_id=1, source_target_pairs={{0,7},{1,0},{2,1},{3,2},{4,3},{5,4},{6,5},{7,6},{8,15},{9,8},{10,9... | collective-permute-start | bytes 31112 | tf_op jit(solution)/shard_map/ppermute | solution.py:59
  11.5 0.4 %fusion.42 = f32[324,132]{0,1:T(8,128)S(1)} fusion(f32[160,324]{1,0:T(8,128)S(1)} %fusion.41, f32[160,132]{1,0:T(8,128)S(1)} %copy-done.2), kind=kOutput, calls=%fused_computation.100 | convolution fusion | flops 41057280 | bytes 462912 | tf_op jit(solution)/shard_map/dot_general | solution.py:315
  11.9 0.4 %fusion.44 = f32[324,132]{0,1:T(8,128)S(1)} fusion(f32[160,324]{1,0:T(8,128)S(1)} %fusion.43, f32[160,132]{1,0:T(8,128)S(1)} %copy-done.2), kind=kOutput, calls=%fused_computation.102 | convolution fusion | flops 41057280 | bytes 462912 | tf_op jit(solution)/shard_map/dot_general | solution.py:315
  12.3 0.3 fusion.46
  12.7 0.3 collective-permute-done.1
  13.0 0.4 %convolution_add_fusion.1 = f32[324,132]{0,1:T(8,128)S(1)} fusion(f32[324,132]{0,1:T(8,128)S(1)} %fusion.44, f32[5,132]{1,0:T(8,128)S(1)} %copy-done.9, f32[4,3,324]{2,1,0:T(4,128)S(1)} %reshape.111, f32[4,2,324]{2,1,0:T(2,128)S(1)} %reshape.113), kind=kOutput, calls=%fused_computation.4 | convolution fusion | flops 2610468 | bytes 370704 | tf_op jit(solution)/shard_map/dot_general | solution.py:328
  13.4 0.1 copy.63
  13.6 0.4 %convolution_add_fusion.2 = f32[324,132]{0,1:T(8,128)S(1)} fusion(f32[324,132]{0,1:T(8,128)S(1)} %fusion.42, f32[5,132]{1,0:T(8,128)S(1)} %copy-done.9, f32[4,3,324]{2,1,0:T(4,128)S(1)} %reshape.111, f32[4,2,324]{2,1,0:T(2,128)S(1)} %reshape.113), kind=kOutput, calls=%fused_computation.5 | convolution fusion | flops 2610468 | bytes 370704 | tf_op jit(solution)/shard_map/dot_general | solution.py:328
  14.1 0.1 copy.62
  14.3 0.8 %constant_dynamic-update-slice_fusion.2 = f32[3,9,36,132]{3,2,1,0:T(8,128)} fusion(f32[1,9,36,132]{3,2,1,0:T(8,128)S(1)} %stack_reshape.13), kind=kLoop, calls=%fused_computation.83 | loop fusion | bytes 539712
  15.0 0.4 %convolution_add_fusion = f32[324,132]{0,1:T(8,128)S(1)} fusion(f32[324,132]{0,1:T(8,128)S(1)} %fusion.46, f32[5,132]{1,0:T(8,128)S(1)} %copy-done.9, f32[4,3,324]{2,1,0:T(4,128)S(1)} %reshape.111, f32[4,2,324]{2,1,0:T(2,128)S(1)} %reshape.113), kind=kOutput, calls=%fused_computation.3 | convolution fusion | flops 2610468 | bytes 370704 | tf_op jit(solution)/shard_map/dot_general | solution.py:328
  15.5 0.1 copy.64
  15.7 0.2 copy.65
  16.0 0.2 add_bitcast_fusion
  16.3 0.1 pad_maximum_fusion
  16.4 0.1 fusion.37
  16.7 0.8 %copy-done = f32[3,9,36,132]{3,2,1,0:T(8,128)S(1)} copy-done((f32[3,9,36,132]{3,2,1,0:T(8,128)S(1)}, f32[3,9,36,132]{3,2,1,0:T(8,128)}, u32[]{:S(2)}) %copy-start) | copy-done | bytes 513240
  17.7 0.1 reshape.115
  17.9 2.1 %collective-permute-start.2 = (f32[616,128]{1,0:T(8,128)S(1)}, f32[616,128]{1,0:T(8,128)}, u32[]{:S(2)}, u32[]{:S(2)}) collective-permute-start(f32[616,128]{1,0:T(8,128)S(1)} %fusion.14), channel_id=1, source_target_pairs={{0,16},{8,24},{16,0},{24,8},{1,17},{9,25},{17,1},{25,9},{2,18},{10... | collective-permute-start | bytes 946184 | tf_op jit(solution)/shard_map/ppermute | solution.py:207
  19.9 0.1 reshape.122
  20.1 0.1 reshape.123
  20.3 1.6 %collective-permute-start.3 = (f32[184,128]{1,0:T(8,128)S(1)}, f32[184,128]{1,0:T(8,128)S(1)}, u32[]{:S(2)}, u32[]{:S(2)}) collective-permute-start(f32[184,128]{1,0:T(8,128)S(1)} %fusion.16), channel_id=1, source_target_pairs={{0,8},{8,0},{16,24},{24,16},{1,9},{9,1},{17,25},{25,17},{2,10},{10... | collective-permute-start | bytes 282632 | tf_op jit(solution)/shard_map/ppermute | solution.py:207
  22.4 0.4 %fusion.10 = f32[3,7,31,128]{3,2,1,0:T(8,128)S(1)} fusion(f32[3,7,31,132]{3,2,1,0:T(8,128)S(1)} %slice_multiply_fusion.1), kind=kLoop, calls=%fused_computation.29 | loop fusion | flops 583296 | bytes 1999872 | tf_op jit(solution)/shard_map/add | solution.py:273
  22.8 6.8 %collective-permute-done.4 = f32[64,128]{1,0:T(8,128)S(1)} collective-permute-done((f32[64,128]{1,0:T(8,128)S(1)}, f32[64,128]{1,0:T(8,128)S(1)}, u32[]{:S(2)}, u32[]{:S(2)}) %collective-permute-start.4) | collective-permute-done | bytes 32800 | tf_op jit(solution)/shard_map/ppermute | solution.py:207
  30.0 0.2 reshape.126
  30.2 0.2 reshape.127
  30.4 0.8 %slice.264 = f32[13068]{0:T(1024)S(1)} slice(f32[78848]{0:T(1024)} %bitcast.17), slice={[32768:45836]} | slice | bytes 104544 | tf_op jit(solution)/shard_map/slice | solution.py:214
  31.2 0.1 reshape.120
  31.3 1.0 %fusion.38 = (f32[256,128]{1,0:T(8,128)S(1)}, f32[256,128]{1,0:T(8,128)S(1)}) fusion(f32[616,128]{1,0:T(8,128)} %collective-permute-done.2), kind=kLoop, calls=%fused_computation.96 | loop fusion | bytes 524288 | tf_op jit(solution)/shard_map/slice | solution.py:214
  32.3 0.4 %pad_add_fusion = f32[4,12,36,132]{3,2,1,0:T(8,128)S(1)} fusion(f32[4,1,2,132]{3,2,1,0:T(2,128)S(1)} %bitcast.101, f32[4,2,1,132]{3,2,1,0:T(1,128)S(1)} %broadcast_in_dim_reshape.20, f32[4,1,2,132]{3,2,1,0:T(2,128)S(1)} %bitcast.100, f32[4,3,1,132]{3,2,1,0:T(1,128)S(1)} %broadcast_in_dim_reshape.19, f32[4,8,2,132]{3,2,1,0:T(2,128)S(1)} %reshape.127, ...), kind=kLoop, calls=%fused_computation | loop fusion | flops 2052864 | bytes 2020912 | tf_op jit(solution)/shard_map/add | solution.py:245
  32.7 0.1 slice_multiply_fusion
  33.0 0.2 fusion.31
  33.2 1.6 %fusion.2 = f32[3,8,32,128]{3,2,1,0:T(8,128)} fusion(f32[3,12,36,132]{3,2,1,0:T(8,128)S(1)} %slice_multiply_fusion, f32[3,7,31,128]{3,2,1,0:T(8,128)S(1)} %fusion.10, f32[3,7,1,128]{3,2,1,0:T(1,128)S(1)} %fusion.31, f32[3,1,32,128]{3,2,1,0:T(8,128)S(1)} %fusion.18), kind=kLoop, calls=%fused_computation.16 | loop fusion | flops 1474560 | bytes 3932160 | tf_op jit(solution)/shard_map/mul | solution.py:264
  (88 shorter events, 3.0 us)
Async XLA Ops:
  0.0 2.7 %copy-start.5 = (f32[2,4,8,5,160]{4,2,3,1,0:T(8,128)S(1)}, f32[2,4,8,5,160]{4,2,3,1,0:T(8,128)}, u32[]{:S(2)}) copy-start(f32[2,4,8,5,160]{4,2,3,1,0:T(8,128)} %param.15) | copy-start | bytes 614404
  2.7 1.0 %copy-start.6 = (f32[2,5,8,4,160]{4,3,2,1,0:T(4,128)S(1)}, f32[2,5,8,4,160]{4,3,2,1,0:T(4,128)}, u32[]{:S(2)}) copy-start(f32[2,5,8,4,160]{4,3,2,1,0:T(4,128)} %param.16) | copy-start | bytes 614404
  2.9 1.1 %copy-start.4 = (f32[324,320]{1,0:T(8,128)S(1)}, f32[324,320]{1,0:T(8,128)}, u32[]{:S(2)}) copy-start(f32[324,320]{1,0:T(8,128)} %constant.22.clone) | copy-start | bytes 1244164
  2.9 1.7 %copy-start.10 = (f32[5,160]{1,0:T(8,128)S(1)}, f32[5,160]{1,0:T(8,128)}, u32[]{:S(2)}) copy-start(f32[5,160]{1,0:T(8,128)} %constant.23.clone) | copy-start | bytes 9604
  3.1 1.8 %copy-start.3 = (f32[324,320]{1,0:T(8,128)S(1)}, f32[324,320]{1,0:T(8,128)}, u32[]{:S(2)}) copy-start(f32[324,320]{1,0:T(8,128)} %constant.24.clone) | copy-start | bytes 1244164
  3.9 2.1 %copy-start.7 = (f32[2,5,8,5,128]{4,2,3,1,0:T(8,128)S(1)}, f32[2,5,8,5,128]{4,2,3,1,0:T(8,128)}, u32[]{:S(2)}) copy-start(f32[2,5,8,5,128]{4,2,3,1,0:T(8,128)} %param.17) | copy-start | bytes 614404
  4.9 1.3 %copy-start.1 = (f32[324,400]{1,0:T(8,128)S(1)}, f32[324,400]{1,0:T(8,128)}, u32[]{:S(2)}) copy-start(f32[324,400]{1,0:T(8,128)} %constant.9.clone) | copy-start | bytes 1555204
  5.8 0.8 %copy-start.11 = (f32[5,128]{1,0:T(8,128)S(1)}, f32[5,128]{1,0:T(8,128)}, u32[]{:S(2)}) copy-start(f32[5,128]{1,0:T(8,128)} %constant.10.clone) | copy-start | bytes 7684
  6.0 5.5 %copy-start.2 = (f32[160,132]{1,0:T(8,128)S(1)}, f32[160,132]{1,0:T(8,128)}, u32[]{:S(2)}) copy-start(f32[160,132]{1,0:T(8,128)} %constant.11.clone) | copy-start | bytes 253444
  6.2 6.1 %copy-start.8 = (f32[128,132]{1,0:T(8,128)S(1)}, f32[128,132]{1,0:T(8,128)}, u32[]{:S(2)}) copy-start(f32[128,132]{1,0:T(8,128)} %constant.12.clone) | copy-start | bytes 202756
  6.2 6.8 %copy-start.9 = (f32[5,132]{1,0:T(8,128)S(1)}, f32[5,132]{1,0:T(8,128)}, u32[]{:S(2)}) copy-start(f32[5,132]{1,0:T(8,128)} %constant.13.clone) | copy-start | bytes 7924
  6.9 6.1 %collective-permute-start = (f32[12,324]{1,0:T(8,128)S(1)}, f32[12,324]{1,0:T(8,128)S(1)}, u32[]{:S(2)}, u32[]{:S(2)}) collective-permute-start(f32[12,324]{1,0:T(8,128)S(1)} %reshape.110), channel_id=1, source_target_pairs={{0,1},{1,2},{2,3},{3,4},{4,5},{5,6},{6,7},{7,0},{8,9},{9,10},{10,1... | collective-permute-start | bytes 46664 | tf_op jit(solution)/shard_map/ppermute | solution.py:59
  7.4 5.5 %collective-permute-start.1 = (f32[8,324]{1,0:T(8,128)S(1)}, f32[8,324]{1,0:T(8,128)S(1)}, u32[]{:S(2)}, u32[]{:S(2)}) collective-permute-start(f32[8,324]{1,0:T(8,128)S(1)} %reshape.112), channel_id=1, source_target_pairs={{0,7},{1,0},{2,1},{3,2},{4,3},{5,4},{6,5},{7,6},{8,15},{9,8},{10,9... | collective-permute-start | bytes 31112 | tf_op jit(solution)/shard_map/ppermute | solution.py:59
  16.3 1.2 %copy-start = (f32[3,9,36,132]{3,2,1,0:T(8,128)S(1)}, f32[3,9,36,132]{3,2,1,0:T(8,128)}, u32[]{:S(2)}) copy-start(f32[3,9,36,132]{3,2,1,0:T(8,128)} %constant_dynamic-update-slice_fusion.2) | copy-start | bytes 1539652
  17.9 12.5 %collective-permute-start.2 = (f32[616,128]{1,0:T(8,128)S(1)}, f32[616,128]{1,0:T(8,128)}, u32[]{:S(2)}, u32[]{:S(2)}) collective-permute-start(f32[616,128]{1,0:T(8,128)S(1)} %fusion.14), channel_id=1, source_target_pairs={{0,16},{8,24},{16,0},{24,8},{1,17},{9,25},{17,1},{25,9},{2,18},{10... | collective-permute-start | bytes 946184 | tf_op jit(solution)/shard_map/ppermute | solution.py:207
  20.3 9.7 %collective-permute-start.3 = (f32[184,128]{1,0:T(8,128)S(1)}, f32[184,128]{1,0:T(8,128)S(1)}, u32[]{:S(2)}, u32[]{:S(2)}) collective-permute-start(f32[184,128]{1,0:T(8,128)S(1)} %fusion.16), channel_id=1, source_target_pairs={{0,8},{8,0},{16,24},{24,16},{1,9},{9,1},{17,25},{25,17},{2,10},{10... | collective-permute-start | bytes 282632 | tf_op jit(solution)/shard_map/ppermute | solution.py:207
  22.3 7.3 %collective-permute-start.4 = (f32[64,128]{1,0:T(8,128)S(1)}, f32[64,128]{1,0:T(8,128)S(1)}, u32[]{:S(2)}, u32[]{:S(2)}) collective-permute-start(f32[64,128]{1,0:T(8,128)S(1)} %pad_maximum_fusion.2), channel_id=1, source_target_pairs={{0,24},{8,16},{16,8},{24,0},{1,25},{9,17},{17,9},{25,1},{2,26},{10... | collective-permute-start | bytes 98312 | tf_op jit(solution)/shard_map/ppermute | solution.py:207

commit v21 on v20

--- a/solution.py
+++ b/solution.py
@@ -195,9 +195,7 @@
         parts = [part for offset in offsets for part in payloads[offset]]
         if previous is not None:
             previous, parts = lax.optimization_barrier((previous, parts))
-        flat = jnp.concatenate([jnp.pad(part.reshape(-1), (0, -part.size % 1024)) for part in parts])
-        length = flat.shape[0]
-        rows = jnp.pad(flat, (0, -length % 128)).reshape(-1, 128)
+        rows = jnp.concatenate([as_rows(part) for part in parts])
         previous = rows
         if any(key):
             pairs = []
@@ -205,16 +203,22 @@
                 target = tuple((c + k) % s for c, k, s in zip(source, key, sizes))
                 pairs.append((int(np.ravel_multi_index(source, sizes)), int(np.ravel_multi_index(target, sizes))))
             rows = lax.ppermute(rows, tuple(axes), pairs)
-        flat = rows.reshape(-1)
         start = 0
         for offset in offsets:
             parts = []
             for part in payloads[offset]:
-                size = int(np.prod(part.shape))
-                parts.append(flat[start : start + size].reshape(part.shape))
-                start += size + (-size % 1024)
+                count = -(-part.size // 128)
+                parts.append(rows[start : start + count].reshape(-1)[: part.size].reshape(part.shape))
+                start += count
             arrived[offset] = parts
     return arrived
+
+
+def as_rows(part):
+    if part.shape[-1] == 128:
+        return part.reshape(-1, 128)
+    flat = part.reshape(-1)
+    return jnp.pad(flat, (0, -flat.shape[0] % 128)).reshape(-1, 128)
 
 
 def placed(block, starts, shape):

time: 35.1 us -> 33 us (0.940)
  local copies, waits for them, and re-layouts: 8.58 us -> 6.81 us
    slice x6 -> x2, local copies, waits for them, and re-layouts: 1.82 us -> 0.03 us  [exchange(): rows[start:start + count].reshape(-1)[:part.size].reshape(part.shape)]
    reshape x10 -> x18, local copies, waits for them, and re-layouts: 1.24 us -> 1.11 us  [the longest x6 0.62 us: as_rows(): flat = part.reshape(-1)]
  transfers between devices with their start and end apart: 5 -> 5, of which waited for: 2 -> 2; matrix products, arithmetic and copies ran while one was open for 8% -> 9% of each run, Pallas kernels for 0% -> 0%
where the time goes in v21:
time: 33 us; the launch traced here: 32.8 us
  starting transfers between devices  8.31 us (25%)
  local copies, waits for them, and re-layouts  6.81 us (21%)
  waiting for transfers between devices  6.79 us (21%)
  other arithmetic  5.24 us (16%)
  matrix products  4.87 us (15%)
  between operations  0.74 us (2%)
    ppermute x3, waiting for transfers between devices, exchange(): rows = lax.ppermute(rows, tuple(axes), pairs)  6.51 us
    ppermute x2, starting transfers between devices, shifted(): lax.ppermute(block, axis, [(i, (i + step) % count) for i in range(count)])  4.61 us
    ppermute x3, starting transfers between devices, exchange(): rows = lax.ppermute(rows, tuple(axes), pairs)  3.7 us
    unnamed x27, local copies, waits for them, and re-layouts  2.14 us
    dot_general x3, matrix products, planar_part(): jnp.dot(jnp.asarray(plane_map, jnp.float32), signed, precision=lax.Precis...  1.97 us
    mul x1, other arithmetic, plane_round_and_stencil(): return 0.25 * result  1.63 us
    dot_general x3, matrix products, body(): lax.dot_general(arrived[comp], place, (((0,), (0,)), ((), ())), precision...  1.28 us
    dot_general x3, matrix products, body(): jnp.dot(planar, jnp.asarray(depth.T, jnp.float32), precision=lax.Precisio...  1.1 us
  transfers between devices with their start and end apart: 5, of which 2 were waited for; matrix products, arithmetic and copies ran while one was open for 9% of the time, Pallas kernels for 0%

profile of v21, /device:TPU:0, one launch (start us, length us, event | category | flops | bytes accessed | tf_op | source)
XLA Modules:
  0.0 32.8 jit_solution(820821035027127321)
XLA Ops:
  0.0 1.0 %subtract_convert_fusion = f32[8,32,128]{2,1,0:T(8,128)S(1)} fusion(s32[8,32,128]{2,1,0:T(8,128)} %param.19), kind=kLoop, calls=%fused_computation.36 | loop fusion | flops 65536 | bytes 262144 | tf_op jit(solution)/shard_map/convert_element_type | solution.py:304
  1.2 0.1 copy.61
  1.6 0.7 %convert_bitcast_fusion.2 = (f32[2,8,32]{2,1,0:T(8,128)S(1)}, f32[2,8,32]{2,1,0:T(8,128)S(1)}, f32[2,8,32]{2,1,0:T(8,128)S(1)}) fusion(s32[3,2,8,32]{3,2,1,0:T(8,128)} %param.18), kind=kLoop, calls=%fused_computation.91 | loop fusion | flops 4608 | bytes 12288 | tf_op jit(solution)/shard_map/convert_element_type | solution.py:44
  2.4 0.1 broadcast_in_dim.12
  2.5 0.2 mul.135
  2.7 0.1 copy.56
  3.0 0.1 broadcast_in_dim.13
  3.1 0.2 mul.139
  3.3 0.4 %copy-done.6 = f32[2,5,8,4,160]{4,3,2,1,0:T(4,128)S(1)} copy-done((f32[2,5,8,4,160]{4,3,2,1,0:T(4,128)S(1)}, f32[2,5,8,4,160]{4,3,2,1,0:T(4,128)}, u32[]{:S(2)}) %copy-start.6) | copy-done | bytes 204824
  3.9 0.8 %fusion.36 = f32[160,324]{1,0:T(8,128)S(1)} fusion(f32[320,160]{1,0:T(8,128)S(1)} %reshape.110, f32[324,320]{1,0:T(8,128)S(1)} %copy-done.4), kind=kOutput, calls=%fused_computation.98 | convolution fusion | flops 99532800 | bytes 826880 | tf_op jit(solution)/shard_map/dot_general | solution.py:48
  4.7 0.2 convolution_bitcast_fusion.2
  4.9 0.8 %fusion.38 = f32[160,324]{1,0:T(8,128)S(1)} fusion(f32[320,160]{1,0:T(8,128)S(1)} %reshape.111, f32[324,320]{1,0:T(8,128)S(1)} %copy-done.3), kind=kOutput, calls=%fused_computation.100 | convolution fusion | flops 99532800 | bytes 826880 | tf_op jit(solution)/shard_map/dot_general | solution.py:48
  5.7 0.2 convolution_bitcast_fusion.1
  6.2 0.4 %fusion.40 = f32[128,324]{0,1:T(8,128)S(1)} fusion(f32[400,128]{1,0:T(8,128)S(1)} %reshape.112, f32[324,400]{1,0:T(8,128)S(1)} %copy-done.1), kind=kOutput, calls=%fused_computation.102 | convolution fusion | flops 99532800 | bytes 889088 | tf_op jit(solution)/shard_map/dot_general | solution.py:48
  6.6 0.2 convolution_bitcast_fusion
  6.9 0.5 %collective-permute-start = (f32[12,324]{1,0:T(8,128)S(1)}, f32[12,324]{1,0:T(8,128)S(1)}, u32[]{:S(2)}, u32[]{:S(2)}) collective-permute-start(f32[12,324]{1,0:T(8,128)S(1)} %reshape.113), channel_id=1, source_target_pairs={{0,1},{1,2},{2,3},{3,4},{4,5},{5,6},{6,7},{7,0},{8,9},{9,10},{10,1... | collective-permute-start | bytes 46664 | tf_op jit(solution)/shard_map/ppermute | solution.py:59
  7.4 4.1 %collective-permute-start.1 = (f32[8,324]{1,0:T(8,128)S(1)}, f32[8,324]{1,0:T(8,128)S(1)}, u32[]{:S(2)}, u32[]{:S(2)}) collective-permute-start(f32[8,324]{1,0:T(8,128)S(1)} %reshape.115), channel_id=1, source_target_pairs={{0,7},{1,0},{2,1},{3,2},{4,3},{5,4},{6,5},{7,6},{8,15},{9,8},{10,9... | collective-permute-start | bytes 31112 | tf_op jit(solution)/shard_map/ppermute | solution.py:59
  11.5 0.4 %fusion.37 = f32[324,132]{0,1:T(8,128)S(1)} fusion(f32[160,324]{1,0:T(8,128)S(1)} %fusion.36, f32[160,132]{1,0:T(8,128)S(1)} %copy-done.2), kind=kOutput, calls=%fused_computation.99 | convolution fusion | flops 41057280 | bytes 462912 | tf_op jit(solution)/shard_map/dot_general | solution.py:319
  11.9 0.4 %fusion.39 = f32[324,132]{0,1:T(8,128)S(1)} fusion(f32[160,324]{1,0:T(8,128)S(1)} %fusion.38, f32[160,132]{1,0:T(8,128)S(1)} %copy-done.2), kind=kOutput, calls=%fused_computation.101 | convolution fusion | flops 41057280 | bytes 462912 | tf_op jit(solution)/shard_map/dot_general | solution.py:319
  12.3 0.3 fusion.41
  12.7 0.3 collective-permute-done.1
  13.0 0.4 %convolution_add_fusion.2 = f32[324,132]{0,1:T(8,128)S(1)} fusion(f32[324,132]{0,1:T(8,128)S(1)} %fusion.37, f32[5,132]{1,0:T(8,128)S(1)} %copy-done.9, f32[4,3,324]{2,1,0:T(4,128)S(1)} %reshape.114, f32[4,2,324]{2,1,0:T(2,128)S(1)} %reshape.116), kind=kOutput, calls=%fused_computation.5 | convolution fusion | flops 2610468 | bytes 370704 | tf_op jit(solution)/shard_map/dot_general | solution.py:332
  13.4 0.1 copy.62
  13.6 0.8 %constant_dynamic-update-slice_fusion.2 = f32[3,9,36,132]{3,2,1,0:T(8,128)} fusion(f32[1,9,36,132]{3,2,1,0:T(8,128)S(1)} %stack_reshape.13), kind=kLoop, calls=%fused_computation.83 | loop fusion | bytes 539712
  14.4 0.4 %convolution_add_fusion.1 = f32[324,132]{0,1:T(8,128)S(1)} fusion(f32[324,132]{0,1:T(8,128)S(1)} %fusion.39, f32[5,132]{1,0:T(8,128)S(1)} %copy-done.9, f32[4,3,324]{2,1,0:T(4,128)S(1)} %reshape.114, f32[4,2,324]{2,1,0:T(2,128)S(1)} %reshape.116), kind=kOutput, calls=%fused_computation.4 | convolution fusion | flops 2610468 | bytes 370704 | tf_op jit(solution)/shard_map/dot_general | solution.py:332
  14.8 0.1 copy.63
  15.0 0.4 %convolution_add_fusion = f32[324,132]{0,1:T(8,128)S(1)} fusion(f32[324,132]{0,1:T(8,128)S(1)} %fusion.41, f32[5,132]{1,0:T(8,128)S(1)} %copy-done.9, f32[4,3,324]{2,1,0:T(4,128)S(1)} %reshape.114, f32[4,2,324]{2,1,0:T(2,128)S(1)} %reshape.116), kind=kOutput, calls=%fused_computation.3 | convolution fusion | flops 2610468 | bytes 370704 | tf_op jit(solution)/shard_map/dot_general | solution.py:332
  15.5 0.1 copy.64
  15.7 0.2 copy.65
  16.0 0.2 add_bitcast_fusion
  16.3 0.1 pad_maximum_fusion
  16.4 0.1 fusion.33
  16.7 0.8 %copy-done = f32[3,9,36,132]{3,2,1,0:T(8,128)S(1)} copy-done((f32[3,9,36,132]{3,2,1,0:T(8,128)S(1)}, f32[3,9,36,132]{3,2,1,0:T(8,128)}, u32[]{:S(2)}) %copy-start) | copy-done | bytes 513240
  17.7 0.1 reshape.118
  17.9 2.0 %collective-permute-start.2 = (f32[615,128]{1,0:T(8,128)S(1)}, f32[615,128]{1,0:T(8,128)S(1)}, u32[]{:S(2)}, u32[]{:S(2)}) collective-permute-start(f32[615,128]{1,0:T(8,128)S(1)} %pad_maximum_fusion.1), channel_id=1, source_target_pairs={{0,16},{8,24},{16,0},{24,8},{1,17},{9,25},{17,1},{25,9},{2,18},{10... | collective-permute-start | bytes 944648 | tf_op jit(solution)/shard_map/ppermute | solution.py:205
  19.9 0.1 reshape.123
  20.1 0.1 reshape.125
  20.3 1.6 %collective-permute-start.3 = (f32[178,128]{1,0:T(8,128)S(1)}, f32[178,128]{1,0:T(8,128)S(1)}, u32[]{:S(2)}, u32[]{:S(2)}) collective-permute-start(f32[178,128]{1,0:T(8,128)S(1)} %pad_maximum_fusion.2), channel_id=1, source_target_pairs={{0,8},{8,0},{16,24},{24,16},{1,9},{9,1},{17,25},{25,17},{2,10},{10... | collective-permute-start | bytes 273416 | tf_op jit(solution)/shard_map/ppermute | solution.py:205
  22.4 0.4 %fusion.10 = f32[3,7,31,128]{3,2,1,0:T(8,128)S(1)} fusion(f32[3,7,31,132]{3,2,1,0:T(8,128)S(1)} %slice_multiply_fusion.1), kind=kLoop, calls=%fused_computation.27 | loop fusion | flops 583296 | bytes 1999872 | tf_op jit(solution)/shard_map/add | solution.py:277
  22.8 6.5 %collective-permute-done.4 = f32[40,128]{1,0:T(8,128)S(1)} collective-permute-done((f32[40,128]{1,0:T(8,128)S(1)}, f32[40,128]{1,0:T(8,128)S(1)}, u32[]{:S(2)}, u32[]{:S(2)}) %collective-permute-start.4) | collective-permute-done | bytes 20512 | tf_op jit(solution)/shard_map/ppermute | solution.py:205
  29.7 0.2 reshape.127
  29.9 0.2 reshape_reshape.11
  30.1 0.1 reshape.122
  30.3 0.4 %pad_add_fusion = f32[4,12,36,132]{3,2,1,0:T(8,128)S(1)} fusion(f32[4,1,2,132]{3,2,1,0:T(2,128)S(1)} %bitcast.117, f32[4,2,1,132]{3,2,1,0:T(1,128)S(1)} %broadcast_in_dim_reshape.20, f32[4,1,2,132]{3,2,1,0:T(2,128)S(1)} %bitcast.116, f32[4,3,1,132]{3,2,1,0:T(1,128)S(1)} %broadcast_in_dim_reshape.19, f32[4,8,2,132]{3,2,1,0:T(2,128)S(1)} %reshape_reshape.11, ...), kind=kLoop, calls=%fused_computation | loop fusion | flops 2052864 | bytes 2020912 | tf_op jit(solution)/shard_map/add | solution.py:249
  30.7 0.1 slice_multiply_fusion
  30.8 0.1 fusion.14
  31.0 0.2 fusion.27
  31.1 1.6 %fusion.2 = f32[3,8,32,128]{3,2,1,0:T(8,128)} fusion(f32[3,12,36,132]{3,2,1,0:T(8,128)S(1)} %slice_multiply_fusion, f32[3,7,31,128]{3,2,1,0:T(8,128)S(1)} %fusion.10, f32[3,7,1,128]{3,2,1,0:T(1,128)S(1)} %fusion.27, f32[3,1,32,128]{3,2,1,0:T(8,128)S(1)} %fusion.14), kind=kLoop, calls=%fused_computation.14 | loop fusion | flops 1474560 | bytes 3932160 | tf_op jit(solution)/shard_map/mul | solution.py:268
  (91 shorter events, 2.8 us)
Async XLA Ops:
  0.0 2.7 %copy-start.5 = (f32[2,4,8,5,160]{4,2,3,1,0:T(8,128)S(1)}, f32[2,4,8,5,160]{4,2,3,1,0:T(8,128)}, u32[]{:S(2)}) copy-start(f32[2,4,8,5,160]{4,2,3,1,0:T(8,128)} %param.15) | copy-start | bytes 614404
  2.7 1.0 %copy-start.6 = (f32[2,5,8,4,160]{4,3,2,1,0:T(4,128)S(1)}, f32[2,5,8,4,160]{4,3,2,1,0:T(4,128)}, u32[]{:S(2)}) copy-start(f32[2,5,8,4,160]{4,3,2,1,0:T(4,128)} %param.16) | copy-start | bytes 614404
  2.9 1.1 %copy-start.4 = (f32[324,320]{1,0:T(8,128)S(1)}, f32[324,320]{1,0:T(8,128)}, u32[]{:S(2)}) copy-start(f32[324,320]{1,0:T(8,128)} %constant.22.clone) | copy-start | bytes 1244164
  2.9 1.7 %copy-start.10 = (f32[5,160]{1,0:T(8,128)S(1)}, f32[5,160]{1,0:T(8,128)}, u32[]{:S(2)}) copy-start(f32[5,160]{1,0:T(8,128)} %constant.23.clone) | copy-start | bytes 9604
  3.1 1.8 %copy-start.3 = (f32[324,320]{1,0:T(8,128)S(1)}, f32[324,320]{1,0:T(8,128)}, u32[]{:S(2)}) copy-start(f32[324,320]{1,0:T(8,128)} %constant.24.clone) | copy-start | bytes 1244164
  3.9 2.1 %copy-start.7 = (f32[2,5,8,5,128]{4,2,3,1,0:T(8,128)S(1)}, f32[2,5,8,5,128]{4,2,3,1,0:T(8,128)}, u32[]{:S(2)}) copy-start(f32[2,5,8,5,128]{4,2,3,1,0:T(8,128)} %param.17) | copy-start | bytes 614404
  4.9 1.3 %copy-start.1 = (f32[324,400]{1,0:T(8,128)S(1)}, f32[324,400]{1,0:T(8,128)}, u32[]{:S(2)}) copy-start(f32[324,400]{1,0:T(8,128)} %constant.9.clone) | copy-start | bytes 1555204
  5.8 0.8 %copy-start.11 = (f32[5,128]{1,0:T(8,128)S(1)}, f32[5,128]{1,0:T(8,128)}, u32[]{:S(2)}) copy-start(f32[5,128]{1,0:T(8,128)} %constant.10.clone) | copy-start | bytes 7684
  6.0 5.5 %copy-start.2 = (f32[160,132]{1,0:T(8,128)S(1)}, f32[160,132]{1,0:T(8,128)}, u32[]{:S(2)}) copy-start(f32[160,132]{1,0:T(8,128)} %constant.11.clone) | copy-start | bytes 253444
  6.2 6.1 %copy-start.8 = (f32[128,132]{1,0:T(8,128)S(1)}, f32[128,132]{1,0:T(8,128)}, u32[]{:S(2)}) copy-start(f32[128,132]{1,0:T(8,128)} %constant.12.clone) | copy-start | bytes 202756
  6.2 6.8 %copy-start.9 = (f32[5,132]{1,0:T(8,128)S(1)}, f32[5,132]{1,0:T(8,128)}, u32[]{:S(2)}) copy-start(f32[5,132]{1,0:T(8,128)} %constant.13.clone) | copy-start | bytes 7924
  6.9 6.1 %collective-permute-start = (f32[12,324]{1,0:T(8,128)S(1)}, f32[12,324]{1,0:T(8,128)S(1)}, u32[]{:S(2)}, u32[]{:S(2)}) collective-permute-start(f32[12,324]{1,0:T(8,128)S(1)} %reshape.113), channel_id=1, source_target_pairs={{0,1},{1,2},{2,3},{3,4},{4,5},{5,6},{6,7},{7,0},{8,9},{9,10},{10,1... | collective-permute-start | bytes 46664 | tf_op jit(solution)/shard_map/ppermute | solution.py:59
  7.4 5.5 %collective-permute-start.1 = (f32[8,324]{1,0:T(8,128)S(1)}, f32[8,324]{1,0:T(8,128)S(1)}, u32[]{:S(2)}, u32[]{:S(2)}) collective-permute-start(f32[8,324]{1,0:T(8,128)S(1)} %reshape.115), channel_id=1, source_target_pairs={{0,7},{1,0},{2,1},{3,2},{4,3},{5,4},{6,5},{7,6},{8,15},{9,8},{10,9... | collective-permute-start | bytes 31112 | tf_op jit(solution)/shard_map/ppermute | solution.py:59
  16.3 1.2 %copy-start = (f32[3,9,36,132]{3,2,1,0:T(8,128)S(1)}, f32[3,9,36,132]{3,2,1,0:T(8,128)}, u32[]{:S(2)}) copy-start(f32[3,9,36,132]{3,2,1,0:T(8,128)} %constant_dynamic-update-slice_fusion.2) | copy-start | bytes 1539652
  17.9 12.2 %collective-permute-start.2 = (f32[615,128]{1,0:T(8,128)S(1)}, f32[615,128]{1,0:T(8,128)S(1)}, u32[]{:S(2)}, u32[]{:S(2)}) collective-permute-start(f32[615,128]{1,0:T(8,128)S(1)} %pad_maximum_fusion.1), channel_id=1, source_target_pairs={{0,16},{8,24},{16,0},{24,8},{1,17},{9,25},{17,1},{25,9},{2,18},{10... | collective-permute-start | bytes 944648 | tf_op jit(solution)/shard_map/ppermute | solution.py:205
  20.3 9.4 %collective-permute-start.3 = (f32[178,128]{1,0:T(8,128)S(1)}, f32[178,128]{1,0:T(8,128)S(1)}, u32[]{:S(2)}, u32[]{:S(2)}) collective-permute-start(f32[178,128]{1,0:T(8,128)S(1)} %pad_maximum_fusion.2), channel_id=1, source_target_pairs={{0,8},{8,0},{16,24},{24,16},{1,9},{9,1},{17,25},{25,17},{2,10},{10... | collective-permute-start | bytes 273416 | tf_op jit(solution)/shard_map/ppermute | solution.py:205
  22.3 7.0 %collective-permute-start.4 = (f32[40,128]{1,0:T(8,128)S(1)}, f32[40,128]{1,0:T(8,128)S(1)}, u32[]{:S(2)}, u32[]{:S(2)}) collective-permute-start(f32[40,128]{1,0:T(8,128)S(1)} %pad_maximum_fusion.4), channel_id=1, source_target_pairs={{0,24},{8,16},{16,8},{24,0},{1,25},{9,17},{17,9},{25,1},{2,26},{10... | collective-permute-start | bytes 61448 | tf_op jit(solution)/shard_map/ppermute | solution.py:205

commit v22 on v21

--- a/solution.py
+++ b/solution.py
@@ -228,7 +228,13 @@
 def plane_round_and_stencil(extended, nx, ny):
     e = extended
     payloads = {
-        (1, 0): (e[:, nx - 2 : nx, 2 : ny + 2, 2:-2], e[:-1, nx : nx + 1, 2 : ny + 3]),
+        (1, 0): (
+            e[:, nx - 2 : nx, 2 : ny + 2, 2:-2],
+            e[:-1, nx : nx + 1, 2 : ny + 2, 2:-2],
+            e[:-1, nx, ny + 2],
+            e[:-1, nx : nx + 1, 2 : ny + 2, 0:2],
+            e[:-1, nx : nx + 1, 2 : ny + 2, -2:],
+        ),
         (-1, 0): (e[:, 0:2, 2 : ny + 2, 2:-2],),
         (0, 1): (e[:, :, ny : ny + 3],),
         (0, -1): (e[:, 0:nx, 2:4],),
@@ -243,12 +249,15 @@
     def at(block, layer, row, col=0):
         return placed(block, (0, layer, row, col), shape)
 
-    halo_x, fold_x = got[(1, 0)]
+    halo_x, fold_own, fold_row, fold_low, fold_high = got[(1, 0)]
     corner_x, corner_y = got[(1, 1)]
     total = (
         at(e, 2, 0)
         + at(halo_x, 0, 2, 2)
-        + at(fold_x, 2, 2)
+        + at(fold_own, 2, 2, 2)
+        + at(fold_row[:, None, None], 2, ny + 2)
+        + at(fold_low, 2, 2)
+        + at(fold_high, 2, 2, depth - 2)
         + at(got[(-1, 0)][0], nx + 2, 2, 2)
         + at(got[(0, 1)][0], 2, 0)
         + at(got[(0, -1)][0], 2, ny + 2)

time: 33 us -> 39.1 us (1.18)
  local copies, waits for them, and re-layouts: 6.81 us -> 10.6 us
  other arithmetic: 5.24 us -> 7.45 us
    slice x2 -> x4, local copies, waits for them, and re-layouts: 0.15 us -> 2.82 us  [the longest x1 0.98 us: plane_round_and_stencil(): e[:-1, nx:nx + 1, 2:ny + 2, 2:-2]]
    mul x1, other arithmetic: 0.11 us -> 1.27 us  [plane_round_and_stencil(): inner = z_terms(e[:-1, 1:nx, 3:ny + 2] * e[-1, 1:nx, 3:ny + 2])]
    add x1, other arithmetic: 0.36 us -> 1.44 us  [plane_round_and_stencil(): at(e, 2, 0) + at(halo_x, 0, 2, 2) + at(fold_own, 2, 2, 2)]
    another operation x4, local copies, waits for them, and re-layouts: 0.13 us -> 0.88 us  [body(): extended = jnp.stack(nodal + [keep])]
    unnamed x27 -> x25, local copies, waits for them, and re-layouts: 2.14 us -> 2.04 us
  transfers between devices with their start and end apart: 5 -> 5, of which waited for: 2 -> 2; matrix products, arithmetic and copies ran while one was open for 9% -> 8% of each run, Pallas kernels for 0% -> 0%
where the time goes in v22:
time: 39.1 us; the launch traced here: 38.8 us
  local copies, waits for them, and re-layouts  10.6 us (27%)
  starting transfers between devices  8.3 us (21%)
  other arithmetic  7.45 us (19%)
  waiting for transfers between devices  6.78 us (17%)
  matrix products  4.88 us (12%)
  between operations  0.74 us (2%)
    ppermute x3, waiting for transfers between devices, exchange(): rows = lax.ppermute(rows, tuple(axes), pairs)  6.5 us
    ppermute x2, starting transfers between devices, shifted(): lax.ppermute(block, axis, [(i, (i + step) % count) for i in range(count)])  4.61 us
    ppermute x3, starting transfers between devices, exchange(): rows = lax.ppermute(rows, tuple(axes), pairs)  3.68 us
    unnamed x25, local copies, waits for them, and re-layouts  2.04 us
    dot_general x3, matrix products, planar_part(): jnp.dot(jnp.asarray(plane_map, jnp.float32), signed, precision=lax.Precis...  1.97 us
    mul x1, other arithmetic, plane_round_and_stencil(): return 0.25 * result  1.63 us
    add x1, other arithmetic, plane_round_and_stencil(): at(e, 2, 0) + at(halo_x, 0, 2, 2) + at(fold_own, 2, 2, 2)  1.44 us
    dot_general x3, matrix products, body(): lax.dot_general(arrived[comp], place, (((0,), (0,)), ((), ())), precision...  1.28 us
  transfers between devices with their start and end apart: 5, of which 2 were waited for; matrix products, arithmetic and copies ran while one was open for 8% of the time, Pallas kernels for 0%

profile of v22, /device:TPU:0, one launch (start us, length us, event | category | flops | bytes accessed | tf_op | source)
XLA Modules:
  0.0 38.8 jit_solution(475081462472550413)
XLA Ops:
  0.0 1.0 %subtract_convert_fusion = f32[8,32,128]{2,1,0:T(8,128)S(1)} fusion(s32[8,32,128]{2,1,0:T(8,128)} %param.19), kind=kLoop, calls=%fused_computation.35 | loop fusion | flops 65536 | bytes 262144 | tf_op jit(solution)/shard_map/convert_element_type | solution.py:313
  1.6 0.7 %convert_bitcast_fusion.2 = (f32[2,8,32]{2,1,0:T(8,128)S(1)}, f32[2,8,32]{2,1,0:T(8,128)S(1)}, f32[2,8,32]{2,1,0:T(8,128)S(1)}) fusion(s32[3,2,8,32]{3,2,1,0:T(8,128)} %param.18), kind=kLoop, calls=%fused_computation.88 | loop fusion | flops 4608 | bytes 12288 | tf_op jit(solution)/shard_map/convert_element_type | solution.py:44
  2.5 0.2 mul.135
  2.7 0.1 copy.43
  3.1 0.2 mul.139
  3.3 0.4 copy-done.5
  3.9 0.8 %fusion.38 = f32[160,324]{1,0:T(8,128)S(1)} fusion(f32[320,160]{1,0:T(8,128)S(1)} %reshape.127, f32[324,320]{1,0:T(8,128)S(1)} %copy-done.3), kind=kOutput, calls=%fused_computation.102 | convolution fusion | flops 99532800 | bytes 826880 | tf_op jit(solution)/shard_map/dot_general | solution.py:48
  4.7 0.2 convolution_bitcast_fusion.2
  4.9 0.8 %fusion.40 = f32[160,324]{1,0:T(8,128)S(1)} fusion(f32[320,160]{1,0:T(8,128)S(1)} %reshape.128, f32[324,320]{1,0:T(8,128)S(1)} %copy-done.2), kind=kOutput, calls=%fused_computation.104 | convolution fusion | flops 99532800 | bytes 826880 | tf_op jit(solution)/shard_map/dot_general | solution.py:48
  5.7 0.2 convolution_bitcast_fusion.1
  6.2 0.4 %fusion.42 = f32[128,324]{0,1:T(8,128)S(1)} fusion(f32[400,128]{1,0:T(8,128)S(1)} %reshape.129, f32[324,400]{1,0:T(8,128)S(1)} %copy-done), kind=kOutput, calls=%fused_computation.106 | convolution fusion | flops 99532800 | bytes 889088 | tf_op jit(solution)/shard_map/dot_general | solution.py:48
  6.6 0.2 convolution_bitcast_fusion
  6.9 0.5 %collective-permute-start = (f32[12,324]{1,0:T(8,128)S(1)}, f32[12,324]{1,0:T(8,128)S(1)}, u32[]{:S(2)}, u32[]{:S(2)}) collective-permute-start(f32[12,324]{1,0:T(8,128)S(1)} %reshape.130), channel_id=1, source_target_pairs={{0,1},{1,2},{2,3},{3,4},{4,5},{5,6},{6,7},{7,0},{8,9},{9,10},{10,1... | collective-permute-start | bytes 46664 | tf_op jit(solution)/shard_map/ppermute | solution.py:59
  7.4 4.1 %collective-permute-start.1 = (f32[8,324]{1,0:T(8,128)S(1)}, f32[8,324]{1,0:T(8,128)S(1)}, u32[]{:S(2)}, u32[]{:S(2)}) collective-permute-start(f32[8,324]{1,0:T(8,128)S(1)} %reshape.132), channel_id=1, source_target_pairs={{0,7},{1,0},{2,1},{3,2},{4,3},{5,4},{6,5},{7,6},{8,15},{9,8},{10,9... | collective-permute-start | bytes 31112 | tf_op jit(solution)/shard_map/ppermute | solution.py:59
  11.5 0.4 fusion.39
  11.9 0.4 %fusion.41 = f32[324,132]{0,1:T(8,128)S(1)} fusion(f32[160,324]{1,0:T(8,128)S(1)} %fusion.40, f32[160,132]{1,0:T(8,128)S(1)} %copy-done.1), kind=kOutput, calls=%fused_computation.105 | convolution fusion | flops 41057280 | bytes 462912 | tf_op jit(solution)/shard_map/dot_general | solution.py:328
  12.3 0.3 fusion.43
  12.7 0.3 collective-permute-done.1
  13.0 0.4 %convolution_add_fusion.2 = f32[324,132]{0,1:T(8,128)S(1)} fusion(f32[324,132]{0,1:T(8,128)S(1)} %fusion.39, f32[5,132]{1,0:T(8,128)S(1)} %copy-done.8, f32[4,3,324]{2,1,0:T(4,128)S(1)} %reshape.131, f32[4,2,324]{2,1,0:T(2,128)S(1)} %reshape.133), kind=kOutput, calls=%fused_computation.5 | convolution fusion | flops 2610468 | bytes 370704 | tf_op jit(solution)/shard_map/dot_general | solution.py:341
  13.4 0.1 copy.49
  13.6 0.8 %constant_dynamic-update-slice_fusion.2 = f32[3,9,36,132]{3,2,1,0:T(8,128)} fusion(f32[1,9,36,132]{3,2,1,0:T(8,128)S(1)} %stack_reshape.13), kind=kLoop, calls=%fused_computation.80 | loop fusion | bytes 539712
  14.4 0.4 %convolution_add_fusion.1 = f32[324,132]{0,1:T(8,128)S(1)} fusion(f32[324,132]{0,1:T(8,128)S(1)} %fusion.41, f32[5,132]{1,0:T(8,128)S(1)} %copy-done.8, f32[4,3,324]{2,1,0:T(4,128)S(1)} %reshape.131, f32[4,2,324]{2,1,0:T(2,128)S(1)} %reshape.133), kind=kOutput, calls=%fused_computation.4 | convolution fusion | flops 2610468 | bytes 370704 | tf_op jit(solution)/shard_map/dot_general | solution.py:341
  14.8 0.1 copy.50
  15.0 0.4 %convolution_add_fusion = f32[324,132]{0,1:T(8,128)S(1)} fusion(f32[324,132]{0,1:T(8,128)S(1)} %fusion.43, f32[5,132]{1,0:T(8,128)S(1)} %copy-done.8, f32[4,3,324]{2,1,0:T(4,128)S(1)} %reshape.131, f32[4,2,324]{2,1,0:T(2,128)S(1)} %reshape.133), kind=kOutput, calls=%fused_computation.3 | convolution fusion | flops 2610468 | bytes 370704 | tf_op jit(solution)/shard_map/dot_general | solution.py:341
  15.5 0.1 copy.51
  15.8 0.2 copy.52
  16.0 0.2 add_bitcast_fusion
  16.3 0.8 %constant_dynamic-update-slice_fusion.1 = f32[3,9,36,132]{3,2,1,0:T(8,128)} fusion(f32[3,9,36,132]{3,2,1,0:T(8,128)} %constant_dynamic-update-slice_fusion.2, f32[1,9,36,132]{3,2,1,0:T(8,128)S(1)} %stack_reshape.14), kind=kLoop, calls=%fused_computation.79 | loop fusion | bytes 539712
  17.0 0.1 pad_maximum_fusion
  17.2 0.8 %constant_dynamic-update-slice_fusion = f32[3,9,36,132]{3,2,1,0:T(8,128)} fusion(f32[3,9,36,132]{3,2,1,0:T(8,128)} %constant_dynamic-update-slice_fusion.1, f32[1,9,36,132]{3,2,1,0:T(8,128)S(1)} %stack_reshape.15), kind=kLoop, calls=%fused_computation.78 | loop fusion | bytes 539712 | tf_op jit(solution)/shard_map/stack | solution.py:347
  17.9 0.9 %fusion.34 = (f32[3,1,32,2]{3,2,1,0:T(8,128)S(1)}, f32[3,1,32,2]{3,2,1,0:T(8,128)S(1)}) fusion(f32[3,9,36,132]{3,2,1,0:T(8,128)} %constant_dynamic-update-slice_fusion), kind=kLoop, calls=%fused_computation.98 | loop fusion | bytes 3072 | tf_op jit(solution)/shard_map/slice | solution.py:236
  18.9 1.0 %slice.325 = f32[3,1,32,128]{3,2,1,0:T(8,128)S(1)} slice(f32[3,9,36,132]{3,2,1,0:T(8,128)} %constant_dynamic-update-slice_fusion), slice={[0:3], [8:9], [2:34], [2:130]} | slice | bytes 98304 | tf_op jit(solution)/shard_map/slice | solution.py:233
  19.9 0.8 %slice_reduce_fusion = f32[3,132]{1,0:T(4,128)S(1)} fusion(f32[3,9,36,132]{3,2,1,0:T(8,128)} %constant_dynamic-update-slice_fusion), kind=kLoop, calls=%fused_computation.89 | loop fusion | bytes 3168 | tf_op jit(solution)/shard_map/slice | solution.py:234
  20.9 1.3 %slice_multiply_fusion.1 = f32[3,7,31,132]{3,2,1,0:T(8,128)S(1)} fusion(f32[3,9,36,132]{3,2,1,0:T(8,128)} %constant_dynamic-update-slice_fusion, f32[7,31,132]{2,1,0:T(8,128)S(1)} %slice_bitcast_fusion.1), kind=kLoop, calls=%fused_computation.9 | loop fusion | flops 85932 | bytes 802032 | tf_op jit(solution)/shard_map/mul | solution.py:270
  22.2 0.1 reshape.137
  22.3 0.1 reshape.139
  22.6 2.0 %collective-permute-start.2 = (f32[616,128]{1,0:T(8,128)S(1)}, f32[616,128]{1,0:T(8,128)S(1)}, u32[]{:S(2)}, u32[]{:S(2)}) collective-permute-start(f32[616,128]{1,0:T(8,128)S(1)} %concatenate.28), channel_id=1, source_target_pairs={{0,16},{8,24},{16,0},{24,8},{1,17},{9,25},{17,1},{25,9},{2,18},{10... | collective-permute-start | bytes 946184 | tf_op jit(solution)/shard_map/ppermute | solution.py:205
  24.6 0.1 reshape.143
  24.8 0.1 reshape.145
  24.9 1.6 %collective-permute-start.3 = (f32[178,128]{1,0:T(8,128)S(1)}, f32[178,128]{1,0:T(8,128)S(1)}, u32[]{:S(2)}, u32[]{:S(2)}) collective-permute-start(f32[178,128]{1,0:T(8,128)S(1)} %pad_maximum_fusion.1), channel_id=1, source_target_pairs={{0,8},{8,0},{16,24},{24,16},{1,9},{9,1},{17,25},{25,17},{2,10},{10... | collective-permute-start | bytes 273416 | tf_op jit(solution)/shard_map/ppermute | solution.py:205
  27.1 0.4 %fusion.10 = f32[3,7,31,128]{3,2,1,0:T(8,128)S(1)} fusion(f32[3,7,31,132]{3,2,1,0:T(8,128)S(1)} %slice_multiply_fusion.1), kind=kLoop, calls=%fused_computation.27 | loop fusion | flops 583296 | bytes 1999872 | tf_op jit(solution)/shard_map/add | solution.py:286
  27.5 6.5 %collective-permute-done.4 = f32[40,128]{1,0:T(8,128)S(1)} collective-permute-done((f32[40,128]{1,0:T(8,128)S(1)}, f32[40,128]{1,0:T(8,128)S(1)}, u32[]{:S(2)}, u32[]{:S(2)}) %collective-permute-start.4) | collective-permute-done | bytes 20512 | tf_op jit(solution)/shard_map/ppermute | solution.py:205
  34.4 0.2 reshape.147
  34.6 0.2 reshape_reshape.15
  34.8 0.1 slice.263
  35.2 1.4 %pad_add_fusion = f32[4,12,36,132]{3,2,1,0:T(8,128)S(1)} fusion(f32[4,1,2,132]{3,2,1,0:T(2,128)S(1)} %bitcast.130, f32[4,2,1,132]{3,2,1,0:T(1,128)S(1)} %broadcast_in_dim_reshape.25, f32[4,1,2,132]{3,2,1,0:T(2,128)S(1)} %bitcast.129, f32[4,3,1,132]{3,2,1,0:T(1,128)S(1)} %broadcast_in_dim_reshape.24, f32[4,8,2,132]{3,2,1,0:T(2,128)S(1)} %reshape_reshape.15, ...), kind=kLoop, calls=%fused_computation | loop fusion | flops 2737152 | bytes 2020912 | tf_op jit(solution)/shard_map/add | solution.py:255
  37.0 0.2 fusion.27
  37.1 1.6 %fusion.2 = f32[3,8,32,128]{3,2,1,0:T(8,128)} fusion(f32[3,12,36,132]{3,2,1,0:T(8,128)S(1)} %slice_multiply_fusion, f32[3,7,31,128]{3,2,1,0:T(8,128)S(1)} %fusion.10, f32[3,7,1,128]{3,2,1,0:T(1,128)S(1)} %fusion.27, f32[3,1,32,128]{3,2,1,0:T(8,128)S(1)} %fusion.14), kind=kLoop, calls=%fused_computation.14 | loop fusion | flops 1474560 | bytes 3932160 | tf_op jit(solution)/shard_map/mul | solution.py:277
  (101 shorter events, 3.7 us)
Async XLA Ops:
  0.0 2.7 %copy-start.4 = (f32[2,4,8,5,160]{4,2,3,1,0:T(8,128)S(1)}, f32[2,4,8,5,160]{4,2,3,1,0:T(8,128)}, u32[]{:S(2)}) copy-start(f32[2,4,8,5,160]{4,2,3,1,0:T(8,128)} %param.15) | copy-start | bytes 614404
  2.7 1.0 %copy-start.5 = (f32[2,5,8,4,160]{4,3,2,1,0:T(4,128)S(1)}, f32[2,5,8,4,160]{4,3,2,1,0:T(4,128)}, u32[]{:S(2)}) copy-start(f32[2,5,8,4,160]{4,3,2,1,0:T(4,128)} %param.16) | copy-start | bytes 614404
  2.9 1.1 %copy-start.3 = (f32[324,320]{1,0:T(8,128)S(1)}, f32[324,320]{1,0:T(8,128)}, u32[]{:S(2)}) copy-start(f32[324,320]{1,0:T(8,128)} %constant.22.clone) | copy-start | bytes 1244164
  2.9 1.7 %copy-start.9 = (f32[5,160]{1,0:T(8,128)S(1)}, f32[5,160]{1,0:T(8,128)}, u32[]{:S(2)}) copy-start(f32[5,160]{1,0:T(8,128)} %constant.23.clone) | copy-start | bytes 9604
  3.1 1.8 %copy-start.2 = (f32[324,320]{1,0:T(8,128)S(1)}, f32[324,320]{1,0:T(8,128)}, u32[]{:S(2)}) copy-start(f32[324,320]{1,0:T(8,128)} %constant.24.clone) | copy-start | bytes 1244164
  3.9 2.1 %copy-start.6 = (f32[2,5,8,5,128]{4,2,3,1,0:T(8,128)S(1)}, f32[2,5,8,5,128]{4,2,3,1,0:T(8,128)}, u32[]{:S(2)}) copy-start(f32[2,5,8,5,128]{4,2,3,1,0:T(8,128)} %param.17) | copy-start | bytes 614404
  4.9 1.3 %copy-start = (f32[324,400]{1,0:T(8,128)S(1)}, f32[324,400]{1,0:T(8,128)}, u32[]{:S(2)}) copy-start(f32[324,400]{1,0:T(8,128)} %constant.9.clone) | copy-start | bytes 1555204
  5.8 0.8 %copy-start.10 = (f32[5,128]{1,0:T(8,128)S(1)}, f32[5,128]{1,0:T(8,128)}, u32[]{:S(2)}) copy-start(f32[5,128]{1,0:T(8,128)} %constant.10.clone) | copy-start | bytes 7684
  6.0 5.5 %copy-start.1 = (f32[160,132]{1,0:T(8,128)S(1)}, f32[160,132]{1,0:T(8,128)}, u32[]{:S(2)}) copy-start(f32[160,132]{1,0:T(8,128)} %constant.11.clone) | copy-start | bytes 253444
  6.2 6.1 %copy-start.7 = (f32[128,132]{1,0:T(8,128)S(1)}, f32[128,132]{1,0:T(8,128)}, u32[]{:S(2)}) copy-start(f32[128,132]{1,0:T(8,128)} %constant.12.clone) | copy-start | bytes 202756
  6.2 6.8 %copy-start.8 = (f32[5,132]{1,0:T(8,128)S(1)}, f32[5,132]{1,0:T(8,128)}, u32[]{:S(2)}) copy-start(f32[5,132]{1,0:T(8,128)} %constant.13.clone) | copy-start | bytes 7924
  6.9 6.1 %collective-permute-start = (f32[12,324]{1,0:T(8,128)S(1)}, f32[12,324]{1,0:T(8,128)S(1)}, u32[]{:S(2)}, u32[]{:S(2)}) collective-permute-start(f32[12,324]{1,0:T(8,128)S(1)} %reshape.130), channel_id=1, source_target_pairs={{0,1},{1,2},{2,3},{3,4},{4,5},{5,6},{6,7},{7,0},{8,9},{9,10},{10,1... | collective-permute-start | bytes 46664 | tf_op jit(solution)/shard_map/ppermute | solution.py:59
  7.4 5.5 %collective-permute-start.1 = (f32[8,324]{1,0:T(8,128)S(1)}, f32[8,324]{1,0:T(8,128)S(1)}, u32[]{:S(2)}, u32[]{:S(2)}) collective-permute-start(f32[8,324]{1,0:T(8,128)S(1)} %reshape.132), channel_id=1, source_target_pairs={{0,7},{1,0},{2,1},{3,2},{4,3},{5,4},{6,5},{7,6},{8,15},{9,8},{10,9... | collective-permute-start | bytes 31112 | tf_op jit(solution)/shard_map/ppermute | solution.py:59
  22.6 12.2 %collective-permute-start.2 = (f32[616,128]{1,0:T(8,128)S(1)}, f32[616,128]{1,0:T(8,128)S(1)}, u32[]{:S(2)}, u32[]{:S(2)}) collective-permute-start(f32[616,128]{1,0:T(8,128)S(1)} %concatenate.28), channel_id=1, source_target_pairs={{0,16},{8,24},{16,0},{24,8},{1,17},{9,25},{17,1},{25,9},{2,18},{10... | collective-permute-start | bytes 946184 | tf_op jit(solution)/shard_map/ppermute | solution.py:205
  24.9 9.5 %collective-permute-start.3 = (f32[178,128]{1,0:T(8,128)S(1)}, f32[178,128]{1,0:T(8,128)S(1)}, u32[]{:S(2)}, u32[]{:S(2)}) collective-permute-start(f32[178,128]{1,0:T(8,128)S(1)} %pad_maximum_fusion.1), channel_id=1, source_target_pairs={{0,8},{8,0},{16,24},{24,16},{1,9},{9,1},{17,25},{25,17},{2,10},{10... | collective-permute-start | bytes 273416 | tf_op jit(solution)/shard_map/ppermute | solution.py:205
  27.0 7.0 %collective-permute-start.4 = (f32[40,128]{1,0:T(8,128)S(1)}, f32[40,128]{1,0:T(8,128)S(1)}, u32[]{:S(2)}, u32[]{:S(2)}) collective-permute-start(f32[40,128]{1,0:T(8,128)S(1)} %pad_maximum_fusion.3), channel_id=1, source_target_pairs={{0,24},{8,16},{16,8},{24,0},{1,25},{9,17},{17,9},{25,1},{2,26},{10... | collective-permute-start | bytes 61448 | tf_op jit(solution)/shard_map/ppermute | solution.py:205

commit v23 on v21

--- a/solution.py
+++ b/solution.py
@@ -329,7 +329,7 @@
     place = jnp.asarray(place, jnp.float32)
     nodal = []
     for comp in range(3):
-        folded = lax.dot_general(arrived[comp], place, (((0,), (0,)), ((), ())), precision=precise)
+        folded = lax.dot_general(arrived[comp], place, (((0,), (0,)), ((), ())), precision=lax.Precision.HIGH)
         nodal.append((own_parts[comp] + folded).reshape(nx + 1, ny + 4, length))
     keep_in = jnp.moveaxis(arrived[3].reshape(5, nx + 1, ny + 4), 0, 2)
     keep = keep + jnp.pad(keep_in[..., :3], ((0, 0), (0, 0), (0, length - 3))) + jnp.pad(

time: 33 us -> 32.7 us (level)
  matrix products: 4.87 us -> 4.54 us
    dot_general x3, matrix products: 1.28 us -> 0.95 us  [body(): lax.dot_general(arrived[comp], place, (((0,), (0,)), ((), ())), precision...]
where the time goes in v23:
time: 32.7 us; the launch traced here: 32.4 us
  starting transfers between devices  8.31 us (25%)
  local copies, waits for them, and re-layouts  6.81 us (21%)
  waiting for transfers between devices  6.79 us (21%)
  other arithmetic  5.24 us (16%)
  matrix products  4.54 us (14%)
  between operations  0.74 us (2%)
    ppermute x3, waiting for transfers between devices, exchange(): rows = lax.ppermute(rows, tuple(axes), pairs)  6.51 us
    ppermute x2, starting transfers between devices, shifted(): lax.ppermute(block, axis, [(i, (i + step) % count) for i in range(count)])  4.61 us
    ppermute x3, starting transfers between devices, exchange(): rows = lax.ppermute(rows, tuple(axes), pairs)  3.7 us
    unnamed x27, local copies, waits for them, and re-layouts  2.14 us
    dot_general x3, matrix products, planar_part(): jnp.dot(jnp.asarray(plane_map, jnp.float32), signed, precision=lax.Precis...  1.97 us
    mul x1, other arithmetic, plane_round_and_stencil(): return 0.25 * result  1.63 us
    dot_general x3, matrix products, body(): jnp.dot(planar, jnp.asarray(depth.T, jnp.float32), precision=lax.Precisio...  1.1 us
    convert_element_type x1, other arithmetic, body(): keep_own = (1 - flags).astype(jnp.float32)  0.96 us
  transfers between devices with their start and end apart: 5, of which 2 were waited for; matrix products, arithmetic and copies ran while one was open for 9% of the time, Pallas kernels for 0%

profile of v23, /device:TPU:0, one launch (start us, length us, event | category | flops | bytes accessed | tf_op | source)
XLA Modules:
  0.0 32.4 jit_solution(13626510825705858673)
XLA Ops:
  0.0 1.0 %subtract_convert_fusion = f32[8,32,128]{2,1,0:T(8,128)S(1)} fusion(s32[8,32,128]{2,1,0:T(8,128)} %param.19), kind=kLoop, calls=%fused_computation.36 | loop fusion | flops 65536 | bytes 262144 | tf_op jit(solution)/shard_map/convert_element_type | solution.py:304
  1.2 0.1 copy.61
  1.6 0.7 %convert_bitcast_fusion.2 = (f32[2,8,32]{2,1,0:T(8,128)S(1)}, f32[2,8,32]{2,1,0:T(8,128)S(1)}, f32[2,8,32]{2,1,0:T(8,128)S(1)}) fusion(s32[3,2,8,32]{3,2,1,0:T(8,128)} %param.18), kind=kLoop, calls=%fused_computation.91 | loop fusion | flops 4608 | bytes 12288 | tf_op jit(solution)/shard_map/convert_element_type | solution.py:44
  2.4 0.1 broadcast_in_dim.12
  2.5 0.2 mul.135
  2.7 0.1 copy.56
  3.0 0.1 broadcast_in_dim.13
  3.1 0.2 mul.139
  3.3 0.4 %copy-done.6 = f32[2,5,8,4,160]{4,3,2,1,0:T(4,128)S(1)} copy-done((f32[2,5,8,4,160]{4,3,2,1,0:T(4,128)S(1)}, f32[2,5,8,4,160]{4,3,2,1,0:T(4,128)}, u32[]{:S(2)}) %copy-start.6) | copy-done | bytes 204824
  3.9 0.8 %fusion.36 = f32[160,324]{1,0:T(8,128)S(1)} fusion(f32[320,160]{1,0:T(8,128)S(1)} %reshape.110, f32[324,320]{1,0:T(8,128)S(1)} %copy-done.4), kind=kOutput, calls=%fused_computation.98 | convolution fusion | flops 99532800 | bytes 826880 | tf_op jit(solution)/shard_map/dot_general | solution.py:48
  4.7 0.2 convolution_bitcast_fusion.2
  4.9 0.8 %fusion.38 = f32[160,324]{1,0:T(8,128)S(1)} fusion(f32[320,160]{1,0:T(8,128)S(1)} %reshape.111, f32[324,320]{1,0:T(8,128)S(1)} %copy-done.3), kind=kOutput, calls=%fused_computation.100 | convolution fusion | flops 99532800 | bytes 826880 | tf_op jit(solution)/shard_map/dot_general | solution.py:48
  5.7 0.2 convolution_bitcast_fusion.1
  6.2 0.4 %fusion.40 = f32[128,324]{0,1:T(8,128)S(1)} fusion(f32[400,128]{1,0:T(8,128)S(1)} %reshape.112, f32[324,400]{1,0:T(8,128)S(1)} %copy-done.1), kind=kOutput, calls=%fused_computation.102 | convolution fusion | flops 99532800 | bytes 889088 | tf_op jit(solution)/shard_map/dot_general | solution.py:48
  6.6 0.2 convolution_bitcast_fusion
  6.9 0.5 %collective-permute-start = (f32[12,324]{1,0:T(8,128)S(1)}, f32[12,324]{1,0:T(8,128)S(1)}, u32[]{:S(2)}, u32[]{:S(2)}) collective-permute-start(f32[12,324]{1,0:T(8,128)S(1)} %reshape.113), channel_id=1, source_target_pairs={{0,1},{1,2},{2,3},{3,4},{4,5},{5,6},{6,7},{7,0},{8,9},{9,10},{10,1... | collective-permute-start | bytes 46664 | tf_op jit(solution)/shard_map/ppermute | solution.py:59
  7.4 4.1 %collective-permute-start.1 = (f32[8,324]{1,0:T(8,128)S(1)}, f32[8,324]{1,0:T(8,128)S(1)}, u32[]{:S(2)}, u32[]{:S(2)}) collective-permute-start(f32[8,324]{1,0:T(8,128)S(1)} %reshape.115), channel_id=1, source_target_pairs={{0,7},{1,0},{2,1},{3,2},{4,3},{5,4},{6,5},{7,6},{8,15},{9,8},{10,9... | collective-permute-start | bytes 31112 | tf_op jit(solution)/shard_map/ppermute | solution.py:59
  11.5 0.4 %fusion.37 = f32[324,132]{0,1:T(8,128)S(1)} fusion(f32[160,324]{1,0:T(8,128)S(1)} %fusion.36, f32[160,132]{1,0:T(8,128)S(1)} %copy-done.2), kind=kOutput, calls=%fused_computation.99 | convolution fusion | flops 41057280 | bytes 462912 | tf_op jit(solution)/shard_map/dot_general | solution.py:319
  11.9 0.4 %fusion.39 = f32[324,132]{0,1:T(8,128)S(1)} fusion(f32[160,324]{1,0:T(8,128)S(1)} %fusion.38, f32[160,132]{1,0:T(8,128)S(1)} %copy-done.2), kind=kOutput, calls=%fused_computation.101 | convolution fusion | flops 41057280 | bytes 462912 | tf_op jit(solution)/shard_map/dot_general | solution.py:319
  12.3 0.3 fusion.41
  12.7 0.3 collective-permute-done.1
  13.0 0.3 convolution_add_fusion.2
  13.3 0.1 copy.62
  13.5 0.8 %constant_dynamic-update-slice_fusion.2 = f32[3,9,36,132]{3,2,1,0:T(8,128)} fusion(f32[1,9,36,132]{3,2,1,0:T(8,128)S(1)} %stack_reshape.13), kind=kLoop, calls=%fused_computation.83 | loop fusion | bytes 539712
  14.3 0.3 convolution_add_fusion.1
  14.6 0.1 copy.63
  14.8 0.3 convolution_add_fusion
  15.1 0.1 copy.64
  15.4 0.2 copy.65
  15.7 0.2 add_bitcast_fusion
  15.9 0.1 pad_maximum_fusion
  16.1 0.1 fusion.33
  16.3 0.8 %copy-done = f32[3,9,36,132]{3,2,1,0:T(8,128)S(1)} copy-done((f32[3,9,36,132]{3,2,1,0:T(8,128)S(1)}, f32[3,9,36,132]{3,2,1,0:T(8,128)}, u32[]{:S(2)}) %copy-start) | copy-done | bytes 513240
  17.4 0.1 reshape.118
  17.6 2.0 %collective-permute-start.2 = (f32[615,128]{1,0:T(8,128)S(1)}, f32[615,128]{1,0:T(8,128)S(1)}, u32[]{:S(2)}, u32[]{:S(2)}) collective-permute-start(f32[615,128]{1,0:T(8,128)S(1)} %pad_maximum_fusion.1), channel_id=1, source_target_pairs={{0,16},{8,24},{16,0},{24,8},{1,17},{9,25},{17,1},{25,9},{2,18},{10... | collective-permute-start | bytes 944648 | tf_op jit(solution)/shard_map/ppermute | solution.py:205
  19.6 0.1 reshape.123
  19.8 0.1 reshape.125
  19.9 1.6 %collective-permute-start.3 = (f32[178,128]{1,0:T(8,128)S(1)}, f32[178,128]{1,0:T(8,128)S(1)}, u32[]{:S(2)}, u32[]{:S(2)}) collective-permute-start(f32[178,128]{1,0:T(8,128)S(1)} %pad_maximum_fusion.2), channel_id=1, source_target_pairs={{0,8},{8,0},{16,24},{24,16},{1,9},{9,1},{17,25},{25,17},{2,10},{10... | collective-permute-start | bytes 273416 | tf_op jit(solution)/shard_map/ppermute | solution.py:205
  22.1 0.4 %fusion.10 = f32[3,7,31,128]{3,2,1,0:T(8,128)S(1)} fusion(f32[3,7,31,132]{3,2,1,0:T(8,128)S(1)} %slice_multiply_fusion.1), kind=kLoop, calls=%fused_computation.27 | loop fusion | flops 583296 | bytes 1999872 | tf_op jit(solution)/shard_map/add | solution.py:277
  22.5 6.5 %collective-permute-done.4 = f32[40,128]{1,0:T(8,128)S(1)} collective-permute-done((f32[40,128]{1,0:T(8,128)S(1)}, f32[40,128]{1,0:T(8,128)S(1)}, u32[]{:S(2)}, u32[]{:S(2)}) %collective-permute-start.4) | collective-permute-done | bytes 20512 | tf_op jit(solution)/shard_map/ppermute | solution.py:205
  29.4 0.2 reshape.127
  29.6 0.2 reshape_reshape.11
  29.8 0.1 reshape.122
  30.0 0.4 %pad_add_fusion = f32[4,12,36,132]{3,2,1,0:T(8,128)S(1)} fusion(f32[4,1,2,132]{3,2,1,0:T(2,128)S(1)} %bitcast.117, f32[4,2,1,132]{3,2,1,0:T(1,128)S(1)} %broadcast_in_dim_reshape.20, f32[4,1,2,132]{3,2,1,0:T(2,128)S(1)} %bitcast.116, f32[4,3,1,132]{3,2,1,0:T(1,128)S(1)} %broadcast_in_dim_reshape.19, f32[4,8,2,132]{3,2,1,0:T(2,128)S(1)} %reshape_reshape.11, ...), kind=kLoop, calls=%fused_computation | loop fusion | flops 2052864 | bytes 2020912 | tf_op jit(solution)/shard_map/add | solution.py:249
  30.4 0.1 slice_multiply_fusion
  30.5 0.1 fusion.14
  30.6 0.2 fusion.27
  30.8 1.6 %fusion.2 = f32[3,8,32,128]{3,2,1,0:T(8,128)} fusion(f32[3,12,36,132]{3,2,1,0:T(8,128)S(1)} %slice_multiply_fusion, f32[3,7,31,128]{3,2,1,0:T(8,128)S(1)} %fusion.10, f32[3,7,1,128]{3,2,1,0:T(1,128)S(1)} %fusion.27, f32[3,1,32,128]{3,2,1,0:T(8,128)S(1)} %fusion.14), kind=kLoop, calls=%fused_computation.14 | loop fusion | flops 1474560 | bytes 3932160 | tf_op jit(solution)/shard_map/mul | solution.py:268
  (91 shorter events, 2.8 us)
Async XLA Ops:
  0.0 2.7 %copy-start.5 = (f32[2,4,8,5,160]{4,2,3,1,0:T(8,128)S(1)}, f32[2,4,8,5,160]{4,2,3,1,0:T(8,128)}, u32[]{:S(2)}) copy-start(f32[2,4,8,5,160]{4,2,3,1,0:T(8,128)} %param.15) | copy-start | bytes 614404
  2.7 1.0 %copy-start.6 = (f32[2,5,8,4,160]{4,3,2,1,0:T(4,128)S(1)}, f32[2,5,8,4,160]{4,3,2,1,0:T(4,128)}, u32[]{:S(2)}) copy-start(f32[2,5,8,4,160]{4,3,2,1,0:T(4,128)} %param.16) | copy-start | bytes 614404
  2.9 1.1 %copy-start.4 = (f32[324,320]{1,0:T(8,128)S(1)}, f32[324,320]{1,0:T(8,128)}, u32[]{:S(2)}) copy-start(f32[324,320]{1,0:T(8,128)} %constant.22.clone) | copy-start | bytes 1244164
  2.9 1.7 %copy-start.10 = (f32[5,160]{1,0:T(8,128)S(1)}, f32[5,160]{1,0:T(8,128)}, u32[]{:S(2)}) copy-start(f32[5,160]{1,0:T(8,128)} %constant.23.clone) | copy-start | bytes 9604
  3.1 1.8 %copy-start.3 = (f32[324,320]{1,0:T(8,128)S(1)}, f32[324,320]{1,0:T(8,128)}, u32[]{:S(2)}) copy-start(f32[324,320]{1,0:T(8,128)} %constant.24.clone) | copy-start | bytes 1244164
  3.9 2.1 %copy-start.7 = (f32[2,5,8,5,128]{4,2,3,1,0:T(8,128)S(1)}, f32[2,5,8,5,128]{4,2,3,1,0:T(8,128)}, u32[]{:S(2)}) copy-start(f32[2,5,8,5,128]{4,2,3,1,0:T(8,128)} %param.17) | copy-start | bytes 614404
  4.9 1.3 %copy-start.1 = (f32[324,400]{1,0:T(8,128)S(1)}, f32[324,400]{1,0:T(8,128)}, u32[]{:S(2)}) copy-start(f32[324,400]{1,0:T(8,128)} %constant.9.clone) | copy-start | bytes 1555204
  5.8 0.8 %copy-start.11 = (f32[5,128]{1,0:T(8,128)S(1)}, f32[5,128]{1,0:T(8,128)}, u32[]{:S(2)}) copy-start(f32[5,128]{1,0:T(8,128)} %constant.10.clone) | copy-start | bytes 7684
  6.0 5.5 %copy-start.2 = (f32[160,132]{1,0:T(8,128)S(1)}, f32[160,132]{1,0:T(8,128)}, u32[]{:S(2)}) copy-start(f32[160,132]{1,0:T(8,128)} %constant.11.clone) | copy-start | bytes 253444
  6.2 6.1 %copy-start.8 = (f32[128,132]{1,0:T(8,128)S(1)}, f32[128,132]{1,0:T(8,128)}, u32[]{:S(2)}) copy-start(f32[128,132]{1,0:T(8,128)} %constant.12.clone) | copy-start | bytes 202756
  6.2 6.8 %copy-start.9 = (f32[5,132]{1,0:T(8,128)S(1)}, f32[5,132]{1,0:T(8,128)}, u32[]{:S(2)}) copy-start(f32[5,132]{1,0:T(8,128)} %constant.13.clone) | copy-start | bytes 7924
  6.9 6.1 %collective-permute-start = (f32[12,324]{1,0:T(8,128)S(1)}, f32[12,324]{1,0:T(8,128)S(1)}, u32[]{:S(2)}, u32[]{:S(2)}) collective-permute-start(f32[12,324]{1,0:T(8,128)S(1)} %reshape.113), channel_id=1, source_target_pairs={{0,1},{1,2},{2,3},{3,4},{4,5},{5,6},{6,7},{7,0},{8,9},{9,10},{10,1... | collective-permute-start | bytes 46664 | tf_op jit(solution)/shard_map/ppermute | solution.py:59
  7.4 5.5 %collective-permute-start.1 = (f32[8,324]{1,0:T(8,128)S(1)}, f32[8,324]{1,0:T(8,128)S(1)}, u32[]{:S(2)}, u32[]{:S(2)}) collective-permute-start(f32[8,324]{1,0:T(8,128)S(1)} %reshape.115), channel_id=1, source_target_pairs={{0,7},{1,0},{2,1},{3,2},{4,3},{5,4},{6,5},{7,6},{8,15},{9,8},{10,9... | collective-permute-start | bytes 31112 | tf_op jit(solution)/shard_map/ppermute | solution.py:59
  15.9 1.2 %copy-start = (f32[3,9,36,132]{3,2,1,0:T(8,128)S(1)}, f32[3,9,36,132]{3,2,1,0:T(8,128)}, u32[]{:S(2)}) copy-start(f32[3,9,36,132]{3,2,1,0:T(8,128)} %constant_dynamic-update-slice_fusion.2) | copy-start | bytes 1539652
  17.6 12.2 %collective-permute-start.2 = (f32[615,128]{1,0:T(8,128)S(1)}, f32[615,128]{1,0:T(8,128)S(1)}, u32[]{:S(2)}, u32[]{:S(2)}) collective-permute-start(f32[615,128]{1,0:T(8,128)S(1)} %pad_maximum_fusion.1), channel_id=1, source_target_pairs={{0,16},{8,24},{16,0},{24,8},{1,17},{9,25},{17,1},{25,9},{2,18},{10... | collective-permute-start | bytes 944648 | tf_op jit(solution)/shard_map/ppermute | solution.py:205
  19.9 9.5 %collective-permute-start.3 = (f32[178,128]{1,0:T(8,128)S(1)}, f32[178,128]{1,0:T(8,128)S(1)}, u32[]{:S(2)}, u32[]{:S(2)}) collective-permute-start(f32[178,128]{1,0:T(8,128)S(1)} %pad_maximum_fusion.2), channel_id=1, source_target_pairs={{0,8},{8,0},{16,24},{24,16},{1,9},{9,1},{17,25},{25,17},{2,10},{10... | collective-permute-start | bytes 273416 | tf_op jit(solution)/shard_map/ppermute | solution.py:205
  22.0 7.0 %collective-permute-start.4 = (f32[40,128]{1,0:T(8,128)S(1)}, f32[40,128]{1,0:T(8,128)S(1)}, u32[]{:S(2)}, u32[]{:S(2)}) collective-permute-start(f32[40,128]{1,0:T(8,128)S(1)} %pad_maximum_fusion.4), channel_id=1, source_target_pairs={{0,24},{8,16},{16,8},{24,0},{1,25},{9,17},{17,9},{25,1},{2,26},{10... | collective-permute-start | bytes 61448 | tf_op jit(solution)/shard_map/ppermute | solution.py:205

commit v24 on v23

--- a/solution.py
+++ b/solution.py
@@ -230,11 +230,11 @@
     payloads = {
         (1, 0): (e[:, nx - 2 : nx, 2 : ny + 2, 2:-2], e[:-1, nx : nx + 1, 2 : ny + 3]),
         (-1, 0): (e[:, 0:2, 2 : ny + 2, 2:-2],),
-        (0, 1): (e[:, :, ny : ny + 3],),
-        (0, -1): (e[:, 0:nx, 2:4],),
         (1, 1): (e[:, nx - 2 : nx + 1, ny + 2], e[:, nx, ny : ny + 2]),
         (-1, 1): (e[:, 0:2, ny + 2],),
         (1, -1): (e[:, nx, 2:4],),
+        (0, 1): (e[:, :, ny : ny + 3],),
+        (0, -1): (e[:, 0:nx, 2:4],),
     }
     got = exchange(payloads, ("gx", "gy"))
     channels, _, _, depth = e.shape

time: 32.7 us -> 33.1 us (1.012)
  waiting for transfers between devices: 6.79 us -> 7.23 us
    ppermute x3, waiting for transfers between devices: 6.51 us -> 6.95 us  [exchange(): rows = lax.ppermute(rows, tuple(axes), pairs)]
  transfers between devices with their start and end apart: 5 -> 5, of which waited for: 2 -> 2; matrix products, arithmetic and copies ran while one was open for 9% -> 8% of each run, Pallas kernels for 0% -> 0%
where the time goes in v24:
time: 33.1 us; the launch traced here: 32.9 us
  starting transfers between devices  8.32 us (25%)
  waiting for transfers between devices  7.23 us (22%)
  local copies, waits for them, and re-layouts  6.82 us (21%)
  other arithmetic  5.21 us (16%)
  matrix products  4.53 us (14%)
  between operations  0.74 us (2%)
    ppermute x3, waiting for transfers between devices, exchange(): rows = lax.ppermute(rows, tuple(axes), pairs)  6.95 us
    ppermute x2, starting transfers between devices, shifted(): lax.ppermute(block, axis, [(i, (i + step) % count) for i in range(count)])  4.61 us
    ppermute x3, starting transfers between devices, exchange(): rows = lax.ppermute(rows, tuple(axes), pairs)  3.71 us
    unnamed x27, local copies, waits for them, and re-layouts  2.15 us
    dot_general x3, matrix products, planar_part(): jnp.dot(jnp.asarray(plane_map, jnp.float32), signed, precision=lax.Precis...  1.97 us
    mul x1, other arithmetic, plane_round_and_stencil(): return 0.25 * result  1.63 us
    dot_general x3, matrix products, body(): jnp.dot(planar, jnp.asarray(depth.T, jnp.float32), precision=lax.Precisio...  1.1 us
    convert_element_type x1, other arithmetic, body(): keep_own = (1 - flags).astype(jnp.float32)  0.96 us
  transfers between devices with their start and end apart: 5, of which 2 were waited for; matrix products, arithmetic and copies ran while one was open for 8% of the time, Pallas kernels for 0%

profile of v24, /device:TPU:0, one launch (start us, length us, event | category | flops | bytes accessed | tf_op | source)
XLA Modules:
  0.0 32.9 jit_solution(3291015195335192065)
XLA Ops:
  0.0 1.0 %subtract_convert_fusion = f32[8,32,128]{2,1,0:T(8,128)S(1)} fusion(s32[8,32,128]{2,1,0:T(8,128)} %param.19), kind=kLoop, calls=%fused_computation.36 | loop fusion | flops 65536 | bytes 262144 | tf_op jit(solution)/shard_map/convert_element_type | solution.py:304
  1.2 0.1 copy.61
  1.6 0.7 %convert_bitcast_fusion.2 = (f32[2,8,32]{2,1,0:T(8,128)S(1)}, f32[2,8,32]{2,1,0:T(8,128)S(1)}, f32[2,8,32]{2,1,0:T(8,128)S(1)}) fusion(s32[3,2,8,32]{3,2,1,0:T(8,128)} %param.18), kind=kLoop, calls=%fused_computation.91 | loop fusion | flops 4608 | bytes 12288 | tf_op jit(solution)/shard_map/convert_element_type | solution.py:44
  2.4 0.1 broadcast_in_dim.12
  2.5 0.2 mul.135
  2.7 0.1 copy.56
  3.0 0.1 broadcast_in_dim.13
  3.1 0.2 mul.139
  3.3 0.4 %copy-done.6 = f32[2,5,8,4,160]{4,3,2,1,0:T(4,128)S(1)} copy-done((f32[2,5,8,4,160]{4,3,2,1,0:T(4,128)S(1)}, f32[2,5,8,4,160]{4,3,2,1,0:T(4,128)}, u32[]{:S(2)}) %copy-start.6) | copy-done | bytes 204824
  3.9 0.8 %fusion.36 = f32[160,324]{1,0:T(8,128)S(1)} fusion(f32[320,160]{1,0:T(8,128)S(1)} %reshape.110, f32[324,320]{1,0:T(8,128)S(1)} %copy-done.4), kind=kOutput, calls=%fused_computation.98 | convolution fusion | flops 99532800 | bytes 826880 | tf_op jit(solution)/shard_map/dot_general | solution.py:48
  4.7 0.2 convolution_bitcast_fusion.2
  4.9 0.8 %fusion.38 = f32[160,324]{1,0:T(8,128)S(1)} fusion(f32[320,160]{1,0:T(8,128)S(1)} %reshape.111, f32[324,320]{1,0:T(8,128)S(1)} %copy-done.3), kind=kOutput, calls=%fused_computation.100 | convolution fusion | flops 99532800 | bytes 826880 | tf_op jit(solution)/shard_map/dot_general | solution.py:48
  5.7 0.2 convolution_bitcast_fusion.1
  6.2 0.4 %fusion.40 = f32[128,324]{0,1:T(8,128)S(1)} fusion(f32[400,128]{1,0:T(8,128)S(1)} %reshape.112, f32[324,400]{1,0:T(8,128)S(1)} %copy-done.1), kind=kOutput, calls=%fused_computation.102 | convolution fusion | flops 99532800 | bytes 889088 | tf_op jit(solution)/shard_map/dot_general | solution.py:48
  6.6 0.2 convolution_bitcast_fusion
  6.9 0.5 %collective-permute-start = (f32[12,324]{1,0:T(8,128)S(1)}, f32[12,324]{1,0:T(8,128)S(1)}, u32[]{:S(2)}, u32[]{:S(2)}) collective-permute-start(f32[12,324]{1,0:T(8,128)S(1)} %reshape.113), channel_id=1, source_target_pairs={{0,1},{1,2},{2,3},{3,4},{4,5},{5,6},{6,7},{7,0},{8,9},{9,10},{10,1... | collective-permute-start | bytes 46664 | tf_op jit(solution)/shard_map/ppermute | solution.py:59
  7.4 4.1 %collective-permute-start.1 = (f32[8,324]{1,0:T(8,128)S(1)}, f32[8,324]{1,0:T(8,128)S(1)}, u32[]{:S(2)}, u32[]{:S(2)}) collective-permute-start(f32[8,324]{1,0:T(8,128)S(1)} %reshape.115), channel_id=1, source_target_pairs={{0,7},{1,0},{2,1},{3,2},{4,3},{5,4},{6,5},{7,6},{8,15},{9,8},{10,9... | collective-permute-start | bytes 31112 | tf_op jit(solution)/shard_map/ppermute | solution.py:59
  11.5 0.4 %fusion.37 = f32[324,132]{0,1:T(8,128)S(1)} fusion(f32[160,324]{1,0:T(8,128)S(1)} %fusion.36, f32[160,132]{1,0:T(8,128)S(1)} %copy-done.2), kind=kOutput, calls=%fused_computation.99 | convolution fusion | flops 41057280 | bytes 462912 | tf_op jit(solution)/shard_map/dot_general | solution.py:319
  11.9 0.4 %fusion.39 = f32[324,132]{0,1:T(8,128)S(1)} fusion(f32[160,324]{1,0:T(8,128)S(1)} %fusion.38, f32[160,132]{1,0:T(8,128)S(1)} %copy-done.2), kind=kOutput, calls=%fused_computation.101 | convolution fusion | flops 41057280 | bytes 462912 | tf_op jit(solution)/shard_map/dot_general | solution.py:319
  12.3 0.3 fusion.41
  12.7 0.3 collective-permute-done.1
  13.0 0.3 convolution_add_fusion.2
  13.3 0.1 copy.62
  13.5 0.8 %constant_dynamic-update-slice_fusion.2 = f32[3,9,36,132]{3,2,1,0:T(8,128)} fusion(f32[1,9,36,132]{3,2,1,0:T(8,128)S(1)} %stack_reshape.13), kind=kLoop, calls=%fused_computation.83 | loop fusion | bytes 539712
  14.3 0.3 convolution_add_fusion.1
  14.6 0.1 copy.63
  14.8 0.3 convolution_add_fusion
  15.1 0.1 copy.64
  15.4 0.2 copy.65
  15.7 0.2 add_bitcast_fusion
  15.9 0.1 pad_maximum_fusion
  16.1 0.1 fusion.33
  16.3 0.8 %copy-done = f32[3,9,36,132]{3,2,1,0:T(8,128)S(1)} copy-done((f32[3,9,36,132]{3,2,1,0:T(8,128)S(1)}, f32[3,9,36,132]{3,2,1,0:T(8,128)}, u32[]{:S(2)}) %copy-start) | copy-done | bytes 513240
  17.4 0.4 %fusion.10 = f32[3,7,31,128]{3,2,1,0:T(8,128)S(1)} fusion(f32[3,7,31,132]{3,2,1,0:T(8,128)S(1)} %slice_multiply_fusion.1), kind=kLoop, calls=%fused_computation.27 | loop fusion | flops 583296 | bytes 1999872 | tf_op jit(solution)/shard_map/add | solution.py:277
  17.8 0.1 reshape.118
  18.0 2.0 %collective-permute-start.2 = (f32[615,128]{1,0:T(8,128)S(1)}, f32[615,128]{1,0:T(8,128)S(1)}, u32[]{:S(2)}, u32[]{:S(2)}) collective-permute-start(f32[615,128]{1,0:T(8,128)S(1)} %pad_maximum_fusion.1), channel_id=1, source_target_pairs={{0,16},{8,24},{16,0},{24,8},{1,17},{9,25},{17,1},{25,9},{2,18},{10... | collective-permute-start | bytes 944648 | tf_op jit(solution)/shard_map/ppermute | solution.py:205
  20.5 1.6 %collective-permute-start.4 = (f32[40,128]{1,0:T(8,128)S(1)}, f32[40,128]{1,0:T(8,128)S(1)}, u32[]{:S(2)}, u32[]{:S(2)}) collective-permute-start(f32[40,128]{1,0:T(8,128)S(1)} %pad_maximum_fusion.4), channel_id=1, source_target_pairs={{0,24},{8,16},{16,8},{24,0},{1,25},{9,17},{17,9},{25,1},{2,26},{10... | collective-permute-start | bytes 61448 | tf_op jit(solution)/shard_map/ppermute | solution.py:205
  22.0 0.1 reshape.131
  22.2 0.1 reshape.133
  22.5 6.9 %collective-permute-done.4 = f32[40,128]{1,0:T(8,128)S(1)} collective-permute-done((f32[40,128]{1,0:T(8,128)S(1)}, f32[40,128]{1,0:T(8,128)S(1)}, u32[]{:S(2)}, u32[]{:S(2)}) %collective-permute-start.4) | collective-permute-done | bytes 20512 | tf_op jit(solution)/shard_map/ppermute | solution.py:205
  29.8 0.2 reshape.135
  30.0 0.2 reshape_reshape.11
  30.2 0.1 reshape.122
  30.4 0.3 %pad_add_fusion = f32[4,12,36,132]{3,2,1,0:T(8,128)S(1)} fusion(f32[4,1,2,132]{3,2,1,0:T(2,128)S(1)} %bitcast.117, f32[4,2,1,132]{3,2,1,0:T(1,128)S(1)} %broadcast_in_dim_reshape.20, f32[4,1,2,132]{3,2,1,0:T(2,128)S(1)} %bitcast.116, f32[4,3,1,132]{3,2,1,0:T(1,128)S(1)} %broadcast_in_dim_reshape.19, f32[4,8,2,132]{3,2,1,0:T(2,128)S(1)} %reshape_reshape.11, ...), kind=kLoop, calls=%fused_computation | loop fusion | flops 2052864 | bytes 2020912 | tf_op jit(solution)/shard_map/add | solution.py:249
  30.8 0.1 slice_multiply_fusion
  30.9 0.1 fusion.14
  31.1 0.2 fusion.27
  31.2 1.6 %fusion.2 = f32[3,8,32,128]{3,2,1,0:T(8,128)} fusion(f32[3,12,36,132]{3,2,1,0:T(8,128)S(1)} %slice_multiply_fusion, f32[3,7,31,128]{3,2,1,0:T(8,128)S(1)} %fusion.10, f32[3,7,1,128]{3,2,1,0:T(1,128)S(1)} %fusion.27, f32[3,1,32,128]{3,2,1,0:T(8,128)S(1)} %fusion.14), kind=kLoop, calls=%fused_computation.14 | loop fusion | flops 1474560 | bytes 3932160 | tf_op jit(solution)/shard_map/mul | solution.py:268
  (91 shorter events, 2.9 us)
Async XLA Ops:
  0.0 2.7 %copy-start.5 = (f32[2,4,8,5,160]{4,2,3,1,0:T(8,128)S(1)}, f32[2,4,8,5,160]{4,2,3,1,0:T(8,128)}, u32[]{:S(2)}) copy-start(f32[2,4,8,5,160]{4,2,3,1,0:T(8,128)} %param.15) | copy-start | bytes 614404
  2.7 1.0 %copy-start.6 = (f32[2,5,8,4,160]{4,3,2,1,0:T(4,128)S(1)}, f32[2,5,8,4,160]{4,3,2,1,0:T(4,128)}, u32[]{:S(2)}) copy-start(f32[2,5,8,4,160]{4,3,2,1,0:T(4,128)} %param.16) | copy-start | bytes 614404
  2.9 1.1 %copy-start.4 = (f32[324,320]{1,0:T(8,128)S(1)}, f32[324,320]{1,0:T(8,128)}, u32[]{:S(2)}) copy-start(f32[324,320]{1,0:T(8,128)} %constant.22.clone) | copy-start | bytes 1244164
  2.9 1.7 %copy-start.10 = (f32[5,160]{1,0:T(8,128)S(1)}, f32[5,160]{1,0:T(8,128)}, u32[]{:S(2)}) copy-start(f32[5,160]{1,0:T(8,128)} %constant.23.clone) | copy-start | bytes 9604
  3.1 1.8 %copy-start.3 = (f32[324,320]{1,0:T(8,128)S(1)}, f32[324,320]{1,0:T(8,128)}, u32[]{:S(2)}) copy-start(f32[324,320]{1,0:T(8,128)} %constant.24.clone) | copy-start | bytes 1244164
  3.9 2.1 %copy-start.7 = (f32[2,5,8,5,128]{4,2,3,1,0:T(8,128)S(1)}, f32[2,5,8,5,128]{4,2,3,1,0:T(8,128)}, u32[]{:S(2)}) copy-start(f32[2,5,8,5,128]{4,2,3,1,0:T(8,128)} %param.17) | copy-start | bytes 614404
  4.9 1.3 %copy-start.1 = (f32[324,400]{1,0:T(8,128)S(1)}, f32[324,400]{1,0:T(8,128)}, u32[]{:S(2)}) copy-start(f32[324,400]{1,0:T(8,128)} %constant.9.clone) | copy-start | bytes 1555204
  5.8 0.8 %copy-start.11 = (f32[5,128]{1,0:T(8,128)S(1)}, f32[5,128]{1,0:T(8,128)}, u32[]{:S(2)}) copy-start(f32[5,128]{1,0:T(8,128)} %constant.10.clone) | copy-start | bytes 7684
  6.0 5.5 %copy-start.2 = (f32[160,132]{1,0:T(8,128)S(1)}, f32[160,132]{1,0:T(8,128)}, u32[]{:S(2)}) copy-start(f32[160,132]{1,0:T(8,128)} %constant.11.clone) | copy-start | bytes 253444
  6.2 6.1 %copy-start.8 = (f32[128,132]{1,0:T(8,128)S(1)}, f32[128,132]{1,0:T(8,128)}, u32[]{:S(2)}) copy-start(f32[128,132]{1,0:T(8,128)} %constant.12.clone) | copy-start | bytes 202756
  6.2 6.8 %copy-start.9 = (f32[5,132]{1,0:T(8,128)S(1)}, f32[5,132]{1,0:T(8,128)}, u32[]{:S(2)}) copy-start(f32[5,132]{1,0:T(8,128)} %constant.13.clone) | copy-start | bytes 7924
  6.9 6.1 %collective-permute-start = (f32[12,324]{1,0:T(8,128)S(1)}, f32[12,324]{1,0:T(8,128)S(1)}, u32[]{:S(2)}, u32[]{:S(2)}) collective-permute-start(f32[12,324]{1,0:T(8,128)S(1)} %reshape.113), channel_id=1, source_target_pairs={{0,1},{1,2},{2,3},{3,4},{4,5},{5,6},{6,7},{7,0},{8,9},{9,10},{10,1... | collective-permute-start | bytes 46664 | tf_op jit(solution)/shard_map/ppermute | solution.py:59
  7.4 5.5 %collective-permute-start.1 = (f32[8,324]{1,0:T(8,128)S(1)}, f32[8,324]{1,0:T(8,128)S(1)}, u32[]{:S(2)}, u32[]{:S(2)}) collective-permute-start(f32[8,324]{1,0:T(8,128)S(1)} %reshape.115), channel_id=1, source_target_pairs={{0,7},{1,0},{2,1},{3,2},{4,3},{5,4},{6,5},{7,6},{8,15},{9,8},{10,9... | collective-permute-start | bytes 31112 | tf_op jit(solution)/shard_map/ppermute | solution.py:59
  15.9 1.2 %copy-start = (f32[3,9,36,132]{3,2,1,0:T(8,128)S(1)}, f32[3,9,36,132]{3,2,1,0:T(8,128)}, u32[]{:S(2)}) copy-start(f32[3,9,36,132]{3,2,1,0:T(8,128)} %constant_dynamic-update-slice_fusion.2) | copy-start | bytes 1539652
  18.0 12.2 %collective-permute-start.2 = (f32[615,128]{1,0:T(8,128)S(1)}, f32[615,128]{1,0:T(8,128)S(1)}, u32[]{:S(2)}, u32[]{:S(2)}) collective-permute-start(f32[615,128]{1,0:T(8,128)S(1)} %pad_maximum_fusion.1), channel_id=1, source_target_pairs={{0,16},{8,24},{16,0},{24,8},{1,17},{9,25},{17,1},{25,9},{2,18},{10... | collective-permute-start | bytes 944648 | tf_op jit(solution)/shard_map/ppermute | solution.py:205
  20.5 8.9 %collective-permute-start.4 = (f32[40,128]{1,0:T(8,128)S(1)}, f32[40,128]{1,0:T(8,128)S(1)}, u32[]{:S(2)}, u32[]{:S(2)}) collective-permute-start(f32[40,128]{1,0:T(8,128)S(1)} %pad_maximum_fusion.4), channel_id=1, source_target_pairs={{0,24},{8,16},{16,8},{24,0},{1,25},{9,17},{17,9},{25,1},{2,26},{10... | collective-permute-start | bytes 61448 | tf_op jit(solution)/shard_map/ppermute | solution.py:205
  22.4 7.4 %collective-permute-start.3 = (f32[178,128]{1,0:T(8,128)S(1)}, f32[178,128]{1,0:T(8,128)S(1)}, u32[]{:S(2)}, u32[]{:S(2)}) collective-permute-start(f32[178,128]{1,0:T(8,128)S(1)} %pad_maximum_fusion.2), channel_id=1, source_target_pairs={{0,8},{8,0},{16,24},{24,16},{1,9},{9,1},{17,25},{25,17},{2,10},{10... | collective-permute-start | bytes 273416 | tf_op jit(solution)/shard_map/ppermute | solution.py:205

commit v25 on v23

--- a/solution.py
+++ b/solution.py
@@ -314,12 +314,10 @@
     up = slabs[:, :3].reshape(-1, slabs.shape[2])
     down = slabs[:, 3:].reshape(-1, slabs.shape[2])
     from_prev, from_next = both_ways(up, down, "gz")
-    own_parts = lax.optimization_barrier(
-        [
-            jnp.dot(planar, jnp.asarray(depth.T, jnp.float32), precision=lax.Precision.HIGH)
-            for planar, depth in zip(planars, depths)
-        ]
-    )
+    own_parts = [
+        jnp.dot(planar, jnp.asarray(depth.T, jnp.float32), precision=lax.Precision.HIGH)
+        for planar, depth in zip(planars, depths)
+    ]
     arrived = jnp.concatenate(
         [from_prev.reshape(4, 3, -1), from_next.reshape(4, 2, -1)], axis=1
     )

time: 32.7 us -> 33.8 us (1.034)
  waiting for transfers between devices: 6.79 us -> 7.92 us
    ppermute x2, waiting for transfers between devices: 0.28 us -> 1.41 us  [shifted(): lax.ppermute(block, axis, [(i, (i + step) % count) for i in range(count)])]
  transfers between devices with their start and end apart: 5 -> 5, of which waited for: 2 -> 2; matrix products, arithmetic and copies ran while one was open for 9% -> 6% of each run, Pallas kernels for 0% -> 0%
where the time goes in v25:
time: 33.8 us; the launch traced here: 33.6 us
  starting transfers between devices  8.31 us (25%)
  waiting for transfers between devices  7.92 us (23%)
  local copies, waits for them, and re-layouts  6.81 us (20%)
  other arithmetic  5.24 us (16%)
  matrix products  4.54 us (13%)
  between operations  0.75 us (2%)
    ppermute x3, waiting for transfers between devices, exchange(): rows = lax.ppermute(rows, tuple(axes), pairs)  6.51 us
    ppermute x2, starting transfers between devices, shifted(): lax.ppermute(block, axis, [(i, (i + step) % count) for i in range(count)])  4.61 us
    ppermute x3, starting transfers between devices, exchange(): rows = lax.ppermute(rows, tuple(axes), pairs)  3.7 us
    unnamed x27, local copies, waits for them, and re-layouts  2.14 us
    dot_general x3, matrix products, planar_part(): jnp.dot(jnp.asarray(plane_map, jnp.float32), signed, precision=lax.Precis...  1.97 us
    mul x1, other arithmetic, plane_round_and_stencil(): return 0.25 * result  1.63 us
    ppermute x2, waiting for transfers between devices, shifted(): lax.ppermute(block, axis, [(i, (i + step) % count) for i in range(count)])  1.41 us
    dot_general x3, matrix products, body(): jnp.dot(planar, jnp.asarray(depth.T, jnp.float32), precision=lax.Precisio...  1.1 us
  transfers between devices with their start and end apart: 5, of which 2 were waited for; matrix products, arithmetic and copies ran while one was open for 6% of the time, Pallas kernels for 0%

profile of v25, /device:TPU:0, one launch (start us, length us, event | category | flops | bytes accessed | tf_op | source)
XLA Modules:
  0.0 33.6 jit_solution(12257845370522554563)
XLA Ops:
  0.0 1.0 %subtract_convert_fusion = f32[8,32,128]{2,1,0:T(8,128)S(1)} fusion(s32[8,32,128]{2,1,0:T(8,128)} %param.19), kind=kLoop, calls=%fused_computation.36 | loop fusion | flops 65536 | bytes 262144 | tf_op jit(solution)/shard_map/convert_element_type | solution.py:304
  1.2 0.1 copy.61
  1.6 0.7 %convert_bitcast_fusion.2 = (f32[2,8,32]{2,1,0:T(8,128)S(1)}, f32[2,8,32]{2,1,0:T(8,128)S(1)}, f32[2,8,32]{2,1,0:T(8,128)S(1)}) fusion(s32[3,2,8,32]{3,2,1,0:T(8,128)} %param.18), kind=kLoop, calls=%fused_computation.94 | loop fusion | flops 4608 | bytes 12288 | tf_op jit(solution)/shard_map/convert_element_type | solution.py:44
  2.4 0.1 broadcast_in_dim.12
  2.5 0.2 mul.135
  2.7 0.1 copy.56
  3.0 0.1 broadcast_in_dim.13
  3.1 0.2 mul.139
  3.3 0.4 %copy-done.6 = f32[2,5,8,4,160]{4,3,2,1,0:T(4,128)S(1)} copy-done((f32[2,5,8,4,160]{4,3,2,1,0:T(4,128)S(1)}, f32[2,5,8,4,160]{4,3,2,1,0:T(4,128)}, u32[]{:S(2)}) %copy-start.6) | copy-done | bytes 204824
  3.9 0.8 %fusion.39 = f32[160,324]{1,0:T(8,128)S(1)} fusion(f32[320,160]{1,0:T(8,128)S(1)} %reshape.110, f32[324,320]{1,0:T(8,128)S(1)} %copy-done.4), kind=kOutput, calls=%fused_computation.101 | convolution fusion | flops 99532800 | bytes 826880 | tf_op jit(solution)/shard_map/dot_general | solution.py:48
  4.7 0.2 convolution_bitcast_fusion.2
  4.9 0.8 %fusion.40 = f32[160,324]{1,0:T(8,128)S(1)} fusion(f32[320,160]{1,0:T(8,128)S(1)} %reshape.111, f32[324,320]{1,0:T(8,128)S(1)} %copy-done.3), kind=kOutput, calls=%fused_computation.102 | convolution fusion | flops 99532800 | bytes 826880 | tf_op jit(solution)/shard_map/dot_general | solution.py:48
  5.7 0.2 convolution_bitcast_fusion.1
  6.2 0.4 %fusion.41 = f32[128,324]{0,1:T(8,128)S(1)} fusion(f32[400,128]{1,0:T(8,128)S(1)} %reshape.112, f32[324,400]{1,0:T(8,128)S(1)} %copy-done.1), kind=kOutput, calls=%fused_computation.103 | convolution fusion | flops 99532800 | bytes 889088 | tf_op jit(solution)/shard_map/dot_general | solution.py:48
  6.6 0.2 convolution_bitcast_fusion
  6.9 0.5 %collective-permute-start = (f32[12,324]{1,0:T(8,128)S(1)}, f32[12,324]{1,0:T(8,128)S(1)}, u32[]{:S(2)}, u32[]{:S(2)}) collective-permute-start(f32[12,324]{1,0:T(8,128)S(1)} %reshape.113), channel_id=1, source_target_pairs={{0,1},{1,2},{2,3},{3,4},{4,5},{5,6},{6,7},{7,0},{8,9},{9,10},{10,1... | collective-permute-start | bytes 46664 | tf_op jit(solution)/shard_map/ppermute | solution.py:59
  7.4 4.1 %collective-permute-start.1 = (f32[8,324]{1,0:T(8,128)S(1)}, f32[8,324]{1,0:T(8,128)S(1)}, u32[]{:S(2)}, u32[]{:S(2)}) collective-permute-start(f32[8,324]{1,0:T(8,128)S(1)} %reshape.115), channel_id=1, source_target_pairs={{0,7},{1,0},{2,1},{3,2},{4,3},{5,4},{6,5},{7,6},{8,15},{9,8},{10,9... | collective-permute-start | bytes 31112 | tf_op jit(solution)/shard_map/ppermute | solution.py:59
  11.5 1.4 %collective-permute-done.1 = f32[8,324]{1,0:T(8,128)S(1)} collective-permute-done((f32[8,324]{1,0:T(8,128)S(1)}, f32[8,324]{1,0:T(8,128)S(1)}, u32[]{:S(2)}, u32[]{:S(2)}) %collective-permute-start.1) | collective-permute-done | bytes 10400 | tf_op jit(solution)/shard_map/ppermute | solution.py:59
  13.0 0.3 fusion.23
  13.3 0.3 fusion.27
  13.6 0.3 fusion.19
  14.0 0.4 %convolution_add_fusion.2 = f32[324,132]{0,1:T(8,128)S(1)} fusion(f32[324,132]{0,1:T(8,128)S(1)} %fusion.23, f32[160,324]{1,0:T(8,128)S(1)} %fusion.39, f32[160,132]{1,0:T(8,128)S(1)} %copy-done.2), kind=kOutput, calls=%fused_computation.5 | convolution fusion | flops 41100048 | bytes 633984 | tf_op jit(solution)/shard_map/dot_general | solution.py:318
  14.4 0.1 copy.62
  14.6 0.8 %constant_dynamic-update-slice_fusion.2 = f32[3,9,36,132]{3,2,1,0:T(8,128)} fusion(f32[1,9,36,132]{3,2,1,0:T(8,128)S(1)} %stack_reshape.13), kind=kLoop, calls=%fused_computation.86 | loop fusion | bytes 539712
  15.3 0.4 %convolution_add_fusion.1 = f32[324,132]{0,1:T(8,128)S(1)} fusion(f32[324,132]{0,1:T(8,128)S(1)} %fusion.27, f32[160,324]{1,0:T(8,128)S(1)} %fusion.40, f32[160,132]{1,0:T(8,128)S(1)} %copy-done.2), kind=kOutput, calls=%fused_computation.4 | convolution fusion | flops 41100048 | bytes 633984 | tf_op jit(solution)/shard_map/dot_general | solution.py:318
  15.7 0.1 copy.63
  15.9 0.3 convolution_add_fusion
  16.3 0.1 copy.64
  16.6 0.2 copy.65
  16.8 0.2 add_bitcast_fusion
  17.1 0.1 pad_maximum_fusion
  17.2 0.1 fusion.36
  17.5 0.8 %copy-done = f32[3,9,36,132]{3,2,1,0:T(8,128)S(1)} copy-done((f32[3,9,36,132]{3,2,1,0:T(8,128)S(1)}, f32[3,9,36,132]{3,2,1,0:T(8,128)}, u32[]{:S(2)}) %copy-start) | copy-done | bytes 513240
  18.5 0.1 reshape.118
  18.7 2.0 %collective-permute-start.2 = (f32[615,128]{1,0:T(8,128)S(1)}, f32[615,128]{1,0:T(8,128)S(1)}, u32[]{:S(2)}, u32[]{:S(2)}) collective-permute-start(f32[615,128]{1,0:T(8,128)S(1)} %pad_maximum_fusion.1), channel_id=1, source_target_pairs={{0,16},{8,24},{16,0},{24,8},{1,17},{9,25},{17,1},{25,9},{2,18},{10... | collective-permute-start | bytes 944648 | tf_op jit(solution)/shard_map/ppermute | solution.py:205
  20.7 0.1 reshape.123
  20.9 0.1 reshape.125
  21.1 1.6 %collective-permute-start.3 = (f32[178,128]{1,0:T(8,128)S(1)}, f32[178,128]{1,0:T(8,128)S(1)}, u32[]{:S(2)}, u32[]{:S(2)}) collective-permute-start(f32[178,128]{1,0:T(8,128)S(1)} %pad_maximum_fusion.2), channel_id=1, source_target_pairs={{0,8},{8,0},{16,24},{24,16},{1,9},{9,1},{17,25},{25,17},{2,10},{10... | collective-permute-start | bytes 273416 | tf_op jit(solution)/shard_map/ppermute | solution.py:205
  23.2 0.4 %fusion.10 = f32[3,7,31,128]{3,2,1,0:T(8,128)S(1)} fusion(f32[3,7,31,132]{3,2,1,0:T(8,128)S(1)} %slice_multiply_fusion.1), kind=kLoop, calls=%fused_computation.27 | loop fusion | flops 583296 | bytes 1999872 | tf_op jit(solution)/shard_map/add | solution.py:277
  23.6 6.5 %collective-permute-done.4 = f32[40,128]{1,0:T(8,128)S(1)} collective-permute-done((f32[40,128]{1,0:T(8,128)S(1)}, f32[40,128]{1,0:T(8,128)S(1)}, u32[]{:S(2)}, u32[]{:S(2)}) %collective-permute-start.4) | collective-permute-done | bytes 20512 | tf_op jit(solution)/shard_map/ppermute | solution.py:205
  30.5 0.2 reshape.127
  30.7 0.2 reshape_reshape.11
  30.9 0.1 reshape.122
  31.1 0.4 %pad_add_fusion = f32[4,12,36,132]{3,2,1,0:T(8,128)S(1)} fusion(f32[4,1,2,132]{3,2,1,0:T(2,128)S(1)} %bitcast.117, f32[4,2,1,132]{3,2,1,0:T(1,128)S(1)} %broadcast_in_dim_reshape.20, f32[4,1,2,132]{3,2,1,0:T(2,128)S(1)} %bitcast.116, f32[4,3,1,132]{3,2,1,0:T(1,128)S(1)} %broadcast_in_dim_reshape.19, f32[4,8,2,132]{3,2,1,0:T(2,128)S(1)} %reshape_reshape.11, ...), kind=kLoop, calls=%fused_computation | loop fusion | flops 2052864 | bytes 2020912 | tf_op jit(solution)/shard_map/add | solution.py:249
  31.5 0.1 slice_multiply_fusion
  31.6 0.1 fusion.14
  31.8 0.2 fusion.30
  31.9 1.6 %fusion.2 = f32[3,8,32,128]{3,2,1,0:T(8,128)} fusion(f32[3,12,36,132]{3,2,1,0:T(8,128)S(1)} %slice_multiply_fusion, f32[3,7,31,128]{3,2,1,0:T(8,128)S(1)} %fusion.10, f32[3,7,1,128]{3,2,1,0:T(1,128)S(1)} %fusion.30, f32[3,1,32,128]{3,2,1,0:T(8,128)S(1)} %fusion.14), kind=kLoop, calls=%fused_computation.14 | loop fusion | flops 1474560 | bytes 3932160 | tf_op jit(solution)/shard_map/mul | solution.py:268
  (91 shorter events, 2.8 us)
Async XLA Ops:
  0.0 2.7 %copy-start.5 = (f32[2,4,8,5,160]{4,2,3,1,0:T(8,128)S(1)}, f32[2,4,8,5,160]{4,2,3,1,0:T(8,128)}, u32[]{:S(2)}) copy-start(f32[2,4,8,5,160]{4,2,3,1,0:T(8,128)} %param.15) | copy-start | bytes 614404
  2.7 1.0 %copy-start.6 = (f32[2,5,8,4,160]{4,3,2,1,0:T(4,128)S(1)}, f32[2,5,8,4,160]{4,3,2,1,0:T(4,128)}, u32[]{:S(2)}) copy-start(f32[2,5,8,4,160]{4,3,2,1,0:T(4,128)} %param.16) | copy-start | bytes 614404
  2.9 1.1 %copy-start.4 = (f32[324,320]{1,0:T(8,128)S(1)}, f32[324,320]{1,0:T(8,128)}, u32[]{:S(2)}) copy-start(f32[324,320]{1,0:T(8,128)} %constant.22.clone) | copy-start | bytes 1244164
  2.9 1.7 %copy-start.10 = (f32[5,160]{1,0:T(8,128)S(1)}, f32[5,160]{1,0:T(8,128)}, u32[]{:S(2)}) copy-start(f32[5,160]{1,0:T(8,128)} %constant.23.clone) | copy-start | bytes 9604
  3.1 1.8 %copy-start.3 = (f32[324,320]{1,0:T(8,128)S(1)}, f32[324,320]{1,0:T(8,128)}, u32[]{:S(2)}) copy-start(f32[324,320]{1,0:T(8,128)} %constant.24.clone) | copy-start | bytes 1244164
  3.9 2.1 %copy-start.7 = (f32[2,5,8,5,128]{4,2,3,1,0:T(8,128)S(1)}, f32[2,5,8,5,128]{4,2,3,1,0:T(8,128)}, u32[]{:S(2)}) copy-start(f32[2,5,8,5,128]{4,2,3,1,0:T(8,128)} %param.17) | copy-start | bytes 614404
  4.9 1.3 %copy-start.1 = (f32[324,400]{1,0:T(8,128)S(1)}, f32[324,400]{1,0:T(8,128)}, u32[]{:S(2)}) copy-start(f32[324,400]{1,0:T(8,128)} %constant.9.clone) | copy-start | bytes 1555204
  5.8 0.8 %copy-start.11 = (f32[5,128]{1,0:T(8,128)S(1)}, f32[5,128]{1,0:T(8,128)}, u32[]{:S(2)}) copy-start(f32[5,128]{1,0:T(8,128)} %constant.10.clone) | copy-start | bytes 7684
  6.0 6.9 %copy-start.9 = (f32[5,132]{1,0:T(8,128)S(1)}, f32[5,132]{1,0:T(8,128)}, u32[]{:S(2)}) copy-start(f32[5,132]{1,0:T(8,128)} %constant.13.clone) | copy-start | bytes 7924
  6.1 7.8 %copy-start.2 = (f32[160,132]{1,0:T(8,128)S(1)}, f32[160,132]{1,0:T(8,128)}, u32[]{:S(2)}) copy-start(f32[160,132]{1,0:T(8,128)} %constant.11.clone) | copy-start | bytes 253444
  6.9 6.1 %collective-permute-start = (f32[12,324]{1,0:T(8,128)S(1)}, f32[12,324]{1,0:T(8,128)S(1)}, u32[]{:S(2)}, u32[]{:S(2)}) collective-permute-start(f32[12,324]{1,0:T(8,128)S(1)} %reshape.113), channel_id=1, source_target_pairs={{0,1},{1,2},{2,3},{3,4},{4,5},{5,6},{6,7},{7,0},{8,9},{9,10},{10,1... | collective-permute-start | bytes 46664 | tf_op jit(solution)/shard_map/ppermute | solution.py:59
  7.4 5.5 %collective-permute-start.1 = (f32[8,324]{1,0:T(8,128)S(1)}, f32[8,324]{1,0:T(8,128)S(1)}, u32[]{:S(2)}, u32[]{:S(2)}) collective-permute-start(f32[8,324]{1,0:T(8,128)S(1)} %reshape.115), channel_id=1, source_target_pairs={{0,7},{1,0},{2,1},{3,2},{4,3},{5,4},{6,5},{7,6},{8,15},{9,8},{10,9... | collective-permute-start | bytes 31112 | tf_op jit(solution)/shard_map/ppermute | solution.py:59
  14.6 1.4 %copy-start.8 = (f32[128,132]{1,0:T(8,128)S(1)}, f32[128,132]{1,0:T(8,128)}, u32[]{:S(2)}) copy-start(f32[128,132]{1,0:T(8,128)} %constant.12.clone) | copy-start | bytes 202756
  17.1 1.2 %copy-start = (f32[3,9,36,132]{3,2,1,0:T(8,128)S(1)}, f32[3,9,36,132]{3,2,1,0:T(8,128)}, u32[]{:S(2)}) copy-start(f32[3,9,36,132]{3,2,1,0:T(8,128)} %constant_dynamic-update-slice_fusion.2) | copy-start | bytes 1539652
  18.7 12.2 %collective-permute-start.2 = (f32[615,128]{1,0:T(8,128)S(1)}, f32[615,128]{1,0:T(8,128)S(1)}, u32[]{:S(2)}, u32[]{:S(2)}) collective-permute-start(f32[615,128]{1,0:T(8,128)S(1)} %pad_maximum_fusion.1), channel_id=1, source_target_pairs={{0,16},{8,24},{16,0},{24,8},{1,17},{9,25},{17,1},{25,9},{2,18},{10... | collective-permute-start | bytes 944648 | tf_op jit(solution)/shard_map/ppermute | solution.py:205
  21.1 9.5 %collective-permute-start.3 = (f32[178,128]{1,0:T(8,128)S(1)}, f32[178,128]{1,0:T(8,128)S(1)}, u32[]{:S(2)}, u32[]{:S(2)}) collective-permute-start(f32[178,128]{1,0:T(8,128)S(1)} %pad_maximum_fusion.2), channel_id=1, source_target_pairs={{0,8},{8,0},{16,24},{24,16},{1,9},{9,1},{17,25},{25,17},{2,10},{10... | collective-permute-start | bytes 273416 | tf_op jit(solution)/shard_map/ppermute | solution.py:205
  23.1 7.0 %collective-permute-start.4 = (f32[40,128]{1,0:T(8,128)S(1)}, f32[40,128]{1,0:T(8,128)S(1)}, u32[]{:S(2)}, u32[]{:S(2)}) collective-permute-start(f32[40,128]{1,0:T(8,128)S(1)} %pad_maximum_fusion.4), channel_id=1, source_target_pairs={{0,24},{8,16},{16,8},{24,0},{1,25},{9,17},{17,9},{25,1},{2,26},{10... | collective-permute-start | bytes 61448 | tf_op jit(solution)/shard_map/ppermute | solution.py:205

commit v26 on v23

--- a/solution.py
+++ b/solution.py
@@ -301,14 +301,12 @@
         slabs.append(
             lax.dot_general(edge_map, planar, (((1,), (1,)), ((), ())), precision=lax.Precision.HIGH)
         )
-    keep_own = (1 - flags).astype(jnp.float32)
-    keep = jnp.pad(keep_own, ((0, 1), (2, 2), (2, 2)))
     keep_layers = [
-        lax.slice_in_dim(keep_own, nz - 2, nz, axis=2),
-        jnp.zeros_like(lax.slice_in_dim(keep_own, 0, 1, axis=2)),
-        lax.slice_in_dim(keep_own, 0, 2, axis=2),
+        lax.slice_in_dim(flags, nz - 2, nz, axis=2),
+        jnp.ones_like(lax.slice_in_dim(flags, 0, 1, axis=2)),
+        lax.slice_in_dim(flags, 0, 2, axis=2),
     ]
-    keep_layers = jnp.moveaxis(jnp.concatenate(keep_layers, axis=2), 2, 0)
+    keep_layers = (1 - jnp.moveaxis(jnp.concatenate(keep_layers, axis=2), 2, 0)).astype(jnp.float32)
     slabs.append(jnp.pad(keep_layers, ((0, 0), (0, 1), (2, 2))).reshape(5, -1))
     slabs = jnp.stack(slabs)
     up = slabs[:, :3].reshape(-1, slabs.shape[2])
@@ -331,6 +329,7 @@
     for comp in range(3):
         folded = lax.dot_general(arrived[comp], place, (((0,), (0,)), ((), ())), precision=lax.Precision.HIGH)
         nodal.append((own_parts[comp] + folded).reshape(nx + 1, ny + 4, length))
+    keep = jnp.pad((1 - flags).astype(jnp.float32), ((0, 1), (2, 2), (2, 2)))
     keep_in = jnp.moveaxis(arrived[3].reshape(5, nx + 1, ny + 4), 0, 2)
     keep = keep + jnp.pad(keep_in[..., :3], ((0, 0), (0, 0), (0, length - 3))) + jnp.pad(
         keep_in[..., 3:], ((0, 0), (0, 0), (nz + 2, 0))

time: 32.7 us -> 32.7 us (level)
    mul x3, other arithmetic: 0.12 us -> 1.14 us  [planar_part(): coef * orient[:, None, :, None, :]]
    convert_element_type x1 -> x2, other arithmetic: 0.96 us -> 0.09 us  [the longest x1 0.08 us: body(): (1 - jnp.moveaxis(jnp.concatenate(keep_layers, axis=2), 2, 0)).astype(jnp...]
    unnamed x27 -> x29, local copies, waits for them, and re-layouts: 2.14 us -> 2.35 us
where the time goes in v26:
time: 32.7 us; the launch traced here: 32.4 us
  starting transfers between devices  8.3 us (25%)
  local copies, waits for them, and re-layouts  6.78 us (21%)
  waiting for transfers between devices  6.78 us (21%)
  other arithmetic  5.3 us (16%)
  matrix products  4.51 us (14%)
  between operations  0.76 us (2%)
    ppermute x3, waiting for transfers between devices, exchange(): rows = lax.ppermute(rows, tuple(axes), pairs)  6.51 us
    ppermute x2, starting transfers between devices, shifted(): lax.ppermute(block, axis, [(i, (i + step) % count) for i in range(count)])  4.61 us
    ppermute x3, starting transfers between devices, exchange(): rows = lax.ppermute(rows, tuple(axes), pairs)  3.69 us
    unnamed x29, local copies, waits for them, and re-layouts  2.35 us
    dot_general x3, matrix products, planar_part(): jnp.dot(jnp.asarray(plane_map, jnp.float32), signed, precision=lax.Precis...  1.95 us
    mul x1, other arithmetic, plane_round_and_stencil(): return 0.25 * result  1.63 us
    mul x3, other arithmetic, planar_part(): coef * orient[:, None, :, None, :]  1.14 us
    dot_general x3, matrix products, body(): jnp.dot(planar, jnp.asarray(depth.T, jnp.float32), precision=lax.Precisio...  1.09 us
  transfers between devices with their start and end apart: 5, of which 2 were waited for; matrix products, arithmetic and copies ran while one was open for 9% of the time, Pallas kernels for 0%

profile of v26, /device:TPU:0, one launch (start us, length us, event | category | flops | bytes accessed | tf_op | source)
XLA Modules:
  0.0 32.4 jit_solution(8227320658673425121)
XLA Ops:
  0.0 0.7 %convert_bitcast_fusion.2 = (f32[2,8,32]{2,1,0:T(8,128)S(1)}, f32[2,8,32]{2,1,0:T(8,128)S(1)}, f32[2,8,32]{2,1,0:T(8,128)S(1)}) fusion(s32[3,2,8,32]{3,2,1,0:T(8,128)} %param.18), kind=kLoop, calls=%fused_computation.93 | loop fusion | flops 4608 | bytes 12288 | tf_op jit(solution)/shard_map/convert_element_type | solution.py:44
  0.7 0.1 broadcast_in_dim.12
  0.9 0.2 mul.135
  1.0 1.0 %broadcast_multiply_fusion.1 = f32[2,4,8,5,160]{4,2,3,1,0:T(8,128)S(1)} fusion(f32[2,4,8,5,160]{4,2,3,1,0:T(8,128)} %param.15, f32[2,8,160]{2,1,0:T(8,128)S(1)} %mul.135), kind=kLoop, calls=%fused_computation.35 | loop fusion | flops 51200 | bytes 419840 | tf_op jit(solution)/shard_map/mul | solution.py:45
  2.1 0.1 copy.56
  2.3 0.1 broadcast_in_dim.13
  2.5 0.2 mul.139
  2.8 0.4 %copy-done.4 = f32[324,320]{1,0:T(8,128)S(1)} copy-done((f32[324,320]{1,0:T(8,128)S(1)}, f32[324,320]{1,0:T(8,128)}, u32[]{:S(2)}) %copy-start.4) | copy-done | bytes 414744
  3.3 0.8 %fusion.38 = f32[160,324]{1,0:T(8,128)S(1)} fusion(f32[320,160]{1,0:T(8,128)S(1)} %reshape.110, f32[324,320]{1,0:T(8,128)S(1)} %copy-done.4), kind=kOutput, calls=%fused_computation.100 | convolution fusion | flops 99532800 | bytes 826880 | tf_op jit(solution)/shard_map/dot_general | solution.py:48
  4.0 0.2 convolution_bitcast_fusion.2
  4.2 0.8 %fusion.40 = f32[160,324]{1,0:T(8,128)S(1)} fusion(f32[320,160]{1,0:T(8,128)S(1)} %reshape.111, f32[324,320]{1,0:T(8,128)S(1)} %copy-done.5), kind=kOutput, calls=%fused_computation.102 | convolution fusion | flops 99532800 | bytes 826880 | tf_op jit(solution)/shard_map/dot_general | solution.py:48
  5.0 0.2 convolution_bitcast_fusion.1
  5.7 0.1 copy.75
  6.2 0.4 %fusion.42 = f32[128,324]{0,1:T(8,128)S(1)} fusion(f32[400,128]{1,0:T(8,128)S(1)} %reshape.112, f32[324,400]{1,0:T(8,128)S(1)} %copy-done.2), kind=kOutput, calls=%fused_computation.104 | convolution fusion | flops 99532800 | bytes 889088 | tf_op jit(solution)/shard_map/dot_general | solution.py:48
  6.7 0.2 convolution_bitcast_fusion
  6.9 0.5 %collective-permute-start = (f32[12,324]{1,0:T(8,128)S(1)}, f32[12,324]{1,0:T(8,128)S(1)}, u32[]{:S(2)}, u32[]{:S(2)}) collective-permute-start(f32[12,324]{1,0:T(8,128)S(1)} %reshape.113), channel_id=1, source_target_pairs={{0,1},{1,2},{2,3},{3,4},{4,5},{5,6},{6,7},{7,0},{8,9},{9,10},{10,1... | collective-permute-start | bytes 46664 | tf_op jit(solution)/shard_map/ppermute | solution.py:59
  7.4 4.1 %collective-permute-start.1 = (f32[8,324]{1,0:T(8,128)S(1)}, f32[8,324]{1,0:T(8,128)S(1)}, u32[]{:S(2)}, u32[]{:S(2)}) collective-permute-start(f32[8,324]{1,0:T(8,128)S(1)} %reshape.115), channel_id=1, source_target_pairs={{0,7},{1,0},{2,1},{3,2},{4,3},{5,4},{6,5},{7,6},{8,15},{9,8},{10,9... | collective-permute-start | bytes 31112 | tf_op jit(solution)/shard_map/ppermute | solution.py:59
  11.6 0.4 %fusion.39 = f32[324,132]{0,1:T(8,128)S(1)} fusion(f32[160,324]{1,0:T(8,128)S(1)} %fusion.38, f32[160,132]{1,0:T(8,128)S(1)} %copy-done.3), kind=kOutput, calls=%fused_computation.101 | convolution fusion | flops 41057280 | bytes 462912 | tf_op jit(solution)/shard_map/dot_general | solution.py:317
  11.9 0.4 %fusion.41 = f32[324,132]{0,1:T(8,128)S(1)} fusion(f32[160,324]{1,0:T(8,128)S(1)} %fusion.40, f32[160,132]{1,0:T(8,128)S(1)} %copy-done.3), kind=kOutput, calls=%fused_computation.103 | convolution fusion | flops 41057280 | bytes 462912 | tf_op jit(solution)/shard_map/dot_general | solution.py:317
  12.3 0.3 fusion.43
  12.7 0.3 collective-permute-done.1
  13.0 0.3 convolution_add_fusion.2
  13.3 0.1 copy.62
  13.5 0.8 %constant_dynamic-update-slice_fusion.2 = f32[3,9,36,132]{3,2,1,0:T(8,128)} fusion(f32[1,9,36,132]{3,2,1,0:T(8,128)S(1)} %stack_reshape.13), kind=kLoop, calls=%fused_computation.85 | loop fusion | bytes 539712
  14.3 0.3 convolution_add_fusion.1
  14.6 0.1 copy.63
  14.8 0.3 convolution_add_fusion
  15.2 0.1 copy.64
  15.4 0.2 copy.65
  15.7 0.2 add_bitcast_fusion
  16.0 0.1 pad_maximum_fusion
  16.1 0.1 fusion.35
  16.4 0.8 %copy-done = f32[3,9,36,132]{3,2,1,0:T(8,128)S(1)} copy-done((f32[3,9,36,132]{3,2,1,0:T(8,128)S(1)}, f32[3,9,36,132]{3,2,1,0:T(8,128)}, u32[]{:S(2)}) %copy-start) | copy-done | bytes 513240
  17.4 0.1 reshape.118
  17.6 2.0 %collective-permute-start.2 = (f32[615,128]{1,0:T(8,128)S(1)}, f32[615,128]{1,0:T(8,128)S(1)}, u32[]{:S(2)}, u32[]{:S(2)}) collective-permute-start(f32[615,128]{1,0:T(8,128)S(1)} %pad_maximum_fusion.1), channel_id=1, source_target_pairs={{0,16},{8,24},{16,0},{24,8},{1,17},{9,25},{17,1},{25,9},{2,18},{10... | collective-permute-start | bytes 944648 | tf_op jit(solution)/shard_map/ppermute | solution.py:205
  19.6 0.1 reshape.123
  19.8 0.1 reshape.125
  19.9 1.6 %collective-permute-start.3 = (f32[178,128]{1,0:T(8,128)S(1)}, f32[178,128]{1,0:T(8,128)S(1)}, u32[]{:S(2)}, u32[]{:S(2)}) collective-permute-start(f32[178,128]{1,0:T(8,128)S(1)} %pad_maximum_fusion.2), channel_id=1, source_target_pairs={{0,8},{8,0},{16,24},{24,16},{1,9},{9,1},{17,25},{25,17},{2,10},{10... | collective-permute-start | bytes 273416 | tf_op jit(solution)/shard_map/ppermute | solution.py:205
  22.1 0.4 %fusion.10 = f32[3,7,31,128]{3,2,1,0:T(8,128)S(1)} fusion(f32[3,7,31,132]{3,2,1,0:T(8,128)S(1)} %slice_multiply_fusion.1), kind=kLoop, calls=%fused_computation.27 | loop fusion | flops 583296 | bytes 1999872 | tf_op jit(solution)/shard_map/add | solution.py:277
  22.5 6.5 %collective-permute-done.4 = f32[40,128]{1,0:T(8,128)S(1)} collective-permute-done((f32[40,128]{1,0:T(8,128)S(1)}, f32[40,128]{1,0:T(8,128)S(1)}, u32[]{:S(2)}, u32[]{:S(2)}) %collective-permute-start.4) | collective-permute-done | bytes 20512 | tf_op jit(solution)/shard_map/ppermute | solution.py:205
  29.4 0.2 reshape.127
  29.6 0.2 reshape_reshape.11
  29.8 0.1 reshape.122
  30.0 0.4 %pad_add_fusion = f32[4,12,36,132]{3,2,1,0:T(8,128)S(1)} fusion(f32[4,1,2,132]{3,2,1,0:T(2,128)S(1)} %bitcast.117, f32[4,2,1,132]{3,2,1,0:T(1,128)S(1)} %broadcast_in_dim_reshape.20, f32[4,1,2,132]{3,2,1,0:T(2,128)S(1)} %bitcast.116, f32[4,3,1,132]{3,2,1,0:T(1,128)S(1)} %broadcast_in_dim_reshape.19, f32[4,8,2,132]{3,2,1,0:T(2,128)S(1)} %reshape_reshape.11, ...), kind=kLoop, calls=%fused_computation | loop fusion | flops 2052864 | bytes 2020912 | tf_op jit(solution)/shard_map/add | solution.py:249
  30.4 0.1 slice_multiply_fusion
  30.5 0.1 fusion.14
  30.6 0.2 fusion.29
  30.8 1.6 %fusion.2 = f32[3,8,32,128]{3,2,1,0:T(8,128)} fusion(f32[3,12,36,132]{3,2,1,0:T(8,128)S(1)} %slice_multiply_fusion, f32[3,7,31,128]{3,2,1,0:T(8,128)S(1)} %fusion.10, f32[3,7,1,128]{3,2,1,0:T(1,128)S(1)} %fusion.29, f32[3,1,32,128]{3,2,1,0:T(8,128)S(1)} %fusion.14), kind=kLoop, calls=%fused_computation.14 | loop fusion | flops 1474560 | bytes 3932160 | tf_op jit(solution)/shard_map/mul | solution.py:268
  (91 shorter events, 2.7 us)
Async XLA Ops:
  1.0 1.6 %copy-start.6 = (f32[2,5,8,4,160]{4,3,2,1,0:T(4,128)S(1)}, f32[2,5,8,4,160]{4,3,2,1,0:T(4,128)}, u32[]{:S(2)}) copy-start(f32[2,5,8,4,160]{4,3,2,1,0:T(4,128)} %param.16) | copy-start | bytes 614404
  2.2 1.0 %copy-start.4 = (f32[324,320]{1,0:T(8,128)S(1)}, f32[324,320]{1,0:T(8,128)}, u32[]{:S(2)}) copy-start(f32[324,320]{1,0:T(8,128)} %constant.22.clone) | copy-start | bytes 1244164
  2.3 1.7 %copy-start.10 = (f32[5,160]{1,0:T(8,128)S(1)}, f32[5,160]{1,0:T(8,128)}, u32[]{:S(2)}) copy-start(f32[5,160]{1,0:T(8,128)} %constant.23.clone) | copy-start | bytes 9604
  2.5 1.8 %copy-start.5 = (f32[324,320]{1,0:T(8,128)S(1)}, f32[324,320]{1,0:T(8,128)}, u32[]{:S(2)}) copy-start(f32[324,320]{1,0:T(8,128)} %constant.24.clone) | copy-start | bytes 1244164
  3.3 2.1 %copy-start.7 = (f32[2,5,8,5,128]{4,2,3,1,0:T(8,128)S(1)}, f32[2,5,8,5,128]{4,2,3,1,0:T(8,128)}, u32[]{:S(2)}) copy-start(f32[2,5,8,5,128]{4,2,3,1,0:T(8,128)} %param.17) | copy-start | bytes 614404
  4.2 1.3 %copy-start.1 = (s32[8,32,128]{2,1,0:T(8,128)S(1)}, s32[8,32,128]{2,1,0:T(8,128)}, u32[]{:S(2)}) copy-start(s32[8,32,128]{2,1,0:T(8,128)} %param.19) | copy-start | bytes 393220
  5.0 1.2 %copy-start.2 = (f32[324,400]{1,0:T(8,128)S(1)}, f32[324,400]{1,0:T(8,128)}, u32[]{:S(2)}) copy-start(f32[324,400]{1,0:T(8,128)} %constant.25.clone) | copy-start | bytes 1555204
  5.4 1.2 %copy-start.11 = (f32[5,128]{1,0:T(8,128)S(1)}, f32[5,128]{1,0:T(8,128)}, u32[]{:S(2)}) copy-start(f32[5,128]{1,0:T(8,128)} %constant.9.clone) | copy-start | bytes 7684
  5.5 6.1 %copy-start.3 = (f32[160,132]{1,0:T(8,128)S(1)}, f32[160,132]{1,0:T(8,128)}, u32[]{:S(2)}) copy-start(f32[160,132]{1,0:T(8,128)} %constant.10.clone) | copy-start | bytes 253444
  5.9 6.5 %copy-start.8 = (f32[128,132]{1,0:T(8,128)S(1)}, f32[128,132]{1,0:T(8,128)}, u32[]{:S(2)}) copy-start(f32[128,132]{1,0:T(8,128)} %constant.11.clone) | copy-start | bytes 202756
  6.6 6.4 %copy-start.9 = (f32[5,132]{1,0:T(8,128)S(1)}, f32[5,132]{1,0:T(8,128)}, u32[]{:S(2)}) copy-start(f32[5,132]{1,0:T(8,128)} %constant.12.clone) | copy-start | bytes 7924
  6.9 6.1 %collective-permute-start = (f32[12,324]{1,0:T(8,128)S(1)}, f32[12,324]{1,0:T(8,128)S(1)}, u32[]{:S(2)}, u32[]{:S(2)}) collective-permute-start(f32[12,324]{1,0:T(8,128)S(1)} %reshape.113), channel_id=1, source_target_pairs={{0,1},{1,2},{2,3},{3,4},{4,5},{5,6},{6,7},{7,0},{8,9},{9,10},{10,1... | collective-permute-start | bytes 46664 | tf_op jit(solution)/shard_map/ppermute | solution.py:59
  7.4 5.5 %collective-permute-start.1 = (f32[8,324]{1,0:T(8,128)S(1)}, f32[8,324]{1,0:T(8,128)S(1)}, u32[]{:S(2)}, u32[]{:S(2)}) collective-permute-start(f32[8,324]{1,0:T(8,128)S(1)} %reshape.115), channel_id=1, source_target_pairs={{0,7},{1,0},{2,1},{3,2},{4,3},{5,4},{6,5},{7,6},{8,15},{9,8},{10,9... | collective-permute-start | bytes 31112 | tf_op jit(solution)/shard_map/ppermute | solution.py:59
  15.9 1.2 %copy-start = (f32[3,9,36,132]{3,2,1,0:T(8,128)S(1)}, f32[3,9,36,132]{3,2,1,0:T(8,128)}, u32[]{:S(2)}) copy-start(f32[3,9,36,132]{3,2,1,0:T(8,128)} %constant_dynamic-update-slice_fusion.2) | copy-start | bytes 1539652
  17.6 12.2 %collective-permute-start.2 = (f32[615,128]{1,0:T(8,128)S(1)}, f32[615,128]{1,0:T(8,128)S(1)}, u32[]{:S(2)}, u32[]{:S(2)}) collective-permute-start(f32[615,128]{1,0:T(8,128)S(1)} %pad_maximum_fusion.1), channel_id=1, source_target_pairs={{0,16},{8,24},{16,0},{24,8},{1,17},{9,25},{17,1},{25,9},{2,18},{10... | collective-permute-start | bytes 944648 | tf_op jit(solution)/shard_map/ppermute | solution.py:205
  19.9 9.5 %collective-permute-start.3 = (f32[178,128]{1,0:T(8,128)S(1)}, f32[178,128]{1,0:T(8,128)S(1)}, u32[]{:S(2)}, u32[]{:S(2)}) collective-permute-start(f32[178,128]{1,0:T(8,128)S(1)} %pad_maximum_fusion.2), channel_id=1, source_target_pairs={{0,8},{8,0},{16,24},{24,16},{1,9},{9,1},{17,25},{25,17},{2,10},{10... | collective-permute-start | bytes 273416 | tf_op jit(solution)/shard_map/ppermute | solution.py:205
  22.0 7.0 %collective-permute-start.4 = (f32[40,128]{1,0:T(8,128)S(1)}, f32[40,128]{1,0:T(8,128)S(1)}, u32[]{:S(2)}, u32[]{:S(2)}) collective-permute-start(f32[40,128]{1,0:T(8,128)S(1)} %pad_maximum_fusion.4), channel_id=1, source_target_pairs={{0,24},{8,16},{16,8},{24,0},{1,25},{9,17},{17,9},{25,1},{2,26},{10... | collective-permute-start | bytes 61448 | tf_op jit(solution)/shard_map/ppermute | solution.py:205
